TPU v7x, 128 devices: a whole 4x4x4 slice. The times are simulated.
128 devices in a mesh: slab: 32 (over x, y, core), pencil: 4 (over z).
Axes of the slice: x: 4, y: 4, z: 4, core: 2. Of those that a mesh axis runs over, the one named last changes fastest.
Arguments:
- cotangent: float32 [128, 512, 512], P('slab', 'pencil'), may hold values from -6 to 6
- seg_rows: int32 [32, 4], replicated, may hold values from 1 to 64, 128 in all within a row
- owners: int32 [32, 4], replicated, may hold values from 0 to 127
- offsets: int32 [32, 4], replicated, may hold values from 0 to 64
Outputs:
- rhs_grad: float32 [128, 512, 512], P('slab', 'pencil')
- parent_grad: float32 [128, 128, 128], P(('slab', 'pencil'))
Inputs may be any that keep to these rules, and one draw needn't show every extreme that they name: `seg_rows`: each tile's 4 row counts sum to 128; in every tile one segment has exactly 64 rows.
All inputs are finite; a program needn't handle non-finite values.
Results may differ from a plain program's by a relative error of at most 0.00002.
Values sent between devices are 32-bit elements; how exact they have to be, the bound alone decides.
No kernel may reach another device: no remote copies, remote signals or barrier semaphores. Data moves between devices by JAX's collectives and lax.ppermute only.
A program may use at most 192 MiB of HBM per device.

v0:
```python
import jax
import jax.numpy as jnp
from jax import lax
from jax.sharding import PartitionSpec as P

TILE = 128
PT_DEV = 1


omega_weight = 2.0 / 3.0


def with_halo(x, sides, width):
    for axis, dim in sides:
        peers, length = (lax.axis_size(axis), x.shape[dim])
        up = [(i, (i + 1) % peers) for i in range(peers - 1)]
        down = [(j, i) for i, j in up]
        last = lax.slice_in_dim(x, length - width, length, axis=dim)
        initial = lax.slice_in_dim(x, 0, width, axis=dim)
        before = lax.ppermute(last, axis, up)
        after = lax.ppermute(initial, axis, down)
        x = jnp.concatenate([before, x, after], axis=dim)
    return x


def neighbour_sum(padded):
    total = padded[2:, 1:-1, 1:-1] + padded[:-2, 1:-1, 1:-1]
    total = total + padded[1:-1, 2:, 1:-1] + padded[1:-1, :-2, 1:-1]
    total = total + padded[1:-1, 1:-1, 2:] + padded[1:-1, 1:-1, :-2]
    return total


def block_neighbours(field):
    padded = with_halo(field, (("slab", 0), ("pencil", 1)), 1)
    return neighbour_sum(jnp.pad(padded, ((0, 0), (0, 0), (1, 1))))


def coarse_neighbours(field):
    padded = with_halo(field, (("slab", 0), ("pencil", 1)), 1)
    return neighbour_sum(jnp.pad(padded, ((0, 0), (0, 0), (1, 1))))


def coefficient(level):
    return omega_weight * 4.0**level / 6.0


def smoothed(field, neighbours):
    return (1.0 - omega_weight) * field + omega_weight / 6.0 * neighbours


def pair_matrix(cells):
    rows = jnp.arange(cells, dtype=jnp.int32)[:, None] // 2
    cols = jnp.arange(cells // 2, dtype=jnp.int32)[None, :]
    return (rows == cols).astype(jnp.float32)


def children_sum(field):
    x_cells, y_cells, z_cells = field.shape
    paired = field.reshape(x_cells // 2, 2, y_cells, z_cells).sum(axis=1)
    flat = paired.reshape(x_cells // 2 * y_cells, z_cells)
    paired = jnp.dot(flat, pair_matrix(z_cells), precision=lax.Precision.HIGHEST)
    paired = paired.reshape(x_cells // 2, y_cells, z_cells // 2)
    to_rows = pair_matrix(y_cells).T
    planes = [
        jnp.dot(to_rows, paired[i], precision=lax.Precision.HIGHEST)
        for i in range(x_cells // 2)
    ]
    return jnp.stack(planes)


def prolong(field):
    return jnp.repeat(jnp.repeat(jnp.repeat(field, 2, axis=0), 2, axis=1), 2, axis=2)


def source_rows(seg_rows, owners, offsets, tile_size):
    starts = jnp.cumsum(seg_rows, axis=1) - seg_rows
    position = jnp.arange(tile_size, dtype=jnp.int32)[None, None, :]
    inside = (position >= starts[:, :, None]) & (position < (starts + seg_rows)[:, :, None])
    value = owners[:, :, None] * tile_size + offsets[:, :, None] + position - starts[:, :, None]
    return jnp.sum(jnp.where(inside, value, 0), axis=1)


def tile_rows(faces, tile_size):
    face_count, y_cells, z_cells = faces.shape
    blocks = faces.reshape(
        face_count, y_cells // tile_size, tile_size, z_cells // tile_size, tile_size
    )
    return blocks.transpose(0, 1, 3, 2, 4).reshape(-1, tile_size)


def add_rows(rows_data, targets, first_row, slot_count):
    shifted = targets - first_row
    segment_ids = jnp.where((shifted >= 0) & (shifted < slot_count), shifted, slot_count)
    summed = jax.ops.segment_sum(rows_data, segment_ids, num_segments=slot_count + 1)
    return summed[:slot_count]


def extend(x, axis, dim, width):
    peers, block = lax.axis_size(axis), x.shape[dim]
    lows, highs = [], []
    distance = 1
    while (distance - 1) * block < width:
        up = [(j, j + distance) for j in range(peers - distance)]
        down = [(j + distance, j) for j in range(peers - distance)]
        low_piece = lax.slice_in_dim(x, max(0, distance * block - width), block, axis=dim)
        high_piece = lax.slice_in_dim(x, 0, min(block, width - (distance - 1) * block), axis=dim)
        lows.insert(0, lax.ppermute(low_piece, axis, up))
        highs.append(lax.ppermute(high_piece, axis, down))
        distance += 1
    return jnp.concatenate(lows + [x] + highs, axis=dim)


def inside(axis, block, width):
    first = lax.axis_index(axis) * block - width
    place = first + jnp.arange(block + 2 * width, dtype=jnp.int32)
    return (place >= 0) & (place < lax.axis_size(axis) * block)


def masked(field, block_x, block_y, width):
    keep = inside("slab", block_x, width)[:, None, None] & inside("pencil", block_y, width)[None, :, None]
    return jnp.where(keep, field, 0.0)


def shrink_neighbours(field):
    centre = field[1:-1, 1:-1]
    total = field[2:, 1:-1] + field[:-2, 1:-1]
    total = total + field[1:-1, 2:] + field[1:-1, :-2]
    padded = jnp.pad(centre, ((0, 0), (0, 0), (1, 1)))
    total = total + padded[:, :, 2:] + padded[:, :, :-2]
    return centre, total


def core(field, width, block_x, block_y):
    return field[width:width + block_x, width:width + block_y]


def shards(cotangent, seg_rows, owners, offsets):
    x_cells, y_cells, z_cells = cotangent.shape
    tile_size = TILE
    depth = 5
    grown = extend(extend(cotangent, "slab", 0, depth), "pencil", 1, depth)
    powers = [grown]
    for width in range(depth - 1, -1, -1):
        centre, total = shrink_neighbours(powers[-1])
        powers.append(masked(smoothed(centre, total), x_cells, y_cells, width))
    rhs_grad = jnp.zeros_like(cotangent)
    for level_power in range(depth + 1):
        part = core(powers[level_power], depth - level_power, x_cells, y_cells)
        rhs_grad = rhs_grad + coefficient(0) * part
    grad_fine = core(powers[3], depth - 3, x_cells, y_cells)
    medium = children_sum(grad_fine)
    grad_medium = jnp.zeros_like(medium)
    for sweep_number in range(3):
        grad_medium = grad_medium + coefficient(1) * medium
        medium = smoothed(medium, block_neighbours(medium))
    coarse_cot = children_sum(medium)
    grad_coarse = coefficient(2) * coarse_cot
    for sweep_number in range(2):
        coarse_cot = smoothed(coarse_cot, coarse_neighbours(coarse_cot))
        grad_coarse = grad_coarse + coefficient(2) * coarse_cot
    back_medium = prolong(grad_coarse) * 0.125
    grad_medium = grad_medium + back_medium
    medium = medium - (6.0 * back_medium - block_neighbours(back_medium)) / 4.0
    for sweep_number in range(3):
        grad_medium = grad_medium + coefficient(1) * medium
        if sweep_number < 2:
            medium = smoothed(medium, block_neighbours(medium))
    grown = extend(extend(grad_medium, "slab", 0, 2), "pencil", 1, 2)
    back_fine = prolong(grown)[1:-1, 1:-1] * 0.125
    rhs_grad = rhs_grad + core(back_fine, 3, x_cells, y_cells)
    centre, total = shrink_neighbours(back_fine)
    stage = masked(6.0 * centre - total, x_cells, y_cells, 2)
    stages = [stage]
    for width in (1, 0):
        centre, total = shrink_neighbours(stages[-1])
        stages.append(masked(smoothed(centre, total), x_cells, y_cells, width))
    for number, stage in enumerate(stages):
        rhs_grad = rhs_grad - coefficient(0) * core(stage, 2 - number, x_cells, y_cells)
    slab_index = lax.axis_index("slab")
    slab_count = lax.axis_size("slab")
    low_face = jnp.where(slab_index == 0, rhs_grad[0], 0.0)
    high_face = jnp.where(slab_index == slab_count - 1, rhs_grad[x_cells - 1], 0.0)
    low_face, high_face = spread_faces(low_face, high_face, slab_index, slab_count)
    pencil_index = lax.axis_index("pencil")
    pencil_count = lax.axis_size("pencil")
    targets = source_rows(seg_rows, owners, offsets, tile_size)
    y_tiles = y_cells * pencil_count // tile_size
    z_tiles = z_cells // tile_size
    targets = targets.reshape(2, y_tiles, z_tiles * tile_size)
    local_targets = lax.dynamic_index_in_dim(targets, pencil_index, axis=1, keepdims=False)
    local_targets = local_targets.reshape(-1)
    faces = jnp.stack([low_face, high_face])
    faces = faces.reshape(2, y_cells, z_tiles, tile_size).transpose(0, 2, 1, 3)
    faces = faces.reshape(-1, tile_size)
    first_parent = slab_index * pencil_count
    wanted = first_parent * tile_size + jnp.arange(pencil_count * tile_size, dtype=jnp.int32)
    picks = (local_targets[None, :] == wanted[:, None]).astype(jnp.float32)
    partial = jnp.dot(picks, faces, precision=lax.Precision.HIGHEST)
    partial = partial.reshape(pencil_count, tile_size, tile_size)
    parent_grad = lax.psum_scatter(partial, "pencil", scatter_dimension=0, tiled=True)
    return (rhs_grad, parent_grad)


def spread_faces(low_face, high_face, slab_index, slab_count):
    stride = slab_count // 2
    while stride >= 1:
        span = 2 * stride
        low_pairs = [(i, i + stride) for i in range(0, slab_count, span)]
        high_pairs = [(slab_count - 1 - i, slab_count - 1 - i - stride) for i in range(0, slab_count, span)]
        low_sender = slab_index % span == 0
        sent = jnp.where(low_sender, low_face, high_face)
        got = lax.ppermute(sent, "slab", low_pairs + high_pairs)
        low_receiver = slab_index % span == stride
        high_receiver = slab_index % span == span - 1 - stride
        low_face = low_face + jnp.where(low_receiver, got, 0.0)
        high_face = high_face + jnp.where(high_receiver, got, 0.0)
        stride //= 2
    return low_face, high_face


def solution(mesh):
    return jax.shard_map(
        shards,
        mesh=mesh,
        in_specs=(P("slab", "pencil", None), P(), P(), P()),
        out_specs=(P("slab", "pencil", None), P(("slab", "pencil"), None, None)),
        check_vma=False,
    )
```

profile of v0, /device:TPU:1, one launch (start us, length us, event | category | flops | bytes accessed | tf_op | source)
XLA Modules:
  0.0 402.5 jit_solution(10446513153266721408)
XLA Ops:
  8.8 4.6 %collective-permute-start.1 = (f32[4,128,512]{1,2,0:T(8,128)S(1)}, f32[4,128,512]{1,2,0:T(8,128)S(1)}, u32[]{:S(2)}, u32[]{:S(2)}) collective-permute-start(f32[4,128,512]{1,2,0:T(8,128)S(1)} %copy.105), channel_id=1, source_target_pairs={{0,4},{4,8},{8,12},{12,16},{16,20},{20,24},{24,28},{28,32},{32,36}... | collective-permute-start | bytes 3145736 | tf_op jit(solution)/shard_map/ppermute | solution.py:107
  21.6 9.2 %collective-permute-done = f32[1,128,512]{1,2,0:T(8,128)} collective-permute-done((f32[1,128,512]{1,2,0:T(8,128)}, f32[1,128,512]{1,2,0:T(8,128)}, u32[]{:S(2)}, u32[]{:S(2)}) %collective-permute-start) | collective-permute-done | bytes 262176 | tf_op jit(solution)/shard_map/ppermute | solution.py:107
  54.5 6.1 %pad_maximum_fusion = f32[14,138,512]{1,2,0:T(8,128)S(1)} fusion(f32[14,5,512]{1,2,0:T(8,128)} %copy.104, f32[14,128,512]{1,2,0:T(8,128)} %copy-done.5, f32[14,5,512]{1,2,0:T(8,128)} %copy.103), kind=kLoop, calls=%fused_computation | loop fusion | flops 1978368 | bytes 7913472 | tf_op jit(solution)/shard_map/concatenate | solution.py:110
  67.9 19.2 %fusion.4 = f32[12,136,512]{1,2,0:T(8,128)S(1)} fusion(f32[14,138,512]{1,2,0:T(8,128)} %copy-done, f32[12,136,512]{1,2,0:T(8,128)} %slice.645, pred[12,136]{1,0:T(8,128)(4,1)S(1)} %broadcast_and_fusion.1), kind=kLoop, calls=%fused_computation.6 | loop fusion | flops 7520256 | bytes 20055648 | tf_op jit(solution)/shard_map/jit(_where)/select_n | solution.py:121
  91.3 10.2 %fusion.9 = f32[10,134,512]{1,2,0:T(8,128)S(1)} fusion(f32[12,136,512]{1,2,0:T(8,128)S(1)} %fusion.4, f32[10,134,512]{1,2,0:T(8,128)} %slice.651, pred[10,134]{1,0:T(8,128)(4,1)S(1)} %broadcast_and_fusion), kind=kLoop, calls=%fused_computation.15 | loop fusion | flops 6174720 | bytes 16467260 | tf_op jit(solution)/shard_map/jit(_where)/select_n | solution.py:121
  111.6 6.6 %collective-permute-start.6 = (f32[1,64,256]{2,1,0:T(8,128)S(1)}, f32[1,64,256]{2,1,0:T(8,128)S(1)}, u32[]{:S(2)}, u32[]{:S(2)}) collective-permute-start(f32[1,64,256]{2,1,0:T(8,128)S(1)} %convolution_bitcast_fusion.1), channel_id=1, source_target_pairs={{4,0},{8,4},{12,8},{16,12},{20,16},{24,20},{28,24},{32,28},{36,32}... | collective-permute-start | bytes 196616 | tf_op jit(solution)/shard_map/ppermute | solution.py:21
  131.1 5.2 %collective-permute-start.11 = (f32[1,64,256]{2,1,0:T(8,128)S(1)}, f32[1,64,256]{2,1,0:T(8,128)S(1)}, u32[]{:S(2)}, u32[]{:S(2)}) collective-permute-start(f32[1,64,256]{2,1,0:T(8,128)S(1)} %get-tuple-element.48), channel_id=1, source_target_pairs={{0,4},{4,8},{8,12},{12,16},{16,20},{20,24},{24,28},{28,32},{32,36}... | collective-permute-start | bytes 196616 | tf_op jit(solution)/shard_map/ppermute | solution.py:20
  138.9 4.5 %collective-permute-start.13 = (f32[4,1,256]{2,1,0:T(1,128)S(1)}, f32[4,1,256]{2,1,0:T(1,128)S(1)}, u32[]{:S(2)}, u32[]{:S(2)}) collective-permute-start(f32[4,1,256]{2,1,0:T(1,128)S(1)} %get-tuple-element.38), channel_id=1, source_target_pairs={{0,1},{1,2},{2,3},{4,5},{5,6},{6,7},{8,9},{9,10},{10,11},{12,13},{... | collective-permute-start | bytes 12296 | tf_op jit(solution)/shard_map/ppermute | solution.py:20
  146.5 5.1 %collective-permute-start.15 = (f32[1,64,256]{2,1,0:T(8,128)S(1)}, f32[1,64,256]{2,1,0:T(8,128)S(1)}, u32[]{:S(2)}, u32[]{:S(2)}) collective-permute-start(f32[1,64,256]{2,1,0:T(8,128)S(1)} %get-tuple-element.46), channel_id=1, source_target_pairs={{0,4},{4,8},{8,12},{12,16},{16,20},{20,24},{24,28},{28,32},{32,36}... | collective-permute-start | bytes 196616 | tf_op jit(solution)/shard_map/ppermute | solution.py:20
  154.2 4.5 %collective-permute-start.17 = (f32[4,1,256]{2,1,0:T(1,128)S(1)}, f32[4,1,256]{2,1,0:T(1,128)S(1)}, u32[]{:S(2)}, u32[]{:S(2)}) collective-permute-start(f32[4,1,256]{2,1,0:T(1,128)S(1)} %get-tuple-element.36), channel_id=1, source_target_pairs={{0,1},{1,2},{2,3},{4,5},{5,6},{6,7},{8,9},{9,10},{10,11},{12,13},{... | collective-permute-start | bytes 12296 | tf_op jit(solution)/shard_map/ppermute | solution.py:20
  162.3 5.1 %collective-permute-start.19 = (f32[1,32,128]{2,1,0:T(8,128)S(1)}, f32[1,32,128]{2,1,0:T(8,128)S(1)}, u32[]{:S(2)}, u32[]{:S(2)}) collective-permute-start(f32[1,32,128]{2,1,0:T(8,128)S(1)} %bitcast.62), channel_id=1, source_target_pairs={{0,4},{4,8},{8,12},{12,16},{16,20},{20,24},{24,28},{28,32},{32,36}... | collective-permute-start | bytes 49160 | tf_op jit(solution)/shard_map/ppermute | solution.py:20
  169.6 4.5 %collective-permute-start.21 = (f32[3,1,128]{2,1,0:T(1,128)S(1)}, f32[3,1,128]{2,1,0:T(1,128)S(1)}, u32[]{:S(2)}, u32[]{:S(2)}) collective-permute-start(f32[3,1,128]{2,1,0:T(1,128)S(1)} %get-tuple-element.52), channel_id=1, source_target_pairs={{0,1},{1,2},{2,3},{4,5},{5,6},{6,7},{8,9},{9,10},{10,11},{12,13},{... | collective-permute-start | bytes 4616 | tf_op jit(solution)/shard_map/ppermute | solution.py:20
  176.9 5.1 %collective-permute-start.23 = (f32[1,32,128]{2,1,0:T(8,128)S(1)}, f32[1,32,128]{2,1,0:T(8,128)S(1)}, u32[]{:S(2)}, u32[]{:S(2)}) collective-permute-start(f32[1,32,128]{2,1,0:T(8,128)S(1)} %fusion.107), channel_id=1, source_target_pairs={{0,4},{4,8},{8,12},{12,16},{16,20},{20,24},{24,28},{28,32},{32,36}... | collective-permute-start | bytes 49160 | tf_op jit(solution)/shard_map/ppermute | solution.py:20
  191.8 5.1 %collective-permute-start.27 = (f32[1,64,256]{2,1,0:T(8,128)S(1)}, f32[1,64,256]{2,1,0:T(8,128)S(1)}, u32[]{:S(2)}, u32[]{:S(2)}) collective-permute-start(f32[1,64,256]{2,1,0:T(8,128)S(1)} %copy.111), channel_id=1, source_target_pairs={{0,4},{4,8},{8,12},{12,16},{16,20},{20,24},{24,28},{28,32},{32,36}... | collective-permute-start | bytes 196616 | tf_op jit(solution)/shard_map/ppermute | solution.py:20
  207.0 5.1 %collective-permute-start.31 = (f32[1,64,256]{2,1,0:T(8,128)S(1)}, f32[1,64,256]{2,1,0:T(8,128)S(1)}, u32[]{:S(2)}, u32[]{:S(2)}) collective-permute-start(f32[1,64,256]{2,1,0:T(8,128)S(1)} %get-tuple-element.44), channel_id=1, source_target_pairs={{0,4},{4,8},{8,12},{12,16},{16,20},{20,24},{24,28},{28,32},{32,36}... | collective-permute-start | bytes 196616 | tf_op jit(solution)/shard_map/ppermute | solution.py:20
  214.8 4.5 %collective-permute-start.33 = (f32[4,1,256]{2,1,0:T(1,128)S(1)}, f32[4,1,256]{2,1,0:T(1,128)S(1)}, u32[]{:S(2)}, u32[]{:S(2)}) collective-permute-start(f32[4,1,256]{2,1,0:T(1,128)S(1)} %get-tuple-element.32), channel_id=1, source_target_pairs={{0,1},{1,2},{2,3},{4,5},{5,6},{6,7},{8,9},{9,10},{10,11},{12,13},{... | collective-permute-start | bytes 12296 | tf_op jit(solution)/shard_map/ppermute | solution.py:20
  222.3 5.1 %collective-permute-start.35 = (f32[1,64,256]{2,1,0:T(8,128)S(1)}, f32[1,64,256]{2,1,0:T(8,128)S(1)}, u32[]{:S(2)}, u32[]{:S(2)}) collective-permute-start(f32[1,64,256]{2,1,0:T(8,128)S(1)} %get-tuple-element.42), channel_id=1, source_target_pairs={{0,4},{4,8},{8,12},{12,16},{16,20},{20,24},{24,28},{28,32},{32,36}... | collective-permute-start | bytes 196616 | tf_op jit(solution)/shard_map/ppermute | solution.py:20
  230.1 4.5 %collective-permute-start.37 = (f32[4,1,256]{2,1,0:T(1,128)S(1)}, f32[4,1,256]{2,1,0:T(1,128)S(1)}, u32[]{:S(2)}, u32[]{:S(2)}) collective-permute-start(f32[4,1,256]{2,1,0:T(1,128)S(1)} %get-tuple-element.30), channel_id=1, source_target_pairs={{0,1},{1,2},{2,3},{4,5},{5,6},{6,7},{8,9},{9,10},{10,11},{12,13},{... | collective-permute-start | bytes 12296 | tf_op jit(solution)/shard_map/ppermute | solution.py:20
  235.8 5.1 %collective-permute-start.38 = (f32[2,64,256]{2,1,0:T(8,128)S(1)}, f32[2,64,256]{2,1,0:T(8,128)S(1)}, u32[]{:S(2)}, u32[]{:S(2)}) collective-permute-start(f32[2,64,256]{2,1,0:T(8,128)S(1)} %fusion.60), channel_id=1, source_target_pairs={{0,4},{4,8},{8,12},{12,16},{16,20},{20,24},{24,28},{28,32},{32,36}... | collective-permute-start | bytes 393224 | tf_op jit(solution)/shard_map/ppermute | solution.py:107
  266.8 8.5 %reshape.485 = f32[12,136,512]{1,2,0:T(8,128)} reshape(f32[12,136,256,2]{1,3,2,0:T(2,128)} %broadcast_in_dim.166) | data formatting | bytes 6684672 | tf_op jit(solution)/shard_map/reshape | solution.py:72
  288.6 21.9 %fusion.28 = (f32[6,130,512]{1,2,0:T(8,128)}, f32[6,130,512]{1,2,0:T(8,128)}) fusion(f32[8,132,512]{1,2,0:T(8,128)} %copy-done.3, f32[6,130,512]{1,2,0:T(8,128)} %slice.663, pred[6,130]{1,0:T(8,128)(4,1)S(1)} %broadcast_and_fusion.2, f32[6,130,512]{1,2,0:T(8,128)} %slice.707, f32[8,132,512]{1,2,0:T(8,128)} %copy-done.4), kind=kLoop, calls=%fused_computation.46 | loop fusion | flops 7188480 | bytes 19170060 | tf_op jit(solution)/shard_map/jit(_where)/select_n | solution.py:121
  314.5 7.9 %fusion.37 = f32[4,128,512]{1,2,0:T(8,128)S(1)} fusion(f32[6,130,512]{1,2,0:T(8,128)} %get-tuple-element.55, f32[8,132,512]{1,2,0:T(8,128)} %copy-done.4, f32[10,134,512]{1,2,0:T(8,128)S(1)} %slice_multiply_fusion, f32[6,130,512]{1,2,0:T(8,128)S(1)} %copy-done.6, f32[4,128,512]{1,2,0:T(8,128)S(1)} %slice.668, f32[10,134,512]{1,2,0:T(8,128)} %copy-done.2, ...), kind=kLoop, calls=%fused_computation.60 | loop fusion | flops 8126464 | bytes 17826304 | tf_op jit(solution)/shard_map/sub | solution.py:178
  326.3 44.2 %collective-permute-done.45 = f32[128,512]{0,1:T(8,128)S(1)} collective-permute-done((f32[128,512]{0,1:T(8,128)S(1)}, f32[128,512]{0,1:T(8,128)S(1)}, u32[]{:S(2)}, u32[]{:S(2)}) %collective-permute-start.45) | collective-permute-done | bytes 262176 | tf_op jit(solution)/shard_map/ppermute | solution.py:212
  375.7 19.8 %reduce-scatter.2.cloned.1.call-done = f32[1,128,128]{2,1,0:T(8,128)} async-done(((f32[4,128,128]{2,1,0:T(8,128)}), f32[1,128,128]{2,1,0:T(8,128)}) %reduce-scatter.2.cloned.1.call-update) | async-done | bytes 65552 | tf_op jit(solution)/shard_map/reduce_scatter | solution.py:200
  (216 shorter events, 165.2 us)
Async XLA Ops:
  7.2 388.3 %reduce-scatter.2.cloned.1.call-start = ((), (), s32[]{:S(2)}) async-start(), calls=%async_computation.1 | async-start | bytes 327680 | tf_op jit(solution)/shard_map/reduce_scatter | solution.py:200
  8.8 23.0 %collective-permute-start.1 = (f32[4,128,512]{1,2,0:T(8,128)S(1)}, f32[4,128,512]{1,2,0:T(8,128)S(1)}, u32[]{:S(2)}, u32[]{:S(2)}) collective-permute-start(f32[4,128,512]{1,2,0:T(8,128)S(1)} %copy.105), channel_id=1, source_target_pairs={{0,4},{4,8},{8,12},{12,16},{16,20},{20,24},{24,28},{28,32},{32,36}... | collective-permute-start | bytes 3145736 | tf_op jit(solution)/shard_map/ppermute | solution.py:107
  13.4 18.9 %collective-permute-start.2 = (f32[4,128,512]{1,2,0:T(8,128)S(1)}, f32[4,128,512]{1,2,0:T(8,128)S(1)}, u32[]{:S(2)}, u32[]{:S(2)}) collective-permute-start(f32[4,128,512]{1,2,0:T(8,128)S(1)} %copy.105), channel_id=1, source_target_pairs={{4,0},{8,4},{12,8},{16,12},{20,16},{24,20},{28,24},{32,28},{36,32}... | collective-permute-start | bytes 3145736 | tf_op jit(solution)/shard_map/ppermute | solution.py:108
  16.1 14.7 %collective-permute-start = (f32[1,128,512]{1,2,0:T(8,128)}, f32[1,128,512]{1,2,0:T(8,128)}, u32[]{:S(2)}, u32[]{:S(2)}) collective-permute-start(f32[1,128,512]{1,2,0:T(8,128)} %get-tuple-element.25), channel_id=1, source_target_pairs={{0,8},{4,12},{8,16},{12,20},{16,24},{20,28},{24,32},{28,36},{32,40... | collective-permute-start | bytes 786440 | tf_op jit(solution)/shard_map/ppermute | solution.py:107
  20.0 12.3 %collective-permute-start.3 = (f32[1,128,512]{1,2,0:T(8,128)}, f32[1,128,512]{1,2,0:T(8,128)S(1)}, u32[]{:S(2)}, u32[]{:S(2)}) collective-permute-start(f32[1,128,512]{1,2,0:T(8,128)} %get-tuple-element.24), channel_id=1, source_target_pairs={{8,0},{12,4},{16,8},{20,12},{24,16},{28,20},{32,24},{36,28},{40,32... | collective-permute-start | bytes 786440 | tf_op jit(solution)/shard_map/ppermute | solution.py:108
  39.5 7.9 %collective-permute-start.4 = (f32[14,5,512]{2,0,1:T(8,128)S(1)}, f32[14,5,512]{2,0,1:T(8,128)S(1)}, u32[]{:S(2)}, u32[]{:S(2)}) collective-permute-start(f32[14,5,512]{2,0,1:T(8,128)S(1)} %copy.101), channel_id=1, source_target_pairs={{0,1},{1,2},{2,3},{4,5},{5,6},{6,7},{8,9},{9,10},{10,11},{12,13},{... | collective-permute-start | bytes 430088 | tf_op jit(solution)/shard_map/ppermute | solution.py:107
  45.8 6.2 %collective-permute-start.5 = (f32[14,5,512]{2,0,1:T(8,128)S(1)}, f32[14,5,512]{2,0,1:T(8,128)S(1)}, u32[]{:S(2)}, u32[]{:S(2)}) collective-permute-start(f32[14,5,512]{2,0,1:T(8,128)S(1)} %copy.102), channel_id=1, source_target_pairs={{1,0},{2,1},{3,2},{5,4},{6,5},{7,6},{9,8},{10,9},{11,10},{13,12},{... | collective-permute-start | bytes 430088 | tf_op jit(solution)/shard_map/ppermute | solution.py:108
  111.6 9.7 %collective-permute-start.6 = (f32[1,64,256]{2,1,0:T(8,128)S(1)}, f32[1,64,256]{2,1,0:T(8,128)S(1)}, u32[]{:S(2)}, u32[]{:S(2)}) collective-permute-start(f32[1,64,256]{2,1,0:T(8,128)S(1)} %convolution_bitcast_fusion.1), channel_id=1, source_target_pairs={{4,0},{8,4},{12,8},{16,12},{20,16},{24,20},{28,24},{32,28},{36,32}... | collective-permute-start | bytes 196616 | tf_op jit(solution)/shard_map/ppermute | solution.py:21
  129.1 7.2 %collective-permute-start.10 = (f32[1,64,256]{2,1,0:T(8,128)S(1)}, f32[1,64,256]{2,1,0:T(8,128)S(1)}, u32[]{:S(2)}, u32[]{:S(2)}) collective-permute-start(f32[1,64,256]{2,1,0:T(8,128)S(1)} %get-tuple-element.49), channel_id=1, source_target_pairs={{4,0},{8,4},{12,8},{16,12},{20,16},{24,20},{28,24},{32,28},{36,32}... | collective-permute-start | bytes 196616 | tf_op jit(solution)/shard_map/ppermute | solution.py:21
  131.1 6.6 %collective-permute-start.11 = (f32[1,64,256]{2,1,0:T(8,128)S(1)}, f32[1,64,256]{2,1,0:T(8,128)S(1)}, u32[]{:S(2)}, u32[]{:S(2)}) collective-permute-start(f32[1,64,256]{2,1,0:T(8,128)S(1)} %get-tuple-element.48), channel_id=1, source_target_pairs={{0,4},{4,8},{8,12},{12,16},{16,20},{20,24},{24,28},{28,32},{32,36}... | collective-permute-start | bytes 196616 | tf_op jit(solution)/shard_map/ppermute | solution.py:20
  144.5 7.1 %collective-permute-start.14 = (f32[1,64,256]{2,1,0:T(8,128)S(1)}, f32[1,64,256]{2,1,0:T(8,128)S(1)}, u32[]{:S(2)}, u32[]{:S(2)}) collective-permute-start(f32[1,64,256]{2,1,0:T(8,128)S(1)} %get-tuple-element.47), channel_id=1, source_target_pairs={{4,0},{8,4},{12,8},{16,12},{20,16},{24,20},{28,24},{32,28},{36,32}... | collective-permute-start | bytes 196616 | tf_op jit(solution)/shard_map/ppermute | solution.py:21
  146.5 6.5 %collective-permute-start.15 = (f32[1,64,256]{2,1,0:T(8,128)S(1)}, f32[1,64,256]{2,1,0:T(8,128)S(1)}, u32[]{:S(2)}, u32[]{:S(2)}) collective-permute-start(f32[1,64,256]{2,1,0:T(8,128)S(1)} %get-tuple-element.46), channel_id=1, source_target_pairs={{0,4},{4,8},{8,12},{12,16},{16,20},{20,24},{24,28},{28,32},{32,36}... | collective-permute-start | bytes 196616 | tf_op jit(solution)/shard_map/ppermute | solution.py:20
  160.3 7.1 %collective-permute-start.18 = (f32[1,32,128]{2,1,0:T(8,128)S(1)}, f32[1,32,128]{2,1,0:T(8,128)S(1)}, u32[]{:S(2)}, u32[]{:S(2)}) collective-permute-start(f32[1,32,128]{2,1,0:T(8,128)S(1)} %bitcast.61), channel_id=1, source_target_pairs={{4,0},{8,4},{12,8},{16,12},{20,16},{24,20},{28,24},{32,28},{36,32}... | collective-permute-start | bytes 49160 | tf_op jit(solution)/shard_map/ppermute | solution.py:21
  175.0 7.0 %collective-permute-start.22 = (f32[1,32,128]{2,1,0:T(8,128)S(1)}, f32[1,32,128]{2,1,0:T(8,128)S(1)}, u32[]{:S(2)}, u32[]{:S(2)}) collective-permute-start(f32[1,32,128]{2,1,0:T(8,128)S(1)} %fusion.107), channel_id=1, source_target_pairs={{4,0},{8,4},{12,8},{16,12},{20,16},{24,20},{28,24},{32,28},{36,32}... | collective-permute-start | bytes 49160 | tf_op jit(solution)/shard_map/ppermute | solution.py:21
  189.9 7.1 %collective-permute-start.26 = (f32[1,64,256]{2,1,0:T(8,128)S(1)}, f32[1,64,256]{2,1,0:T(8,128)S(1)}, u32[]{:S(2)}, u32[]{:S(2)}) collective-permute-start(f32[1,64,256]{2,1,0:T(8,128)S(1)} %copy.111), channel_id=1, source_target_pairs={{4,0},{8,4},{12,8},{16,12},{20,16},{24,20},{28,24},{32,28},{36,32}... | collective-permute-start | bytes 196616 | tf_op jit(solution)/shard_map/ppermute | solution.py:21
  191.8 6.4 %collective-permute-start.27 = (f32[1,64,256]{2,1,0:T(8,128)S(1)}, f32[1,64,256]{2,1,0:T(8,128)S(1)}, u32[]{:S(2)}, u32[]{:S(2)}) collective-permute-start(f32[1,64,256]{2,1,0:T(8,128)S(1)} %copy.111), channel_id=1, source_target_pairs={{0,4},{4,8},{8,12},{12,16},{16,20},{20,24},{24,28},{28,32},{32,36}... | collective-permute-start | bytes 196616 | tf_op jit(solution)/shard_map/ppermute | solution.py:20
  205.1 7.1 %collective-permute-start.30 = (f32[1,64,256]{2,1,0:T(8,128)S(1)}, f32[1,64,256]{2,1,0:T(8,128)S(1)}, u32[]{:S(2)}, u32[]{:S(2)}) collective-permute-start(f32[1,64,256]{2,1,0:T(8,128)S(1)} %get-tuple-element.45), channel_id=1, source_target_pairs={{4,0},{8,4},{12,8},{16,12},{20,16},{24,20},{28,24},{32,28},{36,32}... | collective-permute-start | bytes 196616 | tf_op jit(solution)/shard_map/ppermute | solution.py:21
  207.0 6.4 %collective-permute-start.31 = (f32[1,64,256]{2,1,0:T(8,128)S(1)}, f32[1,64,256]{2,1,0:T(8,128)S(1)}, u32[]{:S(2)}, u32[]{:S(2)}) collective-permute-start(f32[1,64,256]{2,1,0:T(8,128)S(1)} %get-tuple-element.44), channel_id=1, source_target_pairs={{0,4},{4,8},{8,12},{12,16},{16,20},{20,24},{24,28},{28,32},{32,36}... | collective-permute-start | bytes 196616 | tf_op jit(solution)/shard_map/ppermute | solution.py:20
  220.4 7.1 %collective-permute-start.34 = (f32[1,64,256]{2,1,0:T(8,128)S(1)}, f32[1,64,256]{2,1,0:T(8,128)S(1)}, u32[]{:S(2)}, u32[]{:S(2)}) collective-permute-start(f32[1,64,256]{2,1,0:T(8,128)S(1)} %get-tuple-element.43), channel_id=1, source_target_pairs={{4,0},{8,4},{12,8},{16,12},{20,16},{24,20},{28,24},{32,28},{36,32}... | collective-permute-start | bytes 196616 | tf_op jit(solution)/shard_map/ppermute | solution.py:21
  222.3 6.5 %collective-permute-start.35 = (f32[1,64,256]{2,1,0:T(8,128)S(1)}, f32[1,64,256]{2,1,0:T(8,128)S(1)}, u32[]{:S(2)}, u32[]{:S(2)}) collective-permute-start(f32[1,64,256]{2,1,0:T(8,128)S(1)} %get-tuple-element.42), channel_id=1, source_target_pairs={{0,4},{4,8},{8,12},{12,16},{16,20},{20,24},{24,28},{28,32},{32,36}... | collective-permute-start | bytes 196616 | tf_op jit(solution)/shard_map/ppermute | solution.py:20
  235.8 7.1 %collective-permute-start.38 = (f32[2,64,256]{2,1,0:T(8,128)S(1)}, f32[2,64,256]{2,1,0:T(8,128)S(1)}, u32[]{:S(2)}, u32[]{:S(2)}) collective-permute-start(f32[2,64,256]{2,1,0:T(8,128)S(1)} %fusion.60), channel_id=1, source_target_pairs={{0,4},{4,8},{8,12},{12,16},{16,20},{20,24},{24,28},{28,32},{32,36}... | collective-permute-start | bytes 393224 | tf_op jit(solution)/shard_map/ppermute | solution.py:107
  240.9 6.3 %collective-permute-start.39 = (f32[2,64,256]{2,1,0:T(8,128)S(1)}, f32[2,64,256]{2,1,0:T(8,128)S(1)}, u32[]{:S(2)}, u32[]{:S(2)}) collective-permute-start(f32[2,64,256]{2,1,0:T(8,128)S(1)} %fusion.60), channel_id=1, source_target_pairs={{4,0},{8,4},{12,8},{16,12},{20,16},{24,20},{28,24},{32,28},{36,32}... | collective-permute-start | bytes 393224 | tf_op jit(solution)/shard_map/ppermute | solution.py:108
  247.2 9.7 %collective-permute-start.40 = (f32[6,2,256]{2,1,0:T(2,128)S(1)}, f32[6,2,256]{2,1,0:T(2,128)S(1)}, u32[]{:S(2)}, u32[]{:S(2)}) collective-permute-start(f32[6,2,256]{2,1,0:T(2,128)S(1)} %get-tuple-element.28), channel_id=1, source_target_pairs={{0,1},{1,2},{2,3},{4,5},{5,6},{6,7},{8,9},{9,10},{10,11},{12,13},{... | collective-permute-start | bytes 36872 | tf_op jit(solution)/shard_map/ppermute | solution.py:107
  324.9 45.6 %collective-permute-start.45 = (f32[128,512]{0,1:T(8,128)S(1)}, f32[128,512]{0,1:T(8,128)S(1)}, u32[]{:S(2)}, u32[]{:S(2)}) collective-permute-start(f32[128,512]{0,1:T(8,128)S(1)} %get-tuple-element.12), channel_id=1, source_target_pairs={{0,8},{16,24},{32,40},{48,56},{64,72},{80,88},{96,104},{112,120},{... | collective-permute-start | bytes 786440 | tf_op jit(solution)/shard_map/ppermute | solution.py:212
  (36 other events, 175.0 us)
Sparse Core Ops, SparseCore 0:
  374.5 20.9 reduce-scatter.1
where the time goes:
time: 409 us; the launch traced here: 403 us
  starting transfers between devices  138 us (34%)
  waiting for transfers between devices  96.3 us (24%)
  other arithmetic  80.9 us (20%)
  local copies, waits for them, and re-layouts  68.9 us (17%)
  between operations  15.5 us (4%)
    ppermute x16, starting transfers between devices, with_halo(): before = lax.ppermute(last, axis, up)  74.9 us
    select_n x5, other arithmetic, masked(): return jnp.where(keep, field, 0.0)  59.1 us
    ppermute x5, waiting for transfers between devices, spread_faces(): got = lax.ppermute(sent, 'slab', low_pairs + high_pairs)  45.5 us
    ppermute x16, starting transfers between devices, with_halo(): after = lax.ppermute(initial, axis, down)  30.3 us
    ppermute x5, starting transfers between devices, extend(): lows.insert(0, lax.ppermute(low_piece, axis, up))  21.1 us
    reduce_scatter x1, waiting for transfers between devices, shards(): lax.psum_scatter(partial, 'pencil', scatter_dimension=0, tiled=True)  19.8 us
    slice x6, local copies, waits for them, and re-layouts, shrink_neighbours(): centre = field[1:-1, 1:-1]  17.9 us
    ppermute x16, waiting for transfers between devices, with_halo(): before = lax.ppermute(last, axis, up)  14.8 us
  transfers between devices with their start and end apart: 48, of which 23 were waited for; matrix products, arithmetic and copies ran while one was open for 3% of the time, Pallas kernels for 0%

commit v1 on v0

--- a/solution.py
+++ b/solution.py
@@ -69,7 +69,16 @@
 
 
 def prolong(field):
-    return jnp.repeat(jnp.repeat(jnp.repeat(field, 2, axis=0), 2, axis=1), 2, axis=2)
+    x_cells, y_cells, z_cells = field.shape
+    flat = field.reshape(x_cells * y_cells, z_cells)
+    wide = jnp.dot(flat, pair_matrix(2 * z_cells).T, precision=lax.Precision.HIGHEST)
+    wide = wide.reshape(x_cells, y_cells, 2 * z_cells)
+    to_rows = pair_matrix(2 * y_cells)
+    planes = [
+        jnp.dot(to_rows, wide[i], precision=lax.Precision.HIGHEST)
+        for i in range(x_cells)
+    ]
+    return jnp.repeat(jnp.stack(planes), 2, axis=0)
 
 
 def source_rows(seg_rows, owners, offsets, tile_size):
@@ -142,7 +151,7 @@
     powers = [grown]
     for width in range(depth - 1, -1, -1):
         centre, total = shrink_neighbours(powers[-1])
-        powers.append(masked(smoothed(centre, total), x_cells, y_cells, width))
+        powers.append(lax.optimization_barrier(masked(smoothed(centre, total), x_cells, y_cells, width)))
     rhs_grad = jnp.zeros_like(cotangent)
     for level_power in range(depth + 1):
         part = core(powers[level_power], depth - level_power, x_cells, y_cells)
@@ -169,11 +178,11 @@
     back_fine = prolong(grown)[1:-1, 1:-1] * 0.125
     rhs_grad = rhs_grad + core(back_fine, 3, x_cells, y_cells)
     centre, total = shrink_neighbours(back_fine)
-    stage = masked(6.0 * centre - total, x_cells, y_cells, 2)
+    stage = lax.optimization_barrier(masked(6.0 * centre - total, x_cells, y_cells, 2))
     stages = [stage]
     for width in (1, 0):
         centre, total = shrink_neighbours(stages[-1])
-        stages.append(masked(smoothed(centre, total), x_cells, y_cells, width))
+        stages.append(lax.optimization_barrier(masked(smoothed(centre, total), x_cells, y_cells, width)))
     for number, stage in enumerate(stages):
         rhs_grad = rhs_grad - coefficient(0) * core(stage, 2 - number, x_cells, y_cells)
     slab_index = lax.axis_index("slab")

time: 409 us -> 311 us (0.76)
  local copies, waits for them, and re-layouts: 68.9 us -> 16.5 us
  other arithmetic: 80.9 us -> 30.2 us
  matrix products: 3.39 us -> 8.1 us
    select_n x5 -> x6, other arithmetic: 59.1 us -> 14.7 us  [masked(): return jnp.where(keep, field, 0.0)]
    slice x6, local copies, waits for them, and re-layouts: 17.9 us -> 4.77 us  [shrink_neighbours(): centre = field[1:-1, 1:-1]]
    reshape x3 -> x2, local copies, waits for them, and re-layouts: 13.1 us -> 2.71 us  [the longest x1 1.86 us: prolong(): flat = field.reshape(x_cells * y_cells, z_cells)]
    slice x2 -> x1, local copies, waits for them, and re-layouts: 7.03 us -> 0.03 us  [extend(): lax.slice_in_dim(x, max(0, distance * block - width), block, axis=dim)]
    unnamed x30 -> x58, local copies, waits for them, and re-layouts: 12 us -> 6.06 us
    sub x1, other arithmetic: 7.92 us -> 2.63 us  [shards(): rhs_grad - coefficient(0) * core(stage, 2 - number, x_cells, y_cells)]
    ppermute x2 -> x0, local copies, waits for them, and re-layouts: 4.92 us -> none  [the longest x1 2.48 us: extend(): lows.insert(0, lax.ppermute(low_piece, axis, up))]
    broadcast_in_dim x8 -> x1, local copies, waits for them, and re-layouts: 5.28 us -> 0.47 us  [prolong(): return jnp.repeat(jnp.stack(planes), 2, axis=0)]
  transfers between devices with their start and end apart: 48 -> 48, of which waited for: 23 -> 24; matrix products, arithmetic and copies ran while one was open for 3% -> 3% of each run, Pallas kernels for 0% -> 0%
where the time goes in v1:
time: 311 us; the launch traced here: 307 us
  starting transfers between devices  138 us (44%)
  waiting for transfers between devices  99.4 us (32%)
  other arithmetic  30.2 us (10%)
  local copies, waits for them, and re-layouts  16.5 us (5%)
  between operations  15.5 us (5%)
  matrix products  8.1 us (3%)
    ppermute x16, starting transfers between devices, with_halo(): before = lax.ppermute(last, axis, up)  74.8 us
    ppermute x5, waiting for transfers between devices, spread_faces(): got = lax.ppermute(sent, 'slab', low_pairs + high_pairs)  45.5 us
    ppermute x16, starting transfers between devices, with_halo(): after = lax.ppermute(initial, axis, down)  30.2 us
    ppermute x5, starting transfers between devices, extend(): lows.insert(0, lax.ppermute(low_piece, axis, up))  21.3 us
    reduce_scatter x1, waiting for transfers between devices, shards(): lax.psum_scatter(partial, 'pencil', scatter_dimension=0, tiled=True)  20.8 us
    select_n x6, other arithmetic, masked(): return jnp.where(keep, field, 0.0)  14.7 us
    ppermute x16, waiting for transfers between devices, with_halo(): before = lax.ppermute(last, axis, up)  13.5 us
    ppermute x5, waiting for transfers between devices, extend(): lows.insert(0, lax.ppermute(low_piece, axis, up))  9.97 us
  transfers between devices with their start and end apart: 48, of which 24 were waited for; matrix products, arithmetic and copies ran while one was open for 3% of the time, Pallas kernels for 0%

profile of v1, /device:TPU:1, one launch (start us, length us, event | category | flops | bytes accessed | tf_op | source)
XLA Modules:
  0.0 307.2 jit_solution(13113918200835102349)
XLA Ops:
  7.2 4.7 %collective-permute-start.1 = (f32[4,128,512]{2,1,0:T(8,128)}, f32[4,128,512]{2,1,0:T(8,128)S(1)}, u32[]{:S(2)}, u32[]{:S(2)}) collective-permute-start(f32[4,128,512]{2,1,0:T(8,128)} %param.4), channel_id=1, source_target_pairs={{0,4},{4,8},{8,12},{12,16},{16,20},{20,24},{24,28},{28,32},{32,36}... | collective-permute-start | bytes 3145736 | tf_op jit(solution)/shard_map/ppermute | solution.py:116
  21.2 8.3 %collective-permute-done = f32[1,128,512]{2,1,0:T(8,128)} collective-permute-done((f32[1,128,512]{2,1,0:T(8,128)}, f32[1,128,512]{2,1,0:T(8,128)}, u32[]{:S(2)}, u32[]{:S(2)}) %collective-permute-start) | collective-permute-done | bytes 262176 | tf_op jit(solution)/shard_map/ppermute | solution.py:116
  37.7 4.0 %collective-permute-done.5 = f32[14,5,512]{2,1,0:T(8,128)S(1)} collective-permute-done((f32[14,5,512]{2,1,0:T(8,128)S(1)}, f32[14,5,512]{2,1,0:T(8,128)S(1)}, u32[]{:S(2)}, u32[]{:S(2)}) %collective-permute-start.5) | collective-permute-done | bytes 143392 | tf_op jit(solution)/shard_map/ppermute | solution.py:117
  54.3 6.6 %collective-permute-start.6 = (f32[1,64,256]{2,1,0:T(8,128)S(1)}, f32[1,64,256]{2,1,0:T(8,128)S(1)}, u32[]{:S(2)}, u32[]{:S(2)}) collective-permute-start(f32[1,64,256]{2,1,0:T(8,128)S(1)} %convolution_bitcast_fusion.7), channel_id=1, source_target_pairs={{4,0},{8,4},{12,8},{16,12},{20,16},{24,20},{28,24},{32,28},{36,32}... | collective-permute-start | bytes 196616 | tf_op jit(solution)/shard_map/ppermute | solution.py:21
  66.6 4.2 %collective-permute-start.9 = (f32[4,1,256]{2,1,0:T(1,128)S(1)}, f32[4,1,256]{2,1,0:T(1,128)S(1)}, u32[]{:S(2)}, u32[]{:S(2)}) collective-permute-start(f32[4,1,256]{2,1,0:T(1,128)S(1)} %get-tuple-element.28), channel_id=1, source_target_pairs={{0,1},{1,2},{2,3},{4,5},{5,6},{6,7},{8,9},{9,10},{10,11},{12,13},{... | collective-permute-start | bytes 12296 | tf_op jit(solution)/shard_map/ppermute | solution.py:20
  73.8 5.2 %collective-permute-start.11 = (f32[1,64,256]{2,1,0:T(8,128)S(1)}, f32[1,64,256]{2,1,0:T(8,128)S(1)}, u32[]{:S(2)}, u32[]{:S(2)}) collective-permute-start(f32[1,64,256]{2,1,0:T(8,128)S(1)} %get-tuple-element.36), channel_id=1, source_target_pairs={{0,4},{4,8},{8,12},{12,16},{16,20},{20,24},{24,28},{28,32},{32,36}... | collective-permute-start | bytes 196616 | tf_op jit(solution)/shard_map/ppermute | solution.py:20
  81.6 4.5 %collective-permute-start.13 = (f32[4,1,256]{2,1,0:T(1,128)S(1)}, f32[4,1,256]{2,1,0:T(1,128)S(1)}, u32[]{:S(2)}, u32[]{:S(2)}) collective-permute-start(f32[4,1,256]{2,1,0:T(1,128)S(1)} %get-tuple-element.26), channel_id=1, source_target_pairs={{0,1},{1,2},{2,3},{4,5},{5,6},{6,7},{8,9},{9,10},{10,11},{12,13},{... | collective-permute-start | bytes 12296 | tf_op jit(solution)/shard_map/ppermute | solution.py:20
  89.2 5.1 %collective-permute-start.15 = (f32[1,64,256]{2,1,0:T(8,128)S(1)}, f32[1,64,256]{2,1,0:T(8,128)S(1)}, u32[]{:S(2)}, u32[]{:S(2)}) collective-permute-start(f32[1,64,256]{2,1,0:T(8,128)S(1)} %get-tuple-element.34), channel_id=1, source_target_pairs={{0,4},{4,8},{8,12},{12,16},{16,20},{20,24},{24,28},{28,32},{32,36}... | collective-permute-start | bytes 196616 | tf_op jit(solution)/shard_map/ppermute | solution.py:20
  96.9 4.5 %collective-permute-start.17 = (f32[4,1,256]{2,1,0:T(1,128)S(1)}, f32[4,1,256]{2,1,0:T(1,128)S(1)}, u32[]{:S(2)}, u32[]{:S(2)}) collective-permute-start(f32[4,1,256]{2,1,0:T(1,128)S(1)} %get-tuple-element.24), channel_id=1, source_target_pairs={{0,1},{1,2},{2,3},{4,5},{5,6},{6,7},{8,9},{9,10},{10,11},{12,13},{... | collective-permute-start | bytes 12296 | tf_op jit(solution)/shard_map/ppermute | solution.py:20
  105.7 5.1 %collective-permute-start.19 = (f32[1,32,128]{2,1,0:T(8,128)S(1)}, f32[1,32,128]{2,1,0:T(8,128)S(1)}, u32[]{:S(2)}, u32[]{:S(2)}) collective-permute-start(f32[1,32,128]{2,1,0:T(8,128)S(1)} %bitcast.75), channel_id=1, source_target_pairs={{0,4},{4,8},{8,12},{12,16},{16,20},{20,24},{24,28},{28,32},{32,36}... | collective-permute-start | bytes 49160 | tf_op jit(solution)/shard_map/ppermute | solution.py:20
  113.0 4.5 %collective-permute-start.21 = (f32[3,1,128]{2,1,0:T(1,128)S(1)}, f32[3,1,128]{2,1,0:T(1,128)S(1)}, u32[]{:S(2)}, u32[]{:S(2)}) collective-permute-start(f32[3,1,128]{2,1,0:T(1,128)S(1)} %get-tuple-element.43), channel_id=1, source_target_pairs={{0,1},{1,2},{2,3},{4,5},{5,6},{6,7},{8,9},{9,10},{10,11},{12,13},{... | collective-permute-start | bytes 4616 | tf_op jit(solution)/shard_map/ppermute | solution.py:20
  120.3 5.1 %collective-permute-start.23 = (f32[1,32,128]{2,1,0:T(8,128)S(1)}, f32[1,32,128]{2,1,0:T(8,128)S(1)}, u32[]{:S(2)}, u32[]{:S(2)}) collective-permute-start(f32[1,32,128]{2,1,0:T(8,128)S(1)} %fusion.135), channel_id=1, source_target_pairs={{0,4},{4,8},{8,12},{12,16},{16,20},{20,24},{24,28},{28,32},{32,36}... | collective-permute-start | bytes 49160 | tf_op jit(solution)/shard_map/ppermute | solution.py:20
  127.5 4.5 %collective-permute-start.25 = (f32[3,1,128]{2,1,0:T(1,128)S(1)}, f32[3,1,128]{2,1,0:T(1,128)S(1)}, u32[]{:S(2)}, u32[]{:S(2)}) collective-permute-start(f32[3,1,128]{2,1,0:T(1,128)S(1)} %get-tuple-element.41), channel_id=1, source_target_pairs={{0,1},{1,2},{2,3},{4,5},{5,6},{6,7},{8,9},{9,10},{10,11},{12,13},{... | collective-permute-start | bytes 4616 | tf_op jit(solution)/shard_map/ppermute | solution.py:20
  136.0 5.1 %collective-permute-start.27 = (f32[1,64,256]{2,1,0:T(8,128)}, f32[1,64,256]{2,1,0:T(8,128)}, u32[]{:S(2)}, u32[]{:S(2)}) collective-permute-start(f32[1,64,256]{2,1,0:T(8,128)} %get-tuple-element.39), channel_id=1, source_target_pairs={{0,4},{4,8},{8,12},{12,16},{16,20},{20,24},{24,28},{28,32},{32,36}... | collective-permute-start | bytes 196616 | tf_op jit(solution)/shard_map/ppermute | solution.py:20
  146.8 5.1 %collective-permute-start.29 = (f32[4,1,256]{2,1,0:T(1,128)}, f32[4,1,256]{2,1,0:T(1,128)}, u32[]{:S(2)}, u32[]{:S(2)}) collective-permute-start(f32[4,1,256]{2,1,0:T(1,128)} %get-tuple-element.22), channel_id=1, source_target_pairs={{0,1},{1,2},{2,3},{4,5},{5,6},{6,7},{8,9},{9,10},{10,11},{12,13},{... | collective-permute-start | bytes 12296 | tf_op jit(solution)/shard_map/ppermute | solution.py:20
  157.0 4.8 %collective-permute-start.31 = (f32[1,64,256]{2,1,0:T(8,128)S(1)}, f32[1,64,256]{2,1,0:T(8,128)S(1)}, u32[]{:S(2)}, u32[]{:S(2)}) collective-permute-start(f32[1,64,256]{2,1,0:T(8,128)S(1)} %get-tuple-element.32), channel_id=1, source_target_pairs={{0,4},{4,8},{8,12},{12,16},{16,20},{20,24},{24,28},{28,32},{32,36}... | collective-permute-start | bytes 196616 | tf_op jit(solution)/shard_map/ppermute | solution.py:20
  164.4 4.6 %collective-permute-start.33 = (f32[4,1,256]{2,1,0:T(1,128)S(1)}, f32[4,1,256]{2,1,0:T(1,128)S(1)}, u32[]{:S(2)}, u32[]{:S(2)}) collective-permute-start(f32[4,1,256]{2,1,0:T(1,128)S(1)} %get-tuple-element.20), channel_id=1, source_target_pairs={{0,1},{1,2},{2,3},{4,5},{5,6},{6,7},{8,9},{9,10},{10,11},{12,13},{... | collective-permute-start | bytes 12296 | tf_op jit(solution)/shard_map/ppermute | solution.py:20
  172.7 4.6 %collective-permute-start.35 = (f32[1,64,256]{2,1,0:T(8,128)S(1)}, f32[1,64,256]{2,1,0:T(8,128)S(1)}, u32[]{:S(2)}, u32[]{:S(2)}) collective-permute-start(f32[1,64,256]{2,1,0:T(8,128)S(1)} %get-tuple-element.30), channel_id=1, source_target_pairs={{0,4},{4,8},{8,12},{12,16},{16,20},{20,24},{24,28},{28,32},{32,36}... | collective-permute-start | bytes 196616 | tf_op jit(solution)/shard_map/ppermute | solution.py:20
  179.8 4.7 %collective-permute-start.37 = (f32[4,1,256]{2,1,0:T(1,128)S(1)}, f32[4,1,256]{2,1,0:T(1,128)S(1)}, u32[]{:S(2)}, u32[]{:S(2)}) collective-permute-start(f32[4,1,256]{2,1,0:T(1,128)S(1)} %get-tuple-element.18), channel_id=1, source_target_pairs={{0,1},{1,2},{2,3},{4,5},{5,6},{6,7},{8,9},{9,10},{10,11},{12,13},{... | collective-permute-start | bytes 12296 | tf_op jit(solution)/shard_map/ppermute | solution.py:20
  185.6 5.1 %collective-permute-start.38 = (f32[2,64,256]{2,1,0:T(8,128)S(1)}, f32[2,64,256]{2,1,0:T(8,128)S(1)}, u32[]{:S(2)}, u32[]{:S(2)}) collective-permute-start(f32[2,64,256]{2,1,0:T(8,128)S(1)} %fusion.73), channel_id=1, source_target_pairs={{0,4},{4,8},{8,12},{12,16},{16,20},{20,24},{24,28},{28,32},{32,36}... | collective-permute-start | bytes 393224 | tf_op jit(solution)/shard_map/ppermute | solution.py:116
  192.8 4.3 %collective-permute-done.39 = f32[2,64,256]{2,1,0:T(8,128)S(1)} collective-permute-done((f32[2,64,256]{2,1,0:T(8,128)S(1)}, f32[2,64,256]{2,1,0:T(8,128)S(1)}, u32[]{:S(2)}, u32[]{:S(2)}) %collective-permute-start.39) | collective-permute-done | bytes 131104 | tf_op jit(solution)/shard_map/ppermute | solution.py:117
  197.7 4.0 %collective-permute-start.40 = (f32[6,2,256]{2,1,0:T(2,128)S(1)}, f32[6,2,256]{2,1,0:T(2,128)S(1)}, u32[]{:S(2)}, u32[]{:S(2)}) collective-permute-start(f32[6,2,256]{2,1,0:T(2,128)S(1)} %get-tuple-element.16), channel_id=1, source_target_pairs={{0,1},{1,2},{2,3},{4,5},{5,6},{6,7},{8,9},{9,10},{10,11},{12,13},{... | collective-permute-start | bytes 36872 | tf_op jit(solution)/shard_map/ppermute | solution.py:116
  231.5 44.2 %collective-permute-done.45 = f32[128,512]{1,0:T(8,128)S(1)} collective-permute-done((f32[128,512]{1,0:T(8,128)S(1)}, f32[128,512]{1,0:T(8,128)S(1)}, u32[]{:S(2)}, u32[]{:S(2)}) %collective-permute-start.45) | collective-permute-done | bytes 262176 | tf_op jit(solution)/shard_map/ppermute | solution.py:221
  279.6 20.8 %reduce-scatter.2.cloned.1.call-done = f32[1,128,128]{2,1,0:T(8,128)} async-done(((f32[4,128,128]{2,1,0:T(8,128)}), f32[1,128,128]{2,1,0:T(8,128)}) %reduce-scatter.2.cloned.1.call-update) | async-done | bytes 65552 | tf_op jit(solution)/shard_map/reduce_scatter | solution.py:209
  (237 shorter events, 118.0 us)
Async XLA Ops:
  7.2 293.2 %reduce-scatter.2.cloned.1.call-start = ((), (), s32[]{:S(2)}) async-start(), calls=%async_computation.1 | async-start | bytes 327680 | tf_op jit(solution)/shard_map/reduce_scatter | solution.py:209
  7.2 23.4 %collective-permute-start.1 = (f32[4,128,512]{2,1,0:T(8,128)}, f32[4,128,512]{2,1,0:T(8,128)S(1)}, u32[]{:S(2)}, u32[]{:S(2)}) collective-permute-start(f32[4,128,512]{2,1,0:T(8,128)} %param.4), channel_id=1, source_target_pairs={{0,4},{4,8},{8,12},{12,16},{16,20},{20,24},{24,28},{28,32},{32,36}... | collective-permute-start | bytes 3145736 | tf_op jit(solution)/shard_map/ppermute | solution.py:116
  11.9 19.1 %collective-permute-start.2 = (f32[4,128,512]{2,1,0:T(8,128)}, f32[4,128,512]{2,1,0:T(8,128)S(1)}, u32[]{:S(2)}, u32[]{:S(2)}) collective-permute-start(f32[4,128,512]{2,1,0:T(8,128)} %param.4), channel_id=1, source_target_pairs={{4,0},{8,4},{12,8},{16,12},{20,16},{24,20},{28,24},{32,28},{36,32}... | collective-permute-start | bytes 3145736 | tf_op jit(solution)/shard_map/ppermute | solution.py:117
  15.7 13.9 %collective-permute-start = (f32[1,128,512]{2,1,0:T(8,128)}, f32[1,128,512]{2,1,0:T(8,128)}, u32[]{:S(2)}, u32[]{:S(2)}) collective-permute-start(f32[1,128,512]{2,1,0:T(8,128)} %get-tuple-element.13), channel_id=1, source_target_pairs={{0,8},{4,12},{8,16},{12,20},{16,24},{20,28},{24,32},{28,36},{32,40... | collective-permute-start | bytes 786440 | tf_op jit(solution)/shard_map/ppermute | solution.py:116
  19.6 11.5 %collective-permute-start.3 = (f32[1,128,512]{2,1,0:T(8,128)}, f32[1,128,512]{2,1,0:T(8,128)S(1)}, u32[]{:S(2)}, u32[]{:S(2)}) collective-permute-start(f32[1,128,512]{2,1,0:T(8,128)} %get-tuple-element.12), channel_id=1, source_target_pairs={{8,0},{12,4},{16,8},{20,12},{24,16},{28,20},{32,24},{36,28},{40,32... | collective-permute-start | bytes 786440 | tf_op jit(solution)/shard_map/ppermute | solution.py:117
  31.2 6.5 %collective-permute-start.4 = (f32[14,5,512]{2,1,0:T(8,128)S(1)}, f32[14,5,512]{2,1,0:T(8,128)S(1)}, u32[]{:S(2)}, u32[]{:S(2)}) collective-permute-start(f32[14,5,512]{2,1,0:T(8,128)S(1)} %get-tuple-element.10), channel_id=1, source_target_pairs={{0,1},{1,2},{2,3},{4,5},{5,6},{6,7},{8,9},{9,10},{10,11},{12,13},{... | collective-permute-start | bytes 430088 | tf_op jit(solution)/shard_map/ppermute | solution.py:116
  34.8 6.9 %collective-permute-start.5 = (f32[14,5,512]{2,1,0:T(8,128)S(1)}, f32[14,5,512]{2,1,0:T(8,128)S(1)}, u32[]{:S(2)}, u32[]{:S(2)}) collective-permute-start(f32[14,5,512]{2,1,0:T(8,128)S(1)} %get-tuple-element.11), channel_id=1, source_target_pairs={{1,0},{2,1},{3,2},{5,4},{6,5},{7,6},{9,8},{10,9},{11,10},{13,12},{... | collective-permute-start | bytes 430088 | tf_op jit(solution)/shard_map/ppermute | solution.py:117
  54.3 9.7 %collective-permute-start.6 = (f32[1,64,256]{2,1,0:T(8,128)S(1)}, f32[1,64,256]{2,1,0:T(8,128)S(1)}, u32[]{:S(2)}, u32[]{:S(2)}) collective-permute-start(f32[1,64,256]{2,1,0:T(8,128)S(1)} %convolution_bitcast_fusion.7), channel_id=1, source_target_pairs={{4,0},{8,4},{12,8},{16,12},{20,16},{24,20},{28,24},{32,28},{36,32}... | collective-permute-start | bytes 196616 | tf_op jit(solution)/shard_map/ppermute | solution.py:21
  71.9 7.2 %collective-permute-start.10 = (f32[1,64,256]{2,1,0:T(8,128)S(1)}, f32[1,64,256]{2,1,0:T(8,128)S(1)}, u32[]{:S(2)}, u32[]{:S(2)}) collective-permute-start(f32[1,64,256]{2,1,0:T(8,128)S(1)} %get-tuple-element.37), channel_id=1, source_target_pairs={{4,0},{8,4},{12,8},{16,12},{20,16},{24,20},{28,24},{32,28},{36,32}... | collective-permute-start | bytes 196616 | tf_op jit(solution)/shard_map/ppermute | solution.py:21
  73.8 6.5 %collective-permute-start.11 = (f32[1,64,256]{2,1,0:T(8,128)S(1)}, f32[1,64,256]{2,1,0:T(8,128)S(1)}, u32[]{:S(2)}, u32[]{:S(2)}) collective-permute-start(f32[1,64,256]{2,1,0:T(8,128)S(1)} %get-tuple-element.36), channel_id=1, source_target_pairs={{0,4},{4,8},{8,12},{12,16},{16,20},{20,24},{24,28},{28,32},{32,36}... | collective-permute-start | bytes 196616 | tf_op jit(solution)/shard_map/ppermute | solution.py:20
  87.3 7.1 %collective-permute-start.14 = (f32[1,64,256]{2,1,0:T(8,128)S(1)}, f32[1,64,256]{2,1,0:T(8,128)S(1)}, u32[]{:S(2)}, u32[]{:S(2)}) collective-permute-start(f32[1,64,256]{2,1,0:T(8,128)S(1)} %get-tuple-element.35), channel_id=1, source_target_pairs={{4,0},{8,4},{12,8},{16,12},{20,16},{24,20},{28,24},{32,28},{36,32}... | collective-permute-start | bytes 196616 | tf_op jit(solution)/shard_map/ppermute | solution.py:21
  89.2 6.5 %collective-permute-start.15 = (f32[1,64,256]{2,1,0:T(8,128)S(1)}, f32[1,64,256]{2,1,0:T(8,128)S(1)}, u32[]{:S(2)}, u32[]{:S(2)}) collective-permute-start(f32[1,64,256]{2,1,0:T(8,128)S(1)} %get-tuple-element.34), channel_id=1, source_target_pairs={{0,4},{4,8},{8,12},{12,16},{16,20},{20,24},{24,28},{28,32},{32,36}... | collective-permute-start | bytes 196616 | tf_op jit(solution)/shard_map/ppermute | solution.py:20
  103.7 7.1 %collective-permute-start.18 = (f32[1,32,128]{2,1,0:T(8,128)S(1)}, f32[1,32,128]{2,1,0:T(8,128)S(1)}, u32[]{:S(2)}, u32[]{:S(2)}) collective-permute-start(f32[1,32,128]{2,1,0:T(8,128)S(1)} %bitcast.74), channel_id=1, source_target_pairs={{4,0},{8,4},{12,8},{16,12},{20,16},{24,20},{28,24},{32,28},{36,32}... | collective-permute-start | bytes 49160 | tf_op jit(solution)/shard_map/ppermute | solution.py:21
  118.4 7.0 %collective-permute-start.22 = (f32[1,32,128]{2,1,0:T(8,128)S(1)}, f32[1,32,128]{2,1,0:T(8,128)S(1)}, u32[]{:S(2)}, u32[]{:S(2)}) collective-permute-start(f32[1,32,128]{2,1,0:T(8,128)S(1)} %fusion.135), channel_id=1, source_target_pairs={{4,0},{8,4},{12,8},{16,12},{20,16},{24,20},{28,24},{32,28},{36,32}... | collective-permute-start | bytes 49160 | tf_op jit(solution)/shard_map/ppermute | solution.py:21
  134.1 7.3 %collective-permute-start.26 = (f32[1,64,256]{2,1,0:T(8,128)}, f32[1,64,256]{2,1,0:T(8,128)}, u32[]{:S(2)}, u32[]{:S(2)}) collective-permute-start(f32[1,64,256]{2,1,0:T(8,128)} %get-tuple-element.39), channel_id=1, source_target_pairs={{4,0},{8,4},{12,8},{16,12},{20,16},{24,20},{28,24},{32,28},{36,32}... | collective-permute-start | bytes 196616 | tf_op jit(solution)/shard_map/ppermute | solution.py:21
  136.0 6.7 %collective-permute-start.27 = (f32[1,64,256]{2,1,0:T(8,128)}, f32[1,64,256]{2,1,0:T(8,128)}, u32[]{:S(2)}, u32[]{:S(2)}) collective-permute-start(f32[1,64,256]{2,1,0:T(8,128)} %get-tuple-element.39), channel_id=1, source_target_pairs={{0,4},{4,8},{8,12},{12,16},{16,20},{20,24},{24,28},{28,32},{32,36}... | collective-permute-start | bytes 196616 | tf_op jit(solution)/shard_map/ppermute | solution.py:20
  145.5 7.0 %collective-permute-start.28 = (f32[4,1,256]{2,1,0:T(1,128)}, f32[4,1,256]{2,1,0:T(1,128)}, u32[]{:S(2)}, u32[]{:S(2)}) collective-permute-start(f32[4,1,256]{2,1,0:T(1,128)} %get-tuple-element.23), channel_id=1, source_target_pairs={{1,0},{2,1},{3,2},{5,4},{6,5},{7,6},{9,8},{10,9},{11,10},{13,12},{... | collective-permute-start | bytes 12296 | tf_op jit(solution)/shard_map/ppermute | solution.py:21
  155.1 6.7 %collective-permute-start.30 = (f32[1,64,256]{2,1,0:T(8,128)S(1)}, f32[1,64,256]{2,1,0:T(8,128)S(1)}, u32[]{:S(2)}, u32[]{:S(2)}) collective-permute-start(f32[1,64,256]{2,1,0:T(8,128)S(1)} %get-tuple-element.33), channel_id=1, source_target_pairs={{4,0},{8,4},{12,8},{16,12},{20,16},{24,20},{28,24},{32,28},{36,32}... | collective-permute-start | bytes 196616 | tf_op jit(solution)/shard_map/ppermute | solution.py:21
  163.1 7.3 %collective-permute-start.32 = (f32[4,1,256]{2,1,0:T(1,128)S(1)}, f32[4,1,256]{2,1,0:T(1,128)S(1)}, u32[]{:S(2)}, u32[]{:S(2)}) collective-permute-start(f32[4,1,256]{2,1,0:T(1,128)S(1)} %get-tuple-element.21), channel_id=1, source_target_pairs={{1,0},{2,1},{3,2},{5,4},{6,5},{7,6},{9,8},{10,9},{11,10},{13,12},{... | collective-permute-start | bytes 12296 | tf_op jit(solution)/shard_map/ppermute | solution.py:21
  170.7 6.5 %collective-permute-start.34 = (f32[1,64,256]{2,1,0:T(8,128)S(1)}, f32[1,64,256]{2,1,0:T(8,128)S(1)}, u32[]{:S(2)}, u32[]{:S(2)}) collective-permute-start(f32[1,64,256]{2,1,0:T(8,128)S(1)} %get-tuple-element.31), channel_id=1, source_target_pairs={{4,0},{8,4},{12,8},{16,12},{20,16},{24,20},{28,24},{32,28},{36,32}... | collective-permute-start | bytes 196616 | tf_op jit(solution)/shard_map/ppermute | solution.py:21
  185.6 7.1 %collective-permute-start.38 = (f32[2,64,256]{2,1,0:T(8,128)S(1)}, f32[2,64,256]{2,1,0:T(8,128)S(1)}, u32[]{:S(2)}, u32[]{:S(2)}) collective-permute-start(f32[2,64,256]{2,1,0:T(8,128)S(1)} %fusion.73), channel_id=1, source_target_pairs={{0,4},{4,8},{8,12},{12,16},{16,20},{20,24},{24,28},{28,32},{32,36}... | collective-permute-start | bytes 393224 | tf_op jit(solution)/shard_map/ppermute | solution.py:116
  190.7 6.3 %collective-permute-start.39 = (f32[2,64,256]{2,1,0:T(8,128)S(1)}, f32[2,64,256]{2,1,0:T(8,128)S(1)}, u32[]{:S(2)}, u32[]{:S(2)}) collective-permute-start(f32[2,64,256]{2,1,0:T(8,128)S(1)} %fusion.73), channel_id=1, source_target_pairs={{4,0},{8,4},{12,8},{16,12},{20,16},{24,20},{28,24},{32,28},{36,32}... | collective-permute-start | bytes 393224 | tf_op jit(solution)/shard_map/ppermute | solution.py:117
  197.7 8.3 %collective-permute-start.40 = (f32[6,2,256]{2,1,0:T(2,128)S(1)}, f32[6,2,256]{2,1,0:T(2,128)S(1)}, u32[]{:S(2)}, u32[]{:S(2)}) collective-permute-start(f32[6,2,256]{2,1,0:T(2,128)S(1)} %get-tuple-element.16), channel_id=1, source_target_pairs={{0,1},{1,2},{2,3},{4,5},{5,6},{6,7},{8,9},{9,10},{10,11},{12,13},{... | collective-permute-start | bytes 36872 | tf_op jit(solution)/shard_map/ppermute | solution.py:116
  230.2 45.6 %collective-permute-start.45 = (f32[128,512]{1,0:T(8,128)S(1)}, f32[128,512]{1,0:T(8,128)S(1)}, u32[]{:S(2)}, u32[]{:S(2)}) collective-permute-start(f32[128,512]{1,0:T(8,128)S(1)} %get-tuple-element.2), channel_id=1, source_target_pairs={{0,8},{16,24},{32,40},{48,56},{64,72},{80,88},{96,104},{112,120},{... | collective-permute-start | bytes 786440 | tf_op jit(solution)/shard_map/ppermute | solution.py:221
  (51 other events, 484.6 us)
Sparse Core Ops, SparseCore 0:
  279.7 20.5 reduce-scatter.1

commit v2 on v1

--- a/solution.py
+++ b/solution.py
@@ -141,6 +141,60 @@
 
 def core(field, width, block_x, block_y):
     return field[width:width + block_x, width:width + block_y]
+
+
+def shift_planes(x, axis, distance, first, last, upward):
+    peers = lax.axis_size(axis)
+    pairs = [(j, j + distance) for j in range(peers - distance)]
+    if not upward:
+        pairs = [(b, a) for a, b in pairs]
+    return lax.ppermute(x[first:last], axis, pairs)
+
+
+def medium_cycle(medium):
+    block_x, block_y = medium.shape[0], medium.shape[1]
+    grown = extend(extend(medium, "slab", 0, 3), "pencil", 1, 3)
+    powers = [grown]
+    for width in (2, 1, 0):
+        centre, total = shrink_neighbours(powers[-1])
+        powers.append(lax.optimization_barrier(masked(smoothed(centre, total), block_x, block_y, width)))
+    grad_medium = coefficient(1) * core(powers[0], 3, block_x, block_y)
+    grad_medium = grad_medium + coefficient(1) * core(powers[1], 2, block_x, block_y)
+    grad_medium = grad_medium + coefficient(1) * core(powers[2], 1, block_x, block_y)
+    settled = powers[3]
+    coarse_cot = children_sum(settled)
+    coarse_x, coarse_y = coarse_cot.shape[0], coarse_cot.shape[1]
+    grown = extend(extend(coarse_cot, "slab", 0, 2), "pencil", 1, 2)
+    coarse_powers = [grown]
+    for width in (1, 0):
+        centre, total = shrink_neighbours(coarse_powers[-1])
+        coarse_powers.append(lax.optimization_barrier(masked(smoothed(centre, total), coarse_x, coarse_y, width)))
+    grad_coarse = coefficient(2) * core(coarse_powers[0], 2, coarse_x, coarse_y)
+    grad_coarse = grad_coarse + coefficient(2) * core(coarse_powers[1], 1, coarse_x, coarse_y)
+    grad_coarse = grad_coarse + coefficient(2) * coarse_powers[2]
+    back_medium = prolong(grad_coarse) * 0.125
+    both = jnp.concatenate([back_medium, settled], axis=0)
+    near_low = shift_planes(both, "slab", 1, 0, 2 * block_x, True)
+    near_high = shift_planes(both, "slab", 1, 0, 2 * block_x, False)
+    far_low = shift_planes(back_medium, "slab", 2, block_x - 1, block_x, True)
+    far_high = shift_planes(back_medium, "slab", 2, 0, 1, False)
+    back_x = jnp.concatenate(
+        [far_low, near_low[:block_x], back_medium, near_high[:block_x], far_high], axis=0
+    )
+    settled_x = jnp.concatenate([near_low[block_x:], settled, near_high[block_x:]], axis=0)
+    stacked = extend(jnp.concatenate([back_x, settled_x], axis=0), "pencil", 1, 3)
+    back_xy = stacked[:block_x + 6]
+    settled_xy = stacked[block_x + 6:, 1:-1]
+    grad_medium = grad_medium + back_medium
+    centre, total = shrink_neighbours(back_xy)
+    stage = masked(settled_xy - (6.0 * centre - total) / 4.0, block_x, block_y, 2)
+    stage = lax.optimization_barrier(stage)
+    for width in (2, 1, 0):
+        grad_medium = grad_medium + coefficient(1) * core(stage, width, block_x, block_y)
+        if width > 0:
+            centre, total = shrink_neighbours(stage)
+            stage = lax.optimization_barrier(masked(smoothed(centre, total), block_x, block_y, width - 1))
+    return grad_medium
 
 
 def shards(cotangent, seg_rows, owners, offsets):
@@ -158,22 +212,7 @@
         rhs_grad = rhs_grad + coefficient(0) * part
     grad_fine = core(powers[3], depth - 3, x_cells, y_cells)
     medium = children_sum(grad_fine)
-    grad_medium = jnp.zeros_like(medium)
-    for sweep_number in range(3):
-        grad_medium = grad_medium + coefficient(1) * medium
-        medium = smoothed(medium, block_neighbours(medium))
-    coarse_cot = children_sum(medium)
-    grad_coarse = coefficient(2) * coarse_cot
-    for sweep_number in range(2):
-        coarse_cot = smoothed(coarse_cot, coarse_neighbours(coarse_cot))
-        grad_coarse = grad_coarse + coefficient(2) * coarse_cot
-    back_medium = prolong(grad_coarse) * 0.125
-    grad_medium = grad_medium + back_medium
-    medium = medium - (6.0 * back_medium - block_neighbours(back_medium)) / 4.0
-    for sweep_number in range(3):
-        grad_medium = grad_medium + coefficient(1) * medium
-        if sweep_number < 2:
-            medium = smoothed(medium, block_neighbours(medium))
+    grad_medium = medium_cycle(medium)
     grown = extend(extend(grad_medium, "slab", 0, 2), "pencil", 1, 2)
     back_fine = prolong(grown)[1:-1, 1:-1] * 0.125
     rhs_grad = rhs_grad + core(back_fine, 3, x_cells, y_cells)

time: 311 us -> 252 us (0.81)
  starting transfers between devices: 138 us -> 83.5 us
  waiting for transfers between devices: 99.4 us -> 85.5 us
  local copies, waits for them, and re-layouts: 16.5 us -> 22.6 us
    ppermute x32 -> x4, starting transfers between devices: 105 us -> 12.3 us  [shift_planes(): return lax.ppermute(x[first:last], axis, pairs)]
    ppermute x5 -> x12, starting transfers between devices: 21.3 us -> 49.6 us  [extend(): lows.insert(0, lax.ppermute(low_piece, axis, up))]
    ppermute x5, waiting for transfers between devices: 45.5 us -> 27 us  [spread_faces(): got = lax.ppermute(sent, 'slab', low_pairs + high_pairs)]
    ppermute x5 -> x12, waiting for transfers between devices: 9.26 us -> 25.1 us  [extend(): highs.append(lax.ppermute(high_piece, axis, down))]
    ppermute x5 -> x12, starting transfers between devices: 7.71 us -> 18.2 us  [extend(): highs.append(lax.ppermute(high_piece, axis, down))]
    ppermute x32 -> x4, waiting for transfers between devices: 13.9 us -> 5.85 us  [shift_planes(): return lax.ppermute(x[first:last], axis, pairs)]
    unnamed x58 -> x80, local copies, waits for them, and re-layouts: 6.06 us -> 12.2 us
    concatenate x16 -> x1, other arithmetic: 3.87 us -> 0.02 us  [medium_cycle(): both = jnp.concatenate([back_medium, settled], axis=0)]
  transfers between devices with their start and end apart: 48 -> 34, of which waited for: 24 -> 17; matrix products, arithmetic and copies ran while one was open for 3% -> 5% of each run, Pallas kernels for 0% -> 0%
where the time goes in v2:
time: 252 us; the launch traced here: 249 us
  waiting for transfers between devices  85.5 us (34%)
  starting transfers between devices  83.5 us (33%)
  other arithmetic  31.8 us (13%)
  local copies, waits for them, and re-layouts  22.6 us (9%)
  between operations  15.5 us (6%)
  matrix products  10.3 us (4%)
    ppermute x12, starting transfers between devices, extend(): lows.insert(0, lax.ppermute(low_piece, axis, up))  49.6 us
    ppermute x5, waiting for transfers between devices, spread_faces(): got = lax.ppermute(sent, 'slab', low_pairs + high_pairs)  27 us
    ppermute x12, waiting for transfers between devices, extend(): highs.append(lax.ppermute(high_piece, axis, down))  25.1 us
    reduce_scatter x1, waiting for transfers between devices, shards(): lax.psum_scatter(partial, 'pencil', scatter_dimension=0, tiled=True)  18.6 us
    ppermute x12, starting transfers between devices, extend(): highs.append(lax.ppermute(high_piece, axis, down))  18.2 us
    select_n x14, other arithmetic, masked(): return jnp.where(keep, field, 0.0)  17.8 us
    ppermute x4, starting transfers between devices, shift_planes(): return lax.ppermute(x[first:last], axis, pairs)  12.3 us
    unnamed x80, local copies, waits for them, and re-layouts  12.2 us
  transfers between devices with their start and end apart: 34, of which 17 were waited for; matrix products, arithmetic and copies ran while one was open for 5% of the time, Pallas kernels for 0%

profile of v2, /device:TPU:1, one launch (start us, length us, event | category | flops | bytes accessed | tf_op | source)
XLA Modules:
  0.0 249.3 jit_solution(15095190516044255806)
XLA Ops:
  7.2 4.7 %collective-permute-start.1 = (f32[4,128,512]{2,1,0:T(8,128)}, f32[4,128,512]{2,1,0:T(8,128)S(1)}, u32[]{:S(2)}, u32[]{:S(2)}) collective-permute-start(f32[4,128,512]{2,1,0:T(8,128)} %param.4), channel_id=1, source_target_pairs={{0,4},{4,8},{8,12},{12,16},{16,20},{20,24},{24,28},{28,32},{32,36}... | collective-permute-start | bytes 3145736 | tf_op jit(solution)/shard_map/ppermute | solution.py:116
  15.7 3.9 %collective-permute-start = (f32[1,128,512]{2,1,0:T(8,128)}, f32[1,128,512]{2,1,0:T(8,128)}, u32[]{:S(2)}, u32[]{:S(2)}) collective-permute-start(f32[1,128,512]{2,1,0:T(8,128)} %get-tuple-element.11), channel_id=1, source_target_pairs={{0,8},{4,12},{8,16},{12,20},{16,24},{20,28},{24,32},{28,36},{32,40... | collective-permute-start | bytes 786440 | tf_op jit(solution)/shard_map/ppermute | solution.py:116
  22.3 7.3 %collective-permute-done = f32[1,128,512]{2,1,0:T(8,128)} collective-permute-done((f32[1,128,512]{2,1,0:T(8,128)}, f32[1,128,512]{2,1,0:T(8,128)}, u32[]{:S(2)}, u32[]{:S(2)}) %collective-permute-start) | collective-permute-done | bytes 262176 | tf_op jit(solution)/shard_map/ppermute | solution.py:116
  31.2 3.6 %collective-permute-start.4 = (f32[14,5,512]{2,1,0:T(8,128)S(1)}, f32[14,5,512]{2,1,0:T(8,128)S(1)}, u32[]{:S(2)}, u32[]{:S(2)}) collective-permute-start(f32[14,5,512]{2,1,0:T(8,128)S(1)} %get-tuple-element.8), channel_id=1, source_target_pairs={{0,1},{1,2},{2,3},{4,5},{5,6},{6,7},{8,9},{9,10},{10,11},{12,13},{... | collective-permute-start | bytes 430088 | tf_op jit(solution)/shard_map/ppermute | solution.py:116
  37.7 4.0 %collective-permute-done.5 = f32[14,5,512]{2,1,0:T(8,128)S(1)} collective-permute-done((f32[14,5,512]{2,1,0:T(8,128)S(1)}, f32[14,5,512]{2,1,0:T(8,128)S(1)}, u32[]{:S(2)}, u32[]{:S(2)}) %collective-permute-start.5) | collective-permute-done | bytes 143392 | tf_op jit(solution)/shard_map/ppermute | solution.py:117
  43.3 3.1 %fusion.4 = f32[12,136,512]{2,1,0:T(8,128)S(1)} fusion(f32[12,136,512]{2,1,0:T(8,128)S(1)} %slice.617, f32[14,138,512]{2,1,0:T(8,128)S(1)} %pad_maximum_fusion, pred[12,136]{1,0:T(8,128)(4,1)S(1)} %broadcast_and_fusion.1), kind=kLoop, calls=%fused_computation.9 | loop fusion | flops 7520256 | bytes 20055648 | tf_op jit(solution)/shard_map/jit(_where)/select_n | solution.py:130
  55.7 4.1 %collective-permute-start.6 = (f32[1,64,256]{2,1,0:T(8,128)S(1)}, f32[1,64,256]{2,1,0:T(8,128)}, u32[]{:S(2)}, u32[]{:S(2)}) collective-permute-start(f32[1,64,256]{2,1,0:T(8,128)S(1)} %convolution_bitcast_fusion.6), channel_id=1, source_target_pairs={{0,8},{4,12},{8,16},{12,20},{16,24},{20,28},{24,32},{28,36},{32,40... | collective-permute-start | bytes 196616 | tf_op jit(solution)/shard_map/ppermute | solution.py:116
  60.5 6.8 %collective-permute-start.7 = (f32[2,64,256]{2,1,0:T(8,128)}, f32[2,64,256]{2,1,0:T(8,128)}, u32[]{:S(2)}, u32[]{:S(2)}) collective-permute-start(f32[2,64,256]{2,1,0:T(8,128)} %pad_maximum_fusion.6), channel_id=1, source_target_pairs={{0,4},{4,8},{8,12},{12,16},{16,20},{20,24},{24,28},{28,32},{32,36}... | collective-permute-start | bytes 393224 | tf_op jit(solution)/shard_map/ppermute | solution.py:116
  77.8 3.5 %collective-permute-start.10 = (f32[8,3,256]{2,1,0:T(4,128)}, f32[8,3,256]{2,1,0:T(4,128)S(1)}, u32[]{:S(2)}, u32[]{:S(2)}) collective-permute-start(f32[8,3,256]{2,1,0:T(4,128)} %get-tuple-element.16), channel_id=1, source_target_pairs={{0,1},{1,2},{2,3},{4,5},{5,6},{6,7},{8,9},{9,10},{10,11},{12,13},{... | collective-permute-start | bytes 73736 | tf_op jit(solution)/shard_map/ppermute | solution.py:116
  83.2 3.0 %collective-permute-done.11 = f32[8,3,256]{2,1,0:T(4,128)S(1)} collective-permute-done((f32[8,3,256]{2,1,0:T(4,128)}, f32[8,3,256]{2,1,0:T(4,128)S(1)}, u32[]{:S(2)}, u32[]{:S(2)}) %collective-permute-start.11) | collective-permute-done | bytes 24608 | tf_op jit(solution)/shard_map/ppermute | solution.py:117
  92.3 4.9 %collective-permute-start.12 = (f32[1,32,128]{2,1,0:T(8,128)S(1)}, f32[1,32,128]{2,1,0:T(8,128)}, u32[]{:S(2)}, u32[]{:S(2)}) collective-permute-start(f32[1,32,128]{2,1,0:T(8,128)S(1)} %bitcast.76), channel_id=1, source_target_pairs={{0,8},{4,12},{8,16},{12,20},{16,24},{20,28},{24,32},{28,36},{32,40... | collective-permute-start | bytes 49160 | tf_op jit(solution)/shard_map/ppermute | solution.py:116
  97.7 5.0 %collective-permute-start.13 = (f32[1,32,128]{2,1,0:T(8,128)S(1)}, f32[1,32,128]{2,1,0:T(8,128)S(1)}, u32[]{:S(2)}, u32[]{:S(2)}) collective-permute-start(f32[1,32,128]{2,1,0:T(8,128)S(1)} %bitcast.77), channel_id=1, source_target_pairs={{0,4},{4,8},{8,12},{12,16},{16,20},{20,24},{24,28},{28,32},{32,36}... | collective-permute-start | bytes 49160 | tf_op jit(solution)/shard_map/ppermute | solution.py:116
  110.1 3.3 %collective-permute-start.16 = (f32[5,2,128]{2,1,0:T(2,128)S(1)}, f32[5,2,128]{2,1,0:T(2,128)S(1)}, u32[]{:S(2)}, u32[]{:S(2)}) collective-permute-start(f32[5,2,128]{2,1,0:T(2,128)S(1)} %get-tuple-element.20), channel_id=1, source_target_pairs={{0,1},{1,2},{2,3},{4,5},{5,6},{6,7},{8,9},{9,10},{10,11},{12,13},{... | collective-permute-start | bytes 15368 | tf_op jit(solution)/shard_map/ppermute | solution.py:116
  114.7 3.0 %collective-permute-done.17 = f32[5,2,128]{2,1,0:T(2,128)S(1)} collective-permute-done((f32[5,2,128]{2,1,0:T(2,128)S(1)}, f32[5,2,128]{2,1,0:T(2,128)S(1)}, u32[]{:S(2)}, u32[]{:S(2)}) %collective-permute-start.17) | collective-permute-done | bytes 5152 | tf_op jit(solution)/shard_map/ppermute | solution.py:117
  121.2 5.5 %collective-permute-start.19 = (f32[4,64,256]{2,1,0:T(8,128)S(1)}, f32[4,64,256]{2,1,0:T(8,128)S(1)}, u32[]{:S(2)}, u32[]{:S(2)}) collective-permute-start(f32[4,64,256]{2,1,0:T(8,128)S(1)} %pad_maximum_fusion.5), channel_id=1, source_target_pairs={{0,4},{4,8},{8,12},{12,16},{16,20},{20,24},{24,28},{28,32},{32,36}... | collective-permute-start | bytes 786440 | tf_op jit(solution)/shard_map/ppermute | solution.py:151
  127.5 3.6 %collective-permute-start.18 = (f32[1,64,256]{2,1,0:T(8,128)S(1)}, f32[1,64,256]{2,1,0:T(8,128)S(1)}, u32[]{:S(2)}, u32[]{:S(2)}) collective-permute-start(f32[1,64,256]{2,1,0:T(8,128)S(1)} %bitcast.73), channel_id=1, source_target_pairs={{0,8},{4,12},{8,16},{12,20},{16,24},{20,28},{24,32},{28,36},{32,40... | collective-permute-start | bytes 196616 | tf_op jit(solution)/shard_map/ppermute | solution.py:151
  134.4 4.6 %collective-permute-done.20 = f32[4,64,256]{2,1,0:T(8,128)S(1)} collective-permute-done((f32[4,64,256]{2,1,0:T(8,128)S(1)}, f32[4,64,256]{2,1,0:T(8,128)S(1)}, u32[]{:S(2)}, u32[]{:S(2)}) %collective-permute-start.20) | collective-permute-done | bytes 262176 | tf_op jit(solution)/shard_map/ppermute | solution.py:151
  143.4 3.6 %collective-permute-done.23 = f32[14,3,256]{2,1,0:T(4,128)S(1)} collective-permute-done((f32[14,3,256]{2,1,0:T(4,128)S(1)}, f32[14,3,256]{2,1,0:T(4,128)S(1)}, u32[]{:S(2)}, u32[]{:S(2)}) %collective-permute-start.23) | collective-permute-done | bytes 43040 | tf_op jit(solution)/shard_map/ppermute | solution.py:117
  149.4 6.5 %collective-permute-start.24 = (f32[2,64,256]{2,1,0:T(8,128)S(1)}, f32[2,64,256]{2,1,0:T(8,128)S(1)}, u32[]{:S(2)}, u32[]{:S(2)}) collective-permute-start(f32[2,64,256]{2,1,0:T(8,128)S(1)} %fusion.102), channel_id=1, source_target_pairs={{0,4},{4,8},{8,12},{12,16},{16,20},{20,24},{24,28},{28,32},{32,36}... | collective-permute-start | bytes 393224 | tf_op jit(solution)/shard_map/ppermute | solution.py:116
  158.0 4.3 %collective-permute-done.25 = f32[2,64,256]{2,1,0:T(8,128)S(1)} collective-permute-done((f32[2,64,256]{2,1,0:T(8,128)S(1)}, f32[2,64,256]{2,1,0:T(8,128)S(1)}, u32[]{:S(2)}, u32[]{:S(2)}) %collective-permute-start.25) | collective-permute-done | bytes 131104 | tf_op jit(solution)/shard_map/ppermute | solution.py:117
  166.1 3.0 %slice.635 = f32[6,130,512]{2,1,0:T(8,128)} slice(f32[8,132,512]{2,1,0:T(8,128)} %copy-done.1), slice={[1:7], [1:131], [0:512]} | slice | bytes 3194880 | tf_op jit(solution)/shard_map/slice | solution.py:134
  180.4 3.1 %fusion.30 = (f32[6,130,512]{2,1,0:T(8,128)S(1)}, f32[6,130,512]{2,1,0:T(8,128)S(1)}) fusion(f32[6,130,512]{2,1,0:T(8,128)S(1)} %slice.712, f32[8,132,512]{2,1,0:T(8,128)S(1)} %fusion.18, pred[6,130]{1,0:T(8,128)(4,1)S(1)} %broadcast_and_fusion.2, f32[6,130,512]{2,1,0:T(8,128)S(1)} %copy-done.4, f32[8,132,512]{2,1,0:T(8,128)S(1)} %copy-done.2), kind=kLoop, calls=%fused_computation.56 | loop fusion | flops 7188480 | bytes 19170060 | tf_op jit(solution)/shard_map/jit(_where)/select_n | solution.py:130
  194.2 25.7 %collective-permute-done.31 = f32[128,512]{1,0:T(8,128)S(1)} collective-permute-done((f32[128,512]{1,0:T(8,128)S(1)}, f32[128,512]{1,0:T(8,128)S(1)}, u32[]{:S(2)}, u32[]{:S(2)}) %collective-permute-start.31) | collective-permute-done | bytes 262176 | tf_op jit(solution)/shard_map/ppermute | solution.py:260
  223.8 18.6 %reduce-scatter.2.cloned.1.call-done = f32[1,128,128]{2,1,0:T(8,128)} async-done(((f32[4,128,128]{2,1,0:T(8,128)}), f32[1,128,128]{2,1,0:T(8,128)}) %reduce-scatter.2.cloned.1.call-update) | async-done | bytes 65552 | tf_op jit(solution)/shard_map/reduce_scatter | solution.py:248
  (246 shorter events, 95.1 us)
Async XLA Ops:
  7.2 235.2 %reduce-scatter.2.cloned.1.call-start = ((), (), s32[]{:S(2)}) async-start(), calls=%async_computation.1 | async-start | bytes 327680 | tf_op jit(solution)/shard_map/reduce_scatter | solution.py:248
  7.2 23.4 %collective-permute-start.1 = (f32[4,128,512]{2,1,0:T(8,128)}, f32[4,128,512]{2,1,0:T(8,128)S(1)}, u32[]{:S(2)}, u32[]{:S(2)}) collective-permute-start(f32[4,128,512]{2,1,0:T(8,128)} %param.4), channel_id=1, source_target_pairs={{0,4},{4,8},{8,12},{12,16},{16,20},{20,24},{24,28},{28,32},{32,36}... | collective-permute-start | bytes 3145736 | tf_op jit(solution)/shard_map/ppermute | solution.py:116
  11.9 19.1 %collective-permute-start.2 = (f32[4,128,512]{2,1,0:T(8,128)}, f32[4,128,512]{2,1,0:T(8,128)S(1)}, u32[]{:S(2)}, u32[]{:S(2)}) collective-permute-start(f32[4,128,512]{2,1,0:T(8,128)} %param.4), channel_id=1, source_target_pairs={{4,0},{8,4},{12,8},{16,12},{20,16},{24,20},{28,24},{32,28},{36,32}... | collective-permute-start | bytes 3145736 | tf_op jit(solution)/shard_map/ppermute | solution.py:117
  15.7 13.9 %collective-permute-start = (f32[1,128,512]{2,1,0:T(8,128)}, f32[1,128,512]{2,1,0:T(8,128)}, u32[]{:S(2)}, u32[]{:S(2)}) collective-permute-start(f32[1,128,512]{2,1,0:T(8,128)} %get-tuple-element.11), channel_id=1, source_target_pairs={{0,8},{4,12},{8,16},{12,20},{16,24},{20,28},{24,32},{28,36},{32,40... | collective-permute-start | bytes 786440 | tf_op jit(solution)/shard_map/ppermute | solution.py:116
  19.7 11.5 %collective-permute-start.3 = (f32[1,128,512]{2,1,0:T(8,128)}, f32[1,128,512]{2,1,0:T(8,128)S(1)}, u32[]{:S(2)}, u32[]{:S(2)}) collective-permute-start(f32[1,128,512]{2,1,0:T(8,128)} %get-tuple-element.10), channel_id=1, source_target_pairs={{8,0},{12,4},{16,8},{20,12},{24,16},{28,20},{32,24},{36,28},{40,32... | collective-permute-start | bytes 786440 | tf_op jit(solution)/shard_map/ppermute | solution.py:117
  31.2 6.5 %collective-permute-start.4 = (f32[14,5,512]{2,1,0:T(8,128)S(1)}, f32[14,5,512]{2,1,0:T(8,128)S(1)}, u32[]{:S(2)}, u32[]{:S(2)}) collective-permute-start(f32[14,5,512]{2,1,0:T(8,128)S(1)} %get-tuple-element.8), channel_id=1, source_target_pairs={{0,1},{1,2},{2,3},{4,5},{5,6},{6,7},{8,9},{9,10},{10,11},{12,13},{... | collective-permute-start | bytes 430088 | tf_op jit(solution)/shard_map/ppermute | solution.py:116
  34.8 6.9 %collective-permute-start.5 = (f32[14,5,512]{2,1,0:T(8,128)S(1)}, f32[14,5,512]{2,1,0:T(8,128)S(1)}, u32[]{:S(2)}, u32[]{:S(2)}) collective-permute-start(f32[14,5,512]{2,1,0:T(8,128)S(1)} %get-tuple-element.9), channel_id=1, source_target_pairs={{1,0},{2,1},{3,2},{5,4},{6,5},{7,6},{9,8},{10,9},{11,10},{13,12},{... | collective-permute-start | bytes 430088 | tf_op jit(solution)/shard_map/ppermute | solution.py:117
  55.7 15.4 %collective-permute-start.6 = (f32[1,64,256]{2,1,0:T(8,128)S(1)}, f32[1,64,256]{2,1,0:T(8,128)}, u32[]{:S(2)}, u32[]{:S(2)}) collective-permute-start(f32[1,64,256]{2,1,0:T(8,128)S(1)} %convolution_bitcast_fusion.6), channel_id=1, source_target_pairs={{0,8},{4,12},{8,16},{12,20},{16,24},{20,28},{24,32},{28,36},{32,40... | collective-permute-start | bytes 196616 | tf_op jit(solution)/shard_map/ppermute | solution.py:116
  60.5 11.5 %collective-permute-start.7 = (f32[2,64,256]{2,1,0:T(8,128)}, f32[2,64,256]{2,1,0:T(8,128)}, u32[]{:S(2)}, u32[]{:S(2)}) collective-permute-start(f32[2,64,256]{2,1,0:T(8,128)} %pad_maximum_fusion.6), channel_id=1, source_target_pairs={{0,4},{4,8},{8,12},{12,16},{16,20},{20,24},{24,28},{28,32},{32,36}... | collective-permute-start | bytes 393224 | tf_op jit(solution)/shard_map/ppermute | solution.py:116
  67.9 6.5 %collective-permute-start.8 = (f32[2,64,256]{2,1,0:T(8,128)}, f32[2,64,256]{2,1,0:T(8,128)S(1)}, u32[]{:S(2)}, u32[]{:S(2)}) collective-permute-start(f32[2,64,256]{2,1,0:T(8,128)} %pad_maximum_fusion.6), channel_id=1, source_target_pairs={{4,0},{8,4},{12,8},{16,12},{20,16},{24,20},{28,24},{32,28},{36,32}... | collective-permute-start | bytes 393224 | tf_op jit(solution)/shard_map/ppermute | solution.py:117
  69.8 6.5 %collective-permute-start.9 = (f32[1,64,256]{2,1,0:T(8,128)S(1)}, f32[1,64,256]{2,1,0:T(8,128)S(1)}, u32[]{:S(2)}, u32[]{:S(2)}) collective-permute-start(f32[1,64,256]{2,1,0:T(8,128)S(1)} %convolution_bitcast_fusion.7), channel_id=1, source_target_pairs={{8,0},{12,4},{16,8},{20,12},{24,16},{28,20},{32,24},{36,28},{40,32... | collective-permute-start | bytes 196616 | tf_op jit(solution)/shard_map/ppermute | solution.py:117
  77.8 5.4 %collective-permute-start.10 = (f32[8,3,256]{2,1,0:T(4,128)}, f32[8,3,256]{2,1,0:T(4,128)S(1)}, u32[]{:S(2)}, u32[]{:S(2)}) collective-permute-start(f32[8,3,256]{2,1,0:T(4,128)} %get-tuple-element.16), channel_id=1, source_target_pairs={{0,1},{1,2},{2,3},{4,5},{5,6},{6,7},{8,9},{9,10},{10,11},{12,13},{... | collective-permute-start | bytes 73736 | tf_op jit(solution)/shard_map/ppermute | solution.py:116
  92.3 13.6 %collective-permute-start.12 = (f32[1,32,128]{2,1,0:T(8,128)S(1)}, f32[1,32,128]{2,1,0:T(8,128)}, u32[]{:S(2)}, u32[]{:S(2)}) collective-permute-start(f32[1,32,128]{2,1,0:T(8,128)S(1)} %bitcast.76), channel_id=1, source_target_pairs={{0,8},{4,12},{8,16},{12,20},{16,24},{20,28},{24,32},{28,36},{32,40... | collective-permute-start | bytes 49160 | tf_op jit(solution)/shard_map/ppermute | solution.py:116
  97.7 8.9 %collective-permute-start.13 = (f32[1,32,128]{2,1,0:T(8,128)S(1)}, f32[1,32,128]{2,1,0:T(8,128)S(1)}, u32[]{:S(2)}, u32[]{:S(2)}) collective-permute-start(f32[1,32,128]{2,1,0:T(8,128)S(1)} %bitcast.77), channel_id=1, source_target_pairs={{0,4},{4,8},{8,12},{12,16},{16,20},{20,24},{24,28},{28,32},{32,36}... | collective-permute-start | bytes 49160 | tf_op jit(solution)/shard_map/ppermute | solution.py:116
  102.7 5.1 %collective-permute-start.14 = (f32[1,32,128]{2,1,0:T(8,128)S(1)}, f32[1,32,128]{2,1,0:T(8,128)S(1)}, u32[]{:S(2)}, u32[]{:S(2)}) collective-permute-start(f32[1,32,128]{2,1,0:T(8,128)S(1)} %bitcast.78), channel_id=1, source_target_pairs={{4,0},{8,4},{12,8},{16,12},{20,16},{24,20},{28,24},{32,28},{36,32}... | collective-permute-start | bytes 49160 | tf_op jit(solution)/shard_map/ppermute | solution.py:117
  104.6 5.5 %collective-permute-start.15 = (f32[1,32,128]{2,1,0:T(8,128)S(1)}, f32[1,32,128]{2,1,0:T(8,128)S(1)}, u32[]{:S(2)}, u32[]{:S(2)}) collective-permute-start(f32[1,32,128]{2,1,0:T(8,128)S(1)} %bitcast.79), channel_id=1, source_target_pairs={{8,0},{12,4},{16,8},{20,12},{24,16},{28,20},{32,24},{36,28},{40,32... | collective-permute-start | bytes 49160 | tf_op jit(solution)/shard_map/ppermute | solution.py:117
  121.2 13.1 %collective-permute-start.19 = (f32[4,64,256]{2,1,0:T(8,128)S(1)}, f32[4,64,256]{2,1,0:T(8,128)S(1)}, u32[]{:S(2)}, u32[]{:S(2)}) collective-permute-start(f32[4,64,256]{2,1,0:T(8,128)S(1)} %pad_maximum_fusion.5), channel_id=1, source_target_pairs={{0,4},{4,8},{8,12},{12,16},{16,20},{20,24},{24,28},{28,32},{32,36}... | collective-permute-start | bytes 786440 | tf_op jit(solution)/shard_map/ppermute | solution.py:151
  127.5 6.9 %collective-permute-start.18 = (f32[1,64,256]{2,1,0:T(8,128)S(1)}, f32[1,64,256]{2,1,0:T(8,128)S(1)}, u32[]{:S(2)}, u32[]{:S(2)}) collective-permute-start(f32[1,64,256]{2,1,0:T(8,128)S(1)} %bitcast.73), channel_id=1, source_target_pairs={{0,8},{4,12},{8,16},{12,20},{16,24},{20,28},{24,32},{28,36},{32,40... | collective-permute-start | bytes 196616 | tf_op jit(solution)/shard_map/ppermute | solution.py:151
  131.1 7.9 %collective-permute-start.20 = (f32[4,64,256]{2,1,0:T(8,128)S(1)}, f32[4,64,256]{2,1,0:T(8,128)S(1)}, u32[]{:S(2)}, u32[]{:S(2)}) collective-permute-start(f32[4,64,256]{2,1,0:T(8,128)S(1)} %pad_maximum_fusion.5), channel_id=1, source_target_pairs={{4,0},{8,4},{12,8},{16,12},{20,16},{24,20},{28,24},{32,28},{36,32}... | collective-permute-start | bytes 786440 | tf_op jit(solution)/shard_map/ppermute | solution.py:151
  133.0 7.2 %collective-permute-start.21 = (f32[1,64,256]{2,1,0:T(8,128)S(1)}, f32[1,64,256]{2,1,0:T(8,128)S(1)}, u32[]{:S(2)}, u32[]{:S(2)}) collective-permute-start(f32[1,64,256]{2,1,0:T(8,128)S(1)} %bitcast.74), channel_id=1, source_target_pairs={{8,0},{12,4},{16,8},{20,12},{24,16},{28,20},{32,24},{36,28},{40,32... | collective-permute-start | bytes 196616 | tf_op jit(solution)/shard_map/ppermute | solution.py:151
  149.4 8.5 %collective-permute-start.24 = (f32[2,64,256]{2,1,0:T(8,128)S(1)}, f32[2,64,256]{2,1,0:T(8,128)S(1)}, u32[]{:S(2)}, u32[]{:S(2)}) collective-permute-start(f32[2,64,256]{2,1,0:T(8,128)S(1)} %fusion.102), channel_id=1, source_target_pairs={{0,4},{4,8},{8,12},{12,16},{16,20},{20,24},{24,28},{28,32},{32,36}... | collective-permute-start | bytes 393224 | tf_op jit(solution)/shard_map/ppermute | solution.py:116
  156.0 6.3 %collective-permute-start.25 = (f32[2,64,256]{2,1,0:T(8,128)S(1)}, f32[2,64,256]{2,1,0:T(8,128)S(1)}, u32[]{:S(2)}, u32[]{:S(2)}) collective-permute-start(f32[2,64,256]{2,1,0:T(8,128)S(1)} %fusion.102), channel_id=1, source_target_pairs={{4,0},{8,4},{12,8},{16,12},{20,16},{24,20},{28,24},{32,28},{36,32}... | collective-permute-start | bytes 393224 | tf_op jit(solution)/shard_map/ppermute | solution.py:117
  162.9 6.1 %collective-permute-start.26 = (f32[6,2,256]{2,1,0:T(2,128)S(1)}, f32[6,2,256]{2,1,0:T(2,128)S(1)}, u32[]{:S(2)}, u32[]{:S(2)}) collective-permute-start(f32[6,2,256]{2,1,0:T(2,128)S(1)} %get-tuple-element.18), channel_id=1, source_target_pairs={{0,1},{1,2},{2,3},{4,5},{5,6},{6,7},{8,9},{9,10},{10,11},{12,13},{... | collective-permute-start | bytes 36872 | tf_op jit(solution)/shard_map/ppermute | solution.py:116
  192.8 27.1 %collective-permute-start.31 = (f32[128,512]{1,0:T(8,128)S(1)}, f32[128,512]{1,0:T(8,128)S(1)}, u32[]{:S(2)}, u32[]{:S(2)}) collective-permute-start(f32[128,512]{1,0:T(8,128)S(1)} %get-tuple-element.2), channel_id=1, source_target_pairs={{0,8},{16,24},{32,40},{48,56},{64,72},{80,88},{96,104},{112,120},{... | collective-permute-start | bytes 786440 | tf_op jit(solution)/shard_map/ppermute | solution.py:260
  (40 other events, 457.2 us)
Sparse Core Ops, SparseCore 0:
  224.0 18.4 reduce-scatter.1

commit v3 on v2

--- a/solution.py
+++ b/solution.py
@@ -245,25 +245,40 @@
     picks = (local_targets[None, :] == wanted[:, None]).astype(jnp.float32)
     partial = jnp.dot(picks, faces, precision=lax.Precision.HIGHEST)
     partial = partial.reshape(pencil_count, tile_size, tile_size)
-    parent_grad = lax.psum_scatter(partial, "pencil", scatter_dimension=0, tiled=True)
+    parent_grad = scatter_partials(partial, "pencil")
     return (rhs_grad, parent_grad)
 
 
 def spread_faces(low_face, high_face, slab_index, slab_count):
-    stride = slab_count // 2
-    while stride >= 1:
-        span = 2 * stride
-        low_pairs = [(i, i + stride) for i in range(0, slab_count, span)]
-        high_pairs = [(slab_count - 1 - i, slab_count - 1 - i - stride) for i in range(0, slab_count, span)]
-        low_sender = slab_index % span == 0
+    fanouts = []
+    left = slab_count
+    while left > 1:
+        fanouts.append(4 if left % 4 == 0 else 2)
+        left //= fanouts[-1]
+    group = slab_count
+    for fanout in fanouts:
+        stride = group // fanout
+        low_sender = slab_index % group == 0
         sent = jnp.where(low_sender, low_face, high_face)
-        got = lax.ppermute(sent, "slab", low_pairs + high_pairs)
-        low_receiver = slab_index % span == stride
-        high_receiver = slab_index % span == span - 1 - stride
-        low_face = low_face + jnp.where(low_receiver, got, 0.0)
-        high_face = high_face + jnp.where(high_receiver, got, 0.0)
-        stride //= 2
+        for step in range(1, fanout):
+            reach = step * stride
+            low_pairs = [(i, i + reach) for i in range(0, slab_count, group)]
+            high_pairs = [(slab_count - 1 - i, slab_count - 1 - i - reach) for i in range(0, slab_count, group)]
+            got = lax.ppermute(sent, "slab", low_pairs + high_pairs)
+            low_face = low_face + jnp.where(slab_index % group == reach, got, 0.0)
+            high_face = high_face + jnp.where(slab_index % group == group - 1 - reach, got, 0.0)
+        group = stride
     return low_face, high_face
+
+
+def scatter_partials(partial, axis):
+    peers = lax.axis_size(axis)
+    me = lax.axis_index(axis)
+    total = lax.dynamic_index_in_dim(partial, me, axis=0, keepdims=True)
+    for step in range(1, peers):
+        piece = lax.dynamic_index_in_dim(partial, (me + step) % peers, axis=0, keepdims=True)
+        total = total + lax.ppermute(piece, axis, [(j, (j + step) % peers) for j in range(peers)])
+    return total
 
 
 def solution(mesh):

time: 252 us -> 219 us (0.87)
  waiting for transfers between devices: 85.5 us -> 61.2 us
  between operations: 15.5 us -> 2.2 us
  starting transfers between devices: 83.5 us -> 89.5 us
    reduce_scatter x1 -> x0, waiting for transfers between devices: 18.6 us -> none  [shards(): lax.psum_scatter(partial, 'pencil', scatter_dimension=0, tiled=True)]
    ppermute x5 -> x7, waiting for transfers between devices: 27 us -> 19.1 us  [spread_faces(): got = lax.ppermute(sent, 'slab', low_pairs + high_pairs)]
    ppermute x0 -> x3, starting transfers between devices: none -> 4.63 us  [scatter_partials(): lax.ppermute(piece, axis, [(j, (j + step) % peers) for j in range(peers)])]
  transfers between devices with their start and end apart: 34 -> 38, of which waited for: 17 -> 18; matrix products, arithmetic and copies ran while one was open for 5% -> 6% of each run, Pallas kernels for 0% -> 0%
where the time goes in v3:
time: 219 us; the launch traced here: 217 us
  starting transfers between devices  89.5 us (41%)
  waiting for transfers between devices  61.2 us (28%)
  other arithmetic  32.1 us (15%)
  local copies, waits for them, and re-layouts  22.6 us (10%)
  matrix products  9.44 us (4%)
  between operations  2.2 us (1%)
    ppermute x12, starting transfers between devices, extend(): lows.insert(0, lax.ppermute(low_piece, axis, up))  49.6 us
    ppermute x12, waiting for transfers between devices, extend(): highs.append(lax.ppermute(high_piece, axis, down))  25.1 us
    ppermute x7, waiting for transfers between devices, spread_faces(): got = lax.ppermute(sent, 'slab', low_pairs + high_pairs)  19.1 us
    ppermute x12, starting transfers between devices, extend(): highs.append(lax.ppermute(high_piece, axis, down))  18.2 us
    select_n x14, other arithmetic, masked(): return jnp.where(keep, field, 0.0)  17.7 us
    ppermute x4, starting transfers between devices, shift_planes(): return lax.ppermute(x[first:last], axis, pairs)  12.3 us
    unnamed x80, local copies, waits for them, and re-layouts  12.2 us
    ppermute x12, waiting for transfers between devices, extend(): lows.insert(0, lax.ppermute(low_piece, axis, up))  9.01 us
  transfers between devices with their start and end apart: 38, of which 18 were waited for; matrix products, arithmetic and copies ran while one was open for 6% of the time, Pallas kernels for 0%

profile of v3, /device:TPU:1, one launch (start us, length us, event | category | flops | bytes accessed | tf_op | source)
XLA Modules:
  0.0 217.0 jit_solution(4662427502597654407)
XLA Ops:
  0.6 4.7 %collective-permute-start.1 = (f32[4,128,512]{2,1,0:T(8,128)}, f32[4,128,512]{2,1,0:T(8,128)S(1)}, u32[]{:S(2)}, u32[]{:S(2)}) collective-permute-start(f32[4,128,512]{2,1,0:T(8,128)} %param.4), channel_id=1, source_target_pairs={{0,4},{4,8},{8,12},{12,16},{16,20},{20,24},{24,28},{28,32},{32,36}... | collective-permute-start | bytes 3145736 | tf_op jit(solution)/shard_map/ppermute | solution.py:116
  9.1 3.9 %collective-permute-start = (f32[1,128,512]{2,1,0:T(8,128)}, f32[1,128,512]{2,1,0:T(8,128)}, u32[]{:S(2)}, u32[]{:S(2)}) collective-permute-start(f32[1,128,512]{2,1,0:T(8,128)} %get-tuple-element.11), channel_id=1, source_target_pairs={{0,8},{4,12},{8,16},{12,20},{16,24},{20,28},{24,32},{28,36},{32,40... | collective-permute-start | bytes 786440 | tf_op jit(solution)/shard_map/ppermute | solution.py:116
  15.6 7.4 %collective-permute-done = f32[1,128,512]{2,1,0:T(8,128)} collective-permute-done((f32[1,128,512]{2,1,0:T(8,128)}, f32[1,128,512]{2,1,0:T(8,128)}, u32[]{:S(2)}, u32[]{:S(2)}) %collective-permute-start) | collective-permute-done | bytes 262176 | tf_op jit(solution)/shard_map/ppermute | solution.py:116
  24.7 3.6 %collective-permute-start.4 = (f32[14,5,512]{2,1,0:T(8,128)S(1)}, f32[14,5,512]{2,1,0:T(8,128)S(1)}, u32[]{:S(2)}, u32[]{:S(2)}) collective-permute-start(f32[14,5,512]{2,1,0:T(8,128)S(1)} %get-tuple-element.8), channel_id=1, source_target_pairs={{0,1},{1,2},{2,3},{4,5},{5,6},{6,7},{8,9},{9,10},{10,11},{12,13},{... | collective-permute-start | bytes 430088 | tf_op jit(solution)/shard_map/ppermute | solution.py:116
  31.2 4.0 %collective-permute-done.5 = f32[14,5,512]{2,1,0:T(8,128)S(1)} collective-permute-done((f32[14,5,512]{2,1,0:T(8,128)S(1)}, f32[14,5,512]{2,1,0:T(8,128)S(1)}, u32[]{:S(2)}, u32[]{:S(2)}) %collective-permute-start.5) | collective-permute-done | bytes 143392 | tf_op jit(solution)/shard_map/ppermute | solution.py:117
  36.7 3.1 %fusion.4 = f32[12,136,512]{2,1,0:T(8,128)S(1)} fusion(f32[12,136,512]{2,1,0:T(8,128)S(1)} %slice.617, f32[14,138,512]{2,1,0:T(8,128)S(1)} %pad_maximum_fusion, pred[12,136]{1,0:T(8,128)(4,1)S(1)} %broadcast_and_fusion.1), kind=kLoop, calls=%fused_computation.9 | loop fusion | flops 7520256 | bytes 20055648 | tf_op jit(solution)/shard_map/jit(_where)/select_n | solution.py:130
  49.1 4.1 %collective-permute-start.6 = (f32[1,64,256]{2,1,0:T(8,128)S(1)}, f32[1,64,256]{2,1,0:T(8,128)}, u32[]{:S(2)}, u32[]{:S(2)}) collective-permute-start(f32[1,64,256]{2,1,0:T(8,128)S(1)} %convolution_bitcast_fusion.6), channel_id=1, source_target_pairs={{0,8},{4,12},{8,16},{12,20},{16,24},{20,28},{24,32},{28,36},{32,40... | collective-permute-start | bytes 196616 | tf_op jit(solution)/shard_map/ppermute | solution.py:116
  53.9 6.8 %collective-permute-start.7 = (f32[2,64,256]{2,1,0:T(8,128)}, f32[2,64,256]{2,1,0:T(8,128)}, u32[]{:S(2)}, u32[]{:S(2)}) collective-permute-start(f32[2,64,256]{2,1,0:T(8,128)} %pad_maximum_fusion.6), channel_id=1, source_target_pairs={{0,4},{4,8},{8,12},{12,16},{16,20},{20,24},{24,28},{28,32},{32,36}... | collective-permute-start | bytes 393224 | tf_op jit(solution)/shard_map/ppermute | solution.py:116
  71.1 3.5 %collective-permute-start.10 = (f32[8,3,256]{2,1,0:T(4,128)}, f32[8,3,256]{2,1,0:T(4,128)S(1)}, u32[]{:S(2)}, u32[]{:S(2)}) collective-permute-start(f32[8,3,256]{2,1,0:T(4,128)} %get-tuple-element.14), channel_id=1, source_target_pairs={{0,1},{1,2},{2,3},{4,5},{5,6},{6,7},{8,9},{9,10},{10,11},{12,13},{... | collective-permute-start | bytes 73736 | tf_op jit(solution)/shard_map/ppermute | solution.py:116
  76.5 3.0 %collective-permute-done.11 = f32[8,3,256]{2,1,0:T(4,128)S(1)} collective-permute-done((f32[8,3,256]{2,1,0:T(4,128)}, f32[8,3,256]{2,1,0:T(4,128)S(1)}, u32[]{:S(2)}, u32[]{:S(2)}) %collective-permute-start.11) | collective-permute-done | bytes 24608 | tf_op jit(solution)/shard_map/ppermute | solution.py:117
  85.6 4.9 %collective-permute-start.12 = (f32[1,32,128]{2,1,0:T(8,128)S(1)}, f32[1,32,128]{2,1,0:T(8,128)}, u32[]{:S(2)}, u32[]{:S(2)}) collective-permute-start(f32[1,32,128]{2,1,0:T(8,128)S(1)} %bitcast.76), channel_id=1, source_target_pairs={{0,8},{4,12},{8,16},{12,20},{16,24},{20,28},{24,32},{28,36},{32,40... | collective-permute-start | bytes 49160 | tf_op jit(solution)/shard_map/ppermute | solution.py:116
  91.0 5.0 %collective-permute-start.13 = (f32[1,32,128]{2,1,0:T(8,128)S(1)}, f32[1,32,128]{2,1,0:T(8,128)S(1)}, u32[]{:S(2)}, u32[]{:S(2)}) collective-permute-start(f32[1,32,128]{2,1,0:T(8,128)S(1)} %bitcast.77), channel_id=1, source_target_pairs={{0,4},{4,8},{8,12},{12,16},{16,20},{20,24},{24,28},{28,32},{32,36}... | collective-permute-start | bytes 49160 | tf_op jit(solution)/shard_map/ppermute | solution.py:116
  103.4 3.2 %collective-permute-start.16 = (f32[5,2,128]{2,1,0:T(2,128)S(1)}, f32[5,2,128]{2,1,0:T(2,128)S(1)}, u32[]{:S(2)}, u32[]{:S(2)}) collective-permute-start(f32[5,2,128]{2,1,0:T(2,128)S(1)} %get-tuple-element.23), channel_id=1, source_target_pairs={{0,1},{1,2},{2,3},{4,5},{5,6},{6,7},{8,9},{9,10},{10,11},{12,13},{... | collective-permute-start | bytes 15368 | tf_op jit(solution)/shard_map/ppermute | solution.py:116
  108.0 3.0 %collective-permute-done.17 = f32[5,2,128]{2,1,0:T(2,128)S(1)} collective-permute-done((f32[5,2,128]{2,1,0:T(2,128)S(1)}, f32[5,2,128]{2,1,0:T(2,128)S(1)}, u32[]{:S(2)}, u32[]{:S(2)}) %collective-permute-start.17) | collective-permute-done | bytes 5152 | tf_op jit(solution)/shard_map/ppermute | solution.py:117
  114.4 5.5 %collective-permute-start.19 = (f32[4,64,256]{2,1,0:T(8,128)S(1)}, f32[4,64,256]{2,1,0:T(8,128)S(1)}, u32[]{:S(2)}, u32[]{:S(2)}) collective-permute-start(f32[4,64,256]{2,1,0:T(8,128)S(1)} %pad_maximum_fusion.5), channel_id=1, source_target_pairs={{0,4},{4,8},{8,12},{12,16},{16,20},{20,24},{24,28},{28,32},{32,36}... | collective-permute-start | bytes 786440 | tf_op jit(solution)/shard_map/ppermute | solution.py:151
  120.6 3.6 %collective-permute-start.18 = (f32[1,64,256]{2,1,0:T(8,128)S(1)}, f32[1,64,256]{2,1,0:T(8,128)S(1)}, u32[]{:S(2)}, u32[]{:S(2)}) collective-permute-start(f32[1,64,256]{2,1,0:T(8,128)S(1)} %bitcast.73), channel_id=1, source_target_pairs={{0,8},{4,12},{8,16},{12,20},{16,24},{20,28},{24,32},{28,36},{32,40... | collective-permute-start | bytes 196616 | tf_op jit(solution)/shard_map/ppermute | solution.py:151
  127.6 4.6 %collective-permute-done.20 = f32[4,64,256]{2,1,0:T(8,128)S(1)} collective-permute-done((f32[4,64,256]{2,1,0:T(8,128)S(1)}, f32[4,64,256]{2,1,0:T(8,128)S(1)}, u32[]{:S(2)}, u32[]{:S(2)}) %collective-permute-start.20) | collective-permute-done | bytes 262176 | tf_op jit(solution)/shard_map/ppermute | solution.py:151
  136.5 3.6 %collective-permute-done.23 = f32[14,3,256]{2,1,0:T(4,128)S(1)} collective-permute-done((f32[14,3,256]{2,1,0:T(4,128)S(1)}, f32[14,3,256]{2,1,0:T(4,128)S(1)}, u32[]{:S(2)}, u32[]{:S(2)}) %collective-permute-start.23) | collective-permute-done | bytes 43040 | tf_op jit(solution)/shard_map/ppermute | solution.py:117
  142.6 6.5 %collective-permute-start.24 = (f32[2,64,256]{2,1,0:T(8,128)S(1)}, f32[2,64,256]{2,1,0:T(8,128)S(1)}, u32[]{:S(2)}, u32[]{:S(2)}) collective-permute-start(f32[2,64,256]{2,1,0:T(8,128)S(1)} %fusion.102), channel_id=1, source_target_pairs={{0,4},{4,8},{8,12},{12,16},{16,20},{20,24},{24,28},{28,32},{32,36}... | collective-permute-start | bytes 393224 | tf_op jit(solution)/shard_map/ppermute | solution.py:116
  151.1 4.3 %collective-permute-done.25 = f32[2,64,256]{2,1,0:T(8,128)S(1)} collective-permute-done((f32[2,64,256]{2,1,0:T(8,128)S(1)}, f32[2,64,256]{2,1,0:T(8,128)S(1)}, u32[]{:S(2)}, u32[]{:S(2)}) %collective-permute-start.25) | collective-permute-done | bytes 131104 | tf_op jit(solution)/shard_map/ppermute | solution.py:117
  159.2 2.9 %slice.635 = f32[6,130,512]{2,1,0:T(8,128)} slice(f32[8,132,512]{2,1,0:T(8,128)} %copy-done.1), slice={[1:7], [1:131], [0:512]} | slice | bytes 3194880 | tf_op jit(solution)/shard_map/slice | solution.py:134
  173.5 3.1 %fusion.30 = (f32[6,130,512]{2,1,0:T(8,128)S(1)}, f32[6,130,512]{2,1,0:T(8,128)S(1)}) fusion(f32[6,130,512]{2,1,0:T(8,128)S(1)} %slice.712, f32[8,132,512]{2,1,0:T(8,128)S(1)} %fusion.18, pred[6,130]{1,0:T(8,128)(4,1)S(1)} %broadcast_and_fusion.2, f32[6,130,512]{2,1,0:T(8,128)S(1)} %copy-done.4, f32[8,132,512]{2,1,0:T(8,128)S(1)} %copy-done.2), kind=kLoop, calls=%fused_computation.56 | loop fusion | flops 7188480 | bytes 19170060 | tf_op jit(solution)/shard_map/jit(_where)/select_n | solution.py:130
  178.8 2.6 %fusion.49 = f32[4,128,512]{2,1,0:T(8,128)S(1)} fusion(f32[8,132,512]{2,1,0:T(8,128)S(1)} %fusion.18, f32[10,134,512]{2,1,0:T(8,128)S(1)} %slice_multiply_fusion, f32[4,128,512]{2,1,0:T(8,128)S(1)} %get-tuple-element.28, f32[10,134,512]{2,1,0:T(8,128)} %copy-done, f32[4,128,512]{2,1,0:T(8,128)S(1)} %copy-done.6, f32[12,136,512]{2,1,0:T(8,128)S(1)} %fusion.4, ...), kind=kLoop, calls=%fused_computation.98 | loop fusion | flops 3407872 | bytes 11534336 | tf_op jit(solution)/shard_map/sub | solution.py:226
  188.5 17.8 %collective-permute-done.33 = f32[128,512]{1,0:T(8,128)S(1)} collective-permute-done((f32[128,512]{1,0:T(8,128)S(1)}, f32[128,512]{1,0:T(8,128)S(1)}, u32[]{:S(2)}, u32[]{:S(2)}) %collective-permute-start.33) | collective-permute-done | bytes 262176 | tf_op jit(solution)/shard_map/ppermute | solution.py:267
  (253 shorter events, 99.9 us)
Async XLA Ops:
  0.6 23.4 %collective-permute-start.1 = (f32[4,128,512]{2,1,0:T(8,128)}, f32[4,128,512]{2,1,0:T(8,128)S(1)}, u32[]{:S(2)}, u32[]{:S(2)}) collective-permute-start(f32[4,128,512]{2,1,0:T(8,128)} %param.4), channel_id=1, source_target_pairs={{0,4},{4,8},{8,12},{12,16},{16,20},{20,24},{24,28},{28,32},{32,36}... | collective-permute-start | bytes 3145736 | tf_op jit(solution)/shard_map/ppermute | solution.py:116
  5.4 19.1 %collective-permute-start.2 = (f32[4,128,512]{2,1,0:T(8,128)}, f32[4,128,512]{2,1,0:T(8,128)S(1)}, u32[]{:S(2)}, u32[]{:S(2)}) collective-permute-start(f32[4,128,512]{2,1,0:T(8,128)} %param.4), channel_id=1, source_target_pairs={{4,0},{8,4},{12,8},{16,12},{20,16},{24,20},{28,24},{32,28},{36,32}... | collective-permute-start | bytes 3145736 | tf_op jit(solution)/shard_map/ppermute | solution.py:117
  9.1 13.9 %collective-permute-start = (f32[1,128,512]{2,1,0:T(8,128)}, f32[1,128,512]{2,1,0:T(8,128)}, u32[]{:S(2)}, u32[]{:S(2)}) collective-permute-start(f32[1,128,512]{2,1,0:T(8,128)} %get-tuple-element.11), channel_id=1, source_target_pairs={{0,8},{4,12},{8,16},{12,20},{16,24},{20,28},{24,32},{28,36},{32,40... | collective-permute-start | bytes 786440 | tf_op jit(solution)/shard_map/ppermute | solution.py:116
  13.1 11.5 %collective-permute-start.3 = (f32[1,128,512]{2,1,0:T(8,128)}, f32[1,128,512]{2,1,0:T(8,128)S(1)}, u32[]{:S(2)}, u32[]{:S(2)}) collective-permute-start(f32[1,128,512]{2,1,0:T(8,128)} %get-tuple-element.10), channel_id=1, source_target_pairs={{8,0},{12,4},{16,8},{20,12},{24,16},{28,20},{32,24},{36,28},{40,32... | collective-permute-start | bytes 786440 | tf_op jit(solution)/shard_map/ppermute | solution.py:117
  24.7 6.5 %collective-permute-start.4 = (f32[14,5,512]{2,1,0:T(8,128)S(1)}, f32[14,5,512]{2,1,0:T(8,128)S(1)}, u32[]{:S(2)}, u32[]{:S(2)}) collective-permute-start(f32[14,5,512]{2,1,0:T(8,128)S(1)} %get-tuple-element.8), channel_id=1, source_target_pairs={{0,1},{1,2},{2,3},{4,5},{5,6},{6,7},{8,9},{9,10},{10,11},{12,13},{... | collective-permute-start | bytes 430088 | tf_op jit(solution)/shard_map/ppermute | solution.py:116
  28.2 6.9 %collective-permute-start.5 = (f32[14,5,512]{2,1,0:T(8,128)S(1)}, f32[14,5,512]{2,1,0:T(8,128)S(1)}, u32[]{:S(2)}, u32[]{:S(2)}) collective-permute-start(f32[14,5,512]{2,1,0:T(8,128)S(1)} %get-tuple-element.9), channel_id=1, source_target_pairs={{1,0},{2,1},{3,2},{5,4},{6,5},{7,6},{9,8},{10,9},{11,10},{13,12},{... | collective-permute-start | bytes 430088 | tf_op jit(solution)/shard_map/ppermute | solution.py:117
  49.1 15.4 %collective-permute-start.6 = (f32[1,64,256]{2,1,0:T(8,128)S(1)}, f32[1,64,256]{2,1,0:T(8,128)}, u32[]{:S(2)}, u32[]{:S(2)}) collective-permute-start(f32[1,64,256]{2,1,0:T(8,128)S(1)} %convolution_bitcast_fusion.6), channel_id=1, source_target_pairs={{0,8},{4,12},{8,16},{12,20},{16,24},{20,28},{24,32},{28,36},{32,40... | collective-permute-start | bytes 196616 | tf_op jit(solution)/shard_map/ppermute | solution.py:116
  53.9 11.4 %collective-permute-start.7 = (f32[2,64,256]{2,1,0:T(8,128)}, f32[2,64,256]{2,1,0:T(8,128)}, u32[]{:S(2)}, u32[]{:S(2)}) collective-permute-start(f32[2,64,256]{2,1,0:T(8,128)} %pad_maximum_fusion.6), channel_id=1, source_target_pairs={{0,4},{4,8},{8,12},{12,16},{16,20},{20,24},{24,28},{28,32},{32,36}... | collective-permute-start | bytes 393224 | tf_op jit(solution)/shard_map/ppermute | solution.py:116
  61.3 6.5 %collective-permute-start.8 = (f32[2,64,256]{2,1,0:T(8,128)}, f32[2,64,256]{2,1,0:T(8,128)S(1)}, u32[]{:S(2)}, u32[]{:S(2)}) collective-permute-start(f32[2,64,256]{2,1,0:T(8,128)} %pad_maximum_fusion.6), channel_id=1, source_target_pairs={{4,0},{8,4},{12,8},{16,12},{20,16},{24,20},{28,24},{32,28},{36,32}... | collective-permute-start | bytes 393224 | tf_op jit(solution)/shard_map/ppermute | solution.py:117
  63.2 6.5 %collective-permute-start.9 = (f32[1,64,256]{2,1,0:T(8,128)S(1)}, f32[1,64,256]{2,1,0:T(8,128)S(1)}, u32[]{:S(2)}, u32[]{:S(2)}) collective-permute-start(f32[1,64,256]{2,1,0:T(8,128)S(1)} %convolution_bitcast_fusion.7), channel_id=1, source_target_pairs={{8,0},{12,4},{16,8},{20,12},{24,16},{28,20},{32,24},{36,28},{40,32... | collective-permute-start | bytes 196616 | tf_op jit(solution)/shard_map/ppermute | solution.py:117
  71.1 5.4 %collective-permute-start.10 = (f32[8,3,256]{2,1,0:T(4,128)}, f32[8,3,256]{2,1,0:T(4,128)S(1)}, u32[]{:S(2)}, u32[]{:S(2)}) collective-permute-start(f32[8,3,256]{2,1,0:T(4,128)} %get-tuple-element.14), channel_id=1, source_target_pairs={{0,1},{1,2},{2,3},{4,5},{5,6},{6,7},{8,9},{9,10},{10,11},{12,13},{... | collective-permute-start | bytes 73736 | tf_op jit(solution)/shard_map/ppermute | solution.py:116
  85.6 13.6 %collective-permute-start.12 = (f32[1,32,128]{2,1,0:T(8,128)S(1)}, f32[1,32,128]{2,1,0:T(8,128)}, u32[]{:S(2)}, u32[]{:S(2)}) collective-permute-start(f32[1,32,128]{2,1,0:T(8,128)S(1)} %bitcast.76), channel_id=1, source_target_pairs={{0,8},{4,12},{8,16},{12,20},{16,24},{20,28},{24,32},{28,36},{32,40... | collective-permute-start | bytes 49160 | tf_op jit(solution)/shard_map/ppermute | solution.py:116
  91.0 8.9 %collective-permute-start.13 = (f32[1,32,128]{2,1,0:T(8,128)S(1)}, f32[1,32,128]{2,1,0:T(8,128)S(1)}, u32[]{:S(2)}, u32[]{:S(2)}) collective-permute-start(f32[1,32,128]{2,1,0:T(8,128)S(1)} %bitcast.77), channel_id=1, source_target_pairs={{0,4},{4,8},{8,12},{12,16},{16,20},{20,24},{24,28},{28,32},{32,36}... | collective-permute-start | bytes 49160 | tf_op jit(solution)/shard_map/ppermute | solution.py:116
  96.0 5.1 %collective-permute-start.14 = (f32[1,32,128]{2,1,0:T(8,128)S(1)}, f32[1,32,128]{2,1,0:T(8,128)S(1)}, u32[]{:S(2)}, u32[]{:S(2)}) collective-permute-start(f32[1,32,128]{2,1,0:T(8,128)S(1)} %bitcast.78), channel_id=1, source_target_pairs={{4,0},{8,4},{12,8},{16,12},{20,16},{24,20},{28,24},{32,28},{36,32}... | collective-permute-start | bytes 49160 | tf_op jit(solution)/shard_map/ppermute | solution.py:117
  97.9 5.5 %collective-permute-start.15 = (f32[1,32,128]{2,1,0:T(8,128)S(1)}, f32[1,32,128]{2,1,0:T(8,128)S(1)}, u32[]{:S(2)}, u32[]{:S(2)}) collective-permute-start(f32[1,32,128]{2,1,0:T(8,128)S(1)} %bitcast.79), channel_id=1, source_target_pairs={{8,0},{12,4},{16,8},{20,12},{24,16},{28,20},{32,24},{36,28},{40,32... | collective-permute-start | bytes 49160 | tf_op jit(solution)/shard_map/ppermute | solution.py:117
  114.4 13.1 %collective-permute-start.19 = (f32[4,64,256]{2,1,0:T(8,128)S(1)}, f32[4,64,256]{2,1,0:T(8,128)S(1)}, u32[]{:S(2)}, u32[]{:S(2)}) collective-permute-start(f32[4,64,256]{2,1,0:T(8,128)S(1)} %pad_maximum_fusion.5), channel_id=1, source_target_pairs={{0,4},{4,8},{8,12},{12,16},{16,20},{20,24},{24,28},{28,32},{32,36}... | collective-permute-start | bytes 786440 | tf_op jit(solution)/shard_map/ppermute | solution.py:151
  120.6 6.9 %collective-permute-start.18 = (f32[1,64,256]{2,1,0:T(8,128)S(1)}, f32[1,64,256]{2,1,0:T(8,128)S(1)}, u32[]{:S(2)}, u32[]{:S(2)}) collective-permute-start(f32[1,64,256]{2,1,0:T(8,128)S(1)} %bitcast.73), channel_id=1, source_target_pairs={{0,8},{4,12},{8,16},{12,20},{16,24},{20,28},{24,32},{28,36},{32,40... | collective-permute-start | bytes 196616 | tf_op jit(solution)/shard_map/ppermute | solution.py:151
  124.3 7.9 %collective-permute-start.20 = (f32[4,64,256]{2,1,0:T(8,128)S(1)}, f32[4,64,256]{2,1,0:T(8,128)S(1)}, u32[]{:S(2)}, u32[]{:S(2)}) collective-permute-start(f32[4,64,256]{2,1,0:T(8,128)S(1)} %pad_maximum_fusion.5), channel_id=1, source_target_pairs={{4,0},{8,4},{12,8},{16,12},{20,16},{24,20},{28,24},{32,28},{36,32}... | collective-permute-start | bytes 786440 | tf_op jit(solution)/shard_map/ppermute | solution.py:151
  126.2 7.2 %collective-permute-start.21 = (f32[1,64,256]{2,1,0:T(8,128)S(1)}, f32[1,64,256]{2,1,0:T(8,128)S(1)}, u32[]{:S(2)}, u32[]{:S(2)}) collective-permute-start(f32[1,64,256]{2,1,0:T(8,128)S(1)} %bitcast.74), channel_id=1, source_target_pairs={{8,0},{12,4},{16,8},{20,12},{24,16},{28,20},{32,24},{36,28},{40,32... | collective-permute-start | bytes 196616 | tf_op jit(solution)/shard_map/ppermute | solution.py:151
  135.2 4.9 %collective-permute-start.23 = (f32[14,3,256]{2,1,0:T(4,128)S(1)}, f32[14,3,256]{2,1,0:T(4,128)S(1)}, u32[]{:S(2)}, u32[]{:S(2)}) collective-permute-start(f32[14,3,256]{2,1,0:T(4,128)S(1)} %get-tuple-element.13), channel_id=1, source_target_pairs={{1,0},{2,1},{3,2},{5,4},{6,5},{7,6},{9,8},{10,9},{11,10},{13,12},{... | collective-permute-start | bytes 129032 | tf_op jit(solution)/shard_map/ppermute | solution.py:117
  142.6 8.5 %collective-permute-start.24 = (f32[2,64,256]{2,1,0:T(8,128)S(1)}, f32[2,64,256]{2,1,0:T(8,128)S(1)}, u32[]{:S(2)}, u32[]{:S(2)}) collective-permute-start(f32[2,64,256]{2,1,0:T(8,128)S(1)} %fusion.102), channel_id=1, source_target_pairs={{0,4},{4,8},{8,12},{12,16},{16,20},{20,24},{24,28},{28,32},{32,36}... | collective-permute-start | bytes 393224 | tf_op jit(solution)/shard_map/ppermute | solution.py:116
  149.1 6.3 %collective-permute-start.25 = (f32[2,64,256]{2,1,0:T(8,128)S(1)}, f32[2,64,256]{2,1,0:T(8,128)S(1)}, u32[]{:S(2)}, u32[]{:S(2)}) collective-permute-start(f32[2,64,256]{2,1,0:T(8,128)S(1)} %fusion.102), channel_id=1, source_target_pairs={{4,0},{8,4},{12,8},{16,12},{20,16},{24,20},{28,24},{32,28},{36,32}... | collective-permute-start | bytes 393224 | tf_op jit(solution)/shard_map/ppermute | solution.py:117
  156.1 6.1 %collective-permute-start.26 = (f32[6,2,256]{2,1,0:T(2,128)S(1)}, f32[6,2,256]{2,1,0:T(2,128)S(1)}, u32[]{:S(2)}, u32[]{:S(2)}) collective-permute-start(f32[6,2,256]{2,1,0:T(2,128)S(1)} %get-tuple-element.16), channel_id=1, source_target_pairs={{0,1},{1,2},{2,3},{4,5},{5,6},{6,7},{8,9},{9,10},{10,11},{12,13},{... | collective-permute-start | bytes 36872 | tf_op jit(solution)/shard_map/ppermute | solution.py:116
  187.1 19.2 %collective-permute-start.33 = (f32[128,512]{1,0:T(8,128)S(1)}, f32[128,512]{1,0:T(8,128)S(1)}, u32[]{:S(2)}, u32[]{:S(2)}) collective-permute-start(f32[128,512]{1,0:T(8,128)S(1)} %get-tuple-element.5), channel_id=1, source_target_pairs={{0,24},{32,56},{64,88},{96,120},{124,100},{92,68},{60,36},{28,4},{... | collective-permute-start | bytes 786440 | tf_op jit(solution)/shard_map/ppermute | solution.py:267
  (44 other events, 478.6 us)

commit v4 on v3

--- a/solution.py
+++ b/solution.py
@@ -151,21 +151,26 @@
     return lax.ppermute(x[first:last], axis, pairs)
 
 
+def crop(field, have, want, block_x, block_y):
+    lose = have - want
+    return field[lose:lose + block_x + 2 * want, lose:lose + block_y + 2 * want]
+
+
 def medium_cycle(medium):
     block_x, block_y = medium.shape[0], medium.shape[1]
-    grown = extend(extend(medium, "slab", 0, 3), "pencil", 1, 3)
+    depth = 7
+    grown = extend(extend(medium, "slab", 0, depth), "pencil", 1, depth)
     powers = [grown]
-    for width in (2, 1, 0):
+    for width in range(depth - 1, depth - 4, -1):
         centre, total = shrink_neighbours(powers[-1])
         powers.append(lax.optimization_barrier(masked(smoothed(centre, total), block_x, block_y, width)))
-    grad_medium = coefficient(1) * core(powers[0], 3, block_x, block_y)
-    grad_medium = grad_medium + coefficient(1) * core(powers[1], 2, block_x, block_y)
-    grad_medium = grad_medium + coefficient(1) * core(powers[2], 1, block_x, block_y)
+    grad_medium = coefficient(1) * crop(powers[0], depth, 2, block_x, block_y)
+    grad_medium = grad_medium + coefficient(1) * crop(powers[1], depth - 1, 2, block_x, block_y)
+    grad_medium = grad_medium + coefficient(1) * crop(powers[2], depth - 2, 2, block_x, block_y)
     settled = powers[3]
     coarse_cot = children_sum(settled)
-    coarse_x, coarse_y = coarse_cot.shape[0], coarse_cot.shape[1]
-    grown = extend(extend(coarse_cot, "slab", 0, 2), "pencil", 1, 2)
-    coarse_powers = [grown]
+    coarse_x, coarse_y = block_x // 2, block_y // 2
+    coarse_powers = [coarse_cot]
     for width in (1, 0):
         centre, total = shrink_neighbours(coarse_powers[-1])
         coarse_powers.append(lax.optimization_barrier(masked(smoothed(centre, total), coarse_x, coarse_y, width)))
@@ -173,25 +178,14 @@
     grad_coarse = grad_coarse + coefficient(2) * core(coarse_powers[1], 1, coarse_x, coarse_y)
     grad_coarse = grad_coarse + coefficient(2) * coarse_powers[2]
     back_medium = prolong(grad_coarse) * 0.125
-    both = jnp.concatenate([back_medium, settled], axis=0)
-    near_low = shift_planes(both, "slab", 1, 0, 2 * block_x, True)
-    near_high = shift_planes(both, "slab", 1, 0, 2 * block_x, False)
-    far_low = shift_planes(back_medium, "slab", 2, block_x - 1, block_x, True)
-    far_high = shift_planes(back_medium, "slab", 2, 0, 1, False)
-    back_x = jnp.concatenate(
-        [far_low, near_low[:block_x], back_medium, near_high[:block_x], far_high], axis=0
-    )
-    settled_x = jnp.concatenate([near_low[block_x:], settled, near_high[block_x:]], axis=0)
-    stacked = extend(jnp.concatenate([back_x, settled_x], axis=0), "pencil", 1, 3)
-    back_xy = stacked[:block_x + 6]
-    settled_xy = stacked[block_x + 6:, 1:-1]
-    grad_medium = grad_medium + back_medium
+    back_xy = extend(extend(back_medium, "slab", 0, 5), "pencil", 1, 5)
+    grad_medium = grad_medium + crop(back_xy, 5, 2, block_x, block_y)
     centre, total = shrink_neighbours(back_xy)
-    stage = masked(settled_xy - (6.0 * centre - total) / 4.0, block_x, block_y, 2)
+    stage = masked(settled - (6.0 * centre - total) / 4.0, block_x, block_y, 4)
     stage = lax.optimization_barrier(stage)
-    for width in (2, 1, 0):
-        grad_medium = grad_medium + coefficient(1) * core(stage, width, block_x, block_y)
-        if width > 0:
+    for width in (4, 3, 2):
+        grad_medium = grad_medium + coefficient(1) * crop(stage, width, 2, block_x, block_y)
+        if width > 2:
             centre, total = shrink_neighbours(stage)
             stage = lax.optimization_barrier(masked(smoothed(centre, total), block_x, block_y, width - 1))
     return grad_medium
@@ -212,8 +206,7 @@
         rhs_grad = rhs_grad + coefficient(0) * part
     grad_fine = core(powers[3], depth - 3, x_cells, y_cells)
     medium = children_sum(grad_fine)
-    grad_medium = medium_cycle(medium)
-    grown = extend(extend(grad_medium, "slab", 0, 2), "pencil", 1, 2)
+    grown = medium_cycle(medium)
     back_fine = prolong(grown)[1:-1, 1:-1] * 0.125
     rhs_grad = rhs_grad + core(back_fine, 3, x_cells, y_cells)
     centre, total = shrink_neighbours(back_fine)

time: 219 us -> 199 us (0.909)
  starting transfers between devices: 89.5 us -> 77.5 us
  waiting for transfers between devices: 61.2 us -> 51.9 us
  other arithmetic: 32.1 us -> 37.6 us
  local copies, waits for them, and re-layouts: 22.6 us -> 19.3 us
    ppermute x4 -> x0, starting transfers between devices: 12.3 us -> none  [shift_planes(): return lax.ppermute(x[first:last], axis, pairs)]
    ppermute x4 -> x0, waiting for transfers between devices: 5.86 us -> none  [shift_planes(): return lax.ppermute(x[first:last], axis, pairs)]
    ppermute x12, waiting for transfers between devices: 9.01 us -> 5.81 us  [extend(): lows.insert(0, lax.ppermute(low_piece, axis, up))]
    unnamed x80 -> x61, local copies, waits for them, and re-layouts: 12.2 us -> 9.36 us
    slice x11 -> x12, local copies, waits for them, and re-layouts: 4.92 us -> 5.11 us  [shrink_neighbours(): centre = field[1:-1, 1:-1]]
  transfers between devices with their start and end apart: 38 -> 34, of which waited for: 18 -> 17; matrix products, arithmetic and copies ran while one was open for 6% -> 8% of each run, Pallas kernels for 0% -> 0%
where the time goes in v4:
time: 199 us; the launch traced here: 197 us
  starting transfers between devices  77.5 us (39%)
  waiting for transfers between devices  51.9 us (26%)
  other arithmetic  37.6 us (19%)
  local copies, waits for them, and re-layouts  19.3 us (10%)
  matrix products  9 us (5%)
  between operations  2.06 us (1%)
    ppermute x12, starting transfers between devices, extend(): lows.insert(0, lax.ppermute(low_piece, axis, up))  50.1 us
    ppermute x12, waiting for transfers between devices, extend(): highs.append(lax.ppermute(high_piece, axis, down))  23.6 us
    ppermute x7, waiting for transfers between devices, spread_faces(): got = lax.ppermute(sent, 'slab', low_pairs + high_pairs)  20 us
    select_n x14, other arithmetic, masked(): return jnp.where(keep, field, 0.0)  19.4 us
    ppermute x12, starting transfers between devices, extend(): highs.append(lax.ppermute(high_piece, axis, down))  18.4 us
    unnamed x61, local copies, waits for them, and re-layouts  9.36 us
    ppermute x12, waiting for transfers between devices, extend(): lows.insert(0, lax.ppermute(low_piece, axis, up))  5.81 us
    slice x12, local copies, waits for them, and re-layouts, shrink_neighbours(): centre = field[1:-1, 1:-1]  5.11 us
  transfers between devices with their start and end apart: 34, of which 17 were waited for; matrix products, arithmetic and copies ran while one was open for 8% of the time, Pallas kernels for 0%

profile of v4, /device:TPU:1, one launch (start us, length us, event | category | flops | bytes accessed | tf_op | source)
XLA Modules:
  0.0 197.3 jit_solution(17631199371007917284)
XLA Ops:
  0.6 4.7 %collective-permute-start.1 = (f32[4,128,512]{2,1,0:T(8,128)}, f32[4,128,512]{2,1,0:T(8,128)S(1)}, u32[]{:S(2)}, u32[]{:S(2)}) collective-permute-start(f32[4,128,512]{2,1,0:T(8,128)} %param.4), channel_id=1, source_target_pairs={{0,4},{4,8},{8,12},{12,16},{16,20},{20,24},{24,28},{28,32},{32,36}... | collective-permute-start | bytes 3145736 | tf_op jit(solution)/shard_map/ppermute | solution.py:116
  9.1 3.9 %collective-permute-start = (f32[1,128,512]{2,1,0:T(8,128)}, f32[1,128,512]{2,1,0:T(8,128)}, u32[]{:S(2)}, u32[]{:S(2)}) collective-permute-start(f32[1,128,512]{2,1,0:T(8,128)} %get-tuple-element.13), channel_id=1, source_target_pairs={{0,8},{4,12},{8,16},{12,20},{16,24},{20,28},{24,32},{28,36},{32,40... | collective-permute-start | bytes 786440 | tf_op jit(solution)/shard_map/ppermute | solution.py:116
  19.2 3.8 %collective-permute-done = f32[1,128,512]{2,1,0:T(8,128)} collective-permute-done((f32[1,128,512]{2,1,0:T(8,128)}, f32[1,128,512]{2,1,0:T(8,128)}, u32[]{:S(2)}, u32[]{:S(2)}) %collective-permute-start) | collective-permute-done | bytes 262176 | tf_op jit(solution)/shard_map/ppermute | solution.py:116
  24.7 3.6 %collective-permute-start.4 = (f32[14,5,512]{2,1,0:T(8,128)S(1)}, f32[14,5,512]{2,1,0:T(8,128)S(1)}, u32[]{:S(2)}, u32[]{:S(2)}) collective-permute-start(f32[14,5,512]{2,1,0:T(8,128)S(1)} %get-tuple-element.8), channel_id=1, source_target_pairs={{0,1},{1,2},{2,3},{4,5},{5,6},{6,7},{8,9},{9,10},{10,11},{12,13},{... | collective-permute-start | bytes 430088 | tf_op jit(solution)/shard_map/ppermute | solution.py:116
  31.2 4.0 %collective-permute-done.5 = f32[14,5,512]{2,1,0:T(8,128)S(1)} collective-permute-done((f32[14,5,512]{2,1,0:T(8,128)S(1)}, f32[14,5,512]{2,1,0:T(8,128)S(1)}, u32[]{:S(2)}, u32[]{:S(2)}) %collective-permute-start.5) | collective-permute-done | bytes 143392 | tf_op jit(solution)/shard_map/ppermute | solution.py:117
  36.7 3.2 %fusion.4 = f32[12,136,512]{2,1,0:T(8,128)S(1)} fusion(f32[12,136,512]{2,1,0:T(8,128)S(1)} %slice.618, f32[14,138,512]{2,1,0:T(8,128)S(1)} %pad_maximum_fusion, pred[12,136]{1,0:T(8,128)(4,1)S(1)} %broadcast_and_fusion.1), kind=kLoop, calls=%fused_computation.9 | loop fusion | flops 7520256 | bytes 20055648 | tf_op jit(solution)/shard_map/jit(_where)/select_n | solution.py:130
  40.3 2.6 %fusion.9 = f32[10,134,512]{2,1,0:T(8,128)S(1)} fusion(f32[10,134,512]{2,1,0:T(8,128)S(1)} %slice.624, f32[12,136,512]{2,1,0:T(8,128)S(1)} %fusion.4, pred[10,134]{1,0:T(8,128)(4,1)S(1)} %broadcast_and_fusion), kind=kLoop, calls=%fused_computation.21 | loop fusion | flops 6174720 | bytes 16467260 | tf_op jit(solution)/shard_map/jit(_where)/select_n | solution.py:130
  49.1 5.1 %collective-permute-start.6 = (f32[1,64,256]{2,1,0:T(8,128)S(1)}, f32[1,64,256]{2,1,0:T(8,128)S(1)}, u32[]{:S(2)}, u32[]{:S(2)}) collective-permute-start(f32[1,64,256]{2,1,0:T(8,128)S(1)} %convolution_bitcast_fusion.7), channel_id=1, source_target_pairs={{0,16},{4,20},{8,24},{12,28},{16,32},{20,36},{24,40},{28,44},{32,4... | collective-permute-start | bytes 196616 | tf_op jit(solution)/shard_map/ppermute | solution.py:116
  54.9 9.0 %collective-permute-start.7 = (f32[2,64,256]{2,1,0:T(8,128)}, f32[2,64,256]{2,1,0:T(8,128)}, u32[]{:S(2)}, u32[]{:S(2)}) collective-permute-start(f32[2,64,256]{2,1,0:T(8,128)} %pad_maximum_fusion.4), channel_id=1, source_target_pairs={{0,12},{4,16},{8,20},{12,24},{16,28},{20,32},{24,36},{28,40},{32,4... | collective-permute-start | bytes 393224 | tf_op jit(solution)/shard_map/ppermute | solution.py:116
  75.3 2.6 %collective-permute-done.11 = f32[2,64,256]{2,1,0:T(8,128)S(1)} collective-permute-done((f32[2,64,256]{2,1,0:T(8,128)}, f32[2,64,256]{2,1,0:T(8,128)S(1)}, u32[]{:S(2)}, u32[]{:S(2)}) %collective-permute-start.11) | collective-permute-done | bytes 131104 | tf_op jit(solution)/shard_map/ppermute | solution.py:117
  77.9 3.4 %collective-permute-done.12 = f32[2,64,256]{2,1,0:T(8,128)S(1)} collective-permute-done((f32[2,64,256]{2,1,0:T(8,128)}, f32[2,64,256]{2,1,0:T(8,128)S(1)}, u32[]{:S(2)}, u32[]{:S(2)}) %collective-permute-start.12) | collective-permute-done | bytes 131104 | tf_op jit(solution)/shard_map/ppermute | solution.py:117
  81.3 2.5 %collective-permute-done.13 = f32[1,64,256]{2,1,0:T(8,128)S(1)} collective-permute-done((f32[1,64,256]{2,1,0:T(8,128)S(1)}, f32[1,64,256]{2,1,0:T(8,128)S(1)}, u32[]{:S(2)}, u32[]{:S(2)}) %collective-permute-start.13) | collective-permute-done | bytes 65568 | tf_op jit(solution)/shard_map/ppermute | solution.py:117
  83.8 3.5 %collective-permute-start.14 = (f32[16,7,256]{2,1,0:T(8,128)S(1)}, f32[16,7,256]{2,1,0:T(8,128)S(1)}, u32[]{:S(2)}, u32[]{:S(2)}) collective-permute-start(f32[16,7,256]{2,1,0:T(8,128)S(1)} %get-tuple-element.10), channel_id=1, source_target_pairs={{0,1},{1,2},{2,3},{4,5},{5,6},{6,7},{8,9},{9,10},{10,11},{12,13},{... | collective-permute-start | bytes 344072 | tf_op jit(solution)/shard_map/ppermute | solution.py:116
  89.6 3.8 %collective-permute-done.15 = f32[16,7,256]{2,1,0:T(8,128)S(1)} collective-permute-done((f32[16,7,256]{2,1,0:T(8,128)S(1)}, f32[16,7,256]{2,1,0:T(8,128)S(1)}, u32[]{:S(2)}, u32[]{:S(2)}) %collective-permute-start.15) | collective-permute-done | bytes 114720 | tf_op jit(solution)/shard_map/ppermute | solution.py:117
  102.9 8.7 %collective-permute-start.16 = (f32[1,64,256]{2,1,0:T(8,128)S(1)}, f32[1,64,256]{2,1,0:T(8,128)}, u32[]{:S(2)}, u32[]{:S(2)}) collective-permute-start(f32[1,64,256]{2,1,0:T(8,128)S(1)} %bitcast.77), channel_id=1, source_target_pairs={{0,12},{4,16},{8,20},{12,24},{16,28},{20,32},{24,36},{28,40},{32,4... | collective-permute-start | bytes 196616 | tf_op jit(solution)/shard_map/ppermute | solution.py:116
  111.6 2.9 %collective-permute-start.17 = (f32[2,64,256]{2,1,0:T(8,128)S(1)}, f32[2,64,256]{2,1,0:T(8,128)}, u32[]{:S(2)}, u32[]{:S(2)}) collective-permute-start(f32[2,64,256]{2,1,0:T(8,128)S(1)} %reshape.855), channel_id=1, source_target_pairs={{0,8},{4,12},{8,16},{12,20},{16,24},{20,28},{24,32},{28,36},{32,40... | collective-permute-start | bytes 393224 | tf_op jit(solution)/shard_map/ppermute | solution.py:116
  117.1 2.4 %collective-permute-start.19 = (f32[2,64,256]{2,1,0:T(8,128)S(1)}, f32[2,64,256]{2,1,0:T(8,128)S(1)}, u32[]{:S(2)}, u32[]{:S(2)}) collective-permute-start(f32[2,64,256]{2,1,0:T(8,128)S(1)} %reshape.855), channel_id=1, source_target_pairs={{4,0},{8,4},{12,8},{16,12},{20,16},{24,20},{28,24},{32,28},{36,32}... | collective-permute-start | bytes 393224 | tf_op jit(solution)/shard_map/ppermute | solution.py:117
  124.0 2.9 %collective-permute-done.20 = f32[2,64,256]{2,1,0:T(8,128)S(1)} collective-permute-done((f32[2,64,256]{2,1,0:T(8,128)S(1)}, f32[2,64,256]{2,1,0:T(8,128)S(1)}, u32[]{:S(2)}, u32[]{:S(2)}) %collective-permute-start.20) | collective-permute-done | bytes 131104 | tf_op jit(solution)/shard_map/ppermute | solution.py:117
  128.7 3.3 %collective-permute-start.22 = (f32[12,5,256]{2,1,0:T(8,128)S(1)}, f32[12,5,256]{2,1,0:T(8,128)S(1)}, u32[]{:S(2)}, u32[]{:S(2)}) collective-permute-start(f32[12,5,256]{2,1,0:T(8,128)S(1)} %get-tuple-element.14), channel_id=1, source_target_pairs={{0,1},{1,2},{2,3},{4,5},{5,6},{6,7},{8,9},{9,10},{10,11},{12,13},{... | collective-permute-start | bytes 184328 | tf_op jit(solution)/shard_map/ppermute | solution.py:116
  133.2 2.9 %slice.636 = f32[6,130,512]{2,1,0:T(8,128)} slice(f32[8,132,512]{2,1,0:T(8,128)} %copy-done.1), slice={[1:7], [1:131], [0:512]} | slice | bytes 3194880 | tf_op jit(solution)/shard_map/slice | solution.py:134
  140.4 2.4 %fusion.91 = f32[6,68,256]{2,1,0:T(8,128)} fusion(f32[10,72,256]{2,1,0:T(8,128)S(1)} %fusion.76, f32[12,74,256]{2,1,0:T(8,128)S(1)} %pad_maximum_fusion.2, f32[12,74,256]{2,1,0:T(8,128)} %copy-done.5, f32[14,76,256]{2,1,0:T(8,128)} %copy-done.4, f32[16,78,256]{2,1,0:T(8,128)} %copy-done.3, f32[6,68,256]{2,1,0:T(8,128)S(1)} %fusion.88, ...), kind=kLoop, calls=%fused_computation.187 | loop fusion | flops 1044480 | bytes 3342336 | tf_op jit(solution)/shard_map/add | solution.py:187
  153.0 3.1 %fusion.30 = (f32[6,130,512]{2,1,0:T(8,128)S(1)}, f32[6,130,512]{2,1,0:T(8,128)S(1)}) fusion(f32[6,130,512]{2,1,0:T(8,128)S(1)} %slice.715, f32[8,132,512]{2,1,0:T(8,128)S(1)} %fusion.18, pred[6,130]{1,0:T(8,128)(4,1)S(1)} %copy-done.13, f32[6,130,512]{2,1,0:T(8,128)S(1)} %copy-done.6, f32[8,132,512]{2,1,0:T(8,128)S(1)} %copy-done.2), kind=kLoop, calls=%fused_computation.58 | loop fusion | flops 7188480 | bytes 19170060 | tf_op jit(solution)/shard_map/jit(_where)/select_n | solution.py:130
  158.2 2.6 %fusion.54 = f32[4,128,512]{2,1,0:T(8,128)S(1)} fusion(f32[8,132,512]{2,1,0:T(8,128)S(1)} %fusion.18, f32[10,134,512]{2,1,0:T(8,128)S(1)} %slice_multiply_fusion, f32[4,128,512]{2,1,0:T(8,128)S(1)} %get-tuple-element.24, f32[10,134,512]{2,1,0:T(8,128)} %copy-done, f32[4,128,512]{2,1,0:T(8,128)S(1)} %copy-done.9, f32[12,136,512]{2,1,0:T(8,128)S(1)} %fusion.4, ...), kind=kLoop, calls=%fused_computation.120 | loop fusion | flops 3407872 | bytes 11534336 | tf_op jit(solution)/shard_map/sub | solution.py:219
  168.0 18.7 %collective-permute-done.29 = f32[128,512]{1,0:T(8,128)S(1)} collective-permute-done((f32[128,512]{1,0:T(8,128)S(1)}, f32[128,512]{1,0:T(8,128)S(1)}, u32[]{:S(2)}, u32[]{:S(2)}) %collective-permute-start.29) | collective-permute-done | bytes 262176 | tf_op jit(solution)/shard_map/ppermute | solution.py:260
  (231 shorter events, 89.8 us)
Async XLA Ops:
  0.6 23.4 %collective-permute-start.1 = (f32[4,128,512]{2,1,0:T(8,128)}, f32[4,128,512]{2,1,0:T(8,128)S(1)}, u32[]{:S(2)}, u32[]{:S(2)}) collective-permute-start(f32[4,128,512]{2,1,0:T(8,128)} %param.4), channel_id=1, source_target_pairs={{0,4},{4,8},{8,12},{12,16},{16,20},{20,24},{24,28},{28,32},{32,36}... | collective-permute-start | bytes 3145736 | tf_op jit(solution)/shard_map/ppermute | solution.py:116
  5.4 19.1 %collective-permute-start.2 = (f32[4,128,512]{2,1,0:T(8,128)}, f32[4,128,512]{2,1,0:T(8,128)S(1)}, u32[]{:S(2)}, u32[]{:S(2)}) collective-permute-start(f32[4,128,512]{2,1,0:T(8,128)} %param.4), channel_id=1, source_target_pairs={{4,0},{8,4},{12,8},{16,12},{20,16},{24,20},{28,24},{32,28},{36,32}... | collective-permute-start | bytes 3145736 | tf_op jit(solution)/shard_map/ppermute | solution.py:117
  9.1 13.9 %collective-permute-start = (f32[1,128,512]{2,1,0:T(8,128)}, f32[1,128,512]{2,1,0:T(8,128)}, u32[]{:S(2)}, u32[]{:S(2)}) collective-permute-start(f32[1,128,512]{2,1,0:T(8,128)} %get-tuple-element.13), channel_id=1, source_target_pairs={{0,8},{4,12},{8,16},{12,20},{16,24},{20,28},{24,32},{28,36},{32,40... | collective-permute-start | bytes 786440 | tf_op jit(solution)/shard_map/ppermute | solution.py:116
  13.1 11.5 %collective-permute-start.3 = (f32[1,128,512]{2,1,0:T(8,128)}, f32[1,128,512]{2,1,0:T(8,128)S(1)}, u32[]{:S(2)}, u32[]{:S(2)}) collective-permute-start(f32[1,128,512]{2,1,0:T(8,128)} %get-tuple-element.12), channel_id=1, source_target_pairs={{8,0},{12,4},{16,8},{20,12},{24,16},{28,20},{32,24},{36,28},{40,32... | collective-permute-start | bytes 786440 | tf_op jit(solution)/shard_map/ppermute | solution.py:117
  24.7 6.5 %collective-permute-start.4 = (f32[14,5,512]{2,1,0:T(8,128)S(1)}, f32[14,5,512]{2,1,0:T(8,128)S(1)}, u32[]{:S(2)}, u32[]{:S(2)}) collective-permute-start(f32[14,5,512]{2,1,0:T(8,128)S(1)} %get-tuple-element.8), channel_id=1, source_target_pairs={{0,1},{1,2},{2,3},{4,5},{5,6},{6,7},{8,9},{9,10},{10,11},{12,13},{... | collective-permute-start | bytes 430088 | tf_op jit(solution)/shard_map/ppermute | solution.py:116
  28.2 6.9 %collective-permute-start.5 = (f32[14,5,512]{2,1,0:T(8,128)S(1)}, f32[14,5,512]{2,1,0:T(8,128)S(1)}, u32[]{:S(2)}, u32[]{:S(2)}) collective-permute-start(f32[14,5,512]{2,1,0:T(8,128)S(1)} %get-tuple-element.9), channel_id=1, source_target_pairs={{1,0},{2,1},{3,2},{5,4},{6,5},{7,6},{9,8},{10,9},{11,10},{13,12},{... | collective-permute-start | bytes 430088 | tf_op jit(solution)/shard_map/ppermute | solution.py:117
  49.1 21.3 %collective-permute-start.6 = (f32[1,64,256]{2,1,0:T(8,128)S(1)}, f32[1,64,256]{2,1,0:T(8,128)S(1)}, u32[]{:S(2)}, u32[]{:S(2)}) collective-permute-start(f32[1,64,256]{2,1,0:T(8,128)S(1)} %convolution_bitcast_fusion.7), channel_id=1, source_target_pairs={{0,16},{4,20},{8,24},{12,28},{16,32},{20,36},{24,40},{28,44},{32,4... | collective-permute-start | bytes 196616 | tf_op jit(solution)/shard_map/ppermute | solution.py:116
  54.9 16.8 %collective-permute-start.7 = (f32[2,64,256]{2,1,0:T(8,128)}, f32[2,64,256]{2,1,0:T(8,128)}, u32[]{:S(2)}, u32[]{:S(2)}) collective-permute-start(f32[2,64,256]{2,1,0:T(8,128)} %pad_maximum_fusion.4), channel_id=1, source_target_pairs={{0,12},{4,16},{8,20},{12,24},{16,28},{20,32},{24,36},{28,40},{32,4... | collective-permute-start | bytes 393224 | tf_op jit(solution)/shard_map/ppermute | solution.py:116
  64.3 9.6 %collective-permute-start.8 = (f32[2,64,256]{2,1,0:T(8,128)}, f32[2,64,256]{2,1,0:T(8,128)S(1)}, u32[]{:S(2)}, u32[]{:S(2)}) collective-permute-start(f32[2,64,256]{2,1,0:T(8,128)} %pad_maximum_fusion.4), channel_id=1, source_target_pairs={{0,8},{4,12},{8,16},{12,20},{16,24},{20,28},{24,32},{28,36},{32,40... | collective-permute-start | bytes 393224 | tf_op jit(solution)/shard_map/ppermute | solution.py:116
  66.0 9.2 %collective-permute-start.9 = (f32[2,64,256]{2,1,0:T(8,128)}, f32[2,64,256]{2,1,0:T(8,128)S(1)}, u32[]{:S(2)}, u32[]{:S(2)}) collective-permute-start(f32[2,64,256]{2,1,0:T(8,128)} %pad_maximum_fusion.4), channel_id=1, source_target_pairs={{0,4},{4,8},{8,12},{12,16},{16,20},{20,24},{24,28},{28,32},{32,36}... | collective-permute-start | bytes 393224 | tf_op jit(solution)/shard_map/ppermute | solution.py:116
  67.9 7.4 %collective-permute-start.10 = (f32[2,64,256]{2,1,0:T(8,128)}, f32[2,64,256]{2,1,0:T(8,128)S(1)}, u32[]{:S(2)}, u32[]{:S(2)}) collective-permute-start(f32[2,64,256]{2,1,0:T(8,128)} %pad_maximum_fusion.4), channel_id=1, source_target_pairs={{4,0},{8,4},{12,8},{16,12},{20,16},{24,20},{28,24},{32,28},{36,32}... | collective-permute-start | bytes 393224 | tf_op jit(solution)/shard_map/ppermute | solution.py:117
  70.4 7.5 %collective-permute-start.11 = (f32[2,64,256]{2,1,0:T(8,128)}, f32[2,64,256]{2,1,0:T(8,128)S(1)}, u32[]{:S(2)}, u32[]{:S(2)}) collective-permute-start(f32[2,64,256]{2,1,0:T(8,128)} %pad_maximum_fusion.4), channel_id=1, source_target_pairs={{8,0},{12,4},{16,8},{20,12},{24,16},{28,20},{32,24},{36,28},{40,32... | collective-permute-start | bytes 393224 | tf_op jit(solution)/shard_map/ppermute | solution.py:117
  71.7 9.6 %collective-permute-start.12 = (f32[2,64,256]{2,1,0:T(8,128)}, f32[2,64,256]{2,1,0:T(8,128)S(1)}, u32[]{:S(2)}, u32[]{:S(2)}) collective-permute-start(f32[2,64,256]{2,1,0:T(8,128)} %pad_maximum_fusion.4), channel_id=1, source_target_pairs={{12,0},{16,4},{20,8},{24,12},{28,16},{32,20},{36,24},{40,28},{44,3... | collective-permute-start | bytes 393224 | tf_op jit(solution)/shard_map/ppermute | solution.py:117
  73.9 9.9 %collective-permute-start.13 = (f32[1,64,256]{2,1,0:T(8,128)S(1)}, f32[1,64,256]{2,1,0:T(8,128)S(1)}, u32[]{:S(2)}, u32[]{:S(2)}) collective-permute-start(f32[1,64,256]{2,1,0:T(8,128)S(1)} %convolution_bitcast_fusion.6), channel_id=1, source_target_pairs={{16,0},{20,4},{24,8},{28,12},{32,16},{36,20},{40,24},{44,28},{48,3... | collective-permute-start | bytes 196616 | tf_op jit(solution)/shard_map/ppermute | solution.py:117
  87.4 6.1 %collective-permute-start.15 = (f32[16,7,256]{2,1,0:T(8,128)S(1)}, f32[16,7,256]{2,1,0:T(8,128)S(1)}, u32[]{:S(2)}, u32[]{:S(2)}) collective-permute-start(f32[16,7,256]{2,1,0:T(8,128)S(1)} %get-tuple-element.11), channel_id=1, source_target_pairs={{1,0},{2,1},{3,2},{5,4},{6,5},{7,6},{9,8},{10,9},{11,10},{13,12},{... | collective-permute-start | bytes 344072 | tf_op jit(solution)/shard_map/ppermute | solution.py:117
  102.9 17.9 %collective-permute-start.16 = (f32[1,64,256]{2,1,0:T(8,128)S(1)}, f32[1,64,256]{2,1,0:T(8,128)}, u32[]{:S(2)}, u32[]{:S(2)}) collective-permute-start(f32[1,64,256]{2,1,0:T(8,128)S(1)} %bitcast.77), channel_id=1, source_target_pairs={{0,12},{4,16},{8,20},{12,24},{16,28},{20,32},{24,36},{28,40},{32,4... | collective-permute-start | bytes 196616 | tf_op jit(solution)/shard_map/ppermute | solution.py:116
  111.6 11.4 %collective-permute-start.17 = (f32[2,64,256]{2,1,0:T(8,128)S(1)}, f32[2,64,256]{2,1,0:T(8,128)}, u32[]{:S(2)}, u32[]{:S(2)}) collective-permute-start(f32[2,64,256]{2,1,0:T(8,128)S(1)} %reshape.855), channel_id=1, source_target_pairs={{0,8},{4,12},{8,16},{12,20},{16,24},{20,28},{24,32},{28,36},{32,40... | collective-permute-start | bytes 393224 | tf_op jit(solution)/shard_map/ppermute | solution.py:116
  115.2 8.7 %collective-permute-start.18 = (f32[2,64,256]{2,1,0:T(8,128)S(1)}, f32[2,64,256]{2,1,0:T(8,128)S(1)}, u32[]{:S(2)}, u32[]{:S(2)}) collective-permute-start(f32[2,64,256]{2,1,0:T(8,128)S(1)} %reshape.855), channel_id=1, source_target_pairs={{0,4},{4,8},{8,12},{12,16},{16,20},{20,24},{24,28},{28,32},{32,36}... | collective-permute-start | bytes 393224 | tf_op jit(solution)/shard_map/ppermute | solution.py:116
  117.1 6.8 %collective-permute-start.19 = (f32[2,64,256]{2,1,0:T(8,128)S(1)}, f32[2,64,256]{2,1,0:T(8,128)S(1)}, u32[]{:S(2)}, u32[]{:S(2)}) collective-permute-start(f32[2,64,256]{2,1,0:T(8,128)S(1)} %reshape.855), channel_id=1, source_target_pairs={{4,0},{8,4},{12,8},{16,12},{20,16},{24,20},{28,24},{32,28},{36,32}... | collective-permute-start | bytes 393224 | tf_op jit(solution)/shard_map/ppermute | solution.py:117
  119.6 7.3 %collective-permute-start.20 = (f32[2,64,256]{2,1,0:T(8,128)S(1)}, f32[2,64,256]{2,1,0:T(8,128)S(1)}, u32[]{:S(2)}, u32[]{:S(2)}) collective-permute-start(f32[2,64,256]{2,1,0:T(8,128)S(1)} %reshape.855), channel_id=1, source_target_pairs={{8,0},{12,4},{16,8},{20,12},{24,16},{28,20},{32,24},{36,28},{40,32... | collective-permute-start | bytes 393224 | tf_op jit(solution)/shard_map/ppermute | solution.py:117
  120.9 7.8 %collective-permute-start.21 = (f32[1,64,256]{2,1,0:T(8,128)S(1)}, f32[1,64,256]{2,1,0:T(8,128)S(1)}, u32[]{:S(2)}, u32[]{:S(2)}) collective-permute-start(f32[1,64,256]{2,1,0:T(8,128)S(1)} %bitcast.78), channel_id=1, source_target_pairs={{12,0},{16,4},{20,8},{24,12},{28,16},{32,20},{36,24},{40,28},{44,3... | collective-permute-start | bytes 196616 | tf_op jit(solution)/shard_map/ppermute | solution.py:117
  128.7 7.5 %collective-permute-start.22 = (f32[12,5,256]{2,1,0:T(8,128)S(1)}, f32[12,5,256]{2,1,0:T(8,128)S(1)}, u32[]{:S(2)}, u32[]{:S(2)}) collective-permute-start(f32[12,5,256]{2,1,0:T(8,128)S(1)} %get-tuple-element.14), channel_id=1, source_target_pairs={{0,1},{1,2},{2,3},{4,5},{5,6},{6,7},{8,9},{9,10},{10,11},{12,13},{... | collective-permute-start | bytes 184328 | tf_op jit(solution)/shard_map/ppermute | solution.py:116
  131.9 6.5 %collective-permute-start.23 = (f32[12,5,256]{2,1,0:T(8,128)S(1)}, f32[12,5,256]{2,1,0:T(8,128)S(1)}, u32[]{:S(2)}, u32[]{:S(2)}) collective-permute-start(f32[12,5,256]{2,1,0:T(8,128)S(1)} %get-tuple-element.15), channel_id=1, source_target_pairs={{1,0},{2,1},{3,2},{5,4},{6,5},{7,6},{9,8},{10,9},{11,10},{13,12},{... | collective-permute-start | bytes 184328 | tf_op jit(solution)/shard_map/ppermute | solution.py:117
  166.6 20.1 %collective-permute-start.29 = (f32[128,512]{1,0:T(8,128)S(1)}, f32[128,512]{1,0:T(8,128)S(1)}, u32[]{:S(2)}, u32[]{:S(2)}) collective-permute-start(f32[128,512]{1,0:T(8,128)S(1)} %get-tuple-element.5), channel_id=1, source_target_pairs={{0,24},{32,56},{64,88},{96,120},{124,100},{92,68},{60,36},{28,4},{... | collective-permute-start | bytes 786440 | tf_op jit(solution)/shard_map/ppermute | solution.py:260
  (31 other events, 108.8 us)

commit v5 on v4

--- a/solution.py
+++ b/solution.py
@@ -125,8 +125,8 @@
     return (place >= 0) & (place < lax.axis_size(axis) * block)
 
 
-def masked(field, block_x, block_y, width):
-    keep = inside("slab", block_x, width)[:, None, None] & inside("pencil", block_y, width)[None, :, None]
+def masked(field, block_x, block_y, width_x, width_y):
+    keep = inside("slab", block_x, width_x)[:, None, None] & inside("pencil", block_y, width_y)[None, :, None]
     return jnp.where(keep, field, 0.0)
 
 
@@ -139,84 +139,76 @@
     return centre, total
 
 
-def core(field, width, block_x, block_y):
-    return field[width:width + block_x, width:width + block_y]
-
-
-def shift_planes(x, axis, distance, first, last, upward):
-    peers = lax.axis_size(axis)
-    pairs = [(j, j + distance) for j in range(peers - distance)]
-    if not upward:
-        pairs = [(b, a) for a, b in pairs]
-    return lax.ppermute(x[first:last], axis, pairs)
-
-
-def crop(field, have, want, block_x, block_y):
-    lose = have - want
-    return field[lose:lose + block_x + 2 * want, lose:lose + block_y + 2 * want]
-
-
-def medium_cycle(medium):
-    block_x, block_y = medium.shape[0], medium.shape[1]
+def crop(field, have_x, have_y, want_x, want_y, block_x, block_y):
+    lose_x, lose_y = have_x - want_x, have_y - want_y
+    return field[lose_x:lose_x + block_x + 2 * want_x, lose_y:lose_y + block_y + 2 * want_y]
+
+
+def sweep(field, block_x, block_y, width_x, width_y):
+    centre, total = shrink_neighbours(field)
+    return lax.optimization_barrier(masked(smoothed(centre, total), block_x, block_y, width_x, width_y))
+
+
+def medium_cycle(medium, medium_y, block_y):
+    block_x = medium.shape[0]
     depth = 7
-    grown = extend(extend(medium, "slab", 0, depth), "pencil", 1, depth)
-    powers = [grown]
-    for width in range(depth - 1, depth - 4, -1):
-        centre, total = shrink_neighbours(powers[-1])
-        powers.append(lax.optimization_barrier(masked(smoothed(centre, total), block_x, block_y, width)))
-    grad_medium = coefficient(1) * crop(powers[0], depth, 2, block_x, block_y)
-    grad_medium = grad_medium + coefficient(1) * crop(powers[1], depth - 1, 2, block_x, block_y)
-    grad_medium = grad_medium + coefficient(1) * crop(powers[2], depth - 2, 2, block_x, block_y)
+    powers = [extend(medium, "slab", 0, depth)]
+    for step in range(1, 4):
+        powers.append(sweep(powers[-1], block_x, block_y, depth - step, medium_y - step))
+    grad_medium = 0.0
+    for step in range(3):
+        part = crop(powers[step], depth - step, medium_y - step, 2, 2, block_x, block_y)
+        grad_medium = grad_medium + coefficient(1) * part
     settled = powers[3]
+    settled_x, settled_y = depth - 3, medium_y - 3
     coarse_cot = children_sum(settled)
     coarse_x, coarse_y = block_x // 2, block_y // 2
+    coarse_wx, coarse_wy = settled_x // 2, settled_y // 2
     coarse_powers = [coarse_cot]
-    for width in (1, 0):
-        centre, total = shrink_neighbours(coarse_powers[-1])
-        coarse_powers.append(lax.optimization_barrier(masked(smoothed(centre, total), coarse_x, coarse_y, width)))
-    grad_coarse = coefficient(2) * core(coarse_powers[0], 2, coarse_x, coarse_y)
-    grad_coarse = grad_coarse + coefficient(2) * core(coarse_powers[1], 1, coarse_x, coarse_y)
-    grad_coarse = grad_coarse + coefficient(2) * coarse_powers[2]
-    back_medium = prolong(grad_coarse) * 0.125
-    back_xy = extend(extend(back_medium, "slab", 0, 5), "pencil", 1, 5)
-    grad_medium = grad_medium + crop(back_xy, 5, 2, block_x, block_y)
+    for step in (1, 2):
+        coarse_powers.append(sweep(coarse_powers[-1], coarse_x, coarse_y, coarse_wx - step, coarse_wy - step))
+    grad_coarse = 0.0
+    for step in range(3):
+        part = crop(coarse_powers[step], coarse_wx - step, coarse_wy - step, 0, 3, coarse_x, coarse_y)
+        grad_coarse = grad_coarse + coefficient(2) * part
+    back_medium = prolong(grad_coarse)[:, 1:-1] * 0.125
+    back_xy = extend(back_medium, "slab", 0, 5)
+    grad_medium = grad_medium + crop(back_xy, 5, 5, 2, 2, block_x, block_y)
     centre, total = shrink_neighbours(back_xy)
-    stage = masked(settled - (6.0 * centre - total) / 4.0, block_x, block_y, 4)
+    near = crop(settled, settled_x, settled_y, 4, 4, block_x, block_y)
+    stage = masked(near - (6.0 * centre - total) / 4.0, block_x, block_y, 4, 4)
     stage = lax.optimization_barrier(stage)
     for width in (4, 3, 2):
-        grad_medium = grad_medium + coefficient(1) * crop(stage, width, 2, block_x, block_y)
+        grad_medium = grad_medium + coefficient(1) * crop(stage, width, width, 2, 2, block_x, block_y)
         if width > 2:
-            centre, total = shrink_neighbours(stage)
-            stage = lax.optimization_barrier(masked(smoothed(centre, total), block_x, block_y, width - 1))
+            stage = sweep(stage, block_x, block_y, width - 1, width - 1)
     return grad_medium
 
 
 def shards(cotangent, seg_rows, owners, offsets):
     x_cells, y_cells, z_cells = cotangent.shape
     tile_size = TILE
-    depth = 5
-    grown = extend(extend(cotangent, "slab", 0, depth), "pencil", 1, depth)
+    depth_x, depth_y = 5, 29
+    grown = extend(extend(cotangent, "slab", 0, depth_x), "pencil", 1, depth_y)
     powers = [grown]
-    for width in range(depth - 1, -1, -1):
-        centre, total = shrink_neighbours(powers[-1])
-        powers.append(lax.optimization_barrier(masked(smoothed(centre, total), x_cells, y_cells, width)))
+    for step in range(1, 6):
+        powers.append(sweep(powers[-1], x_cells, y_cells, depth_x - step, depth_y - step))
     rhs_grad = jnp.zeros_like(cotangent)
-    for level_power in range(depth + 1):
-        part = core(powers[level_power], depth - level_power, x_cells, y_cells)
+    for step in range(6):
+        part = crop(powers[step], depth_x - step, depth_y - step, 0, 0, x_cells, y_cells)
         rhs_grad = rhs_grad + coefficient(0) * part
-    grad_fine = core(powers[3], depth - 3, x_cells, y_cells)
-    medium = children_sum(grad_fine)
-    grown = medium_cycle(medium)
+    settled = crop(powers[3], depth_x - 3, depth_y - 3, 0, depth_y - 3, x_cells, y_cells)
+    medium = children_sum(settled)
+    grown = medium_cycle(medium, (depth_y - 3) // 2, y_cells // 2)
     back_fine = prolong(grown)[1:-1, 1:-1] * 0.125
-    rhs_grad = rhs_grad + core(back_fine, 3, x_cells, y_cells)
+    rhs_grad = rhs_grad + crop(back_fine, 3, 3, 0, 0, x_cells, y_cells)
     centre, total = shrink_neighbours(back_fine)
-    stage = lax.optimization_barrier(masked(6.0 * centre - total, x_cells, y_cells, 2))
+    stage = lax.optimization_barrier(masked(6.0 * centre - total, x_cells, y_cells, 2, 2))
     stages = [stage]
     for width in (1, 0):
-        centre, total = shrink_neighbours(stages[-1])
-        stages.append(lax.optimization_barrier(masked(smoothed(centre, total), x_cells, y_cells, width)))
+        stages.append(sweep(stages[-1], x_cells, y_cells, width, width))
     for number, stage in enumerate(stages):
-        rhs_grad = rhs_grad - coefficient(0) * core(stage, 2 - number, x_cells, y_cells)
+        rhs_grad = rhs_grad - coefficient(0) * crop(stage, 2 - number, 2 - number, 0, 0, x_cells, y_cells)
     slab_index = lax.axis_index("slab")
     slab_count = lax.axis_size("slab")
     low_face = jnp.where(slab_index == 0, rhs_grad[0], 0.0)

time: 199 us -> 210 us (1.055)
  waiting for transfers between devices: 51.9 us -> 56.2 us
  other arithmetic: 37.6 us -> 41.5 us
    select_n x14 -> x16, other arithmetic: 19.4 us -> 27.3 us  [masked(): return jnp.where(keep, field, 0.0)]
    ppermute x7, waiting for transfers between devices: 20 us -> 13.8 us  [spread_faces(): got = lax.ppermute(sent, 'slab', low_pairs + high_pairs)]
    ppermute x12 -> x10, waiting for transfers between devices: 23.6 us -> 28.9 us  [extend(): highs.append(lax.ppermute(high_piece, axis, down))]
    and x12 -> x16, other arithmetic: 4.25 us -> 1.13 us  [masked(): inside('slab', block_x, width_x)[:, None, None]]
    ppermute x7, starting transfers between devices: 4.98 us -> 7.95 us  [spread_faces(): got = lax.ppermute(sent, 'slab', low_pairs + high_pairs)]
    ppermute x12 -> x10, starting transfers between devices: 18.4 us -> 15.4 us  [extend(): highs.append(lax.ppermute(high_piece, axis, down))]
    reshape x0 -> x2, local copies, waits for them, and re-layouts: none -> 2.89 us  [children_sum(): flat = paired.reshape(x_cells // 2 * y_cells, z_cells)]
    ppermute x3, waiting for transfers between devices: 2.46 us -> 5.24 us  [scatter_partials(): lax.ppermute(piece, axis, [(j, (j + step) % peers) for j in range(peers)])]
  transfers between devices with their start and end apart: 34 -> 30, of which waited for: 17 -> 15; matrix products, arithmetic and copies ran while one was open for 8% -> 7% of each run, Pallas kernels for 0% -> 0%
where the time goes in v5:
time: 210 us; the launch traced here: 207 us
  starting transfers between devices  76.8 us (37%)
  waiting for transfers between devices  56.2 us (27%)
  other arithmetic  41.5 us (20%)
  local copies, waits for them, and re-layouts  20.2 us (10%)
  matrix products  10.5 us (5%)
  between operations  2.15 us (1%)
    ppermute x10, starting transfers between devices, extend(): lows.insert(0, lax.ppermute(low_piece, axis, up))  48.1 us
    ppermute x10, waiting for transfers between devices, extend(): highs.append(lax.ppermute(high_piece, axis, down))  28.9 us
    select_n x16, other arithmetic, masked(): return jnp.where(keep, field, 0.0)  27.3 us
    ppermute x10, starting transfers between devices, extend(): highs.append(lax.ppermute(high_piece, axis, down))  15.4 us
    ppermute x7, waiting for transfers between devices, spread_faces(): got = lax.ppermute(sent, 'slab', low_pairs + high_pairs)  13.8 us
    unnamed x65, local copies, waits for them, and re-layouts  8.94 us
    ppermute x10, waiting for transfers between devices, extend(): lows.insert(0, lax.ppermute(low_piece, axis, up))  8.24 us
    ppermute x7, starting transfers between devices, spread_faces(): got = lax.ppermute(sent, 'slab', low_pairs + high_pairs)  7.95 us
  transfers between devices with their start and end apart: 30, of which 15 were waited for; matrix products, arithmetic and copies ran while one was open for 7% of the time, Pallas kernels for 0%

profile of v5, /device:TPU:1, one launch (start us, length us, event | category | flops | bytes accessed | tf_op | source)
XLA Modules:
  0.0 207.4 jit_solution(325124995486764955)
XLA Ops:
  0.6 4.7 %collective-permute-start.1 = (f32[4,128,512]{2,1,0:T(8,128)}, f32[4,128,512]{2,1,0:T(8,128)S(1)}, u32[]{:S(2)}, u32[]{:S(2)}) collective-permute-start(f32[4,128,512]{2,1,0:T(8,128)} %param.4), channel_id=1, source_target_pairs={{0,4},{4,8},{8,12},{12,16},{16,20},{20,24},{24,28},{28,32},{32,36}... | collective-permute-start | bytes 3145736 | tf_op jit(solution)/shard_map/ppermute | solution.py:116
  9.2 3.9 %collective-permute-start = (f32[1,128,512]{2,1,0:T(8,128)}, f32[1,128,512]{2,1,0:T(8,128)}, u32[]{:S(2)}, u32[]{:S(2)}) collective-permute-start(f32[1,128,512]{2,1,0:T(8,128)} %get-tuple-element.11), channel_id=1, source_target_pairs={{0,8},{4,12},{8,16},{12,20},{16,24},{20,28},{24,32},{28,36},{32,40... | collective-permute-start | bytes 786440 | tf_op jit(solution)/shard_map/ppermute | solution.py:116
  15.7 7.3 %collective-permute-done = f32[1,128,512]{2,1,0:T(8,128)} collective-permute-done((f32[1,128,512]{2,1,0:T(8,128)}, f32[1,128,512]{2,1,0:T(8,128)}, u32[]{:S(2)}, u32[]{:S(2)}) %collective-permute-start) | collective-permute-done | bytes 262176 | tf_op jit(solution)/shard_map/ppermute | solution.py:116
  27.7 5.1 %collective-permute-start.4 = (f32[14,29,512]{2,1,0:T(8,128)S(1)}, f32[14,29,512]{2,1,0:T(8,128)}, u32[]{:S(2)}, u32[]{:S(2)}) collective-permute-start(f32[14,29,512]{2,1,0:T(8,128)S(1)} %get-tuple-element.8), channel_id=1, source_target_pairs={{0,1},{1,2},{2,3},{4,5},{5,6},{6,7},{8,9},{9,10},{10,11},{12,13},{... | collective-permute-start | bytes 2494472 | tf_op jit(solution)/shard_map/ppermute | solution.py:116
  33.1 14.1 %collective-permute-done.5 = f32[14,29,512]{2,1,0:T(8,128)S(1)} collective-permute-done((f32[14,29,512]{2,1,0:T(8,128)S(1)}, f32[14,29,512]{2,1,0:T(8,128)S(1)}, u32[]{:S(2)}, u32[]{:S(2)}) %collective-permute-start.5) | collective-permute-done | bytes 831520 | tf_op jit(solution)/shard_map/ppermute | solution.py:117
  48.1 3.0 %pad_maximum_fusion = f32[14,186,512]{2,1,0:T(8,128)S(1)} fusion(f32[14,29,512]{2,1,0:T(8,128)S(1)} %collective-permute-done.5, f32[14,128,512]{2,1,0:T(8,128)} %copy-done.6, f32[14,29,512]{2,1,0:T(8,128)} %collective-permute-done.4), kind=kLoop, calls=%fused_computation.2 | loop fusion | flops 2666496 | bytes 10665984 | tf_op jit(solution)/shard_map/concatenate | solution.py:119
  51.9 4.3 %fusion.4 = f32[12,184,512]{2,1,0:T(8,128)S(1)} fusion(f32[12,184,512]{2,1,0:T(8,128)S(1)} %slice.634, f32[14,186,512]{2,1,0:T(8,128)S(1)} %pad_maximum_fusion, pred[12,184]{1,0:T(8,128)(4,1)S(1)} %broadcast_and_fusion.1), kind=kLoop, calls=%fused_computation.9 | loop fusion | flops 10174464 | bytes 27134112 | tf_op jit(solution)/shard_map/jit(_where)/select_n | solution.py:130
  58.3 3.7 %fusion.9 = f32[10,182,512]{2,1,0:T(8,128)S(1)} fusion(f32[10,182,512]{2,1,0:T(8,128)S(1)} %slice.640, f32[12,184,512]{2,1,0:T(8,128)S(1)} %fusion.4, pred[10,182]{1,0:T(8,128)(4,1)S(1)} %broadcast_and_fusion), kind=kLoop, calls=%fused_computation.19 | loop fusion | flops 8386560 | bytes 22365980 | tf_op jit(solution)/shard_map/jit(_where)/select_n | solution.py:130
  63.8 3.0 %fusion.14 = f32[8,180,512]{2,1,0:T(8,128)S(1)} fusion(f32[8,180,512]{2,1,0:T(8,128)S(1)} %slice.646, f32[10,182,512]{2,1,0:T(8,128)S(1)} %fusion.9, pred[8,180]{1,0:T(8,128)(4,1)S(1)} %broadcast_and_fusion.9), kind=kLoop, calls=%fused_computation.27 | loop fusion | flops 6635520 | bytes 17696160 | tf_op jit(solution)/shard_map/jit(_where)/select_n | solution.py:130
  72.3 5.8 %collective-permute-start.13 = (f32[1,90,256]{2,1,0:T(8,128)S(1)}, f32[1,90,256]{2,1,0:T(8,128)S(1)}, u32[]{:S(2)}, u32[]{:S(2)}) collective-permute-start(f32[1,90,256]{2,1,0:T(8,128)S(1)} %convolution_bitcast_fusion.6), channel_id=1, source_target_pairs={{0,16},{4,20},{8,24},{12,28},{16,32},{20,36},{24,40},{28,44},{32,4... | collective-permute-start | bytes 276488 | tf_op jit(solution)/shard_map/ppermute | solution.py:116
  78.1 8.9 %collective-permute-start.8 = (f32[2,90,256]{2,1,0:T(8,128)S(1)}, f32[2,90,256]{2,1,0:T(8,128)S(1)}, u32[]{:S(2)}, u32[]{:S(2)}) collective-permute-start(f32[2,90,256]{2,1,0:T(8,128)S(1)} %pad_maximum_fusion.7), channel_id=1, source_target_pairs={{0,12},{4,16},{8,20},{12,24},{16,28},{20,32},{24,36},{28,40},{32,4... | collective-permute-start | bytes 552968 | tf_op jit(solution)/shard_map/ppermute | solution.py:116
  88.3 2.5 %collective-permute-start.6 = (f32[2,90,256]{2,1,0:T(8,128)S(1)}, f32[2,90,256]{2,1,0:T(8,128)S(1)}, u32[]{:S(2)}, u32[]{:S(2)}) collective-permute-start(f32[2,90,256]{2,1,0:T(8,128)S(1)} %pad_maximum_fusion.7), channel_id=1, source_target_pairs={{0,4},{4,8},{8,12},{12,16},{16,20},{20,24},{24,28},{28,32},{32,36}... | collective-permute-start | bytes 552968 | tf_op jit(solution)/shard_map/ppermute | solution.py:116
  101.0 3.8 %collective-permute-done.10 = f32[2,90,256]{2,1,0:T(8,128)S(1)} collective-permute-done((f32[2,90,256]{2,1,0:T(8,128)S(1)}, f32[2,90,256]{2,1,0:T(8,128)S(1)}, u32[]{:S(2)}, u32[]{:S(2)}) %collective-permute-start.10) | collective-permute-done | bytes 184352 | tf_op jit(solution)/shard_map/ppermute | solution.py:117
  104.9 3.2 %collective-permute-done.11 = f32[2,90,256]{2,1,0:T(8,128)S(1)} collective-permute-done((f32[2,90,256]{2,1,0:T(8,128)S(1)}, f32[2,90,256]{2,1,0:T(8,128)S(1)}, u32[]{:S(2)}, u32[]{:S(2)}) %collective-permute-start.11) | collective-permute-done | bytes 184352 | tf_op jit(solution)/shard_map/ppermute | solution.py:117
  119.3 7.1 %collective-permute-start.16 = (f32[2,74,256]{2,1,0:T(8,128)S(1)}, f32[2,74,256]{2,1,0:T(8,128)S(1)}, u32[]{:S(2)}, u32[]{:S(2)}) collective-permute-start(f32[2,74,256]{2,1,0:T(8,128)S(1)} %reshape.1011), channel_id=1, source_target_pairs={{0,8},{4,12},{8,16},{12,20},{16,24},{20,28},{24,32},{28,36},{32,40... | collective-permute-start | bytes 454664 | tf_op jit(solution)/shard_map/ppermute | solution.py:116
  126.4 6.9 %collective-permute-start.19 = (f32[1,74,256]{2,1,0:T(8,128)S(1)}, f32[1,74,256]{2,1,0:T(8,128)S(1)}, u32[]{:S(2)}, u32[]{:S(2)}) collective-permute-start(f32[1,74,256]{2,1,0:T(8,128)S(1)} %bitcast.73), channel_id=1, source_target_pairs={{0,12},{4,16},{8,20},{12,24},{16,28},{20,32},{24,36},{28,40},{32,4... | collective-permute-start | bytes 227336 | tf_op jit(solution)/shard_map/ppermute | solution.py:116
  133.4 4.7 %fusion.35 = f32[4,176,512]{2,1,0:T(8,128)} fusion(f32[4,176,512]{2,1,0:T(8,128)} %slice.658, f32[6,178,512]{2,1,0:T(8,128)S(1)} %copy-done.3, pred[4,176]{1,0:T(4,128)(4,1)S(1)} %broadcast_and_fusion.12), kind=kLoop, calls=%fused_computation.76 | loop fusion | flops 3244032 | bytes 8651456 | tf_op jit(solution)/shard_map/jit(_where)/select_n | solution.py:130
  140.0 2.4 %collective-permute-start.15 = (f32[2,74,256]{2,1,0:T(8,128)S(1)}, f32[2,74,256]{2,1,0:T(8,128)S(1)}, u32[]{:S(2)}, u32[]{:S(2)}) collective-permute-start(f32[2,74,256]{2,1,0:T(8,128)S(1)} %reshape.1011), channel_id=1, source_target_pairs={{4,0},{8,4},{12,8},{16,12},{20,16},{24,20},{28,24},{32,28},{36,32}... | collective-permute-start | bytes 454664 | tf_op jit(solution)/shard_map/ppermute | solution.py:117
  146.7 3.8 %collective-permute-done.17 = f32[2,74,256]{2,1,0:T(8,128)S(1)} collective-permute-done((f32[2,74,256]{2,1,0:T(8,128)S(1)}, f32[2,74,256]{2,1,0:T(8,128)S(1)}, u32[]{:S(2)}, u32[]{:S(2)}) %collective-permute-start.17) | collective-permute-done | bytes 151584 | tf_op jit(solution)/shard_map/ppermute | solution.py:117
  166.8 3.3 %fusion.59 = f32[4,128,512]{2,1,0:T(8,128)S(1)} fusion(f32[8,132,512]{2,1,0:T(8,128)S(1)} %fusion.23, f32[10,134,512]{2,1,0:T(8,128)S(1)} %slice_multiply_fusion, f32[4,176,512]{2,1,0:T(8,128)S(1)} %copy-done.10, f32[6,178,512]{2,1,0:T(8,128)} %copy-done.2, f32[8,180,512]{2,1,0:T(8,128)S(1)} %fusion.14, f32[10,182,512]{2,1,0:T(8,128)} %copy-done.1, ...), kind=kLoop, calls=%fused_computation.131 | loop fusion | flops 3407872 | bytes 11534336 | tf_op jit(solution)/shard_map/sub | solution.py:211
  177.3 12.9 %collective-permute-done.25 = f32[128,512]{1,0:T(8,128)S(1)} collective-permute-done((f32[128,512]{1,0:T(8,128)S(1)}, f32[128,512]{1,0:T(8,128)S(1)}, u32[]{:S(2)}, u32[]{:S(2)}) %collective-permute-start.25) | collective-permute-done | bytes 262176 | tf_op jit(solution)/shard_map/ppermute | solution.py:252
  190.3 3.3 %collective-permute-start.26 = (f32[128,512]{1,0:T(8,128)S(1)}, f32[128,512]{1,0:T(8,128)S(1)}, u32[]{:S(2)}, u32[]{:S(2)}) collective-permute-start(f32[128,512]{1,0:T(8,128)S(1)} %get-tuple-element.2), channel_id=1, source_target_pairs={{0,4},{8,12},{16,20},{24,28},{32,36},{40,44},{48,52},{56,60},{64,6... | collective-permute-start | bytes 786440 | tf_op jit(solution)/shard_map/ppermute | solution.py:252
  196.2 4.7 %collective-permute-start.29 = (f32[1,128,128]{2,1,0:T(8,128)S(1)}, f32[1,128,128]{2,1,0:T(8,128)S(1)}, u32[]{:S(2)}, u32[]{:S(2)}) collective-permute-start(f32[1,128,128]{2,1,0:T(8,128)S(1)} %get-tuple-element.13), channel_id=1, source_target_pairs={{0,3},{1,0},{2,1},{3,2},{4,7},{5,4},{6,5},{7,6},{8,11},{9,8},{10,9... | collective-permute-start | bytes 196616 | tf_op jit(solution)/shard_map/ppermute | solution.py:265
  202.8 2.7 %collective-permute-done.28 = f32[1,128,128]{2,1,0:T(8,128)S(1)} collective-permute-done((f32[1,128,128]{2,1,0:T(8,128)S(1)}, f32[1,128,128]{2,1,0:T(8,128)S(1)}, u32[]{:S(2)}, u32[]{:S(2)}) %collective-permute-start.28) | collective-permute-done | bytes 65568 | tf_op jit(solution)/shard_map/ppermute | solution.py:265
  (236 shorter events, 80.5 us)
Async XLA Ops:
  0.6 23.4 %collective-permute-start.1 = (f32[4,128,512]{2,1,0:T(8,128)}, f32[4,128,512]{2,1,0:T(8,128)S(1)}, u32[]{:S(2)}, u32[]{:S(2)}) collective-permute-start(f32[4,128,512]{2,1,0:T(8,128)} %param.4), channel_id=1, source_target_pairs={{0,4},{4,8},{8,12},{12,16},{16,20},{20,24},{24,28},{28,32},{32,36}... | collective-permute-start | bytes 3145736 | tf_op jit(solution)/shard_map/ppermute | solution.py:116
  5.4 19.1 %collective-permute-start.2 = (f32[4,128,512]{2,1,0:T(8,128)}, f32[4,128,512]{2,1,0:T(8,128)S(1)}, u32[]{:S(2)}, u32[]{:S(2)}) collective-permute-start(f32[4,128,512]{2,1,0:T(8,128)} %param.4), channel_id=1, source_target_pairs={{4,0},{8,4},{12,8},{16,12},{20,16},{24,20},{28,24},{32,28},{36,32}... | collective-permute-start | bytes 3145736 | tf_op jit(solution)/shard_map/ppermute | solution.py:117
  9.2 13.9 %collective-permute-start = (f32[1,128,512]{2,1,0:T(8,128)}, f32[1,128,512]{2,1,0:T(8,128)}, u32[]{:S(2)}, u32[]{:S(2)}) collective-permute-start(f32[1,128,512]{2,1,0:T(8,128)} %get-tuple-element.11), channel_id=1, source_target_pairs={{0,8},{4,12},{8,16},{12,20},{16,24},{20,28},{24,32},{28,36},{32,40... | collective-permute-start | bytes 786440 | tf_op jit(solution)/shard_map/ppermute | solution.py:116
  13.1 11.5 %collective-permute-start.3 = (f32[1,128,512]{2,1,0:T(8,128)}, f32[1,128,512]{2,1,0:T(8,128)S(1)}, u32[]{:S(2)}, u32[]{:S(2)}) collective-permute-start(f32[1,128,512]{2,1,0:T(8,128)} %get-tuple-element.10), channel_id=1, source_target_pairs={{8,0},{12,4},{16,8},{20,12},{24,16},{28,20},{32,24},{36,28},{40,32... | collective-permute-start | bytes 786440 | tf_op jit(solution)/shard_map/ppermute | solution.py:117
  26.4 20.8 %collective-permute-start.5 = (f32[14,29,512]{2,1,0:T(8,128)S(1)}, f32[14,29,512]{2,1,0:T(8,128)S(1)}, u32[]{:S(2)}, u32[]{:S(2)}) collective-permute-start(f32[14,29,512]{2,1,0:T(8,128)S(1)} %get-tuple-element.9), channel_id=1, source_target_pairs={{1,0},{2,1},{3,2},{5,4},{6,5},{7,6},{9,8},{10,9},{11,10},{13,12},{... | collective-permute-start | bytes 2494472 | tf_op jit(solution)/shard_map/ppermute | solution.py:117
  27.7 20.4 %collective-permute-start.4 = (f32[14,29,512]{2,1,0:T(8,128)S(1)}, f32[14,29,512]{2,1,0:T(8,128)}, u32[]{:S(2)}, u32[]{:S(2)}) collective-permute-start(f32[14,29,512]{2,1,0:T(8,128)S(1)} %get-tuple-element.8), channel_id=1, source_target_pairs={{0,1},{1,2},{2,3},{4,5},{5,6},{6,7},{8,9},{9,10},{10,11},{12,13},{... | collective-permute-start | bytes 2494472 | tf_op jit(solution)/shard_map/ppermute | solution.py:116
  72.3 24.3 %collective-permute-start.13 = (f32[1,90,256]{2,1,0:T(8,128)S(1)}, f32[1,90,256]{2,1,0:T(8,128)S(1)}, u32[]{:S(2)}, u32[]{:S(2)}) collective-permute-start(f32[1,90,256]{2,1,0:T(8,128)S(1)} %convolution_bitcast_fusion.6), channel_id=1, source_target_pairs={{0,16},{4,20},{8,24},{12,28},{16,32},{20,36},{24,40},{28,44},{32,4... | collective-permute-start | bytes 276488 | tf_op jit(solution)/shard_map/ppermute | solution.py:116
  78.1 19.8 %collective-permute-start.8 = (f32[2,90,256]{2,1,0:T(8,128)S(1)}, f32[2,90,256]{2,1,0:T(8,128)S(1)}, u32[]{:S(2)}, u32[]{:S(2)}) collective-permute-start(f32[2,90,256]{2,1,0:T(8,128)S(1)} %pad_maximum_fusion.7), channel_id=1, source_target_pairs={{0,12},{4,16},{8,20},{12,24},{16,28},{20,32},{24,36},{28,40},{32,4... | collective-permute-start | bytes 552968 | tf_op jit(solution)/shard_map/ppermute | solution.py:116
  87.0 12.3 %collective-permute-start.9 = (f32[2,90,256]{2,1,0:T(8,128)S(1)}, f32[2,90,256]{2,1,0:T(8,128)S(1)}, u32[]{:S(2)}, u32[]{:S(2)}) collective-permute-start(f32[2,90,256]{2,1,0:T(8,128)S(1)} %pad_maximum_fusion.7), channel_id=1, source_target_pairs={{0,8},{4,12},{8,16},{12,20},{16,24},{20,28},{24,32},{28,36},{32,40... | collective-permute-start | bytes 552968 | tf_op jit(solution)/shard_map/ppermute | solution.py:116
  88.3 12.5 %collective-permute-start.6 = (f32[2,90,256]{2,1,0:T(8,128)S(1)}, f32[2,90,256]{2,1,0:T(8,128)S(1)}, u32[]{:S(2)}, u32[]{:S(2)}) collective-permute-start(f32[2,90,256]{2,1,0:T(8,128)S(1)} %pad_maximum_fusion.7), channel_id=1, source_target_pairs={{0,4},{4,8},{8,12},{12,16},{16,20},{20,24},{24,28},{28,32},{32,36}... | collective-permute-start | bytes 552968 | tf_op jit(solution)/shard_map/ppermute | solution.py:116
  90.8 10.2 %collective-permute-start.7 = (f32[2,90,256]{2,1,0:T(8,128)S(1)}, f32[2,90,256]{2,1,0:T(8,128)S(1)}, u32[]{:S(2)}, u32[]{:S(2)}) collective-permute-start(f32[2,90,256]{2,1,0:T(8,128)S(1)} %pad_maximum_fusion.7), channel_id=1, source_target_pairs={{4,0},{8,4},{12,8},{16,12},{20,16},{24,20},{28,24},{32,28},{36,32}... | collective-permute-start | bytes 552968 | tf_op jit(solution)/shard_map/ppermute | solution.py:117
  96.6 8.2 %collective-permute-start.10 = (f32[2,90,256]{2,1,0:T(8,128)S(1)}, f32[2,90,256]{2,1,0:T(8,128)S(1)}, u32[]{:S(2)}, u32[]{:S(2)}) collective-permute-start(f32[2,90,256]{2,1,0:T(8,128)S(1)} %pad_maximum_fusion.7), channel_id=1, source_target_pairs={{8,0},{12,4},{16,8},{20,12},{24,16},{28,20},{32,24},{36,28},{40,32... | collective-permute-start | bytes 552968 | tf_op jit(solution)/shard_map/ppermute | solution.py:117
  97.9 10.2 %collective-permute-start.11 = (f32[2,90,256]{2,1,0:T(8,128)S(1)}, f32[2,90,256]{2,1,0:T(8,128)S(1)}, u32[]{:S(2)}, u32[]{:S(2)}) collective-permute-start(f32[2,90,256]{2,1,0:T(8,128)S(1)} %pad_maximum_fusion.7), channel_id=1, source_target_pairs={{12,0},{16,4},{20,8},{24,12},{28,16},{32,20},{36,24},{40,28},{44,3... | collective-permute-start | bytes 552968 | tf_op jit(solution)/shard_map/ppermute | solution.py:117
  99.3 10.2 %collective-permute-start.12 = (f32[1,90,256]{2,1,0:T(8,128)S(1)}, f32[1,90,256]{2,1,0:T(8,128)S(1)}, u32[]{:S(2)}, u32[]{:S(2)}) collective-permute-start(f32[1,90,256]{2,1,0:T(8,128)S(1)} %convolution_bitcast_fusion.7), channel_id=1, source_target_pairs={{16,0},{20,4},{24,8},{28,12},{32,16},{36,20},{40,24},{44,28},{48,3... | collective-permute-start | bytes 276488 | tf_op jit(solution)/shard_map/ppermute | solution.py:117
  119.3 25.7 %collective-permute-start.16 = (f32[2,74,256]{2,1,0:T(8,128)S(1)}, f32[2,74,256]{2,1,0:T(8,128)S(1)}, u32[]{:S(2)}, u32[]{:S(2)}) collective-permute-start(f32[2,74,256]{2,1,0:T(8,128)S(1)} %reshape.1011), channel_id=1, source_target_pairs={{0,8},{4,12},{8,16},{12,20},{16,24},{20,28},{24,32},{28,36},{32,40... | collective-permute-start | bytes 454664 | tf_op jit(solution)/shard_map/ppermute | solution.py:116
  126.4 17.3 %collective-permute-start.19 = (f32[1,74,256]{2,1,0:T(8,128)S(1)}, f32[1,74,256]{2,1,0:T(8,128)S(1)}, u32[]{:S(2)}, u32[]{:S(2)}) collective-permute-start(f32[1,74,256]{2,1,0:T(8,128)S(1)} %bitcast.73), channel_id=1, source_target_pairs={{0,12},{4,16},{8,20},{12,24},{16,28},{20,32},{24,36},{28,40},{32,4... | collective-permute-start | bytes 227336 | tf_op jit(solution)/shard_map/ppermute | solution.py:116
  138.1 7.0 %collective-permute-start.14 = (f32[2,74,256]{2,1,0:T(8,128)S(1)}, f32[2,74,256]{2,1,0:T(8,128)S(1)}, u32[]{:S(2)}, u32[]{:S(2)}) collective-permute-start(f32[2,74,256]{2,1,0:T(8,128)S(1)} %reshape.1011), channel_id=1, source_target_pairs={{0,4},{4,8},{8,12},{12,16},{16,20},{20,24},{24,28},{28,32},{32,36}... | collective-permute-start | bytes 454664 | tf_op jit(solution)/shard_map/ppermute | solution.py:116
  140.0 6.6 %collective-permute-start.15 = (f32[2,74,256]{2,1,0:T(8,128)S(1)}, f32[2,74,256]{2,1,0:T(8,128)S(1)}, u32[]{:S(2)}, u32[]{:S(2)}) collective-permute-start(f32[2,74,256]{2,1,0:T(8,128)S(1)} %reshape.1011), channel_id=1, source_target_pairs={{4,0},{8,4},{12,8},{16,12},{20,16},{24,20},{28,24},{32,28},{36,32}... | collective-permute-start | bytes 454664 | tf_op jit(solution)/shard_map/ppermute | solution.py:117
  142.4 8.0 %collective-permute-start.17 = (f32[2,74,256]{2,1,0:T(8,128)S(1)}, f32[2,74,256]{2,1,0:T(8,128)S(1)}, u32[]{:S(2)}, u32[]{:S(2)}) collective-permute-start(f32[2,74,256]{2,1,0:T(8,128)S(1)} %reshape.1011), channel_id=1, source_target_pairs={{8,0},{12,4},{16,8},{20,12},{24,16},{28,20},{32,24},{36,28},{40,32... | collective-permute-start | bytes 454664 | tf_op jit(solution)/shard_map/ppermute | solution.py:117
  143.7 8.0 %collective-permute-start.18 = (f32[1,74,256]{2,1,0:T(8,128)S(1)}, f32[1,74,256]{2,1,0:T(8,128)S(1)}, u32[]{:S(2)}, u32[]{:S(2)}) collective-permute-start(f32[1,74,256]{2,1,0:T(8,128)S(1)} %bitcast.74), channel_id=1, source_target_pairs={{12,0},{16,4},{20,8},{24,12},{28,16},{32,20},{36,24},{40,28},{44,3... | collective-permute-start | bytes 227336 | tf_op jit(solution)/shard_map/ppermute | solution.py:117
  174.5 15.6 %collective-permute-start.25 = (f32[128,512]{1,0:T(8,128)S(1)}, f32[128,512]{1,0:T(8,128)S(1)}, u32[]{:S(2)}, u32[]{:S(2)}) collective-permute-start(f32[128,512]{1,0:T(8,128)S(1)} %get-tuple-element.5), channel_id=1, source_target_pairs={{0,24},{32,56},{64,88},{96,120},{124,100},{92,68},{60,36},{28,4},{... | collective-permute-start | bytes 786440 | tf_op jit(solution)/shard_map/ppermute | solution.py:252
  175.8 14.4 %collective-permute-start.24 = (f32[128,512]{1,0:T(8,128)S(1)}, f32[128,512]{1,0:T(8,128)S(1)}, u32[]{:S(2)}, u32[]{:S(2)}) collective-permute-start(f32[128,512]{1,0:T(8,128)S(1)} %get-tuple-element.5), channel_id=1, source_target_pairs={{0,16},{32,48},{64,80},{96,112},{124,108},{92,76},{60,44},{28,12},... | collective-permute-start | bytes 786440 | tf_op jit(solution)/shard_map/ppermute | solution.py:252
  176.5 13.7 %collective-permute-start.23 = (f32[128,512]{1,0:T(8,128)S(1)}, f32[128,512]{1,0:T(8,128)S(1)}, u32[]{:S(2)}, u32[]{:S(2)}) collective-permute-start(f32[128,512]{1,0:T(8,128)S(1)} %get-tuple-element.5), channel_id=1, source_target_pairs={{0,8},{32,40},{64,72},{96,104},{124,116},{92,84},{60,52},{28,20},{... | collective-permute-start | bytes 786440 | tf_op jit(solution)/shard_map/ppermute | solution.py:252
  196.2 6.6 %collective-permute-start.29 = (f32[1,128,128]{2,1,0:T(8,128)S(1)}, f32[1,128,128]{2,1,0:T(8,128)S(1)}, u32[]{:S(2)}, u32[]{:S(2)}) collective-permute-start(f32[1,128,128]{2,1,0:T(8,128)S(1)} %get-tuple-element.13), channel_id=1, source_target_pairs={{0,3},{1,0},{2,1},{3,2},{4,7},{5,4},{6,5},{7,6},{8,11},{9,8},{10,9... | collective-permute-start | bytes 196616 | tf_op jit(solution)/shard_map/ppermute | solution.py:265
  (29 other events, 178.1 us)

commit v6 on v4

--- a/solution.py
+++ b/solution.py
@@ -143,14 +143,6 @@
     return field[width:width + block_x, width:width + block_y]
 
 
-def shift_planes(x, axis, distance, first, last, upward):
-    peers = lax.axis_size(axis)
-    pairs = [(j, j + distance) for j in range(peers - distance)]
-    if not upward:
-        pairs = [(b, a) for a, b in pairs]
-    return lax.ppermute(x[first:last], axis, pairs)
-
-
 def crop(field, have, want, block_x, block_y):
     lose = have - want
     return field[lose:lose + block_x + 2 * want, lose:lose + block_y + 2 * want]
@@ -158,7 +150,7 @@
 
 def medium_cycle(medium):
     block_x, block_y = medium.shape[0], medium.shape[1]
-    depth = 7
+    depth = 13
     grown = extend(extend(medium, "slab", 0, depth), "pencil", 1, depth)
     powers = [grown]
     for width in range(depth - 1, depth - 4, -1):
@@ -168,20 +160,23 @@
     grad_medium = grad_medium + coefficient(1) * crop(powers[1], depth - 1, 2, block_x, block_y)
     grad_medium = grad_medium + coefficient(1) * crop(powers[2], depth - 2, 2, block_x, block_y)
     settled = powers[3]
+    settled_width = depth - 3
     coarse_cot = children_sum(settled)
     coarse_x, coarse_y = block_x // 2, block_y // 2
+    coarse_width = settled_width // 2
     coarse_powers = [coarse_cot]
-    for width in (1, 0):
+    for step in (1, 2):
         centre, total = shrink_neighbours(coarse_powers[-1])
-        coarse_powers.append(lax.optimization_barrier(masked(smoothed(centre, total), coarse_x, coarse_y, width)))
-    grad_coarse = coefficient(2) * core(coarse_powers[0], 2, coarse_x, coarse_y)
-    grad_coarse = grad_coarse + coefficient(2) * core(coarse_powers[1], 1, coarse_x, coarse_y)
-    grad_coarse = grad_coarse + coefficient(2) * coarse_powers[2]
-    back_medium = prolong(grad_coarse) * 0.125
-    back_xy = extend(extend(back_medium, "slab", 0, 5), "pencil", 1, 5)
+        coarse_powers.append(lax.optimization_barrier(masked(smoothed(centre, total), coarse_x, coarse_y, coarse_width - step)))
+    grad_coarse = 0.0
+    for step in range(3):
+        part = crop(coarse_powers[step], coarse_width - step, 3, coarse_x, coarse_y)
+        grad_coarse = grad_coarse + coefficient(2) * part
+    back_xy = prolong(grad_coarse)[1:-1, 1:-1] * 0.125
     grad_medium = grad_medium + crop(back_xy, 5, 2, block_x, block_y)
     centre, total = shrink_neighbours(back_xy)
-    stage = masked(settled - (6.0 * centre - total) / 4.0, block_x, block_y, 4)
+    near = crop(settled, settled_width, 4, block_x, block_y)
+    stage = masked(near - (6.0 * centre - total) / 4.0, block_x, block_y, 4)
     stage = lax.optimization_barrier(stage)
     for width in (4, 3, 2):
         grad_medium = grad_medium + coefficient(1) * crop(stage, width, 2, block_x, block_y)

time: 199 us -> 214 us (1.075)
  other arithmetic: 37.6 us -> 48.1 us
  local copies, waits for them, and re-layouts: 19.3 us -> 27.5 us
  starting transfers between devices: 77.5 us -> 69.8 us
  matrix products: 9 us -> 13.5 us
    select_n x14, other arithmetic: 19.4 us -> 25 us  [masked(): return jnp.where(keep, field, 0.0)]
    ppermute x12 -> x11, starting transfers between devices: 50.1 us -> 45.9 us  [extend(): lows.insert(0, lax.ppermute(low_piece, axis, up))]
    unnamed x61 -> x73, local copies, waits for them, and re-layouts: 9.36 us -> 13.1 us
    ppermute x7, waiting for transfers between devices: 20 us -> 16.3 us  [spread_faces(): got = lax.ppermute(sent, 'slab', low_pairs + high_pairs)]
    concatenate x3 -> x2, other arithmetic: 1.19 us -> 4.23 us  [extend(): return jnp.concatenate(lows + [x] + highs, axis=dim)]
    ppermute x12 -> x11, starting transfers between devices: 18.4 us -> 15.4 us  [extend(): highs.append(lax.ppermute(high_piece, axis, down))]
    reshape x1, local copies, waits for them, and re-layouts: 0.01 us -> 2.25 us  [children_sum(): flat = paired.reshape(x_cells // 2 * y_cells, z_cells)]
    ppermute x12 -> x11, waiting for transfers between devices: 5.81 us -> 8.03 us  [extend(): lows.insert(0, lax.ppermute(low_piece, axis, up))]
  transfers between devices with their start and end apart: 34 -> 32, of which waited for: 17 -> 17; matrix products, arithmetic and copies ran while one was open for 8% -> 7% of each run, Pallas kernels for 0% -> 0%
where the time goes in v6:
time: 214 us; the launch traced here: 211 us
  starting transfers between devices  69.8 us (33%)
  waiting for transfers between devices  49.9 us (23%)
  other arithmetic  48.1 us (22%)
  local copies, waits for them, and re-layouts  27.5 us (13%)
  matrix products  13.5 us (6%)
  between operations  2.24 us (1%)
    ppermute x11, starting transfers between devices, extend(): lows.insert(0, lax.ppermute(low_piece, axis, up))  45.9 us
    select_n x14, other arithmetic, masked(): return jnp.where(keep, field, 0.0)  25 us
    ppermute x11, waiting for transfers between devices, extend(): highs.append(lax.ppermute(high_piece, axis, down))  22.6 us
    ppermute x7, waiting for transfers between devices, spread_faces(): got = lax.ppermute(sent, 'slab', low_pairs + high_pairs)  16.3 us
    ppermute x11, starting transfers between devices, extend(): highs.append(lax.ppermute(high_piece, axis, down))  15.4 us
    unnamed x73, local copies, waits for them, and re-layouts  13.1 us
    ppermute x11, waiting for transfers between devices, extend(): lows.insert(0, lax.ppermute(low_piece, axis, up))  8.03 us
    and x13, other arithmetic, masked(): inside('slab', block_x, width)[:, None, None]  6.23 us
  transfers between devices with their start and end apart: 32, of which 17 were waited for; matrix products, arithmetic and copies ran while one was open for 7% of the time, Pallas kernels for 0%

profile of v6, /device:TPU:1, one launch (start us, length us, event | category | flops | bytes accessed | tf_op | source)
XLA Modules:
  0.0 211.0 jit_solution(8059746532749213690)
XLA Ops:
  0.6 4.7 %collective-permute-start.1 = (f32[4,128,512]{2,1,0:T(8,128)}, f32[4,128,512]{2,1,0:T(8,128)S(1)}, u32[]{:S(2)}, u32[]{:S(2)}) collective-permute-start(f32[4,128,512]{2,1,0:T(8,128)} %param.4), channel_id=1, source_target_pairs={{0,4},{4,8},{8,12},{12,16},{16,20},{20,24},{24,28},{28,32},{32,36}... | collective-permute-start | bytes 3145736 | tf_op jit(solution)/shard_map/ppermute | solution.py:116
  9.1 3.9 %collective-permute-start = (f32[1,128,512]{2,1,0:T(8,128)}, f32[1,128,512]{2,1,0:T(8,128)}, u32[]{:S(2)}, u32[]{:S(2)}) collective-permute-start(f32[1,128,512]{2,1,0:T(8,128)} %get-tuple-element.13), channel_id=1, source_target_pairs={{0,8},{4,12},{8,16},{12,20},{16,24},{20,28},{24,32},{28,36},{32,40... | collective-permute-start | bytes 786440 | tf_op jit(solution)/shard_map/ppermute | solution.py:116
  26.5 3.6 %collective-permute-start.4 = (f32[14,5,512]{2,1,0:T(8,128)S(1)}, f32[14,5,512]{2,1,0:T(8,128)S(1)}, u32[]{:S(2)}, u32[]{:S(2)}) collective-permute-start(f32[14,5,512]{2,1,0:T(8,128)S(1)} %get-tuple-element.8), channel_id=1, source_target_pairs={{0,1},{1,2},{2,3},{4,5},{5,6},{6,7},{8,9},{9,10},{10,11},{12,13},{... | collective-permute-start | bytes 430088 | tf_op jit(solution)/shard_map/ppermute | solution.py:116
  33.0 4.0 %collective-permute-done.5 = f32[14,5,512]{2,1,0:T(8,128)S(1)} collective-permute-done((f32[14,5,512]{2,1,0:T(8,128)S(1)}, f32[14,5,512]{2,1,0:T(8,128)S(1)}, u32[]{:S(2)}, u32[]{:S(2)}) %collective-permute-start.5) | collective-permute-done | bytes 143392 | tf_op jit(solution)/shard_map/ppermute | solution.py:117
  37.0 2.8 %pad_maximum_fusion = f32[14,138,512]{2,1,0:T(8,128)S(1)} fusion(f32[14,5,512]{2,1,0:T(8,128)S(1)} %collective-permute-done.5, f32[14,128,512]{2,1,0:T(8,128)} %copy-done.11, f32[14,5,512]{2,1,0:T(8,128)S(1)} %collective-permute-done.4), kind=kLoop, calls=%fused_computation.2 | loop fusion | flops 1978368 | bytes 7913472 | tf_op jit(solution)/shard_map/concatenate | solution.py:119
  40.4 3.2 %fusion.4 = f32[12,136,512]{2,1,0:T(8,128)S(1)} fusion(f32[12,136,512]{2,1,0:T(8,128)S(1)} %slice.679, f32[14,138,512]{2,1,0:T(8,128)S(1)} %pad_maximum_fusion, pred[12,136]{1,0:T(8,128)(4,1)S(1)} %broadcast_and_fusion.2), kind=kLoop, calls=%fused_computation.13 | loop fusion | flops 7520256 | bytes 20055648 | tf_op jit(solution)/shard_map/jit(_where)/select_n | solution.py:130
  43.9 2.6 %fusion.9 = f32[10,134,512]{2,1,0:T(8,128)S(1)} fusion(f32[10,134,512]{2,1,0:T(8,128)S(1)} %slice.685, f32[12,136,512]{2,1,0:T(8,128)S(1)} %fusion.4, pred[10,134]{1,0:T(8,128)(4,1)S(1)} %broadcast_and_fusion.1), kind=kLoop, calls=%fused_computation.27 | loop fusion | flops 6174720 | bytes 16467260 | tf_op jit(solution)/shard_map/jit(_where)/select_n | solution.py:130
  52.7 8.6 %collective-permute-start.6 = (f32[1,64,256]{2,1,0:T(8,128)S(1)}, f32[1,64,256]{2,1,0:T(8,128)S(1)}, u32[]{:S(2)}, u32[]{:S(2)}) collective-permute-start(f32[1,64,256]{2,1,0:T(8,128)S(1)} %convolution_bitcast_fusion.14), channel_id=1, source_target_pairs={{0,28},{4,32},{8,36},{12,40},{16,44},{20,48},{24,52},{28,56},{32,6... | collective-permute-start | bytes 196616 | tf_op jit(solution)/shard_map/ppermute | solution.py:116
  62.0 6.1 %collective-permute-start.7 = (f32[2,64,256]{2,1,0:T(8,128)}, f32[2,64,256]{2,1,0:T(8,128)}, u32[]{:S(2)}, u32[]{:S(2)}) collective-permute-start(f32[2,64,256]{2,1,0:T(8,128)} %pad_maximum_fusion.3), channel_id=1, source_target_pairs={{0,24},{4,28},{8,32},{12,36},{16,40},{20,44},{24,48},{28,52},{32,5... | collective-permute-start | bytes 393224 | tf_op jit(solution)/shard_map/ppermute | solution.py:116
  69.9 2.6 %collective-permute-start.9 = (f32[2,64,256]{2,1,0:T(8,128)}, f32[2,64,256]{2,1,0:T(8,128)S(1)}, u32[]{:S(2)}, u32[]{:S(2)}) collective-permute-start(f32[2,64,256]{2,1,0:T(8,128)} %pad_maximum_fusion.3), channel_id=1, source_target_pairs={{0,16},{4,20},{8,24},{12,28},{16,32},{20,36},{24,40},{28,44},{32,4... | collective-permute-start | bytes 393224 | tf_op jit(solution)/shard_map/ppermute | solution.py:116
  72.4 5.1 %collective-permute-start.10 = (f32[2,64,256]{2,1,0:T(8,128)}, f32[2,64,256]{2,1,0:T(8,128)S(1)}, u32[]{:S(2)}, u32[]{:S(2)}) collective-permute-start(f32[2,64,256]{2,1,0:T(8,128)} %pad_maximum_fusion.3), channel_id=1, source_target_pairs={{0,12},{4,16},{8,20},{12,24},{16,28},{20,32},{24,36},{28,40},{32,4... | collective-permute-start | bytes 393224 | tf_op jit(solution)/shard_map/ppermute | solution.py:116
  77.6 2.8 %collective-permute-start.11 = (f32[2,64,256]{2,1,0:T(8,128)}, f32[2,64,256]{2,1,0:T(8,128)S(1)}, u32[]{:S(2)}, u32[]{:S(2)}) collective-permute-start(f32[2,64,256]{2,1,0:T(8,128)} %pad_maximum_fusion.3), channel_id=1, source_target_pairs={{0,8},{4,12},{8,16},{12,20},{16,24},{20,28},{24,32},{28,36},{32,40... | collective-permute-start | bytes 393224 | tf_op jit(solution)/shard_map/ppermute | solution.py:116
  80.4 3.1 %collective-permute-start.12 = (f32[2,64,256]{2,1,0:T(8,128)}, f32[2,64,256]{2,1,0:T(8,128)S(1)}, u32[]{:S(2)}, u32[]{:S(2)}) collective-permute-start(f32[2,64,256]{2,1,0:T(8,128)} %pad_maximum_fusion.3), channel_id=1, source_target_pairs={{0,4},{4,8},{8,12},{12,16},{16,20},{20,24},{24,28},{28,32},{32,36}... | collective-permute-start | bytes 393224 | tf_op jit(solution)/shard_map/ppermute | solution.py:116
  99.4 4.2 %collective-permute-done.17 = f32[2,64,256]{2,1,0:T(8,128)S(1)} collective-permute-done((f32[2,64,256]{2,1,0:T(8,128)}, f32[2,64,256]{2,1,0:T(8,128)S(1)}, u32[]{:S(2)}, u32[]{:S(2)}) %collective-permute-start.17) | collective-permute-done | bytes 131104 | tf_op jit(solution)/shard_map/ppermute | solution.py:117
  104.5 3.4 %collective-permute-done.19 = f32[1,64,256]{2,1,0:T(8,128)S(1)} collective-permute-done((f32[1,64,256]{2,1,0:T(8,128)S(1)}, f32[1,64,256]{2,1,0:T(8,128)S(1)}, u32[]{:S(2)}, u32[]{:S(2)}) %collective-permute-start.19) | collective-permute-done | bytes 65568 | tf_op jit(solution)/shard_map/ppermute | solution.py:117
  110.1 4.3 %collective-permute-start.20 = (f32[28,13,256]{2,1,0:T(8,128)}, f32[28,13,256]{2,1,0:T(8,128)}, u32[]{:S(2)}, u32[]{:S(2)}) collective-permute-start(f32[28,13,256]{2,1,0:T(8,128)} %get-tuple-element.10), channel_id=1, source_target_pairs={{0,1},{1,2},{2,3},{4,5},{5,6},{6,7},{8,9},{9,10},{10,11},{12,13},{... | collective-permute-start | bytes 1118216 | tf_op jit(solution)/shard_map/ppermute | solution.py:116
  115.8 3.0 %slice.697 = f32[6,130,512]{2,1,0:T(8,128)} slice(f32[8,132,512]{2,1,0:T(8,128)} %copy-done.3), slice={[1:7], [1:131], [0:512]} | slice | bytes 3194880 | tf_op jit(solution)/shard_map/slice | solution.py:134
  118.8 4.8 %collective-permute-done.20 = f32[28,13,256]{2,1,0:T(8,128)} collective-permute-done((f32[28,13,256]{2,1,0:T(8,128)}, f32[28,13,256]{2,1,0:T(8,128)}, u32[]{:S(2)}, u32[]{:S(2)}) %collective-permute-start.20) | collective-permute-done | bytes 372768 | tf_op jit(solution)/shard_map/ppermute | solution.py:116
  123.6 4.8 %collective-permute-done.21 = f32[28,13,256]{2,1,0:T(8,128)} collective-permute-done((f32[28,13,256]{2,1,0:T(8,128)}, f32[28,13,256]{2,1,0:T(8,128)}, u32[]{:S(2)}, u32[]{:S(2)}) %collective-permute-start.21) | collective-permute-done | bytes 372768 | tf_op jit(solution)/shard_map/ppermute | solution.py:117
  136.1 2.8 %fusion.35 = f32[22,84,256]{2,1,0:T(8,128)} fusion(f32[22,84,256]{2,1,0:T(8,128)S(1)} %slice.723, f32[24,86,256]{2,1,0:T(8,128)S(1)} %fusion.28, pred[22,84]{1,0:T(8,128)(4,1)S(1)} %copy-done.13), kind=kLoop, calls=%fused_computation.74 | loop fusion | flops 4257792 | bytes 11355960 | tf_op jit(solution)/shard_map/jit(_where)/select_n | solution.py:130
  138.9 2.7 %reduce_sum.28 = f32[11,84,256]{2,1,0:T(8,128)} reduce(f32[11,2,84,256]{3,2,1,0:T(8,128)} %bitcast.114, f32[]{:T(128)} %constant.300.clone.1), dimensions={1}, to_apply=%region_1.2 | reduce | flops 236544 | bytes 2838532 | tf_op jit(solution)/shard_map/reduce_sum | solution.py:59
  170.1 3.1 %fusion.45 = (f32[6,130,512]{2,1,0:T(8,128)S(1)}, f32[6,130,512]{2,1,0:T(8,128)S(1)}) fusion(f32[6,130,512]{2,1,0:T(8,128)S(1)} %slice.790, f32[8,132,512]{2,1,0:T(8,128)S(1)} %fusion.23, pred[6,130]{1,0:T(8,128)(4,1)S(1)} %copy-done.18, f32[6,130,512]{2,1,0:T(8,128)S(1)} %copy-done.8, f32[8,132,512]{2,1,0:T(8,128)S(1)} %copy-done.4), kind=kLoop, calls=%fused_computation.87 | loop fusion | flops 7188480 | bytes 19170060 | tf_op jit(solution)/shard_map/jit(_where)/select_n | solution.py:130
  175.7 2.6 %fusion.73 = f32[4,128,512]{2,1,0:T(8,128)S(1)} fusion(f32[8,132,512]{2,1,0:T(8,128)S(1)} %fusion.23, f32[10,134,512]{2,1,0:T(8,128)S(1)} %slice_multiply_fusion, f32[4,128,512]{2,1,0:T(8,128)S(1)} %get-tuple-element.54, f32[10,134,512]{2,1,0:T(8,128)} %copy-done, f32[4,128,512]{2,1,0:T(8,128)S(1)} %copy-done.10, f32[12,136,512]{2,1,0:T(8,128)S(1)} %fusion.4, ...), kind=kLoop, calls=%fused_computation.157 | loop fusion | flops 3407872 | bytes 11534336 | tf_op jit(solution)/shard_map/sub | solution.py:214
  185.4 15.4 %collective-permute-done.27 = f32[128,512]{1,0:T(8,128)S(1)} collective-permute-done((f32[128,512]{1,0:T(8,128)S(1)}, f32[128,512]{1,0:T(8,128)S(1)}, u32[]{:S(2)}, u32[]{:S(2)}) %collective-permute-start.27) | collective-permute-done | bytes 262176 | tf_op jit(solution)/shard_map/ppermute | solution.py:255
  (255 shorter events, 104.7 us)
Async XLA Ops:
  0.6 23.4 %collective-permute-start.1 = (f32[4,128,512]{2,1,0:T(8,128)}, f32[4,128,512]{2,1,0:T(8,128)S(1)}, u32[]{:S(2)}, u32[]{:S(2)}) collective-permute-start(f32[4,128,512]{2,1,0:T(8,128)} %param.4), channel_id=1, source_target_pairs={{0,4},{4,8},{8,12},{12,16},{16,20},{20,24},{24,28},{28,32},{32,36}... | collective-permute-start | bytes 3145736 | tf_op jit(solution)/shard_map/ppermute | solution.py:116
  5.4 19.1 %collective-permute-start.2 = (f32[4,128,512]{2,1,0:T(8,128)}, f32[4,128,512]{2,1,0:T(8,128)S(1)}, u32[]{:S(2)}, u32[]{:S(2)}) collective-permute-start(f32[4,128,512]{2,1,0:T(8,128)} %param.4), channel_id=1, source_target_pairs={{4,0},{8,4},{12,8},{16,12},{20,16},{24,20},{28,24},{32,28},{36,32}... | collective-permute-start | bytes 3145736 | tf_op jit(solution)/shard_map/ppermute | solution.py:117
  9.1 13.9 %collective-permute-start = (f32[1,128,512]{2,1,0:T(8,128)}, f32[1,128,512]{2,1,0:T(8,128)}, u32[]{:S(2)}, u32[]{:S(2)}) collective-permute-start(f32[1,128,512]{2,1,0:T(8,128)} %get-tuple-element.13), channel_id=1, source_target_pairs={{0,8},{4,12},{8,16},{12,20},{16,24},{20,28},{24,32},{28,36},{32,40... | collective-permute-start | bytes 786440 | tf_op jit(solution)/shard_map/ppermute | solution.py:116
  13.1 11.5 %collective-permute-start.3 = (f32[1,128,512]{2,1,0:T(8,128)}, f32[1,128,512]{2,1,0:T(8,128)S(1)}, u32[]{:S(2)}, u32[]{:S(2)}) collective-permute-start(f32[1,128,512]{2,1,0:T(8,128)} %get-tuple-element.12), channel_id=1, source_target_pairs={{8,0},{12,4},{16,8},{20,12},{24,16},{28,20},{32,24},{36,28},{40,32... | collective-permute-start | bytes 786440 | tf_op jit(solution)/shard_map/ppermute | solution.py:117
  26.5 6.5 %collective-permute-start.4 = (f32[14,5,512]{2,1,0:T(8,128)S(1)}, f32[14,5,512]{2,1,0:T(8,128)S(1)}, u32[]{:S(2)}, u32[]{:S(2)}) collective-permute-start(f32[14,5,512]{2,1,0:T(8,128)S(1)} %get-tuple-element.8), channel_id=1, source_target_pairs={{0,1},{1,2},{2,3},{4,5},{5,6},{6,7},{8,9},{9,10},{10,11},{12,13},{... | collective-permute-start | bytes 430088 | tf_op jit(solution)/shard_map/ppermute | solution.py:116
  30.0 6.9 %collective-permute-start.5 = (f32[14,5,512]{2,1,0:T(8,128)S(1)}, f32[14,5,512]{2,1,0:T(8,128)S(1)}, u32[]{:S(2)}, u32[]{:S(2)}) collective-permute-start(f32[14,5,512]{2,1,0:T(8,128)S(1)} %get-tuple-element.9), channel_id=1, source_target_pairs={{1,0},{2,1},{3,2},{5,4},{6,5},{7,6},{9,8},{10,9},{11,10},{13,12},{... | collective-permute-start | bytes 430088 | tf_op jit(solution)/shard_map/ppermute | solution.py:117
  52.7 24.8 %collective-permute-start.6 = (f32[1,64,256]{2,1,0:T(8,128)S(1)}, f32[1,64,256]{2,1,0:T(8,128)S(1)}, u32[]{:S(2)}, u32[]{:S(2)}) collective-permute-start(f32[1,64,256]{2,1,0:T(8,128)S(1)} %convolution_bitcast_fusion.14), channel_id=1, source_target_pairs={{0,28},{4,32},{8,36},{12,40},{16,44},{20,48},{24,52},{28,56},{32,6... | collective-permute-start | bytes 196616 | tf_op jit(solution)/shard_map/ppermute | solution.py:116
  62.0 18.4 %collective-permute-start.7 = (f32[2,64,256]{2,1,0:T(8,128)}, f32[2,64,256]{2,1,0:T(8,128)}, u32[]{:S(2)}, u32[]{:S(2)}) collective-permute-start(f32[2,64,256]{2,1,0:T(8,128)} %pad_maximum_fusion.3), channel_id=1, source_target_pairs={{0,24},{4,28},{8,32},{12,36},{16,40},{20,44},{24,48},{28,52},{32,5... | collective-permute-start | bytes 393224 | tf_op jit(solution)/shard_map/ppermute | solution.py:116
  68.6 15.8 %collective-permute-start.8 = (f32[2,64,256]{2,1,0:T(8,128)}, f32[2,64,256]{2,1,0:T(8,128)S(1)}, u32[]{:S(2)}, u32[]{:S(2)}) collective-permute-start(f32[2,64,256]{2,1,0:T(8,128)} %pad_maximum_fusion.3), channel_id=1, source_target_pairs={{0,20},{4,24},{8,28},{12,32},{16,36},{20,40},{24,44},{28,48},{32,5... | collective-permute-start | bytes 393224 | tf_op jit(solution)/shard_map/ppermute | solution.py:116
  69.9 16.5 %collective-permute-start.9 = (f32[2,64,256]{2,1,0:T(8,128)}, f32[2,64,256]{2,1,0:T(8,128)S(1)}, u32[]{:S(2)}, u32[]{:S(2)}) collective-permute-start(f32[2,64,256]{2,1,0:T(8,128)} %pad_maximum_fusion.3), channel_id=1, source_target_pairs={{0,16},{4,20},{8,24},{12,28},{16,32},{20,36},{24,40},{28,44},{32,4... | collective-permute-start | bytes 393224 | tf_op jit(solution)/shard_map/ppermute | solution.py:116
  72.4 15.2 %collective-permute-start.10 = (f32[2,64,256]{2,1,0:T(8,128)}, f32[2,64,256]{2,1,0:T(8,128)S(1)}, u32[]{:S(2)}, u32[]{:S(2)}) collective-permute-start(f32[2,64,256]{2,1,0:T(8,128)} %pad_maximum_fusion.3), channel_id=1, source_target_pairs={{0,12},{4,16},{8,20},{12,24},{16,28},{20,32},{24,36},{28,40},{32,4... | collective-permute-start | bytes 393224 | tf_op jit(solution)/shard_map/ppermute | solution.py:116
  77.6 11.4 %collective-permute-start.11 = (f32[2,64,256]{2,1,0:T(8,128)}, f32[2,64,256]{2,1,0:T(8,128)S(1)}, u32[]{:S(2)}, u32[]{:S(2)}) collective-permute-start(f32[2,64,256]{2,1,0:T(8,128)} %pad_maximum_fusion.3), channel_id=1, source_target_pairs={{0,8},{4,12},{8,16},{12,20},{16,24},{20,28},{24,32},{28,36},{32,40... | collective-permute-start | bytes 393224 | tf_op jit(solution)/shard_map/ppermute | solution.py:116
  80.4 10.0 %collective-permute-start.12 = (f32[2,64,256]{2,1,0:T(8,128)}, f32[2,64,256]{2,1,0:T(8,128)S(1)}, u32[]{:S(2)}, u32[]{:S(2)}) collective-permute-start(f32[2,64,256]{2,1,0:T(8,128)} %pad_maximum_fusion.3), channel_id=1, source_target_pairs={{0,4},{4,8},{8,12},{12,16},{16,20},{20,24},{24,28},{28,32},{32,36}... | collective-permute-start | bytes 393224 | tf_op jit(solution)/shard_map/ppermute | solution.py:116
  84.4 7.3 %collective-permute-start.13 = (f32[2,64,256]{2,1,0:T(8,128)}, f32[2,64,256]{2,1,0:T(8,128)S(1)}, u32[]{:S(2)}, u32[]{:S(2)}) collective-permute-start(f32[2,64,256]{2,1,0:T(8,128)} %pad_maximum_fusion.3), channel_id=1, source_target_pairs={{4,0},{8,4},{12,8},{16,12},{20,16},{24,20},{28,24},{32,28},{36,32}... | collective-permute-start | bytes 393224 | tf_op jit(solution)/shard_map/ppermute | solution.py:117
  86.3 7.1 %collective-permute-start.14 = (f32[2,64,256]{2,1,0:T(8,128)}, f32[2,64,256]{2,1,0:T(8,128)S(1)}, u32[]{:S(2)}, u32[]{:S(2)}) collective-permute-start(f32[2,64,256]{2,1,0:T(8,128)} %pad_maximum_fusion.3), channel_id=1, source_target_pairs={{8,0},{12,4},{16,8},{20,12},{24,16},{28,20},{32,24},{36,28},{40,32... | collective-permute-start | bytes 393224 | tf_op jit(solution)/shard_map/ppermute | solution.py:117
  87.7 9.2 %collective-permute-start.15 = (f32[2,64,256]{2,1,0:T(8,128)}, f32[2,64,256]{2,1,0:T(8,128)S(1)}, u32[]{:S(2)}, u32[]{:S(2)}) collective-permute-start(f32[2,64,256]{2,1,0:T(8,128)} %pad_maximum_fusion.3), channel_id=1, source_target_pairs={{12,0},{16,4},{20,8},{24,12},{28,16},{32,20},{36,24},{40,28},{44,3... | collective-permute-start | bytes 393224 | tf_op jit(solution)/shard_map/ppermute | solution.py:117
  89.0 10.4 %collective-permute-start.16 = (f32[2,64,256]{2,1,0:T(8,128)}, f32[2,64,256]{2,1,0:T(8,128)S(1)}, u32[]{:S(2)}, u32[]{:S(2)}) collective-permute-start(f32[2,64,256]{2,1,0:T(8,128)} %pad_maximum_fusion.3), channel_id=1, source_target_pairs={{16,0},{20,4},{24,8},{28,12},{32,16},{36,20},{40,24},{44,28},{48,3... | collective-permute-start | bytes 393224 | tf_op jit(solution)/shard_map/ppermute | solution.py:117
  90.3 13.3 %collective-permute-start.17 = (f32[2,64,256]{2,1,0:T(8,128)}, f32[2,64,256]{2,1,0:T(8,128)S(1)}, u32[]{:S(2)}, u32[]{:S(2)}) collective-permute-start(f32[2,64,256]{2,1,0:T(8,128)} %pad_maximum_fusion.3), channel_id=1, source_target_pairs={{20,0},{24,4},{28,8},{32,12},{36,16},{40,20},{44,24},{48,28},{52,3... | collective-permute-start | bytes 393224 | tf_op jit(solution)/shard_map/ppermute | solution.py:117
  91.7 12.7 %collective-permute-start.18 = (f32[2,64,256]{2,1,0:T(8,128)}, f32[2,64,256]{2,1,0:T(8,128)S(1)}, u32[]{:S(2)}, u32[]{:S(2)}) collective-permute-start(f32[2,64,256]{2,1,0:T(8,128)} %pad_maximum_fusion.3), channel_id=1, source_target_pairs={{24,0},{28,4},{32,8},{36,12},{40,16},{44,20},{48,24},{52,28},{56,3... | collective-permute-start | bytes 393224 | tf_op jit(solution)/shard_map/ppermute | solution.py:117
  93.4 14.4 %collective-permute-start.19 = (f32[1,64,256]{2,1,0:T(8,128)S(1)}, f32[1,64,256]{2,1,0:T(8,128)S(1)}, u32[]{:S(2)}, u32[]{:S(2)}) collective-permute-start(f32[1,64,256]{2,1,0:T(8,128)S(1)} %convolution_bitcast_fusion.13), channel_id=1, source_target_pairs={{28,0},{32,4},{36,8},{40,12},{44,16},{48,20},{52,24},{56,28},{60,3... | collective-permute-start | bytes 196616 | tf_op jit(solution)/shard_map/ppermute | solution.py:117
  110.1 13.5 %collective-permute-start.20 = (f32[28,13,256]{2,1,0:T(8,128)}, f32[28,13,256]{2,1,0:T(8,128)}, u32[]{:S(2)}, u32[]{:S(2)}) collective-permute-start(f32[28,13,256]{2,1,0:T(8,128)} %get-tuple-element.10), channel_id=1, source_target_pairs={{0,1},{1,2},{2,3},{4,5},{5,6},{6,7},{8,9},{9,10},{10,11},{12,13},{... | collective-permute-start | bytes 1118216 | tf_op jit(solution)/shard_map/ppermute | solution.py:116
  114.4 14.0 %collective-permute-start.21 = (f32[28,13,256]{2,1,0:T(8,128)}, f32[28,13,256]{2,1,0:T(8,128)}, u32[]{:S(2)}, u32[]{:S(2)}) collective-permute-start(f32[28,13,256]{2,1,0:T(8,128)} %get-tuple-element.11), channel_id=1, source_target_pairs={{1,0},{2,1},{3,2},{5,4},{6,5},{7,6},{9,8},{10,9},{11,10},{13,12},{... | collective-permute-start | bytes 1118216 | tf_op jit(solution)/shard_map/ppermute | solution.py:117
  184.0 16.8 %collective-permute-start.27 = (f32[128,512]{1,0:T(8,128)S(1)}, f32[128,512]{1,0:T(8,128)S(1)}, u32[]{:S(2)}, u32[]{:S(2)}) collective-permute-start(f32[128,512]{1,0:T(8,128)S(1)} %get-tuple-element.5), channel_id=1, source_target_pairs={{0,24},{32,56},{64,88},{96,120},{124,100},{92,68},{60,36},{28,4},{... | collective-permute-start | bytes 786440 | tf_op jit(solution)/shard_map/ppermute | solution.py:255
  205.4 4.9 %collective-permute-start.31 = (f32[1,128,128]{2,1,0:T(8,128)S(1)}, f32[1,128,128]{2,1,0:T(8,128)S(1)}, u32[]{:S(2)}, u32[]{:S(2)}) collective-permute-start(f32[1,128,128]{2,1,0:T(8,128)S(1)} %get-tuple-element.15), channel_id=1, source_target_pairs={{0,3},{1,0},{2,1},{3,2},{4,7},{5,4},{6,5},{7,6},{8,11},{9,8},{10,9... | collective-permute-start | bytes 196616 | tf_op jit(solution)/shard_map/ppermute | solution.py:268
  (35 other events, 146.0 us)

commit v7 on v4

--- a/solution.py
+++ b/solution.py
@@ -191,6 +191,25 @@
     return grad_medium
 
 
+def face_value(partial_plane, quad):
+    block_y = partial_plane.shape[0]
+    back = prolong(quad)[1:, 1:-1] * 0.125
+    place = jnp.arange(back.shape[0], dtype=jnp.int32)
+    centre, total = shrink_neighbours(back)
+    keep = (place[1:-1] >= 3)[:, None, None] & inside("pencil", block_y, 2)[None, :, None]
+    first = lax.optimization_barrier(jnp.where(keep, 6.0 * centre - total, 0.0))
+    centre, total = shrink_neighbours(first)
+    keep = (place[2:-2] >= 3)[:, None, None] & inside("pencil", block_y, 1)[None, :, None]
+    second = lax.optimization_barrier(jnp.where(keep, smoothed(centre, total), 0.0))
+    centre, total = shrink_neighbours(second)
+    third = smoothed(centre, total)
+    value = partial_plane + back[3, 3:3 + block_y]
+    value = value - coefficient(0) * first[2, 2:2 + block_y]
+    value = value - coefficient(0) * second[1, 1:1 + block_y]
+    value = value - coefficient(0) * third[0]
+    return value
+
+
 def shards(cotangent, seg_rows, owners, offsets):
     x_cells, y_cells, z_cells = cotangent.shape
     tile_size = TILE
@@ -207,6 +226,8 @@
     grad_fine = core(powers[3], depth - 3, x_cells, y_cells)
     medium = children_sum(grad_fine)
     grown = medium_cycle(medium)
+    low_face = face_value(rhs_grad[0], grown[0:4])
+    high_face = face_value(rhs_grad[x_cells - 1], grown[5:1:-1])
     back_fine = prolong(grown)[1:-1, 1:-1] * 0.125
     rhs_grad = rhs_grad + core(back_fine, 3, x_cells, y_cells)
     centre, total = shrink_neighbours(back_fine)
@@ -219,8 +240,8 @@
         rhs_grad = rhs_grad - coefficient(0) * core(stage, 2 - number, x_cells, y_cells)
     slab_index = lax.axis_index("slab")
     slab_count = lax.axis_size("slab")
-    low_face = jnp.where(slab_index == 0, rhs_grad[0], 0.0)
-    high_face = jnp.where(slab_index == slab_count - 1, rhs_grad[x_cells - 1], 0.0)
+    low_face = jnp.where(slab_index == 0, low_face, 0.0)
+    high_face = jnp.where(slab_index == slab_count - 1, high_face, 0.0)
     low_face, high_face = spread_faces(low_face, high_face, slab_index, slab_count)
     pencil_index = lax.axis_index("pencil")
     pencil_count = lax.axis_size("pencil")

time: 199 us -> 240 us (1.21)
  local copies, waits for them, and re-layouts: 19.3 us -> 37.1 us
  other arithmetic: 37.6 us -> 53.6 us
  waiting for transfers between devices: 51.9 us -> 41.1 us
  starting transfers between devices: 77.5 us -> 86.4 us
  matrix products: 9 us -> 16.4 us
    select_n x0 -> x2, other arithmetic: none -> 10.3 us  [the longest x1 9.18 us: face_value(): first = lax.optimization_barrier(jnp.where(keep, 6.0 * centre - total, 0.0))]
    ppermute x12, waiting for transfers between devices: 23.6 us -> 15.6 us  [extend(): highs.append(lax.ppermute(high_piece, axis, down))]
    unnamed x61 -> x93, local copies, waits for them, and re-layouts: 9.36 us -> 15.6 us
    ppermute x7, starting transfers between devices: 4.98 us -> 10.4 us  [spread_faces(): got = lax.ppermute(sent, 'slab', low_pairs + high_pairs)]
    dot_general x7 -> x15, matrix products: 2.12 us -> 7.52 us  [prolong(): jnp.dot(to_rows, wide[i], precision=lax.Precision.HIGHEST)]
    ppermute x7, waiting for transfers between devices: 20 us -> 15.2 us  [spread_faces(): got = lax.ppermute(sent, 'slab', low_pairs + high_pairs)]
    slice x12 -> x16, local copies, waits for them, and re-layouts: 5.11 us -> 9.14 us  [shrink_neighbours(): centre = field[1:-1, 1:-1]]
    reshape x1 -> x3, local copies, waits for them, and re-layouts: 1.81 us -> 5.19 us  [prolong(): flat = field.reshape(x_cells * y_cells, z_cells)]
  transfers between devices with their start and end apart: 34 -> 34, of which waited for: 17 -> 16; matrix products, arithmetic and copies ran while one was open for 8% -> 7% of each run, Pallas kernels for 0% -> 0%
where the time goes in v7:
time: 240 us; the launch traced here: 237 us
  starting transfers between devices  86.4 us (36%)
  other arithmetic  53.6 us (22%)
  waiting for transfers between devices  41.1 us (17%)
  local copies, waits for them, and re-layouts  37.1 us (15%)
  matrix products  16.4 us (7%)
    ppermute x12, starting transfers between devices, extend(): lows.insert(0, lax.ppermute(low_piece, axis, up))  53 us
    select_n x14, other arithmetic, masked(): return jnp.where(keep, field, 0.0)  20.5 us
    ppermute x12, starting transfers between devices, extend(): highs.append(lax.ppermute(high_piece, axis, down))  18.4 us
    ppermute x12, waiting for transfers between devices, extend(): highs.append(lax.ppermute(high_piece, axis, down))  15.6 us
    unnamed x93, local copies, waits for them, and re-layouts  15.6 us
    ppermute x7, waiting for transfers between devices, spread_faces(): got = lax.ppermute(sent, 'slab', low_pairs + high_pairs)  15.2 us
    ppermute x7, starting transfers between devices, spread_faces(): got = lax.ppermute(sent, 'slab', low_pairs + high_pairs)  10.4 us
    select_n x1, other arithmetic, face_value(): first = lax.optimization_barrier(jnp.where(keep, 6.0 * centre - total, 0.0))  9.18 us
  transfers between devices with their start and end apart: 34, of which 16 were waited for; matrix products, arithmetic and copies ran while one was open for 7% of the time, Pallas kernels for 0%

profile of v7, /device:TPU:1, one launch (start us, length us, event | category | flops | bytes accessed | tf_op | source)
XLA Modules:
  0.0 236.8 jit_solution(11986134988375818265)
XLA Ops:
  0.6 4.7 %collective-permute-start.1 = (f32[4,128,512]{2,1,0:T(8,128)}, f32[4,128,512]{2,1,0:T(8,128)S(1)}, u32[]{:S(2)}, u32[]{:S(2)}) collective-permute-start(f32[4,128,512]{2,1,0:T(8,128)} %param.4), channel_id=1, source_target_pairs={{0,4},{4,8},{8,12},{12,16},{16,20},{20,24},{24,28},{28,32},{32,36}... | collective-permute-start | bytes 3145736 | tf_op jit(solution)/shard_map/ppermute | solution.py:116
  9.2 3.9 %collective-permute-start = (f32[1,128,512]{2,1,0:T(8,128)}, f32[1,128,512]{2,1,0:T(8,128)}, u32[]{:S(2)}, u32[]{:S(2)}) collective-permute-start(f32[1,128,512]{2,1,0:T(8,128)} %get-tuple-element.18), channel_id=1, source_target_pairs={{0,8},{4,12},{8,16},{12,20},{16,24},{20,28},{24,32},{28,36},{32,40... | collective-permute-start | bytes 786440 | tf_op jit(solution)/shard_map/ppermute | solution.py:116
  26.0 4.2 %collective-permute-start.4 = (f32[14,5,512]{2,1,0:T(8,128)S(1)}, f32[14,5,512]{2,1,0:T(8,128)S(1)}, u32[]{:S(2)}, u32[]{:S(2)}) collective-permute-start(f32[14,5,512]{2,1,0:T(8,128)S(1)} %get-tuple-element.13), channel_id=1, source_target_pairs={{0,1},{1,2},{2,3},{4,5},{5,6},{6,7},{8,9},{9,10},{10,11},{12,13},{... | collective-permute-start | bytes 430088 | tf_op jit(solution)/shard_map/ppermute | solution.py:116
  34.7 3.2 %fusion.4 = f32[12,136,512]{2,1,0:T(8,128)S(1)} fusion(f32[12,136,512]{2,1,0:T(8,128)S(1)} %slice.870, f32[14,138,512]{2,1,0:T(8,128)S(1)} %pad_maximum_fusion, pred[12,136]{1,0:T(8,128)(4,1)S(1)} %broadcast_and_fusion.1), kind=kLoop, calls=%fused_computation.9 | loop fusion | flops 7520256 | bytes 20055648 | tf_op jit(solution)/shard_map/jit(_where)/select_n | solution.py:130
  38.2 2.6 %fusion.9 = f32[10,134,512]{2,1,0:T(8,128)S(1)} fusion(f32[10,134,512]{2,1,0:T(8,128)S(1)} %slice.876, f32[12,136,512]{2,1,0:T(8,128)S(1)} %fusion.4, pred[10,134]{1,0:T(8,128)(4,1)S(1)} %broadcast_and_fusion), kind=kLoop, calls=%fused_computation.21 | loop fusion | flops 6174720 | bytes 16467260 | tf_op jit(solution)/shard_map/jit(_where)/select_n | solution.py:130
  47.0 5.1 %collective-permute-start.6 = (f32[1,64,256]{2,1,0:T(8,128)S(1)}, f32[1,64,256]{2,1,0:T(8,128)S(1)}, u32[]{:S(2)}, u32[]{:S(2)}) collective-permute-start(f32[1,64,256]{2,1,0:T(8,128)S(1)} %convolution_bitcast_fusion.15), channel_id=1, source_target_pairs={{0,16},{4,20},{8,24},{12,28},{16,32},{20,36},{24,40},{28,44},{32,4... | collective-permute-start | bytes 196616 | tf_op jit(solution)/shard_map/ppermute | solution.py:116
  52.8 8.7 %collective-permute-start.7 = (f32[2,64,256]{2,1,0:T(8,128)}, f32[2,64,256]{2,1,0:T(8,128)}, u32[]{:S(2)}, u32[]{:S(2)}) collective-permute-start(f32[2,64,256]{2,1,0:T(8,128)} %pad_maximum_fusion.6), channel_id=1, source_target_pairs={{0,12},{4,16},{8,20},{12,24},{16,28},{20,32},{24,36},{28,40},{32,4... | collective-permute-start | bytes 393224 | tf_op jit(solution)/shard_map/ppermute | solution.py:116
  73.0 2.6 %collective-permute-done.11 = f32[2,64,256]{2,1,0:T(8,128)S(1)} collective-permute-done((f32[2,64,256]{2,1,0:T(8,128)}, f32[2,64,256]{2,1,0:T(8,128)S(1)}, u32[]{:S(2)}, u32[]{:S(2)}) %collective-permute-start.11) | collective-permute-done | bytes 131104 | tf_op jit(solution)/shard_map/ppermute | solution.py:117
  75.6 3.4 %collective-permute-done.12 = f32[2,64,256]{2,1,0:T(8,128)S(1)} collective-permute-done((f32[2,64,256]{2,1,0:T(8,128)}, f32[2,64,256]{2,1,0:T(8,128)S(1)}, u32[]{:S(2)}, u32[]{:S(2)}) %collective-permute-start.12) | collective-permute-done | bytes 131104 | tf_op jit(solution)/shard_map/ppermute | solution.py:117
  78.9 2.5 %collective-permute-done.13 = f32[1,64,256]{2,1,0:T(8,128)S(1)} collective-permute-done((f32[1,64,256]{2,1,0:T(8,128)S(1)}, f32[1,64,256]{2,1,0:T(8,128)S(1)}, u32[]{:S(2)}, u32[]{:S(2)}) %collective-permute-start.13) | collective-permute-done | bytes 65568 | tf_op jit(solution)/shard_map/ppermute | solution.py:117
  82.8 4.7 %collective-permute-start.14 = (f32[16,7,256]{2,1,0:T(8,128)S(1)}, f32[16,7,256]{2,1,0:T(8,128)S(1)}, u32[]{:S(2)}, u32[]{:S(2)}) collective-permute-start(f32[16,7,256]{2,1,0:T(8,128)S(1)} %get-tuple-element.15), channel_id=1, source_target_pairs={{0,1},{1,2},{2,3},{4,5},{5,6},{6,7},{8,9},{9,10},{10,11},{12,13},{... | collective-permute-start | bytes 344072 | tf_op jit(solution)/shard_map/ppermute | solution.py:116
  99.6 8.6 %collective-permute-start.16 = (f32[1,64,256]{2,1,0:T(8,128)S(1)}, f32[1,64,256]{2,1,0:T(8,128)}, u32[]{:S(2)}, u32[]{:S(2)}) collective-permute-start(f32[1,64,256]{2,1,0:T(8,128)S(1)} %bitcast.91), channel_id=1, source_target_pairs={{0,12},{4,16},{8,20},{12,24},{16,28},{20,32},{24,36},{28,40},{32,4... | collective-permute-start | bytes 196616 | tf_op jit(solution)/shard_map/ppermute | solution.py:116
  108.2 2.9 %collective-permute-start.17 = (f32[2,64,256]{2,1,0:T(8,128)S(1)}, f32[2,64,256]{2,1,0:T(8,128)}, u32[]{:S(2)}, u32[]{:S(2)}) collective-permute-start(f32[2,64,256]{2,1,0:T(8,128)S(1)} %reshape.965), channel_id=1, source_target_pairs={{0,8},{4,12},{8,16},{12,20},{16,24},{20,28},{24,32},{28,36},{32,40... | collective-permute-start | bytes 393224 | tf_op jit(solution)/shard_map/ppermute | solution.py:116
  120.6 2.9 %collective-permute-done.20 = f32[2,64,256]{2,1,0:T(8,128)S(1)} collective-permute-done((f32[2,64,256]{2,1,0:T(8,128)S(1)}, f32[2,64,256]{2,1,0:T(8,128)S(1)}, u32[]{:S(2)}, u32[]{:S(2)}) %collective-permute-start.20) | collective-permute-done | bytes 131104 | tf_op jit(solution)/shard_map/ppermute | solution.py:117
  126.6 4.7 %collective-permute-start.22 = (f32[12,5,256]{2,1,0:T(8,128)S(1)}, f32[12,5,256]{2,1,0:T(8,128)S(1)}, u32[]{:S(2)}, u32[]{:S(2)}) collective-permute-start(f32[12,5,256]{2,1,0:T(8,128)S(1)} %get-tuple-element.19), channel_id=1, source_target_pairs={{0,1},{1,2},{2,3},{4,5},{5,6},{6,7},{8,9},{9,10},{10,11},{12,13},{... | collective-permute-start | bytes 184328 | tf_op jit(solution)/shard_map/ppermute | solution.py:116
  131.3 2.9 %slice.888 = f32[6,130,512]{2,1,0:T(8,128)} slice(f32[8,132,512]{2,1,0:T(8,128)} %copy-done.1), slice={[1:7], [1:131], [0:512]} | slice | bytes 3194880 | tf_op jit(solution)/shard_map/slice | solution.py:134
  165.0 3.1 %fusion.25 = (f32[6,130,512]{2,1,0:T(8,128)S(1)}, f32[6,130,512]{2,1,0:T(8,128)S(1)}) fusion(f32[6,130,512]{2,1,0:T(8,128)S(1)} %copy-done.14, f32[8,132,512]{2,1,0:T(8,128)S(1)} %copy-done.2, pred[6,130]{1,0:T(8,128)(4,1)S(1)} %copy-done.28, f32[6,130,512]{2,1,0:T(8,128)S(1)} %slice.967, f32[8,132,512]{2,1,0:T(8,128)S(1)} %fusion.18), kind=kLoop, calls=%fused_computation.59 | loop fusion | flops 7188480 | bytes 19170060 | tf_op jit(solution)/shard_map/jit(_where)/select_n | solution.py:130
  169.9 2.8 %fusion.54 = (f32[4,128,512]{2,1,0:T(8,128)}, f32[4,128,512]{2,1,0:T(8,128)}) fusion(f32[4,128,512]{2,1,0:T(8,128)S(1)} %slice.893, f32[6,130,512]{2,1,0:T(8,128)S(1)} %get-tuple-element.30, pred[4,128]{1,0:T(4,128)(4,1)S(1)} %broadcast_and_fusion.12, f32[4,128,512]{2,1,0:T(8,128)S(1)} %slice.972, f32[6,130,512]{2,1,0:T(8,128)S(1)} %get-tuple-element.31), kind=kLoop, calls=%fused_computation.142 | loop fusion | flops 4718592 | bytes 12583424 | tf_op jit(solution)/shard_map/jit(_where)/select_n | solution.py:130
  178.0 9.2 %fusion.34 = (f32[5,132,512]{2,1,0:T(8,128)}, f32[5,132,512]{2,1,0:T(8,128)}) fusion(f32[5,132,512]{2,1,0:T(8,128)} %slice.985, f32[7,134,512]{2,1,0:T(8,128)S(1)} %slice_multiply_fusion.2, pred[5,132]{1,0:T(8,128)(4,1)S(1)} %copy-done.25, f32[5,132,512]{2,1,0:T(8,128)} %slice.1009, f32[7,134,512]{2,1,0:T(8,128)} %copy-done.4), kind=kLoop, calls=%fused_computation.76 | loop fusion | flops 5406720 | bytes 16220820 | tf_op jit(solution)/shard_map/jit(_where)/select_n | solution.py:200
  192.3 4.3 %fusion.62 = (f32[4,128,512]{2,1,0:T(8,128)}, f32[4,128,512]{2,1,0:T(8,128)S(1)}) fusion(f32[8,132,512]{2,1,0:T(8,128)} %copy-done.3, f32[10,134,512]{2,1,0:T(8,128)S(1)} %slice_multiply_fusion, f32[4,128,512]{2,1,0:T(8,128)S(1)} %copy-done.19, f32[6,130,512]{2,1,0:T(8,128)S(1)} %copy-done.9, f32[4,128,512]{2,1,0:T(8,128)S(1)} %copy-done.18, ...), kind=kLoop, calls=%fused_computation.154 | loop fusion | flops 3407872 | bytes 12582912 | tf_op jit(solution)/shard_map/sub | solution.py:240
  203.3 14.3 %collective-permute-done.29 = f32[128,512]{1,0:T(8,128)S(1)} collective-permute-done((f32[128,512]{1,0:T(8,128)S(1)}, f32[128,512]{1,0:T(8,128)S(1)}, u32[]{:S(2)}, u32[]{:S(2)}) %collective-permute-start.29) | collective-permute-done | bytes 262176 | tf_op jit(solution)/shard_map/ppermute | solution.py:281
  217.7 5.6 %collective-permute-start.30 = (f32[128,512]{1,0:T(8,128)S(1)}, f32[128,512]{1,0:T(8,128)S(1)}, u32[]{:S(2)}, u32[]{:S(2)}) collective-permute-start(f32[128,512]{1,0:T(8,128)S(1)} %get-tuple-element.2), channel_id=1, source_target_pairs={{0,4},{8,12},{16,20},{24,28},{32,36},{40,44},{48,52},{56,60},{64,6... | collective-permute-start | bytes 786440 | tf_op jit(solution)/shard_map/ppermute | solution.py:281
  226.0 3.6 %collective-permute-start.33 = (f32[1,128,128]{2,1,0:T(8,128)S(1)}, f32[1,128,128]{2,1,0:T(8,128)S(1)}, u32[]{:S(2)}, u32[]{:S(2)}) collective-permute-start(f32[1,128,128]{2,1,0:T(8,128)S(1)} %get-tuple-element.24), channel_id=1, source_target_pairs={{0,3},{1,0},{2,1},{3,2},{4,7},{5,4},{6,5},{7,6},{8,11},{9,8},{10,9... | collective-permute-start | bytes 196616 | tf_op jit(solution)/shard_map/ppermute | solution.py:294
  230.9 3.4 %collective-permute-done.32 = f32[1,128,128]{2,1,0:T(8,128)S(1)} collective-permute-done((f32[1,128,128]{2,1,0:T(8,128)S(1)}, f32[1,128,128]{2,1,0:T(8,128)S(1)}, u32[]{:S(2)}, u32[]{:S(2)}) %collective-permute-start.32) | collective-permute-done | bytes 65568 | tf_op jit(solution)/shard_map/ppermute | solution.py:294
  (297 shorter events, 120.8 us)
Async XLA Ops:
  0.6 23.4 %collective-permute-start.1 = (f32[4,128,512]{2,1,0:T(8,128)}, f32[4,128,512]{2,1,0:T(8,128)S(1)}, u32[]{:S(2)}, u32[]{:S(2)}) collective-permute-start(f32[4,128,512]{2,1,0:T(8,128)} %param.4), channel_id=1, source_target_pairs={{0,4},{4,8},{8,12},{12,16},{16,20},{20,24},{24,28},{28,32},{32,36}... | collective-permute-start | bytes 3145736 | tf_op jit(solution)/shard_map/ppermute | solution.py:116
  5.4 19.1 %collective-permute-start.2 = (f32[4,128,512]{2,1,0:T(8,128)}, f32[4,128,512]{2,1,0:T(8,128)S(1)}, u32[]{:S(2)}, u32[]{:S(2)}) collective-permute-start(f32[4,128,512]{2,1,0:T(8,128)} %param.4), channel_id=1, source_target_pairs={{4,0},{8,4},{12,8},{16,12},{20,16},{24,20},{28,24},{32,28},{36,32}... | collective-permute-start | bytes 3145736 | tf_op jit(solution)/shard_map/ppermute | solution.py:117
  9.2 13.9 %collective-permute-start = (f32[1,128,512]{2,1,0:T(8,128)}, f32[1,128,512]{2,1,0:T(8,128)}, u32[]{:S(2)}, u32[]{:S(2)}) collective-permute-start(f32[1,128,512]{2,1,0:T(8,128)} %get-tuple-element.18), channel_id=1, source_target_pairs={{0,8},{4,12},{8,16},{12,20},{16,24},{20,28},{24,32},{28,36},{32,40... | collective-permute-start | bytes 786440 | tf_op jit(solution)/shard_map/ppermute | solution.py:116
  13.0 11.5 %collective-permute-start.3 = (f32[1,128,512]{2,1,0:T(8,128)}, f32[1,128,512]{2,1,0:T(8,128)S(1)}, u32[]{:S(2)}, u32[]{:S(2)}) collective-permute-start(f32[1,128,512]{2,1,0:T(8,128)} %get-tuple-element.17), channel_id=1, source_target_pairs={{8,0},{12,4},{16,8},{20,12},{24,16},{28,20},{32,24},{36,28},{40,32... | collective-permute-start | bytes 786440 | tf_op jit(solution)/shard_map/ppermute | solution.py:117
  26.0 7.1 %collective-permute-start.4 = (f32[14,5,512]{2,1,0:T(8,128)S(1)}, f32[14,5,512]{2,1,0:T(8,128)S(1)}, u32[]{:S(2)}, u32[]{:S(2)}) collective-permute-start(f32[14,5,512]{2,1,0:T(8,128)S(1)} %get-tuple-element.13), channel_id=1, source_target_pairs={{0,1},{1,2},{2,3},{4,5},{5,6},{6,7},{8,9},{9,10},{10,11},{12,13},{... | collective-permute-start | bytes 430088 | tf_op jit(solution)/shard_map/ppermute | solution.py:116
  47.0 21.0 %collective-permute-start.6 = (f32[1,64,256]{2,1,0:T(8,128)S(1)}, f32[1,64,256]{2,1,0:T(8,128)S(1)}, u32[]{:S(2)}, u32[]{:S(2)}) collective-permute-start(f32[1,64,256]{2,1,0:T(8,128)S(1)} %convolution_bitcast_fusion.15), channel_id=1, source_target_pairs={{0,16},{4,20},{8,24},{12,28},{16,32},{20,36},{24,40},{28,44},{32,4... | collective-permute-start | bytes 196616 | tf_op jit(solution)/shard_map/ppermute | solution.py:116
  52.8 16.6 %collective-permute-start.7 = (f32[2,64,256]{2,1,0:T(8,128)}, f32[2,64,256]{2,1,0:T(8,128)}, u32[]{:S(2)}, u32[]{:S(2)}) collective-permute-start(f32[2,64,256]{2,1,0:T(8,128)} %pad_maximum_fusion.6), channel_id=1, source_target_pairs={{0,12},{4,16},{8,20},{12,24},{16,28},{20,32},{24,36},{28,40},{32,4... | collective-permute-start | bytes 393224 | tf_op jit(solution)/shard_map/ppermute | solution.py:116
  62.0 9.6 %collective-permute-start.8 = (f32[2,64,256]{2,1,0:T(8,128)}, f32[2,64,256]{2,1,0:T(8,128)S(1)}, u32[]{:S(2)}, u32[]{:S(2)}) collective-permute-start(f32[2,64,256]{2,1,0:T(8,128)} %pad_maximum_fusion.6), channel_id=1, source_target_pairs={{0,8},{4,12},{8,16},{12,20},{16,24},{20,28},{24,32},{28,36},{32,40... | collective-permute-start | bytes 393224 | tf_op jit(solution)/shard_map/ppermute | solution.py:116
  63.7 9.2 %collective-permute-start.9 = (f32[2,64,256]{2,1,0:T(8,128)}, f32[2,64,256]{2,1,0:T(8,128)S(1)}, u32[]{:S(2)}, u32[]{:S(2)}) collective-permute-start(f32[2,64,256]{2,1,0:T(8,128)} %pad_maximum_fusion.6), channel_id=1, source_target_pairs={{0,4},{4,8},{8,12},{12,16},{16,20},{20,24},{24,28},{28,32},{32,36}... | collective-permute-start | bytes 393224 | tf_op jit(solution)/shard_map/ppermute | solution.py:116
  65.6 7.4 %collective-permute-start.10 = (f32[2,64,256]{2,1,0:T(8,128)}, f32[2,64,256]{2,1,0:T(8,128)S(1)}, u32[]{:S(2)}, u32[]{:S(2)}) collective-permute-start(f32[2,64,256]{2,1,0:T(8,128)} %pad_maximum_fusion.6), channel_id=1, source_target_pairs={{4,0},{8,4},{12,8},{16,12},{20,16},{24,20},{28,24},{32,28},{36,32}... | collective-permute-start | bytes 393224 | tf_op jit(solution)/shard_map/ppermute | solution.py:117
  68.0 7.5 %collective-permute-start.11 = (f32[2,64,256]{2,1,0:T(8,128)}, f32[2,64,256]{2,1,0:T(8,128)S(1)}, u32[]{:S(2)}, u32[]{:S(2)}) collective-permute-start(f32[2,64,256]{2,1,0:T(8,128)} %pad_maximum_fusion.6), channel_id=1, source_target_pairs={{8,0},{12,4},{16,8},{20,12},{24,16},{28,20},{32,24},{36,28},{40,32... | collective-permute-start | bytes 393224 | tf_op jit(solution)/shard_map/ppermute | solution.py:117
  69.3 9.6 %collective-permute-start.12 = (f32[2,64,256]{2,1,0:T(8,128)}, f32[2,64,256]{2,1,0:T(8,128)S(1)}, u32[]{:S(2)}, u32[]{:S(2)}) collective-permute-start(f32[2,64,256]{2,1,0:T(8,128)} %pad_maximum_fusion.6), channel_id=1, source_target_pairs={{12,0},{16,4},{20,8},{24,12},{28,16},{32,20},{36,24},{40,28},{44,3... | collective-permute-start | bytes 393224 | tf_op jit(solution)/shard_map/ppermute | solution.py:117
  71.6 9.9 %collective-permute-start.13 = (f32[1,64,256]{2,1,0:T(8,128)S(1)}, f32[1,64,256]{2,1,0:T(8,128)S(1)}, u32[]{:S(2)}, u32[]{:S(2)}) collective-permute-start(f32[1,64,256]{2,1,0:T(8,128)S(1)} %convolution_bitcast_fusion.14), channel_id=1, source_target_pairs={{16,0},{20,4},{24,8},{28,12},{32,16},{36,20},{40,24},{44,28},{48,3... | collective-permute-start | bytes 196616 | tf_op jit(solution)/shard_map/ppermute | solution.py:117
  81.5 7.4 %collective-permute-start.15 = (f32[16,7,256]{2,1,0:T(8,128)S(1)}, f32[16,7,256]{2,1,0:T(8,128)S(1)}, u32[]{:S(2)}, u32[]{:S(2)}) collective-permute-start(f32[16,7,256]{2,1,0:T(8,128)S(1)} %get-tuple-element.16), channel_id=1, source_target_pairs={{1,0},{2,1},{3,2},{5,4},{6,5},{7,6},{9,8},{10,9},{11,10},{13,12},{... | collective-permute-start | bytes 344072 | tf_op jit(solution)/shard_map/ppermute | solution.py:117
  99.6 17.9 %collective-permute-start.16 = (f32[1,64,256]{2,1,0:T(8,128)S(1)}, f32[1,64,256]{2,1,0:T(8,128)}, u32[]{:S(2)}, u32[]{:S(2)}) collective-permute-start(f32[1,64,256]{2,1,0:T(8,128)S(1)} %bitcast.91), channel_id=1, source_target_pairs={{0,12},{4,16},{8,20},{12,24},{16,28},{20,32},{24,36},{28,40},{32,4... | collective-permute-start | bytes 196616 | tf_op jit(solution)/shard_map/ppermute | solution.py:116
  108.2 11.5 %collective-permute-start.17 = (f32[2,64,256]{2,1,0:T(8,128)S(1)}, f32[2,64,256]{2,1,0:T(8,128)}, u32[]{:S(2)}, u32[]{:S(2)}) collective-permute-start(f32[2,64,256]{2,1,0:T(8,128)S(1)} %reshape.965), channel_id=1, source_target_pairs={{0,8},{4,12},{8,16},{12,20},{16,24},{20,28},{24,32},{28,36},{32,40... | collective-permute-start | bytes 393224 | tf_op jit(solution)/shard_map/ppermute | solution.py:116
  111.8 8.7 %collective-permute-start.18 = (f32[2,64,256]{2,1,0:T(8,128)S(1)}, f32[2,64,256]{2,1,0:T(8,128)S(1)}, u32[]{:S(2)}, u32[]{:S(2)}) collective-permute-start(f32[2,64,256]{2,1,0:T(8,128)S(1)} %reshape.965), channel_id=1, source_target_pairs={{0,4},{4,8},{8,12},{12,16},{16,20},{20,24},{24,28},{28,32},{32,36}... | collective-permute-start | bytes 393224 | tf_op jit(solution)/shard_map/ppermute | solution.py:116
  116.1 7.3 %collective-permute-start.20 = (f32[2,64,256]{2,1,0:T(8,128)S(1)}, f32[2,64,256]{2,1,0:T(8,128)S(1)}, u32[]{:S(2)}, u32[]{:S(2)}) collective-permute-start(f32[2,64,256]{2,1,0:T(8,128)S(1)} %reshape.965), channel_id=1, source_target_pairs={{8,0},{12,4},{16,8},{20,12},{24,16},{28,20},{32,24},{36,28},{40,32... | collective-permute-start | bytes 393224 | tf_op jit(solution)/shard_map/ppermute | solution.py:117
  117.5 7.8 %collective-permute-start.21 = (f32[1,64,256]{2,1,0:T(8,128)S(1)}, f32[1,64,256]{2,1,0:T(8,128)S(1)}, u32[]{:S(2)}, u32[]{:S(2)}) collective-permute-start(f32[1,64,256]{2,1,0:T(8,128)S(1)} %bitcast.92), channel_id=1, source_target_pairs={{12,0},{16,4},{20,8},{24,12},{28,16},{32,20},{36,24},{40,28},{44,3... | collective-permute-start | bytes 196616 | tf_op jit(solution)/shard_map/ppermute | solution.py:117
  125.3 9.0 %collective-permute-start.23 = (f32[12,5,256]{2,1,0:T(8,128)S(1)}, f32[12,5,256]{2,1,0:T(8,128)S(1)}, u32[]{:S(2)}, u32[]{:S(2)}) collective-permute-start(f32[12,5,256]{2,1,0:T(8,128)S(1)} %get-tuple-element.20), channel_id=1, source_target_pairs={{1,0},{2,1},{3,2},{5,4},{6,5},{7,6},{9,8},{10,9},{11,10},{13,12},{... | collective-permute-start | bytes 184328 | tf_op jit(solution)/shard_map/ppermute | solution.py:117
  126.6 7.7 %collective-permute-start.22 = (f32[12,5,256]{2,1,0:T(8,128)S(1)}, f32[12,5,256]{2,1,0:T(8,128)S(1)}, u32[]{:S(2)}, u32[]{:S(2)}) collective-permute-start(f32[12,5,256]{2,1,0:T(8,128)S(1)} %get-tuple-element.19), channel_id=1, source_target_pairs={{0,1},{1,2},{2,3},{4,5},{5,6},{6,7},{8,9},{9,10},{10,11},{12,13},{... | collective-permute-start | bytes 184328 | tf_op jit(solution)/shard_map/ppermute | solution.py:116
  200.5 17.0 %collective-permute-start.29 = (f32[128,512]{1,0:T(8,128)S(1)}, f32[128,512]{1,0:T(8,128)S(1)}, u32[]{:S(2)}, u32[]{:S(2)}) collective-permute-start(f32[128,512]{1,0:T(8,128)S(1)} %get-tuple-element.5), channel_id=1, source_target_pairs={{0,24},{32,56},{64,88},{96,120},{124,100},{92,68},{60,36},{28,4},{... | collective-permute-start | bytes 786440 | tf_op jit(solution)/shard_map/ppermute | solution.py:281
  201.8 15.7 %collective-permute-start.28 = (f32[128,512]{1,0:T(8,128)S(1)}, f32[128,512]{1,0:T(8,128)S(1)}, u32[]{:S(2)}, u32[]{:S(2)}) collective-permute-start(f32[128,512]{1,0:T(8,128)S(1)} %get-tuple-element.5), channel_id=1, source_target_pairs={{0,16},{32,48},{64,80},{96,112},{124,108},{92,76},{60,44},{28,12},... | collective-permute-start | bytes 786440 | tf_op jit(solution)/shard_map/ppermute | solution.py:281
  202.5 15.1 %collective-permute-start.27 = (f32[128,512]{1,0:T(8,128)S(1)}, f32[128,512]{1,0:T(8,128)S(1)}, u32[]{:S(2)}, u32[]{:S(2)}) collective-permute-start(f32[128,512]{1,0:T(8,128)S(1)} %get-tuple-element.5), channel_id=1, source_target_pairs={{0,8},{32,40},{64,72},{96,104},{124,116},{92,84},{60,52},{28,20},{... | collective-permute-start | bytes 786440 | tf_op jit(solution)/shard_map/ppermute | solution.py:281
  (47 other events, 157.1 us)

commit v8 on v4

--- a/solution.py
+++ b/solution.py
@@ -238,7 +238,8 @@
     picks = (local_targets[None, :] == wanted[:, None]).astype(jnp.float32)
     partial = jnp.dot(picks, faces, precision=lax.Precision.HIGHEST)
     partial = partial.reshape(pencil_count, tile_size, tile_size)
-    parent_grad = scatter_partials(partial, "pencil")
+    gathered = lax.all_to_all(partial, "pencil", 0, 0, tiled=True)
+    parent_grad = jnp.sum(gathered, axis=0, keepdims=True)
     return (rhs_grad, parent_grad)
 
 

time: 199 us -> 201 us (1.010)
  blocking collectives: 0 us -> 9.23 us
  starting transfers between devices: 77.5 us -> 73.4 us
  waiting for transfers between devices: 51.9 us -> 49.5 us
    all_to_all x0 -> x1, blocking collectives: none -> 9.23 us  [shards(): gathered = lax.all_to_all(partial, 'pencil', 0, 0, tiled=True)]
    ppermute x3 -> x0, starting transfers between devices: 4.04 us -> none  [scatter_partials(): lax.ppermute(piece, axis, [(j, (j + step) % peers) for j in range(peers)])]
    ppermute x3 -> x0, waiting for transfers between devices: 2.46 us -> none  [scatter_partials(): lax.ppermute(piece, axis, [(j, (j + step) % peers) for j in range(peers)])]
  transfers between devices with their start and end apart: 34 -> 31, of which waited for: 17 -> 14; matrix products, arithmetic and copies ran while one was open for 8% -> 8% of each run, Pallas kernels for 0% -> 0%
where the time goes in v8:
time: 201 us; the launch traced here: 200 us
  starting transfers between devices  73.4 us (37%)
  waiting for transfers between devices  49.5 us (25%)
  other arithmetic  37.6 us (19%)
  local copies, waits for them, and re-layouts  19.3 us (10%)
  blocking collectives  9.23 us (5%)
  matrix products  9 us (4%)
    ppermute x12, starting transfers between devices, extend(): lows.insert(0, lax.ppermute(low_piece, axis, up))  50.3 us
    ppermute x12, waiting for transfers between devices, extend(): highs.append(lax.ppermute(high_piece, axis, down))  23.6 us
    ppermute x7, waiting for transfers between devices, spread_faces(): got = lax.ppermute(sent, 'slab', low_pairs + high_pairs)  20 us
    select_n x14, other arithmetic, masked(): return jnp.where(keep, field, 0.0)  19.4 us
    ppermute x12, starting transfers between devices, extend(): highs.append(lax.ppermute(high_piece, axis, down))  18.4 us
    unnamed x61, local copies, waits for them, and re-layouts  9.39 us
    all_to_all x1, blocking collectives, shards(): gathered = lax.all_to_all(partial, 'pencil', 0, 0, tiled=True)  9.23 us
    ppermute x12, waiting for transfers between devices, extend(): lows.insert(0, lax.ppermute(low_piece, axis, up))  5.86 us
  transfers between devices with their start and end apart: 31, of which 14 were waited for; matrix products, arithmetic and copies ran while one was open for 8% of the time, Pallas kernels for 0%

profile of v8, /device:TPU:1, one launch (start us, length us, event | category | flops | bytes accessed | tf_op | source)
XLA Modules:
  0.0 200.0 jit_solution(3554473397197534155)
XLA Ops:
  0.6 4.7 %collective-permute-start.1 = (f32[4,128,512]{2,1,0:T(8,128)}, f32[4,128,512]{2,1,0:T(8,128)S(1)}, u32[]{:S(2)}, u32[]{:S(2)}) collective-permute-start(f32[4,128,512]{2,1,0:T(8,128)} %param.4), channel_id=1, source_target_pairs={{0,4},{4,8},{8,12},{12,16},{16,20},{20,24},{24,28},{28,32},{32,36}... | collective-permute-start | bytes 3145736 | tf_op jit(solution)/shard_map/ppermute | solution.py:116
  9.2 3.9 %collective-permute-start = (f32[1,128,512]{2,1,0:T(8,128)}, f32[1,128,512]{2,1,0:T(8,128)}, u32[]{:S(2)}, u32[]{:S(2)}) collective-permute-start(f32[1,128,512]{2,1,0:T(8,128)} %get-tuple-element.13), channel_id=1, source_target_pairs={{0,8},{4,12},{8,16},{12,20},{16,24},{20,28},{24,32},{28,36},{32,40... | collective-permute-start | bytes 786440 | tf_op jit(solution)/shard_map/ppermute | solution.py:116
  19.1 3.9 %collective-permute-done = f32[1,128,512]{2,1,0:T(8,128)} collective-permute-done((f32[1,128,512]{2,1,0:T(8,128)}, f32[1,128,512]{2,1,0:T(8,128)}, u32[]{:S(2)}, u32[]{:S(2)}) %collective-permute-start) | collective-permute-done | bytes 262176 | tf_op jit(solution)/shard_map/ppermute | solution.py:116
  24.7 3.6 %collective-permute-start.4 = (f32[14,5,512]{2,1,0:T(8,128)S(1)}, f32[14,5,512]{2,1,0:T(8,128)S(1)}, u32[]{:S(2)}, u32[]{:S(2)}) collective-permute-start(f32[14,5,512]{2,1,0:T(8,128)S(1)} %get-tuple-element.8), channel_id=1, source_target_pairs={{0,1},{1,2},{2,3},{4,5},{5,6},{6,7},{8,9},{9,10},{10,11},{12,13},{... | collective-permute-start | bytes 430088 | tf_op jit(solution)/shard_map/ppermute | solution.py:116
  31.2 4.0 %collective-permute-done.5 = f32[14,5,512]{2,1,0:T(8,128)S(1)} collective-permute-done((f32[14,5,512]{2,1,0:T(8,128)S(1)}, f32[14,5,512]{2,1,0:T(8,128)S(1)}, u32[]{:S(2)}, u32[]{:S(2)}) %collective-permute-start.5) | collective-permute-done | bytes 143392 | tf_op jit(solution)/shard_map/ppermute | solution.py:117
  36.7 3.2 %fusion.4 = f32[12,136,512]{2,1,0:T(8,128)S(1)} fusion(f32[12,136,512]{2,1,0:T(8,128)S(1)} %slice.618, f32[14,138,512]{2,1,0:T(8,128)S(1)} %pad_maximum_fusion, pred[12,136]{1,0:T(8,128)(4,1)S(1)} %broadcast_and_fusion.1), kind=kLoop, calls=%fused_computation.9 | loop fusion | flops 7520256 | bytes 20055648 | tf_op jit(solution)/shard_map/jit(_where)/select_n | solution.py:130
  40.3 2.6 %fusion.9 = f32[10,134,512]{2,1,0:T(8,128)S(1)} fusion(f32[10,134,512]{2,1,0:T(8,128)S(1)} %slice.624, f32[12,136,512]{2,1,0:T(8,128)S(1)} %fusion.4, pred[10,134]{1,0:T(8,128)(4,1)S(1)} %broadcast_and_fusion), kind=kLoop, calls=%fused_computation.21 | loop fusion | flops 6174720 | bytes 16467260 | tf_op jit(solution)/shard_map/jit(_where)/select_n | solution.py:130
  49.1 5.1 %collective-permute-start.6 = (f32[1,64,256]{2,1,0:T(8,128)S(1)}, f32[1,64,256]{2,1,0:T(8,128)S(1)}, u32[]{:S(2)}, u32[]{:S(2)}) collective-permute-start(f32[1,64,256]{2,1,0:T(8,128)S(1)} %convolution_bitcast_fusion.7), channel_id=1, source_target_pairs={{0,16},{4,20},{8,24},{12,28},{16,32},{20,36},{24,40},{28,44},{32,4... | collective-permute-start | bytes 196616 | tf_op jit(solution)/shard_map/ppermute | solution.py:116
  54.9 9.0 %collective-permute-start.7 = (f32[2,64,256]{2,1,0:T(8,128)}, f32[2,64,256]{2,1,0:T(8,128)}, u32[]{:S(2)}, u32[]{:S(2)}) collective-permute-start(f32[2,64,256]{2,1,0:T(8,128)} %pad_maximum_fusion.4), channel_id=1, source_target_pairs={{0,12},{4,16},{8,20},{12,24},{16,28},{20,32},{24,36},{28,40},{32,4... | collective-permute-start | bytes 393224 | tf_op jit(solution)/shard_map/ppermute | solution.py:116
  75.4 2.6 %collective-permute-done.11 = f32[2,64,256]{2,1,0:T(8,128)S(1)} collective-permute-done((f32[2,64,256]{2,1,0:T(8,128)}, f32[2,64,256]{2,1,0:T(8,128)S(1)}, u32[]{:S(2)}, u32[]{:S(2)}) %collective-permute-start.11) | collective-permute-done | bytes 131104 | tf_op jit(solution)/shard_map/ppermute | solution.py:117
  78.0 3.4 %collective-permute-done.12 = f32[2,64,256]{2,1,0:T(8,128)S(1)} collective-permute-done((f32[2,64,256]{2,1,0:T(8,128)}, f32[2,64,256]{2,1,0:T(8,128)S(1)}, u32[]{:S(2)}, u32[]{:S(2)}) %collective-permute-start.12) | collective-permute-done | bytes 131104 | tf_op jit(solution)/shard_map/ppermute | solution.py:117
  81.4 2.5 %collective-permute-done.13 = f32[1,64,256]{2,1,0:T(8,128)S(1)} collective-permute-done((f32[1,64,256]{2,1,0:T(8,128)S(1)}, f32[1,64,256]{2,1,0:T(8,128)S(1)}, u32[]{:S(2)}, u32[]{:S(2)}) %collective-permute-start.13) | collective-permute-done | bytes 65568 | tf_op jit(solution)/shard_map/ppermute | solution.py:117
  83.9 3.5 %collective-permute-start.14 = (f32[16,7,256]{2,1,0:T(8,128)S(1)}, f32[16,7,256]{2,1,0:T(8,128)S(1)}, u32[]{:S(2)}, u32[]{:S(2)}) collective-permute-start(f32[16,7,256]{2,1,0:T(8,128)S(1)} %get-tuple-element.10), channel_id=1, source_target_pairs={{0,1},{1,2},{2,3},{4,5},{5,6},{6,7},{8,9},{9,10},{10,11},{12,13},{... | collective-permute-start | bytes 344072 | tf_op jit(solution)/shard_map/ppermute | solution.py:116
  89.7 3.8 %collective-permute-done.15 = f32[16,7,256]{2,1,0:T(8,128)S(1)} collective-permute-done((f32[16,7,256]{2,1,0:T(8,128)S(1)}, f32[16,7,256]{2,1,0:T(8,128)S(1)}, u32[]{:S(2)}, u32[]{:S(2)}) %collective-permute-start.15) | collective-permute-done | bytes 114720 | tf_op jit(solution)/shard_map/ppermute | solution.py:117
  103.0 8.6 %collective-permute-start.16 = (f32[1,64,256]{2,1,0:T(8,128)S(1)}, f32[1,64,256]{2,1,0:T(8,128)}, u32[]{:S(2)}, u32[]{:S(2)}) collective-permute-start(f32[1,64,256]{2,1,0:T(8,128)S(1)} %bitcast.78), channel_id=1, source_target_pairs={{0,12},{4,16},{8,20},{12,24},{16,28},{20,32},{24,36},{28,40},{32,4... | collective-permute-start | bytes 196616 | tf_op jit(solution)/shard_map/ppermute | solution.py:116
  111.6 3.1 %collective-permute-start.17 = (f32[2,64,256]{2,1,0:T(8,128)S(1)}, f32[2,64,256]{2,1,0:T(8,128)}, u32[]{:S(2)}, u32[]{:S(2)}) collective-permute-start(f32[2,64,256]{2,1,0:T(8,128)S(1)} %reshape.855), channel_id=1, source_target_pairs={{0,8},{4,12},{8,16},{12,20},{16,24},{20,28},{24,32},{28,36},{32,40... | collective-permute-start | bytes 393224 | tf_op jit(solution)/shard_map/ppermute | solution.py:116
  124.3 2.9 %collective-permute-done.20 = f32[2,64,256]{2,1,0:T(8,128)S(1)} collective-permute-done((f32[2,64,256]{2,1,0:T(8,128)S(1)}, f32[2,64,256]{2,1,0:T(8,128)S(1)}, u32[]{:S(2)}, u32[]{:S(2)}) %collective-permute-start.20) | collective-permute-done | bytes 131104 | tf_op jit(solution)/shard_map/ppermute | solution.py:117
  128.9 3.2 %collective-permute-start.22 = (f32[12,5,256]{2,1,0:T(8,128)S(1)}, f32[12,5,256]{2,1,0:T(8,128)S(1)}, u32[]{:S(2)}, u32[]{:S(2)}) collective-permute-start(f32[12,5,256]{2,1,0:T(8,128)S(1)} %get-tuple-element.14), channel_id=1, source_target_pairs={{0,1},{1,2},{2,3},{4,5},{5,6},{6,7},{8,9},{9,10},{10,11},{12,13},{... | collective-permute-start | bytes 184328 | tf_op jit(solution)/shard_map/ppermute | solution.py:116
  133.5 2.9 %slice.636 = f32[6,130,512]{2,1,0:T(8,128)} slice(f32[8,132,512]{2,1,0:T(8,128)} %copy-done.1), slice={[1:7], [1:131], [0:512]} | slice | bytes 3194880 | tf_op jit(solution)/shard_map/slice | solution.py:134
  140.6 2.4 %fusion.91 = f32[6,68,256]{2,1,0:T(8,128)} fusion(f32[10,72,256]{2,1,0:T(8,128)S(1)} %fusion.76, f32[12,74,256]{2,1,0:T(8,128)S(1)} %pad_maximum_fusion.2, f32[12,74,256]{2,1,0:T(8,128)} %copy-done.5, f32[14,76,256]{2,1,0:T(8,128)} %copy-done.4, f32[16,78,256]{2,1,0:T(8,128)} %copy-done.3, f32[6,68,256]{2,1,0:T(8,128)S(1)} %fusion.88, ...), kind=kLoop, calls=%fused_computation.187 | loop fusion | flops 1044480 | bytes 3342336 | tf_op jit(solution)/shard_map/add | solution.py:187
  153.3 3.1 %fusion.30 = (f32[6,130,512]{2,1,0:T(8,128)S(1)}, f32[6,130,512]{2,1,0:T(8,128)S(1)}) fusion(f32[6,130,512]{2,1,0:T(8,128)S(1)} %slice.715, f32[8,132,512]{2,1,0:T(8,128)S(1)} %fusion.18, pred[6,130]{1,0:T(8,128)(4,1)S(1)} %copy-done.13, f32[6,130,512]{2,1,0:T(8,128)S(1)} %copy-done.6, f32[8,132,512]{2,1,0:T(8,128)S(1)} %copy-done.2), kind=kLoop, calls=%fused_computation.58 | loop fusion | flops 7188480 | bytes 19170060 | tf_op jit(solution)/shard_map/jit(_where)/select_n | solution.py:130
  158.5 2.6 %fusion.54 = f32[4,128,512]{2,1,0:T(8,128)S(1)} fusion(f32[8,132,512]{2,1,0:T(8,128)S(1)} %fusion.18, f32[10,134,512]{2,1,0:T(8,128)S(1)} %slice_multiply_fusion, f32[4,128,512]{2,1,0:T(8,128)S(1)} %get-tuple-element.21, f32[10,134,512]{2,1,0:T(8,128)} %copy-done, f32[4,128,512]{2,1,0:T(8,128)S(1)} %copy-done.9, f32[12,136,512]{2,1,0:T(8,128)S(1)} %fusion.4, ...), kind=kLoop, calls=%fused_computation.120 | loop fusion | flops 3407872 | bytes 11534336 | tf_op jit(solution)/shard_map/sub | solution.py:219
  168.3 18.7 %collective-permute-done.29 = f32[128,512]{1,0:T(8,128)S(1)} collective-permute-done((f32[128,512]{1,0:T(8,128)S(1)}, f32[128,512]{1,0:T(8,128)S(1)}, u32[]{:S(2)}, u32[]{:S(2)}) %collective-permute-start.29) | collective-permute-done | bytes 262176 | tf_op jit(solution)/shard_map/ppermute | solution.py:261
  190.2 9.2 %all_to_all.5 = f32[4,128,128]{2,1,0:T(8,128)S(1)} all-to-all(f32[4,128,128]{2,1,0:T(8,128)S(1)} %fusion.19), channel_id=1, replica_groups=mesh['slab'=32,'pencil'=4] {'pencil'}, dimensions={0} | all-to-all | bytes 524288 | tf_op jit(solution)/shard_map/all_to_all | solution.py:241
  (226 shorter events, 85.4 us)
Async XLA Ops:
  0.6 23.4 %collective-permute-start.1 = (f32[4,128,512]{2,1,0:T(8,128)}, f32[4,128,512]{2,1,0:T(8,128)S(1)}, u32[]{:S(2)}, u32[]{:S(2)}) collective-permute-start(f32[4,128,512]{2,1,0:T(8,128)} %param.4), channel_id=1, source_target_pairs={{0,4},{4,8},{8,12},{12,16},{16,20},{20,24},{24,28},{28,32},{32,36}... | collective-permute-start | bytes 3145736 | tf_op jit(solution)/shard_map/ppermute | solution.py:116
  5.4 19.1 %collective-permute-start.2 = (f32[4,128,512]{2,1,0:T(8,128)}, f32[4,128,512]{2,1,0:T(8,128)S(1)}, u32[]{:S(2)}, u32[]{:S(2)}) collective-permute-start(f32[4,128,512]{2,1,0:T(8,128)} %param.4), channel_id=1, source_target_pairs={{4,0},{8,4},{12,8},{16,12},{20,16},{24,20},{28,24},{32,28},{36,32}... | collective-permute-start | bytes 3145736 | tf_op jit(solution)/shard_map/ppermute | solution.py:117
  9.2 13.9 %collective-permute-start = (f32[1,128,512]{2,1,0:T(8,128)}, f32[1,128,512]{2,1,0:T(8,128)}, u32[]{:S(2)}, u32[]{:S(2)}) collective-permute-start(f32[1,128,512]{2,1,0:T(8,128)} %get-tuple-element.13), channel_id=1, source_target_pairs={{0,8},{4,12},{8,16},{12,20},{16,24},{20,28},{24,32},{28,36},{32,40... | collective-permute-start | bytes 786440 | tf_op jit(solution)/shard_map/ppermute | solution.py:116
  13.1 11.5 %collective-permute-start.3 = (f32[1,128,512]{2,1,0:T(8,128)}, f32[1,128,512]{2,1,0:T(8,128)S(1)}, u32[]{:S(2)}, u32[]{:S(2)}) collective-permute-start(f32[1,128,512]{2,1,0:T(8,128)} %get-tuple-element.12), channel_id=1, source_target_pairs={{8,0},{12,4},{16,8},{20,12},{24,16},{28,20},{32,24},{36,28},{40,32... | collective-permute-start | bytes 786440 | tf_op jit(solution)/shard_map/ppermute | solution.py:117
  24.7 6.5 %collective-permute-start.4 = (f32[14,5,512]{2,1,0:T(8,128)S(1)}, f32[14,5,512]{2,1,0:T(8,128)S(1)}, u32[]{:S(2)}, u32[]{:S(2)}) collective-permute-start(f32[14,5,512]{2,1,0:T(8,128)S(1)} %get-tuple-element.8), channel_id=1, source_target_pairs={{0,1},{1,2},{2,3},{4,5},{5,6},{6,7},{8,9},{9,10},{10,11},{12,13},{... | collective-permute-start | bytes 430088 | tf_op jit(solution)/shard_map/ppermute | solution.py:116
  28.2 6.9 %collective-permute-start.5 = (f32[14,5,512]{2,1,0:T(8,128)S(1)}, f32[14,5,512]{2,1,0:T(8,128)S(1)}, u32[]{:S(2)}, u32[]{:S(2)}) collective-permute-start(f32[14,5,512]{2,1,0:T(8,128)S(1)} %get-tuple-element.9), channel_id=1, source_target_pairs={{1,0},{2,1},{3,2},{5,4},{6,5},{7,6},{9,8},{10,9},{11,10},{13,12},{... | collective-permute-start | bytes 430088 | tf_op jit(solution)/shard_map/ppermute | solution.py:117
  49.1 21.3 %collective-permute-start.6 = (f32[1,64,256]{2,1,0:T(8,128)S(1)}, f32[1,64,256]{2,1,0:T(8,128)S(1)}, u32[]{:S(2)}, u32[]{:S(2)}) collective-permute-start(f32[1,64,256]{2,1,0:T(8,128)S(1)} %convolution_bitcast_fusion.7), channel_id=1, source_target_pairs={{0,16},{4,20},{8,24},{12,28},{16,32},{20,36},{24,40},{28,44},{32,4... | collective-permute-start | bytes 196616 | tf_op jit(solution)/shard_map/ppermute | solution.py:116
  54.9 16.8 %collective-permute-start.7 = (f32[2,64,256]{2,1,0:T(8,128)}, f32[2,64,256]{2,1,0:T(8,128)}, u32[]{:S(2)}, u32[]{:S(2)}) collective-permute-start(f32[2,64,256]{2,1,0:T(8,128)} %pad_maximum_fusion.4), channel_id=1, source_target_pairs={{0,12},{4,16},{8,20},{12,24},{16,28},{20,32},{24,36},{28,40},{32,4... | collective-permute-start | bytes 393224 | tf_op jit(solution)/shard_map/ppermute | solution.py:116
  64.4 9.6 %collective-permute-start.8 = (f32[2,64,256]{2,1,0:T(8,128)}, f32[2,64,256]{2,1,0:T(8,128)S(1)}, u32[]{:S(2)}, u32[]{:S(2)}) collective-permute-start(f32[2,64,256]{2,1,0:T(8,128)} %pad_maximum_fusion.4), channel_id=1, source_target_pairs={{0,8},{4,12},{8,16},{12,20},{16,24},{20,28},{24,32},{28,36},{32,40... | collective-permute-start | bytes 393224 | tf_op jit(solution)/shard_map/ppermute | solution.py:116
  66.1 9.2 %collective-permute-start.9 = (f32[2,64,256]{2,1,0:T(8,128)}, f32[2,64,256]{2,1,0:T(8,128)S(1)}, u32[]{:S(2)}, u32[]{:S(2)}) collective-permute-start(f32[2,64,256]{2,1,0:T(8,128)} %pad_maximum_fusion.4), channel_id=1, source_target_pairs={{0,4},{4,8},{8,12},{12,16},{16,20},{20,24},{24,28},{28,32},{32,36}... | collective-permute-start | bytes 393224 | tf_op jit(solution)/shard_map/ppermute | solution.py:116
  68.0 7.4 %collective-permute-start.10 = (f32[2,64,256]{2,1,0:T(8,128)}, f32[2,64,256]{2,1,0:T(8,128)S(1)}, u32[]{:S(2)}, u32[]{:S(2)}) collective-permute-start(f32[2,64,256]{2,1,0:T(8,128)} %pad_maximum_fusion.4), channel_id=1, source_target_pairs={{4,0},{8,4},{12,8},{16,12},{20,16},{24,20},{28,24},{32,28},{36,32}... | collective-permute-start | bytes 393224 | tf_op jit(solution)/shard_map/ppermute | solution.py:117
  70.4 7.5 %collective-permute-start.11 = (f32[2,64,256]{2,1,0:T(8,128)}, f32[2,64,256]{2,1,0:T(8,128)S(1)}, u32[]{:S(2)}, u32[]{:S(2)}) collective-permute-start(f32[2,64,256]{2,1,0:T(8,128)} %pad_maximum_fusion.4), channel_id=1, source_target_pairs={{8,0},{12,4},{16,8},{20,12},{24,16},{28,20},{32,24},{36,28},{40,32... | collective-permute-start | bytes 393224 | tf_op jit(solution)/shard_map/ppermute | solution.py:117
  71.8 9.6 %collective-permute-start.12 = (f32[2,64,256]{2,1,0:T(8,128)}, f32[2,64,256]{2,1,0:T(8,128)S(1)}, u32[]{:S(2)}, u32[]{:S(2)}) collective-permute-start(f32[2,64,256]{2,1,0:T(8,128)} %pad_maximum_fusion.4), channel_id=1, source_target_pairs={{12,0},{16,4},{20,8},{24,12},{28,16},{32,20},{36,24},{40,28},{44,3... | collective-permute-start | bytes 393224 | tf_op jit(solution)/shard_map/ppermute | solution.py:117
  74.0 9.9 %collective-permute-start.13 = (f32[1,64,256]{2,1,0:T(8,128)S(1)}, f32[1,64,256]{2,1,0:T(8,128)S(1)}, u32[]{:S(2)}, u32[]{:S(2)}) collective-permute-start(f32[1,64,256]{2,1,0:T(8,128)S(1)} %convolution_bitcast_fusion.6), channel_id=1, source_target_pairs={{16,0},{20,4},{24,8},{28,12},{32,16},{36,20},{40,24},{44,28},{48,3... | collective-permute-start | bytes 196616 | tf_op jit(solution)/shard_map/ppermute | solution.py:117
  87.5 6.1 %collective-permute-start.15 = (f32[16,7,256]{2,1,0:T(8,128)S(1)}, f32[16,7,256]{2,1,0:T(8,128)S(1)}, u32[]{:S(2)}, u32[]{:S(2)}) collective-permute-start(f32[16,7,256]{2,1,0:T(8,128)S(1)} %get-tuple-element.11), channel_id=1, source_target_pairs={{1,0},{2,1},{3,2},{5,4},{6,5},{7,6},{9,8},{10,9},{11,10},{13,12},{... | collective-permute-start | bytes 344072 | tf_op jit(solution)/shard_map/ppermute | solution.py:117
  103.0 18.1 %collective-permute-start.16 = (f32[1,64,256]{2,1,0:T(8,128)S(1)}, f32[1,64,256]{2,1,0:T(8,128)}, u32[]{:S(2)}, u32[]{:S(2)}) collective-permute-start(f32[1,64,256]{2,1,0:T(8,128)S(1)} %bitcast.78), channel_id=1, source_target_pairs={{0,12},{4,16},{8,20},{12,24},{16,28},{20,32},{24,36},{28,40},{32,4... | collective-permute-start | bytes 196616 | tf_op jit(solution)/shard_map/ppermute | solution.py:116
  111.6 11.6 %collective-permute-start.17 = (f32[2,64,256]{2,1,0:T(8,128)S(1)}, f32[2,64,256]{2,1,0:T(8,128)}, u32[]{:S(2)}, u32[]{:S(2)}) collective-permute-start(f32[2,64,256]{2,1,0:T(8,128)S(1)} %reshape.855), channel_id=1, source_target_pairs={{0,8},{4,12},{8,16},{12,20},{16,24},{20,28},{24,32},{28,36},{32,40... | collective-permute-start | bytes 393224 | tf_op jit(solution)/shard_map/ppermute | solution.py:116
  115.5 8.7 %collective-permute-start.18 = (f32[2,64,256]{2,1,0:T(8,128)S(1)}, f32[2,64,256]{2,1,0:T(8,128)S(1)}, u32[]{:S(2)}, u32[]{:S(2)}) collective-permute-start(f32[2,64,256]{2,1,0:T(8,128)S(1)} %reshape.855), channel_id=1, source_target_pairs={{0,4},{4,8},{8,12},{12,16},{16,20},{20,24},{24,28},{28,32},{32,36}... | collective-permute-start | bytes 393224 | tf_op jit(solution)/shard_map/ppermute | solution.py:116
  117.4 6.8 %collective-permute-start.19 = (f32[2,64,256]{2,1,0:T(8,128)S(1)}, f32[2,64,256]{2,1,0:T(8,128)S(1)}, u32[]{:S(2)}, u32[]{:S(2)}) collective-permute-start(f32[2,64,256]{2,1,0:T(8,128)S(1)} %reshape.855), channel_id=1, source_target_pairs={{4,0},{8,4},{12,8},{16,12},{20,16},{24,20},{28,24},{32,28},{36,32}... | collective-permute-start | bytes 393224 | tf_op jit(solution)/shard_map/ppermute | solution.py:117
  119.8 7.3 %collective-permute-start.20 = (f32[2,64,256]{2,1,0:T(8,128)S(1)}, f32[2,64,256]{2,1,0:T(8,128)S(1)}, u32[]{:S(2)}, u32[]{:S(2)}) collective-permute-start(f32[2,64,256]{2,1,0:T(8,128)S(1)} %reshape.855), channel_id=1, source_target_pairs={{8,0},{12,4},{16,8},{20,12},{24,16},{28,20},{32,24},{36,28},{40,32... | collective-permute-start | bytes 393224 | tf_op jit(solution)/shard_map/ppermute | solution.py:117
  121.1 7.8 %collective-permute-start.21 = (f32[1,64,256]{2,1,0:T(8,128)S(1)}, f32[1,64,256]{2,1,0:T(8,128)S(1)}, u32[]{:S(2)}, u32[]{:S(2)}) collective-permute-start(f32[1,64,256]{2,1,0:T(8,128)S(1)} %bitcast.79), channel_id=1, source_target_pairs={{12,0},{16,4},{20,8},{24,12},{28,16},{32,20},{36,24},{40,28},{44,3... | collective-permute-start | bytes 196616 | tf_op jit(solution)/shard_map/ppermute | solution.py:117
  128.9 7.5 %collective-permute-start.22 = (f32[12,5,256]{2,1,0:T(8,128)S(1)}, f32[12,5,256]{2,1,0:T(8,128)S(1)}, u32[]{:S(2)}, u32[]{:S(2)}) collective-permute-start(f32[12,5,256]{2,1,0:T(8,128)S(1)} %get-tuple-element.14), channel_id=1, source_target_pairs={{0,1},{1,2},{2,3},{4,5},{5,6},{6,7},{8,9},{9,10},{10,11},{12,13},{... | collective-permute-start | bytes 184328 | tf_op jit(solution)/shard_map/ppermute | solution.py:116
  132.2 6.5 %collective-permute-start.23 = (f32[12,5,256]{2,1,0:T(8,128)S(1)}, f32[12,5,256]{2,1,0:T(8,128)S(1)}, u32[]{:S(2)}, u32[]{:S(2)}) collective-permute-start(f32[12,5,256]{2,1,0:T(8,128)S(1)} %get-tuple-element.15), channel_id=1, source_target_pairs={{1,0},{2,1},{3,2},{5,4},{6,5},{7,6},{9,8},{10,9},{11,10},{13,12},{... | collective-permute-start | bytes 184328 | tf_op jit(solution)/shard_map/ppermute | solution.py:117
  166.8 20.1 %collective-permute-start.29 = (f32[128,512]{1,0:T(8,128)S(1)}, f32[128,512]{1,0:T(8,128)S(1)}, u32[]{:S(2)}, u32[]{:S(2)}) collective-permute-start(f32[128,512]{1,0:T(8,128)S(1)} %get-tuple-element.5), channel_id=1, source_target_pairs={{0,24},{32,56},{64,88},{96,120},{124,100},{92,68},{60,36},{28,4},{... | collective-permute-start | bytes 786440 | tf_op jit(solution)/shard_map/ppermute | solution.py:261
  (28 other events, 94.5 us)

commit v9 on v5

--- a/solution.py
+++ b/solution.py
@@ -188,7 +188,7 @@
 def shards(cotangent, seg_rows, owners, offsets):
     x_cells, y_cells, z_cells = cotangent.shape
     tile_size = TILE
-    depth_x, depth_y = 5, 29
+    depth_x, depth_y = 5, 5
     grown = extend(extend(cotangent, "slab", 0, depth_x), "pencil", 1, depth_y)
     powers = [grown]
     for step in range(1, 6):
@@ -197,9 +197,10 @@
     for step in range(6):
         part = crop(powers[step], depth_x - step, depth_y - step, 0, 0, x_cells, y_cells)
         rhs_grad = rhs_grad + coefficient(0) * part
-    settled = crop(powers[3], depth_x - 3, depth_y - 3, 0, depth_y - 3, x_cells, y_cells)
+    settled = crop(powers[3], depth_x - 3, depth_y - 3, 0, 0, x_cells, y_cells)
     medium = children_sum(settled)
-    grown = medium_cycle(medium, (depth_y - 3) // 2, y_cells // 2)
+    medium_y = 13
+    grown = medium_cycle(extend(medium, "pencil", 1, medium_y), medium_y, y_cells // 2)
     back_fine = prolong(grown)[1:-1, 1:-1] * 0.125
     rhs_grad = rhs_grad + crop(back_fine, 3, 3, 0, 0, x_cells, y_cells)
     centre, total = shrink_neighbours(back_fine)

time: 210 us -> 198 us (0.943)
  waiting for transfers between devices: 56.2 us -> 47.9 us
  other arithmetic: 41.5 us -> 37.3 us
  local copies, waits for them, and re-layouts: 20.2 us -> 23.3 us
    ppermute x10 -> x11, waiting for transfers between devices: 28.9 us -> 20.4 us  [extend(): highs.append(lax.ppermute(high_piece, axis, down))]
    select_n x16 -> x14, other arithmetic: 27.3 us -> 20.1 us  [masked(): return jnp.where(keep, field, 0.0)]
    ppermute x7, waiting for transfers between devices: 13.8 us -> 18.6 us  [spread_faces(): got = lax.ppermute(sent, 'slab', low_pairs + high_pairs)]
    ppermute x7, starting transfers between devices: 7.95 us -> 4.98 us  [spread_faces(): got = lax.ppermute(sent, 'slab', low_pairs + high_pairs)]
    ppermute x3, waiting for transfers between devices: 5.24 us -> 2.58 us  [scatter_partials(): lax.ppermute(piece, axis, [(j, (j + step) % peers) for j in range(peers)])]
    and x16 -> x13, other arithmetic: 1.13 us -> 3.64 us  [masked(): inside('slab', block_x, width_x)[:, None, None]]
    ppermute x10 -> x11, starting transfers between devices: 48.1 us -> 50.6 us  [extend(): lows.insert(0, lax.ppermute(low_piece, axis, up))]
    ppermute x10 -> x11, waiting for transfers between devices: 8.24 us -> 6.29 us  [extend(): lows.insert(0, lax.ppermute(low_piece, axis, up))]
  transfers between devices with their start and end apart: 30 -> 32, of which waited for: 15 -> 16; matrix products, arithmetic and copies ran while one was open for 7% -> 7% of each run, Pallas kernels for 0% -> 0%
where the time goes in v9:
time: 198 us; the launch traced here: 196 us
  starting transfers between devices  76.6 us (39%)
  waiting for transfers between devices  47.9 us (24%)
  other arithmetic  37.3 us (19%)
  local copies, waits for them, and re-layouts  23.3 us (12%)
  matrix products  9.04 us (5%)
  between operations  2.23 us (1%)
    ppermute x11, starting transfers between devices, extend(): lows.insert(0, lax.ppermute(low_piece, axis, up))  50.6 us
    ppermute x11, waiting for transfers between devices, extend(): highs.append(lax.ppermute(high_piece, axis, down))  20.4 us
    select_n x14, other arithmetic, masked(): return jnp.where(keep, field, 0.0)  20.1 us
    ppermute x7, waiting for transfers between devices, spread_faces(): got = lax.ppermute(sent, 'slab', low_pairs + high_pairs)  18.6 us
    ppermute x11, starting transfers between devices, extend(): highs.append(lax.ppermute(high_piece, axis, down))  17.2 us
    unnamed x83, local copies, waits for them, and re-layouts  10.3 us
    ppermute x11, waiting for transfers between devices, extend(): lows.insert(0, lax.ppermute(low_piece, axis, up))  6.29 us
    slice x12, local copies, waits for them, and re-layouts, shrink_neighbours(): centre = field[1:-1, 1:-1]  5.09 us
  transfers between devices with their start and end apart: 32, of which 16 were waited for; matrix products, arithmetic and copies ran while one was open for 7% of the time, Pallas kernels for 0%

profile of v9, /device:TPU:1, one launch (start us, length us, event | category | flops | bytes accessed | tf_op | source)
XLA Modules:
  0.0 196.3 jit_solution(3030536867604078429)
XLA Ops:
  0.6 4.7 %collective-permute-start.1 = (f32[4,128,512]{2,1,0:T(8,128)}, f32[4,128,512]{2,1,0:T(8,128)S(1)}, u32[]{:S(2)}, u32[]{:S(2)}) collective-permute-start(f32[4,128,512]{2,1,0:T(8,128)} %param.4), channel_id=1, source_target_pairs={{0,4},{4,8},{8,12},{12,16},{16,20},{20,24},{24,28},{28,32},{32,36}... | collective-permute-start | bytes 3145736 | tf_op jit(solution)/shard_map/ppermute | solution.py:116
  9.2 3.9 %collective-permute-start = (f32[1,128,512]{2,1,0:T(8,128)}, f32[1,128,512]{2,1,0:T(8,128)}, u32[]{:S(2)}, u32[]{:S(2)}) collective-permute-start(f32[1,128,512]{2,1,0:T(8,128)} %get-tuple-element.11), channel_id=1, source_target_pairs={{0,8},{4,12},{8,16},{12,20},{16,24},{20,28},{24,32},{28,36},{32,40... | collective-permute-start | bytes 786440 | tf_op jit(solution)/shard_map/ppermute | solution.py:116
  18.4 4.7 %collective-permute-done = f32[1,128,512]{2,1,0:T(8,128)} collective-permute-done((f32[1,128,512]{2,1,0:T(8,128)}, f32[1,128,512]{2,1,0:T(8,128)}, u32[]{:S(2)}, u32[]{:S(2)}) %collective-permute-start) | collective-permute-done | bytes 262176 | tf_op jit(solution)/shard_map/ppermute | solution.py:116
  26.5 3.6 %collective-permute-start.4 = (f32[14,5,512]{2,1,0:T(8,128)S(1)}, f32[14,5,512]{2,1,0:T(8,128)S(1)}, u32[]{:S(2)}, u32[]{:S(2)}) collective-permute-start(f32[14,5,512]{2,1,0:T(8,128)S(1)} %get-tuple-element.8), channel_id=1, source_target_pairs={{0,1},{1,2},{2,3},{4,5},{5,6},{6,7},{8,9},{9,10},{10,11},{12,13},{... | collective-permute-start | bytes 430088 | tf_op jit(solution)/shard_map/ppermute | solution.py:116
  33.0 4.0 %collective-permute-done.5 = f32[14,5,512]{2,1,0:T(8,128)S(1)} collective-permute-done((f32[14,5,512]{2,1,0:T(8,128)S(1)}, f32[14,5,512]{2,1,0:T(8,128)S(1)}, u32[]{:S(2)}, u32[]{:S(2)}) %collective-permute-start.5) | collective-permute-done | bytes 143392 | tf_op jit(solution)/shard_map/ppermute | solution.py:117
  37.0 2.8 %pad_maximum_fusion = f32[14,138,512]{2,1,0:T(8,128)S(1)} fusion(f32[14,5,512]{2,1,0:T(8,128)S(1)} %collective-permute-done.5, f32[14,128,512]{2,1,0:T(8,128)} %copy-done.9, f32[14,5,512]{2,1,0:T(8,128)S(1)} %collective-permute-done.4), kind=kLoop, calls=%fused_computation.2 | loop fusion | flops 1978368 | bytes 7913472 | tf_op jit(solution)/shard_map/concatenate | solution.py:119
  40.4 3.1 %fusion.4 = f32[12,136,512]{2,1,0:T(8,128)S(1)} fusion(f32[12,136,512]{2,1,0:T(8,128)S(1)} %slice.640, f32[14,138,512]{2,1,0:T(8,128)S(1)} %pad_maximum_fusion, pred[12,136]{1,0:T(8,128)(4,1)S(1)} %broadcast_and_fusion.1), kind=kLoop, calls=%fused_computation.9 | loop fusion | flops 7520256 | bytes 20055648 | tf_op jit(solution)/shard_map/jit(_where)/select_n | solution.py:130
  43.9 2.6 %fusion.9 = f32[10,134,512]{2,1,0:T(8,128)S(1)} fusion(f32[10,134,512]{2,1,0:T(8,128)S(1)} %slice.646, f32[12,136,512]{2,1,0:T(8,128)S(1)} %fusion.4, pred[10,134]{1,0:T(8,128)(4,1)S(1)} %broadcast_and_fusion), kind=kLoop, calls=%fused_computation.21 | loop fusion | flops 6174720 | bytes 16467260 | tf_op jit(solution)/shard_map/jit(_where)/select_n | solution.py:130
  51.4 3.7 %collective-permute-start.6 = (f32[2,13,256]{2,1,0:T(8,128)S(1)}, f32[2,13,256]{2,1,0:T(8,128)S(1)}, u32[]{:S(2)}, u32[]{:S(2)}) collective-permute-start(f32[2,13,256]{2,1,0:T(8,128)S(1)} %get-tuple-element.52), channel_id=1, source_target_pairs={{0,1},{1,2},{2,3},{4,5},{5,6},{6,7},{8,9},{9,10},{10,11},{12,13},{... | collective-permute-start | bytes 79880 | tf_op jit(solution)/shard_map/ppermute | solution.py:116
  56.9 2.7 %collective-permute-done.7 = f32[2,13,256]{2,1,0:T(8,128)S(1)} collective-permute-done((f32[2,13,256]{2,1,0:T(8,128)S(1)}, f32[2,13,256]{2,1,0:T(8,128)S(1)}, u32[]{:S(2)}, u32[]{:S(2)}) %collective-permute-start.7) | collective-permute-done | bytes 26656 | tf_op jit(solution)/shard_map/ppermute | solution.py:117
  59.7 10.4 %collective-permute-start.10 = (f32[2,90,256]{2,1,0:T(8,128)S(1)}, f32[2,90,256]{2,1,0:T(8,128)S(1)}, u32[]{:S(2)}, u32[]{:S(2)}) collective-permute-start(f32[2,90,256]{2,1,0:T(8,128)S(1)} %pad_maximum_fusion.10), channel_id=1, source_target_pairs={{0,12},{4,16},{8,20},{12,24},{16,28},{20,32},{24,36},{28,40},{32,4... | collective-permute-start | bytes 552968 | tf_op jit(solution)/shard_map/ppermute | solution.py:116
  70.1 3.9 %collective-permute-start.15 = (f32[1,90,256]{2,1,0:T(8,128)S(1)}, f32[1,90,256]{2,1,0:T(8,128)S(1)}, u32[]{:S(2)}, u32[]{:S(2)}) collective-permute-start(f32[1,90,256]{2,1,0:T(8,128)S(1)} %get-tuple-element.18), channel_id=1, source_target_pairs={{0,16},{4,20},{8,24},{12,28},{16,32},{20,36},{24,40},{28,44},{32,4... | collective-permute-start | bytes 276488 | tf_op jit(solution)/shard_map/ppermute | solution.py:116
  74.1 2.5 %collective-permute-start.11 = (f32[2,90,256]{2,1,0:T(8,128)S(1)}, f32[2,90,256]{2,1,0:T(8,128)S(1)}, u32[]{:S(2)}, u32[]{:S(2)}) collective-permute-start(f32[2,90,256]{2,1,0:T(8,128)S(1)} %pad_maximum_fusion.10), channel_id=1, source_target_pairs={{0,8},{4,12},{8,16},{12,20},{16,24},{20,28},{24,32},{28,36},{32,40... | collective-permute-start | bytes 552968 | tf_op jit(solution)/shard_map/ppermute | solution.py:116
  86.0 3.8 %collective-permute-done.12 = f32[2,90,256]{2,1,0:T(8,128)S(1)} collective-permute-done((f32[2,90,256]{2,1,0:T(8,128)S(1)}, f32[2,90,256]{2,1,0:T(8,128)S(1)}, u32[]{:S(2)}, u32[]{:S(2)}) %collective-permute-start.12) | collective-permute-done | bytes 184352 | tf_op jit(solution)/shard_map/ppermute | solution.py:117
  89.8 2.8 %collective-permute-done.13 = f32[2,90,256]{2,1,0:T(8,128)S(1)} collective-permute-done((f32[2,90,256]{2,1,0:T(8,128)S(1)}, f32[2,90,256]{2,1,0:T(8,128)S(1)}, u32[]{:S(2)}, u32[]{:S(2)}) %collective-permute-start.13) | collective-permute-done | bytes 184352 | tf_op jit(solution)/shard_map/ppermute | solution.py:117
  105.9 12.1 %collective-permute-start.21 = (f32[1,74,256]{2,1,0:T(8,128)S(1)}, f32[1,74,256]{2,1,0:T(8,128)}, u32[]{:S(2)}, u32[]{:S(2)}) collective-permute-start(f32[1,74,256]{2,1,0:T(8,128)S(1)} %bitcast.75), channel_id=1, source_target_pairs={{0,12},{4,16},{8,20},{12,24},{16,28},{20,32},{24,36},{28,40},{32,4... | collective-permute-start | bytes 227336 | tf_op jit(solution)/shard_map/ppermute | solution.py:116
  121.2 2.9 %slice.658 = f32[6,130,512]{2,1,0:T(8,128)} slice(f32[8,132,512]{2,1,0:T(8,128)} %copy-done.1), slice={[1:7], [1:131], [0:512]} | slice | bytes 3194880 | tf_op jit(solution)/shard_map/slice | solution.py:134
  126.0 2.4 %collective-permute-start.17 = (f32[2,74,256]{2,1,0:T(8,128)}, f32[2,74,256]{2,1,0:T(8,128)S(1)}, u32[]{:S(2)}, u32[]{:S(2)}) collective-permute-start(f32[2,74,256]{2,1,0:T(8,128)} %reshape.894), channel_id=1, source_target_pairs={{4,0},{8,4},{12,8},{16,12},{20,16},{24,20},{28,24},{32,28},{36,32}... | collective-permute-start | bytes 454664 | tf_op jit(solution)/shard_map/ppermute | solution.py:117
  133.0 3.6 %collective-permute-done.19 = f32[2,74,256]{2,1,0:T(8,128)S(1)} collective-permute-done((f32[2,74,256]{2,1,0:T(8,128)}, f32[2,74,256]{2,1,0:T(8,128)S(1)}, u32[]{:S(2)}, u32[]{:S(2)}) %collective-permute-start.19) | collective-permute-done | bytes 151584 | tf_op jit(solution)/shard_map/ppermute | solution.py:117
  140.1 2.4 %fusion.91 = f32[6,68,256]{2,1,0:T(8,128)} fusion(f32[10,72,256]{2,1,0:T(8,128)S(1)} %fusion.76, f32[2,74,256]{2,1,0:T(8,128)S(1)} %collective-permute-done.17, f32[2,74,256]{2,1,0:T(8,128)} %reshape.894, f32[2,74,256]{2,1,0:T(8,128)S(1)} %collective-permute-done.16, f32[12,86,256]{2,1,0:T(8,128)} %copy-done.4, f32[14,88,256]{2,1,0:T(8,128)} %copy-done.3, ...), kind=kLoop, calls=%fused_computation.185 | loop fusion | flops 1775616 | bytes 3514368 | tf_op jit(solution)/shard_map/add | solution.py:182
  153.1 3.1 %fusion.30 = (f32[6,130,512]{2,1,0:T(8,128)S(1)}, f32[6,130,512]{2,1,0:T(8,128)S(1)}) fusion(f32[6,130,512]{2,1,0:T(8,128)S(1)} %slice.739, f32[8,132,512]{2,1,0:T(8,128)S(1)} %fusion.18, pred[6,130]{1,0:T(8,128)(4,1)S(1)} %copy-done.26, f32[6,130,512]{2,1,0:T(8,128)S(1)} %copy-done.6, f32[8,132,512]{2,1,0:T(8,128)S(1)} %copy-done.2), kind=kLoop, calls=%fused_computation.60 | loop fusion | flops 7188480 | bytes 19170060 | tf_op jit(solution)/shard_map/jit(_where)/select_n | solution.py:130
  158.6 2.6 %fusion.59 = f32[4,128,512]{2,1,0:T(8,128)S(1)} fusion(f32[8,132,512]{2,1,0:T(8,128)S(1)} %fusion.18, f32[10,134,512]{2,1,0:T(8,128)S(1)} %slice_multiply_fusion, f32[4,128,512]{2,1,0:T(8,128)S(1)} %get-tuple-element.60, f32[10,134,512]{2,1,0:T(8,128)} %copy-done, f32[4,128,512]{2,1,0:T(8,128)S(1)} %copy-done.8, f32[12,136,512]{2,1,0:T(8,128)S(1)} %fusion.4, ...), kind=kLoop, calls=%fused_computation.127 | loop fusion | flops 3407872 | bytes 11534336 | tf_op jit(solution)/shard_map/sub | solution.py:212
  168.4 17.3 %collective-permute-done.27 = f32[128,512]{1,0:T(8,128)S(1)} collective-permute-done((f32[128,512]{1,0:T(8,128)S(1)}, f32[128,512]{1,0:T(8,128)S(1)}, u32[]{:S(2)}, u32[]{:S(2)}) %collective-permute-start.27) | collective-permute-done | bytes 262176 | tf_op jit(solution)/shard_map/ppermute | solution.py:253
  190.8 2.3 %collective-permute-start.31 = (f32[1,128,128]{2,1,0:T(8,128)S(1)}, f32[1,128,128]{2,1,0:T(8,128)S(1)}, u32[]{:S(2)}, u32[]{:S(2)}) collective-permute-start(f32[1,128,128]{2,1,0:T(8,128)S(1)} %get-tuple-element.13), channel_id=1, source_target_pairs={{0,3},{1,0},{2,1},{3,2},{4,7},{5,4},{6,5},{7,6},{8,11},{9,8},{10,9... | collective-permute-start | bytes 196616 | tf_op jit(solution)/shard_map/ppermute | solution.py:266
  (253 shorter events, 86.2 us)
Async XLA Ops:
  0.6 23.4 %collective-permute-start.1 = (f32[4,128,512]{2,1,0:T(8,128)}, f32[4,128,512]{2,1,0:T(8,128)S(1)}, u32[]{:S(2)}, u32[]{:S(2)}) collective-permute-start(f32[4,128,512]{2,1,0:T(8,128)} %param.4), channel_id=1, source_target_pairs={{0,4},{4,8},{8,12},{12,16},{16,20},{20,24},{24,28},{28,32},{32,36}... | collective-permute-start | bytes 3145736 | tf_op jit(solution)/shard_map/ppermute | solution.py:116
  5.4 19.1 %collective-permute-start.2 = (f32[4,128,512]{2,1,0:T(8,128)}, f32[4,128,512]{2,1,0:T(8,128)S(1)}, u32[]{:S(2)}, u32[]{:S(2)}) collective-permute-start(f32[4,128,512]{2,1,0:T(8,128)} %param.4), channel_id=1, source_target_pairs={{4,0},{8,4},{12,8},{16,12},{20,16},{24,20},{28,24},{32,28},{36,32}... | collective-permute-start | bytes 3145736 | tf_op jit(solution)/shard_map/ppermute | solution.py:117
  9.2 13.9 %collective-permute-start = (f32[1,128,512]{2,1,0:T(8,128)}, f32[1,128,512]{2,1,0:T(8,128)}, u32[]{:S(2)}, u32[]{:S(2)}) collective-permute-start(f32[1,128,512]{2,1,0:T(8,128)} %get-tuple-element.11), channel_id=1, source_target_pairs={{0,8},{4,12},{8,16},{12,20},{16,24},{20,28},{24,32},{28,36},{32,40... | collective-permute-start | bytes 786440 | tf_op jit(solution)/shard_map/ppermute | solution.py:116
  13.1 11.5 %collective-permute-start.3 = (f32[1,128,512]{2,1,0:T(8,128)}, f32[1,128,512]{2,1,0:T(8,128)S(1)}, u32[]{:S(2)}, u32[]{:S(2)}) collective-permute-start(f32[1,128,512]{2,1,0:T(8,128)} %get-tuple-element.10), channel_id=1, source_target_pairs={{8,0},{12,4},{16,8},{20,12},{24,16},{28,20},{32,24},{36,28},{40,32... | collective-permute-start | bytes 786440 | tf_op jit(solution)/shard_map/ppermute | solution.py:117
  26.5 6.5 %collective-permute-start.4 = (f32[14,5,512]{2,1,0:T(8,128)S(1)}, f32[14,5,512]{2,1,0:T(8,128)S(1)}, u32[]{:S(2)}, u32[]{:S(2)}) collective-permute-start(f32[14,5,512]{2,1,0:T(8,128)S(1)} %get-tuple-element.8), channel_id=1, source_target_pairs={{0,1},{1,2},{2,3},{4,5},{5,6},{6,7},{8,9},{9,10},{10,11},{12,13},{... | collective-permute-start | bytes 430088 | tf_op jit(solution)/shard_map/ppermute | solution.py:116
  30.0 6.9 %collective-permute-start.5 = (f32[14,5,512]{2,1,0:T(8,128)S(1)}, f32[14,5,512]{2,1,0:T(8,128)S(1)}, u32[]{:S(2)}, u32[]{:S(2)}) collective-permute-start(f32[14,5,512]{2,1,0:T(8,128)S(1)} %get-tuple-element.9), channel_id=1, source_target_pairs={{1,0},{2,1},{3,2},{5,4},{6,5},{7,6},{9,8},{10,9},{11,10},{13,12},{... | collective-permute-start | bytes 430088 | tf_op jit(solution)/shard_map/ppermute | solution.py:117
  51.4 5.6 %collective-permute-start.6 = (f32[2,13,256]{2,1,0:T(8,128)S(1)}, f32[2,13,256]{2,1,0:T(8,128)S(1)}, u32[]{:S(2)}, u32[]{:S(2)}) collective-permute-start(f32[2,13,256]{2,1,0:T(8,128)S(1)} %get-tuple-element.52), channel_id=1, source_target_pairs={{0,1},{1,2},{2,3},{4,5},{5,6},{6,7},{8,9},{9,10},{10,11},{12,13},{... | collective-permute-start | bytes 79880 | tf_op jit(solution)/shard_map/ppermute | solution.py:116
  59.7 22.5 %collective-permute-start.10 = (f32[2,90,256]{2,1,0:T(8,128)S(1)}, f32[2,90,256]{2,1,0:T(8,128)S(1)}, u32[]{:S(2)}, u32[]{:S(2)}) collective-permute-start(f32[2,90,256]{2,1,0:T(8,128)S(1)} %pad_maximum_fusion.10), channel_id=1, source_target_pairs={{0,12},{4,16},{8,20},{12,24},{16,28},{20,32},{24,36},{28,40},{32,4... | collective-permute-start | bytes 552968 | tf_op jit(solution)/shard_map/ppermute | solution.py:116
  70.1 10.8 %collective-permute-start.15 = (f32[1,90,256]{2,1,0:T(8,128)S(1)}, f32[1,90,256]{2,1,0:T(8,128)S(1)}, u32[]{:S(2)}, u32[]{:S(2)}) collective-permute-start(f32[1,90,256]{2,1,0:T(8,128)S(1)} %get-tuple-element.18), channel_id=1, source_target_pairs={{0,16},{4,20},{8,24},{12,28},{16,32},{20,36},{24,40},{28,44},{32,4... | collective-permute-start | bytes 276488 | tf_op jit(solution)/shard_map/ppermute | solution.py:116
  74.1 9.5 %collective-permute-start.11 = (f32[2,90,256]{2,1,0:T(8,128)S(1)}, f32[2,90,256]{2,1,0:T(8,128)S(1)}, u32[]{:S(2)}, u32[]{:S(2)}) collective-permute-start(f32[2,90,256]{2,1,0:T(8,128)S(1)} %pad_maximum_fusion.10), channel_id=1, source_target_pairs={{0,8},{4,12},{8,16},{12,20},{16,24},{20,28},{24,32},{28,36},{32,40... | collective-permute-start | bytes 552968 | tf_op jit(solution)/shard_map/ppermute | solution.py:116
  76.6 8.6 %collective-permute-start.8 = (f32[2,90,256]{2,1,0:T(8,128)S(1)}, f32[2,90,256]{2,1,0:T(8,128)S(1)}, u32[]{:S(2)}, u32[]{:S(2)}) collective-permute-start(f32[2,90,256]{2,1,0:T(8,128)S(1)} %pad_maximum_fusion.10), channel_id=1, source_target_pairs={{0,4},{4,8},{8,12},{12,16},{16,20},{20,24},{24,28},{28,32},{32,36}... | collective-permute-start | bytes 552968 | tf_op jit(solution)/shard_map/ppermute | solution.py:116
  78.6 7.3 %collective-permute-start.9 = (f32[2,90,256]{2,1,0:T(8,128)S(1)}, f32[2,90,256]{2,1,0:T(8,128)S(1)}, u32[]{:S(2)}, u32[]{:S(2)}) collective-permute-start(f32[2,90,256]{2,1,0:T(8,128)S(1)} %pad_maximum_fusion.10), channel_id=1, source_target_pairs={{4,0},{8,4},{12,8},{16,12},{20,16},{24,20},{28,24},{32,28},{36,32}... | collective-permute-start | bytes 552968 | tf_op jit(solution)/shard_map/ppermute | solution.py:117
  80.9 8.8 %collective-permute-start.12 = (f32[2,90,256]{2,1,0:T(8,128)S(1)}, f32[2,90,256]{2,1,0:T(8,128)S(1)}, u32[]{:S(2)}, u32[]{:S(2)}) collective-permute-start(f32[2,90,256]{2,1,0:T(8,128)S(1)} %pad_maximum_fusion.10), channel_id=1, source_target_pairs={{8,0},{12,4},{16,8},{20,12},{24,16},{28,20},{32,24},{36,28},{40,32... | collective-permute-start | bytes 552968 | tf_op jit(solution)/shard_map/ppermute | solution.py:117
  82.3 10.4 %collective-permute-start.13 = (f32[2,90,256]{2,1,0:T(8,128)S(1)}, f32[2,90,256]{2,1,0:T(8,128)S(1)}, u32[]{:S(2)}, u32[]{:S(2)}) collective-permute-start(f32[2,90,256]{2,1,0:T(8,128)S(1)} %pad_maximum_fusion.10), channel_id=1, source_target_pairs={{12,0},{16,4},{20,8},{24,12},{28,16},{32,20},{36,24},{40,28},{44,3... | collective-permute-start | bytes 552968 | tf_op jit(solution)/shard_map/ppermute | solution.py:117
  83.6 10.8 %collective-permute-start.14 = (f32[1,90,256]{2,1,0:T(8,128)S(1)}, f32[1,90,256]{2,1,0:T(8,128)S(1)}, u32[]{:S(2)}, u32[]{:S(2)}) collective-permute-start(f32[1,90,256]{2,1,0:T(8,128)S(1)} %get-tuple-element.17), channel_id=1, source_target_pairs={{16,0},{20,4},{24,8},{28,12},{32,16},{36,20},{40,24},{44,28},{48,3... | collective-permute-start | bytes 276488 | tf_op jit(solution)/shard_map/ppermute | solution.py:117
  105.9 23.7 %collective-permute-start.21 = (f32[1,74,256]{2,1,0:T(8,128)S(1)}, f32[1,74,256]{2,1,0:T(8,128)}, u32[]{:S(2)}, u32[]{:S(2)}) collective-permute-start(f32[1,74,256]{2,1,0:T(8,128)S(1)} %bitcast.75), channel_id=1, source_target_pairs={{0,12},{4,16},{8,20},{12,24},{16,28},{20,32},{24,36},{28,40},{32,4... | collective-permute-start | bytes 227336 | tf_op jit(solution)/shard_map/ppermute | solution.py:116
  118.7 13.2 %collective-permute-start.18 = (f32[2,74,256]{2,1,0:T(8,128)}, f32[2,74,256]{2,1,0:T(8,128)}, u32[]{:S(2)}, u32[]{:S(2)}) collective-permute-start(f32[2,74,256]{2,1,0:T(8,128)} %reshape.894), channel_id=1, source_target_pairs={{0,8},{4,12},{8,16},{12,20},{16,24},{20,28},{24,32},{28,36},{32,40... | collective-permute-start | bytes 454664 | tf_op jit(solution)/shard_map/ppermute | solution.py:116
  124.0 8.8 %collective-permute-start.16 = (f32[2,74,256]{2,1,0:T(8,128)}, f32[2,74,256]{2,1,0:T(8,128)S(1)}, u32[]{:S(2)}, u32[]{:S(2)}) collective-permute-start(f32[2,74,256]{2,1,0:T(8,128)} %reshape.894), channel_id=1, source_target_pairs={{0,4},{4,8},{8,12},{12,16},{16,20},{20,24},{24,28},{28,32},{32,36}... | collective-permute-start | bytes 454664 | tf_op jit(solution)/shard_map/ppermute | solution.py:116
  126.0 7.0 %collective-permute-start.17 = (f32[2,74,256]{2,1,0:T(8,128)}, f32[2,74,256]{2,1,0:T(8,128)S(1)}, u32[]{:S(2)}, u32[]{:S(2)}) collective-permute-start(f32[2,74,256]{2,1,0:T(8,128)} %reshape.894), channel_id=1, source_target_pairs={{4,0},{8,4},{12,8},{16,12},{20,16},{24,20},{28,24},{32,28},{36,32}... | collective-permute-start | bytes 454664 | tf_op jit(solution)/shard_map/ppermute | solution.py:117
  128.4 8.2 %collective-permute-start.19 = (f32[2,74,256]{2,1,0:T(8,128)}, f32[2,74,256]{2,1,0:T(8,128)S(1)}, u32[]{:S(2)}, u32[]{:S(2)}) collective-permute-start(f32[2,74,256]{2,1,0:T(8,128)} %reshape.894), channel_id=1, source_target_pairs={{8,0},{12,4},{16,8},{20,12},{24,16},{28,20},{32,24},{36,28},{40,32... | collective-permute-start | bytes 454664 | tf_op jit(solution)/shard_map/ppermute | solution.py:117
  129.7 8.0 %collective-permute-start.20 = (f32[1,74,256]{2,1,0:T(8,128)S(1)}, f32[1,74,256]{2,1,0:T(8,128)S(1)}, u32[]{:S(2)}, u32[]{:S(2)}) collective-permute-start(f32[1,74,256]{2,1,0:T(8,128)S(1)} %bitcast.76), channel_id=1, source_target_pairs={{12,0},{16,4},{20,8},{24,12},{28,16},{32,20},{36,24},{40,28},{44,3... | collective-permute-start | bytes 227336 | tf_op jit(solution)/shard_map/ppermute | solution.py:117
  167.0 18.8 %collective-permute-start.27 = (f32[128,512]{1,0:T(8,128)S(1)}, f32[128,512]{1,0:T(8,128)S(1)}, u32[]{:S(2)}, u32[]{:S(2)}) collective-permute-start(f32[128,512]{1,0:T(8,128)S(1)} %get-tuple-element.5), channel_id=1, source_target_pairs={{0,24},{32,56},{64,88},{96,120},{124,100},{92,68},{60,36},{28,4},{... | collective-permute-start | bytes 786440 | tf_op jit(solution)/shard_map/ppermute | solution.py:253
  189.2 4.8 %collective-permute-start.29 = (f32[1,128,128]{2,1,0:T(8,128)S(1)}, f32[1,128,128]{2,1,0:T(8,128)S(1)}, u32[]{:S(2)}, u32[]{:S(2)}) collective-permute-start(f32[1,128,128]{2,1,0:T(8,128)S(1)} %get-tuple-element.12), channel_id=1, source_target_pairs={{0,1},{1,2},{2,3},{3,0},{4,5},{5,6},{6,7},{7,4},{8,9},{9,10},{10,1... | collective-permute-start | bytes 196616 | tf_op jit(solution)/shard_map/ppermute | solution.py:266
  190.8 4.9 %collective-permute-start.31 = (f32[1,128,128]{2,1,0:T(8,128)S(1)}, f32[1,128,128]{2,1,0:T(8,128)S(1)}, u32[]{:S(2)}, u32[]{:S(2)}) collective-permute-start(f32[1,128,128]{2,1,0:T(8,128)S(1)} %get-tuple-element.13), channel_id=1, source_target_pairs={{0,3},{1,0},{2,1},{3,2},{4,7},{5,4},{6,5},{7,6},{8,11},{9,8},{10,9... | collective-permute-start | bytes 196616 | tf_op jit(solution)/shard_map/ppermute | solution.py:266
  (41 other events, 231.8 us)

commit v10 on v9

--- a/solution.py
+++ b/solution.py
@@ -171,8 +171,7 @@
     for step in range(3):
         part = crop(coarse_powers[step], coarse_wx - step, coarse_wy - step, 0, 3, coarse_x, coarse_y)
         grad_coarse = grad_coarse + coefficient(2) * part
-    back_medium = prolong(grad_coarse)[:, 1:-1] * 0.125
-    back_xy = extend(back_medium, "slab", 0, 5)
+    back_xy = prolong(extend(grad_coarse, "slab", 0, 3))[1:-1, 1:-1] * 0.125
     grad_medium = grad_medium + crop(back_xy, 5, 5, 2, 2, block_x, block_y)
     centre, total = shrink_neighbours(back_xy)
     near = crop(settled, settled_x, settled_y, 4, 4, block_x, block_y)

time: 198 us -> 204 us (1.030)
  waiting for transfers between devices: 47.9 us -> 41.7 us
  local copies, waits for them, and re-layouts: 23.3 us -> 29 us
  other arithmetic: 37.3 us -> 42.3 us
  matrix products: 9.04 us -> 11.4 us
    unnamed x83 -> x71, local copies, waits for them, and re-layouts: 10.3 us -> 15 us
    ppermute x11, waiting for transfers between devices: 6.29 us -> 2.97 us  [extend(): lows.insert(0, lax.ppermute(low_piece, axis, up))]
    ppermute x11, waiting for transfers between devices: 20.4 us -> 17.5 us  [extend(): highs.append(lax.ppermute(high_piece, axis, down))]
    and x13, other arithmetic: 3.64 us -> 6.47 us  [masked(): inside('slab', block_x, width_x)[:, None, None]]
  transfers between devices with their start and end apart: 32 -> 32, of which waited for: 16 -> 15; matrix products, arithmetic and copies ran while one was open for 7% -> 10% of each run, Pallas kernels for 0% -> 0%
where the time goes in v10:
time: 204 us; the launch traced here: 202 us
  starting transfers between devices  75.7 us (37%)
  other arithmetic  42.3 us (21%)
  waiting for transfers between devices  41.7 us (20%)
  local copies, waits for them, and re-layouts  29 us (14%)
  matrix products  11.4 us (6%)
  between operations  2.15 us (1%)
    ppermute x11, starting transfers between devices, extend(): lows.insert(0, lax.ppermute(low_piece, axis, up))  50.1 us
    select_n x14, other arithmetic, masked(): return jnp.where(keep, field, 0.0)  21.1 us
    ppermute x7, waiting for transfers between devices, spread_faces(): got = lax.ppermute(sent, 'slab', low_pairs + high_pairs)  18.7 us
    ppermute x11, waiting for transfers between devices, extend(): highs.append(lax.ppermute(high_piece, axis, down))  17.5 us
    ppermute x11, starting transfers between devices, extend(): highs.append(lax.ppermute(high_piece, axis, down))  16.8 us
    unnamed x71, local copies, waits for them, and re-layouts  15 us
    and x13, other arithmetic, masked(): inside('slab', block_x, width_x)[:, None, None]  6.47 us
    slice x12, local copies, waits for them, and re-layouts, shrink_neighbours(): centre = field[1:-1, 1:-1]  5.13 us
  transfers between devices with their start and end apart: 32, of which 15 were waited for; matrix products, arithmetic and copies ran while one was open for 10% of the time, Pallas kernels for 0%

profile of v10, /device:TPU:1, one launch (start us, length us, event | category | flops | bytes accessed | tf_op | source)
XLA Modules:
  0.0 202.3 jit_solution(11543825322615419354)
XLA Ops:
  0.6 4.7 %collective-permute-start.1 = (f32[4,128,512]{2,1,0:T(8,128)}, f32[4,128,512]{2,1,0:T(8,128)S(1)}, u32[]{:S(2)}, u32[]{:S(2)}) collective-permute-start(f32[4,128,512]{2,1,0:T(8,128)} %param.4), channel_id=1, source_target_pairs={{0,4},{4,8},{8,12},{12,16},{16,20},{20,24},{24,28},{28,32},{32,36}... | collective-permute-start | bytes 3145736 | tf_op jit(solution)/shard_map/ppermute | solution.py:116
  9.2 3.9 %collective-permute-start = (f32[1,128,512]{2,1,0:T(8,128)}, f32[1,128,512]{2,1,0:T(8,128)}, u32[]{:S(2)}, u32[]{:S(2)}) collective-permute-start(f32[1,128,512]{2,1,0:T(8,128)} %get-tuple-element.11), channel_id=1, source_target_pairs={{0,8},{4,12},{8,16},{12,20},{16,24},{20,28},{24,32},{28,36},{32,40... | collective-permute-start | bytes 786440 | tf_op jit(solution)/shard_map/ppermute | solution.py:116
  26.5 3.6 %collective-permute-start.4 = (f32[14,5,512]{2,1,0:T(8,128)S(1)}, f32[14,5,512]{2,1,0:T(8,128)S(1)}, u32[]{:S(2)}, u32[]{:S(2)}) collective-permute-start(f32[14,5,512]{2,1,0:T(8,128)S(1)} %get-tuple-element.8), channel_id=1, source_target_pairs={{0,1},{1,2},{2,3},{4,5},{5,6},{6,7},{8,9},{9,10},{10,11},{12,13},{... | collective-permute-start | bytes 430088 | tf_op jit(solution)/shard_map/ppermute | solution.py:116
  33.0 4.0 %collective-permute-done.5 = f32[14,5,512]{2,1,0:T(8,128)S(1)} collective-permute-done((f32[14,5,512]{2,1,0:T(8,128)S(1)}, f32[14,5,512]{2,1,0:T(8,128)S(1)}, u32[]{:S(2)}, u32[]{:S(2)}) %collective-permute-start.5) | collective-permute-done | bytes 143392 | tf_op jit(solution)/shard_map/ppermute | solution.py:117
  37.0 2.8 %pad_maximum_fusion = f32[14,138,512]{2,1,0:T(8,128)S(1)} fusion(f32[14,5,512]{2,1,0:T(8,128)S(1)} %collective-permute-done.5, f32[14,128,512]{2,1,0:T(8,128)} %copy-done.9, f32[14,5,512]{2,1,0:T(8,128)S(1)} %collective-permute-done.4), kind=kLoop, calls=%fused_computation.2 | loop fusion | flops 1978368 | bytes 7913472 | tf_op jit(solution)/shard_map/concatenate | solution.py:119
  40.4 3.2 %fusion.4 = f32[12,136,512]{2,1,0:T(8,128)S(1)} fusion(f32[12,136,512]{2,1,0:T(8,128)S(1)} %slice.662, f32[14,138,512]{2,1,0:T(8,128)S(1)} %pad_maximum_fusion, pred[12,136]{1,0:T(8,128)(4,1)S(1)} %broadcast_and_fusion.1), kind=kLoop, calls=%fused_computation.9 | loop fusion | flops 7520256 | bytes 20055648 | tf_op jit(solution)/shard_map/jit(_where)/select_n | solution.py:130
  43.9 2.6 %fusion.9 = f32[10,134,512]{2,1,0:T(8,128)S(1)} fusion(f32[10,134,512]{2,1,0:T(8,128)S(1)} %slice.668, f32[12,136,512]{2,1,0:T(8,128)S(1)} %fusion.4, pred[10,134]{1,0:T(8,128)(4,1)S(1)} %broadcast_and_fusion), kind=kLoop, calls=%fused_computation.21 | loop fusion | flops 6174720 | bytes 16467260 | tf_op jit(solution)/shard_map/jit(_where)/select_n | solution.py:130
  51.4 3.7 %collective-permute-start.6 = (f32[2,13,256]{2,1,0:T(8,128)S(1)}, f32[2,13,256]{2,1,0:T(8,128)S(1)}, u32[]{:S(2)}, u32[]{:S(2)}) collective-permute-start(f32[2,13,256]{2,1,0:T(8,128)S(1)} %get-tuple-element.40), channel_id=1, source_target_pairs={{0,1},{1,2},{2,3},{4,5},{5,6},{6,7},{8,9},{9,10},{10,11},{12,13},{... | collective-permute-start | bytes 79880 | tf_op jit(solution)/shard_map/ppermute | solution.py:116
  56.9 2.8 %collective-permute-done.7 = f32[2,13,256]{2,1,0:T(8,128)S(1)} collective-permute-done((f32[2,13,256]{2,1,0:T(8,128)S(1)}, f32[2,13,256]{2,1,0:T(8,128)S(1)}, u32[]{:S(2)}, u32[]{:S(2)}) %collective-permute-start.7) | collective-permute-done | bytes 26656 | tf_op jit(solution)/shard_map/ppermute | solution.py:117
  59.8 10.4 %collective-permute-start.10 = (f32[2,90,256]{2,1,0:T(8,128)S(1)}, f32[2,90,256]{2,1,0:T(8,128)S(1)}, u32[]{:S(2)}, u32[]{:S(2)}) collective-permute-start(f32[2,90,256]{2,1,0:T(8,128)S(1)} %pad_maximum_fusion.8), channel_id=1, source_target_pairs={{0,12},{4,16},{8,20},{12,24},{16,28},{20,32},{24,36},{28,40},{32,4... | collective-permute-start | bytes 552968 | tf_op jit(solution)/shard_map/ppermute | solution.py:116
  70.1 3.9 %collective-permute-start.15 = (f32[1,90,256]{2,1,0:T(8,128)S(1)}, f32[1,90,256]{2,1,0:T(8,128)S(1)}, u32[]{:S(2)}, u32[]{:S(2)}) collective-permute-start(f32[1,90,256]{2,1,0:T(8,128)S(1)} %get-tuple-element.18), channel_id=1, source_target_pairs={{0,16},{4,20},{8,24},{12,28},{16,32},{20,36},{24,40},{28,44},{32,4... | collective-permute-start | bytes 276488 | tf_op jit(solution)/shard_map/ppermute | solution.py:116
  74.1 2.5 %collective-permute-start.11 = (f32[2,90,256]{2,1,0:T(8,128)S(1)}, f32[2,90,256]{2,1,0:T(8,128)S(1)}, u32[]{:S(2)}, u32[]{:S(2)}) collective-permute-start(f32[2,90,256]{2,1,0:T(8,128)S(1)} %pad_maximum_fusion.8), channel_id=1, source_target_pairs={{0,8},{4,12},{8,16},{12,20},{16,24},{20,28},{24,32},{28,36},{32,40... | collective-permute-start | bytes 552968 | tf_op jit(solution)/shard_map/ppermute | solution.py:116
  78.6 2.3 %collective-permute-start.9 = (f32[2,90,256]{2,1,0:T(8,128)S(1)}, f32[2,90,256]{2,1,0:T(8,128)S(1)}, u32[]{:S(2)}, u32[]{:S(2)}) collective-permute-start(f32[2,90,256]{2,1,0:T(8,128)S(1)} %pad_maximum_fusion.8), channel_id=1, source_target_pairs={{4,0},{8,4},{12,8},{16,12},{20,16},{24,20},{28,24},{32,28},{36,32}... | collective-permute-start | bytes 552968 | tf_op jit(solution)/shard_map/ppermute | solution.py:117
  86.0 3.8 %collective-permute-done.12 = f32[2,90,256]{2,1,0:T(8,128)S(1)} collective-permute-done((f32[2,90,256]{2,1,0:T(8,128)S(1)}, f32[2,90,256]{2,1,0:T(8,128)S(1)}, u32[]{:S(2)}, u32[]{:S(2)}) %collective-permute-start.12) | collective-permute-done | bytes 184352 | tf_op jit(solution)/shard_map/ppermute | solution.py:117
  89.8 2.8 %collective-permute-done.13 = f32[2,90,256]{2,1,0:T(8,128)S(1)} collective-permute-done((f32[2,90,256]{2,1,0:T(8,128)S(1)}, f32[2,90,256]{2,1,0:T(8,128)S(1)}, u32[]{:S(2)}, u32[]{:S(2)}) %collective-permute-start.13) | collective-permute-done | bytes 184352 | tf_op jit(solution)/shard_map/ppermute | solution.py:117
  108.3 12.0 %collective-permute-start.16 = (f32[1,38,128]{2,1,0:T(8,128)}, f32[1,38,128]{2,1,0:T(8,128)}, u32[]{:S(2)}, u32[]{:S(2)}) collective-permute-start(f32[1,38,128]{2,1,0:T(8,128)} %fusion.157), channel_id=1, source_target_pairs={{0,12},{4,16},{8,20},{12,24},{16,28},{20,32},{24,36},{28,40},{32,4... | collective-permute-start | bytes 58376 | tf_op jit(solution)/shard_map/ppermute | solution.py:116
  120.4 2.9 %slice.680 = f32[6,130,512]{2,1,0:T(8,128)} slice(f32[8,132,512]{2,1,0:T(8,128)} %copy-done.1), slice={[1:7], [1:131], [0:512]} | slice | bytes 3194880 | tf_op jit(solution)/shard_map/slice | solution.py:134
  124.5 2.1 %collective-permute-start.18 = (f32[1,38,128]{2,1,0:T(8,128)}, f32[1,38,128]{2,1,0:T(8,128)S(1)}, u32[]{:S(2)}, u32[]{:S(2)}) collective-permute-start(f32[1,38,128]{2,1,0:T(8,128)} %fusion.157), channel_id=1, source_target_pairs={{0,4},{4,8},{8,12},{12,16},{16,20},{20,24},{24,28},{28,32},{32,36}... | collective-permute-start | bytes 58376 | tf_op jit(solution)/shard_map/ppermute | solution.py:116
  126.7 2.2 %collective-permute-start.19 = (f32[1,38,128]{2,1,0:T(8,128)}, f32[1,38,128]{2,1,0:T(8,128)S(1)}, u32[]{:S(2)}, u32[]{:S(2)}) collective-permute-start(f32[1,38,128]{2,1,0:T(8,128)} %fusion.157), channel_id=1, source_target_pairs={{4,0},{8,4},{12,8},{16,12},{20,16},{24,20},{28,24},{32,28},{36,32}... | collective-permute-start | bytes 58376 | tf_op jit(solution)/shard_map/ppermute | solution.py:117
  146.5 2.3 %fusion.98 = f32[6,68,256]{2,1,0:T(8,128)} fusion(f32[10,72,256]{2,1,0:T(8,128)S(1)} %fusion.83, f32[12,74,256]{2,1,0:T(8,128)S(1)} %slice_multiply_fusion.2, f32[12,86,256]{2,1,0:T(8,128)} %copy-done.4, f32[14,88,256]{2,1,0:T(8,128)} %copy-done.3, f32[2,90,256]{2,1,0:T(8,128)S(1)} %copy-done.14, f32[2,90,256]{2,1,0:T(8,128)S(1)} %copy-done.12, ...), kind=kLoop, calls=%fused_computation.199 | loop fusion | flops 1566720 | bytes 3477504 | tf_op jit(solution)/shard_map/add | solution.py:181
  159.0 3.1 %fusion.30 = (f32[6,130,512]{2,1,0:T(8,128)S(1)}, f32[6,130,512]{2,1,0:T(8,128)S(1)}) fusion(f32[6,130,512]{2,1,0:T(8,128)S(1)} %slice.769, f32[8,132,512]{2,1,0:T(8,128)S(1)} %fusion.18, pred[6,130]{1,0:T(8,128)(4,1)S(1)} %copy-done.20, f32[6,130,512]{2,1,0:T(8,128)S(1)} %copy-done.6, f32[8,132,512]{2,1,0:T(8,128)S(1)} %copy-done.2), kind=kLoop, calls=%fused_computation.60 | loop fusion | flops 7188480 | bytes 19170060 | tf_op jit(solution)/shard_map/jit(_where)/select_n | solution.py:130
  164.6 2.6 %fusion.66 = f32[4,128,512]{2,1,0:T(8,128)S(1)} fusion(f32[8,132,512]{2,1,0:T(8,128)S(1)} %fusion.18, f32[10,134,512]{2,1,0:T(8,128)S(1)} %slice_multiply_fusion, f32[4,128,512]{2,1,0:T(8,128)S(1)} %get-tuple-element.45, f32[10,134,512]{2,1,0:T(8,128)} %copy-done, f32[4,128,512]{2,1,0:T(8,128)S(1)} %copy-done.8, f32[12,136,512]{2,1,0:T(8,128)S(1)} %fusion.4, ...), kind=kLoop, calls=%fused_computation.140 | loop fusion | flops 3407872 | bytes 11534336 | tf_op jit(solution)/shard_map/sub | solution.py:211
  174.6 17.4 %collective-permute-done.27 = f32[128,512]{1,0:T(8,128)S(1)} collective-permute-done((f32[128,512]{1,0:T(8,128)S(1)}, f32[128,512]{1,0:T(8,128)S(1)}, u32[]{:S(2)}, u32[]{:S(2)}) %collective-permute-start.27) | collective-permute-done | bytes 262176 | tf_op jit(solution)/shard_map/ppermute | solution.py:252
  196.8 2.3 %collective-permute-start.31 = (f32[1,128,128]{2,1,0:T(8,128)S(1)}, f32[1,128,128]{2,1,0:T(8,128)S(1)}, u32[]{:S(2)}, u32[]{:S(2)}) collective-permute-start(f32[1,128,128]{2,1,0:T(8,128)S(1)} %get-tuple-element.13), channel_id=1, source_target_pairs={{0,3},{1,0},{2,1},{3,2},{4,7},{5,4},{6,5},{7,6},{8,11},{9,8},{10,9... | collective-permute-start | bytes 196616 | tf_op jit(solution)/shard_map/ppermute | solution.py:265
  (248 shorter events, 96.3 us)
Async XLA Ops:
  0.6 23.4 %collective-permute-start.1 = (f32[4,128,512]{2,1,0:T(8,128)}, f32[4,128,512]{2,1,0:T(8,128)S(1)}, u32[]{:S(2)}, u32[]{:S(2)}) collective-permute-start(f32[4,128,512]{2,1,0:T(8,128)} %param.4), channel_id=1, source_target_pairs={{0,4},{4,8},{8,12},{12,16},{16,20},{20,24},{24,28},{28,32},{32,36}... | collective-permute-start | bytes 3145736 | tf_op jit(solution)/shard_map/ppermute | solution.py:116
  5.4 19.1 %collective-permute-start.2 = (f32[4,128,512]{2,1,0:T(8,128)}, f32[4,128,512]{2,1,0:T(8,128)S(1)}, u32[]{:S(2)}, u32[]{:S(2)}) collective-permute-start(f32[4,128,512]{2,1,0:T(8,128)} %param.4), channel_id=1, source_target_pairs={{4,0},{8,4},{12,8},{16,12},{20,16},{24,20},{28,24},{32,28},{36,32}... | collective-permute-start | bytes 3145736 | tf_op jit(solution)/shard_map/ppermute | solution.py:117
  9.2 13.9 %collective-permute-start = (f32[1,128,512]{2,1,0:T(8,128)}, f32[1,128,512]{2,1,0:T(8,128)}, u32[]{:S(2)}, u32[]{:S(2)}) collective-permute-start(f32[1,128,512]{2,1,0:T(8,128)} %get-tuple-element.11), channel_id=1, source_target_pairs={{0,8},{4,12},{8,16},{12,20},{16,24},{20,28},{24,32},{28,36},{32,40... | collective-permute-start | bytes 786440 | tf_op jit(solution)/shard_map/ppermute | solution.py:116
  13.1 11.5 %collective-permute-start.3 = (f32[1,128,512]{2,1,0:T(8,128)}, f32[1,128,512]{2,1,0:T(8,128)S(1)}, u32[]{:S(2)}, u32[]{:S(2)}) collective-permute-start(f32[1,128,512]{2,1,0:T(8,128)} %get-tuple-element.10), channel_id=1, source_target_pairs={{8,0},{12,4},{16,8},{20,12},{24,16},{28,20},{32,24},{36,28},{40,32... | collective-permute-start | bytes 786440 | tf_op jit(solution)/shard_map/ppermute | solution.py:117
  26.5 6.5 %collective-permute-start.4 = (f32[14,5,512]{2,1,0:T(8,128)S(1)}, f32[14,5,512]{2,1,0:T(8,128)S(1)}, u32[]{:S(2)}, u32[]{:S(2)}) collective-permute-start(f32[14,5,512]{2,1,0:T(8,128)S(1)} %get-tuple-element.8), channel_id=1, source_target_pairs={{0,1},{1,2},{2,3},{4,5},{5,6},{6,7},{8,9},{9,10},{10,11},{12,13},{... | collective-permute-start | bytes 430088 | tf_op jit(solution)/shard_map/ppermute | solution.py:116
  30.0 6.9 %collective-permute-start.5 = (f32[14,5,512]{2,1,0:T(8,128)S(1)}, f32[14,5,512]{2,1,0:T(8,128)S(1)}, u32[]{:S(2)}, u32[]{:S(2)}) collective-permute-start(f32[14,5,512]{2,1,0:T(8,128)S(1)} %get-tuple-element.9), channel_id=1, source_target_pairs={{1,0},{2,1},{3,2},{5,4},{6,5},{7,6},{9,8},{10,9},{11,10},{13,12},{... | collective-permute-start | bytes 430088 | tf_op jit(solution)/shard_map/ppermute | solution.py:117
  51.4 5.5 %collective-permute-start.6 = (f32[2,13,256]{2,1,0:T(8,128)S(1)}, f32[2,13,256]{2,1,0:T(8,128)S(1)}, u32[]{:S(2)}, u32[]{:S(2)}) collective-permute-start(f32[2,13,256]{2,1,0:T(8,128)S(1)} %get-tuple-element.40), channel_id=1, source_target_pairs={{0,1},{1,2},{2,3},{4,5},{5,6},{6,7},{8,9},{9,10},{10,11},{12,13},{... | collective-permute-start | bytes 79880 | tf_op jit(solution)/shard_map/ppermute | solution.py:116
  59.8 22.5 %collective-permute-start.10 = (f32[2,90,256]{2,1,0:T(8,128)S(1)}, f32[2,90,256]{2,1,0:T(8,128)S(1)}, u32[]{:S(2)}, u32[]{:S(2)}) collective-permute-start(f32[2,90,256]{2,1,0:T(8,128)S(1)} %pad_maximum_fusion.8), channel_id=1, source_target_pairs={{0,12},{4,16},{8,20},{12,24},{16,28},{20,32},{24,36},{28,40},{32,4... | collective-permute-start | bytes 552968 | tf_op jit(solution)/shard_map/ppermute | solution.py:116
  70.1 10.8 %collective-permute-start.15 = (f32[1,90,256]{2,1,0:T(8,128)S(1)}, f32[1,90,256]{2,1,0:T(8,128)S(1)}, u32[]{:S(2)}, u32[]{:S(2)}) collective-permute-start(f32[1,90,256]{2,1,0:T(8,128)S(1)} %get-tuple-element.18), channel_id=1, source_target_pairs={{0,16},{4,20},{8,24},{12,28},{16,32},{20,36},{24,40},{28,44},{32,4... | collective-permute-start | bytes 276488 | tf_op jit(solution)/shard_map/ppermute | solution.py:116
  74.1 9.5 %collective-permute-start.11 = (f32[2,90,256]{2,1,0:T(8,128)S(1)}, f32[2,90,256]{2,1,0:T(8,128)S(1)}, u32[]{:S(2)}, u32[]{:S(2)}) collective-permute-start(f32[2,90,256]{2,1,0:T(8,128)S(1)} %pad_maximum_fusion.8), channel_id=1, source_target_pairs={{0,8},{4,12},{8,16},{12,20},{16,24},{20,28},{24,32},{28,36},{32,40... | collective-permute-start | bytes 552968 | tf_op jit(solution)/shard_map/ppermute | solution.py:116
  76.6 8.4 %collective-permute-start.8 = (f32[2,90,256]{2,1,0:T(8,128)S(1)}, f32[2,90,256]{2,1,0:T(8,128)S(1)}, u32[]{:S(2)}, u32[]{:S(2)}) collective-permute-start(f32[2,90,256]{2,1,0:T(8,128)S(1)} %pad_maximum_fusion.8), channel_id=1, source_target_pairs={{0,4},{4,8},{8,12},{12,16},{16,20},{20,24},{24,28},{28,32},{32,36}... | collective-permute-start | bytes 552968 | tf_op jit(solution)/shard_map/ppermute | solution.py:116
  78.6 7.3 %collective-permute-start.9 = (f32[2,90,256]{2,1,0:T(8,128)S(1)}, f32[2,90,256]{2,1,0:T(8,128)S(1)}, u32[]{:S(2)}, u32[]{:S(2)}) collective-permute-start(f32[2,90,256]{2,1,0:T(8,128)S(1)} %pad_maximum_fusion.8), channel_id=1, source_target_pairs={{4,0},{8,4},{12,8},{16,12},{20,16},{24,20},{28,24},{32,28},{36,32}... | collective-permute-start | bytes 552968 | tf_op jit(solution)/shard_map/ppermute | solution.py:117
  80.9 8.8 %collective-permute-start.12 = (f32[2,90,256]{2,1,0:T(8,128)S(1)}, f32[2,90,256]{2,1,0:T(8,128)S(1)}, u32[]{:S(2)}, u32[]{:S(2)}) collective-permute-start(f32[2,90,256]{2,1,0:T(8,128)S(1)} %pad_maximum_fusion.8), channel_id=1, source_target_pairs={{8,0},{12,4},{16,8},{20,12},{24,16},{28,20},{32,24},{36,28},{40,32... | collective-permute-start | bytes 552968 | tf_op jit(solution)/shard_map/ppermute | solution.py:117
  82.3 10.4 %collective-permute-start.13 = (f32[2,90,256]{2,1,0:T(8,128)S(1)}, f32[2,90,256]{2,1,0:T(8,128)S(1)}, u32[]{:S(2)}, u32[]{:S(2)}) collective-permute-start(f32[2,90,256]{2,1,0:T(8,128)S(1)} %pad_maximum_fusion.8), channel_id=1, source_target_pairs={{12,0},{16,4},{20,8},{24,12},{28,16},{32,20},{36,24},{40,28},{44,3... | collective-permute-start | bytes 552968 | tf_op jit(solution)/shard_map/ppermute | solution.py:117
  83.6 10.8 %collective-permute-start.14 = (f32[1,90,256]{2,1,0:T(8,128)S(1)}, f32[1,90,256]{2,1,0:T(8,128)S(1)}, u32[]{:S(2)}, u32[]{:S(2)}) collective-permute-start(f32[1,90,256]{2,1,0:T(8,128)S(1)} %get-tuple-element.17), channel_id=1, source_target_pairs={{16,0},{20,4},{24,8},{28,12},{32,16},{36,20},{40,24},{44,28},{48,3... | collective-permute-start | bytes 276488 | tf_op jit(solution)/shard_map/ppermute | solution.py:117
  108.3 21.9 %collective-permute-start.16 = (f32[1,38,128]{2,1,0:T(8,128)}, f32[1,38,128]{2,1,0:T(8,128)}, u32[]{:S(2)}, u32[]{:S(2)}) collective-permute-start(f32[1,38,128]{2,1,0:T(8,128)} %fusion.157), channel_id=1, source_target_pairs={{0,12},{4,16},{8,20},{12,24},{16,28},{20,32},{24,36},{28,40},{32,4... | collective-permute-start | bytes 58376 | tf_op jit(solution)/shard_map/ppermute | solution.py:116
  123.3 9.6 %collective-permute-start.17 = (f32[1,38,128]{2,1,0:T(8,128)}, f32[1,38,128]{2,1,0:T(8,128)S(1)}, u32[]{:S(2)}, u32[]{:S(2)}) collective-permute-start(f32[1,38,128]{2,1,0:T(8,128)} %fusion.157), channel_id=1, source_target_pairs={{0,8},{4,12},{8,16},{12,20},{16,24},{20,28},{24,32},{28,36},{32,40... | collective-permute-start | bytes 58376 | tf_op jit(solution)/shard_map/ppermute | solution.py:116
  124.5 8.9 %collective-permute-start.18 = (f32[1,38,128]{2,1,0:T(8,128)}, f32[1,38,128]{2,1,0:T(8,128)S(1)}, u32[]{:S(2)}, u32[]{:S(2)}) collective-permute-start(f32[1,38,128]{2,1,0:T(8,128)} %fusion.157), channel_id=1, source_target_pairs={{0,4},{4,8},{8,12},{12,16},{16,20},{20,24},{24,28},{28,32},{32,36}... | collective-permute-start | bytes 58376 | tf_op jit(solution)/shard_map/ppermute | solution.py:116
  126.7 8.7 %collective-permute-start.19 = (f32[1,38,128]{2,1,0:T(8,128)}, f32[1,38,128]{2,1,0:T(8,128)S(1)}, u32[]{:S(2)}, u32[]{:S(2)}) collective-permute-start(f32[1,38,128]{2,1,0:T(8,128)} %fusion.157), channel_id=1, source_target_pairs={{4,0},{8,4},{12,8},{16,12},{20,16},{24,20},{28,24},{32,28},{36,32}... | collective-permute-start | bytes 58376 | tf_op jit(solution)/shard_map/ppermute | solution.py:117
  128.9 7.1 %collective-permute-start.20 = (f32[1,38,128]{2,1,0:T(8,128)}, f32[1,38,128]{2,1,0:T(8,128)S(1)}, u32[]{:S(2)}, u32[]{:S(2)}) collective-permute-start(f32[1,38,128]{2,1,0:T(8,128)} %fusion.157), channel_id=1, source_target_pairs={{8,0},{12,4},{16,8},{20,12},{24,16},{28,20},{32,24},{36,28},{40,32... | collective-permute-start | bytes 58376 | tf_op jit(solution)/shard_map/ppermute | solution.py:117
  130.2 7.7 %collective-permute-start.21 = (f32[1,38,128]{2,1,0:T(8,128)}, f32[1,38,128]{2,1,0:T(8,128)S(1)}, u32[]{:S(2)}, u32[]{:S(2)}) collective-permute-start(f32[1,38,128]{2,1,0:T(8,128)} %fusion.157), channel_id=1, source_target_pairs={{12,0},{16,4},{20,8},{24,12},{28,16},{32,20},{36,24},{40,28},{44,3... | collective-permute-start | bytes 58376 | tf_op jit(solution)/shard_map/ppermute | solution.py:117
  173.2 18.8 %collective-permute-start.27 = (f32[128,512]{1,0:T(8,128)S(1)}, f32[128,512]{1,0:T(8,128)S(1)}, u32[]{:S(2)}, u32[]{:S(2)}) collective-permute-start(f32[128,512]{1,0:T(8,128)S(1)} %get-tuple-element.5), channel_id=1, source_target_pairs={{0,24},{32,56},{64,88},{96,120},{124,100},{92,68},{60,36},{28,4},{... | collective-permute-start | bytes 786440 | tf_op jit(solution)/shard_map/ppermute | solution.py:252
  195.2 4.8 %collective-permute-start.29 = (f32[1,128,128]{2,1,0:T(8,128)S(1)}, f32[1,128,128]{2,1,0:T(8,128)S(1)}, u32[]{:S(2)}, u32[]{:S(2)}) collective-permute-start(f32[1,128,128]{2,1,0:T(8,128)S(1)} %get-tuple-element.12), channel_id=1, source_target_pairs={{0,1},{1,2},{2,3},{3,0},{4,5},{5,6},{6,7},{7,4},{8,9},{9,10},{10,1... | collective-permute-start | bytes 196616 | tf_op jit(solution)/shard_map/ppermute | solution.py:265
  196.8 4.9 %collective-permute-start.31 = (f32[1,128,128]{2,1,0:T(8,128)S(1)}, f32[1,128,128]{2,1,0:T(8,128)S(1)}, u32[]{:S(2)}, u32[]{:S(2)}) collective-permute-start(f32[1,128,128]{2,1,0:T(8,128)S(1)} %get-tuple-element.13), channel_id=1, source_target_pairs={{0,3},{1,0},{2,1},{3,2},{4,7},{5,4},{6,5},{7,6},{8,11},{9,8},{10,9... | collective-permute-start | bytes 196616 | tf_op jit(solution)/shard_map/ppermute | solution.py:265
  (35 other events, 117.2 us)

commit v11 on v9

--- a/solution.py
+++ b/solution.py
@@ -189,7 +189,7 @@
     x_cells, y_cells, z_cells = cotangent.shape
     tile_size = TILE
     depth_x, depth_y = 5, 5
-    grown = extend(extend(cotangent, "slab", 0, depth_x), "pencil", 1, depth_y)
+    grown = extend(extend(cotangent, "pencil", 1, depth_y), "slab", 0, depth_x)
     powers = [grown]
     for step in range(1, 6):
         powers.append(sweep(powers[-1], x_cells, y_cells, depth_x - step, depth_y - step))

time: 198 us -> 200 us (1.010)
  other arithmetic: 37.3 us -> 42.1 us
  local copies, waits for them, and re-layouts: 23.3 us -> 19.3 us
  waiting for transfers between devices: 47.9 us -> 50 us
    select_n x14, other arithmetic: 20.1 us -> 25.7 us  [masked(): return jnp.where(keep, field, 0.0)]
    unnamed x83 -> x77, local copies, waits for them, and re-layouts: 10.3 us -> 7.25 us
  transfers between devices with their start and end apart: 32 -> 32, of which waited for: 16 -> 15; matrix products, arithmetic and copies ran while one was open for 7% -> 6% of each run, Pallas kernels for 0% -> 0%
where the time goes in v11:
time: 200 us; the launch traced here: 199 us
  starting transfers between devices  76.6 us (38%)
  waiting for transfers between devices  50 us (25%)
  other arithmetic  42.1 us (21%)
  local copies, waits for them, and re-layouts  19.3 us (10%)
  matrix products  9.04 us (5%)
  between operations  2.2 us (1%)
    ppermute x11, starting transfers between devices, extend(): lows.insert(0, lax.ppermute(low_piece, axis, up))  49.8 us
    select_n x14, other arithmetic, masked(): return jnp.where(keep, field, 0.0)  25.7 us
    ppermute x11, waiting for transfers between devices, extend(): highs.append(lax.ppermute(high_piece, axis, down))  21.1 us
    ppermute x7, waiting for transfers between devices, spread_faces(): got = lax.ppermute(sent, 'slab', low_pairs + high_pairs)  18.6 us
    ppermute x11, starting transfers between devices, extend(): highs.append(lax.ppermute(high_piece, axis, down))  17.2 us
    ppermute x11, waiting for transfers between devices, extend(): lows.insert(0, lax.ppermute(low_piece, axis, up))  8.19 us
    unnamed x77, local copies, waits for them, and re-layouts  7.25 us
    slice x12, local copies, waits for them, and re-layouts, shrink_neighbours(): centre = field[1:-1, 1:-1]  5.09 us
  transfers between devices with their start and end apart: 32, of which 15 were waited for; matrix products, arithmetic and copies ran while one was open for 6% of the time, Pallas kernels for 0%

profile of v11, /device:TPU:1, one launch (start us, length us, event | category | flops | bytes accessed | tf_op | source)
XLA Modules:
  0.0 199.1 jit_solution(3754384357333561132)
XLA Ops:
  1.5 4.4 %collective-permute-start = (f32[4,5,512]{2,1,0:T(8,128)S(1)}, f32[4,5,512]{2,1,0:T(8,128)S(1)}, u32[]{:S(2)}, u32[]{:S(2)}) collective-permute-start(f32[4,5,512]{2,1,0:T(8,128)S(1)} %get-tuple-element.10), channel_id=1, source_target_pairs={{0,1},{1,2},{2,3},{4,5},{5,6},{6,7},{8,9},{9,10},{10,11},{12,13},{... | collective-permute-start | bytes 122888 | tf_op jit(solution)/shard_map/ppermute | solution.py:116
  12.5 5.0 %collective-permute-start.2 = (f32[4,138,512]{2,1,0:T(8,128)S(1)}, f32[4,138,512]{2,1,0:T(8,128)S(1)}, u32[]{:S(2)}, u32[]{:S(2)}) collective-permute-start(f32[4,138,512]{2,1,0:T(8,128)S(1)} %pad_maximum_fusion.10), channel_id=1, source_target_pairs={{0,4},{4,8},{8,12},{12,16},{16,20},{20,24},{24,28},{28,32},{32,36}... | collective-permute-start | bytes 3391496 | tf_op jit(solution)/shard_map/ppermute | solution.py:116
  21.6 4.0 %collective-permute-start.5 = (f32[1,138,512]{2,1,0:T(8,128)S(1)}, f32[1,138,512]{2,1,0:T(8,128)S(1)}, u32[]{:S(2)}, u32[]{:S(2)}) collective-permute-start(f32[1,138,512]{2,1,0:T(8,128)S(1)} %get-tuple-element.9), channel_id=1, source_target_pairs={{0,8},{4,12},{8,16},{12,20},{16,24},{20,28},{24,32},{28,36},{32,40... | collective-permute-start | bytes 847880 | tf_op jit(solution)/shard_map/ppermute | solution.py:116
  25.7 8.2 %collective-permute-done.2 = f32[4,138,512]{2,1,0:T(8,128)S(1)} collective-permute-done((f32[4,138,512]{2,1,0:T(8,128)S(1)}, f32[4,138,512]{2,1,0:T(8,128)S(1)}, u32[]{:S(2)}, u32[]{:S(2)}) %collective-permute-start.2) | collective-permute-done | bytes 1130528 | tf_op jit(solution)/shard_map/ppermute | solution.py:116
  33.8 4.4 %collective-permute-done.3 = f32[4,138,512]{2,1,0:T(8,128)S(1)} collective-permute-done((f32[4,138,512]{2,1,0:T(8,128)S(1)}, f32[4,138,512]{2,1,0:T(8,128)S(1)}, u32[]{:S(2)}, u32[]{:S(2)}) %collective-permute-start.3) | collective-permute-done | bytes 1130528 | tf_op jit(solution)/shard_map/ppermute | solution.py:117
  39.4 8.7 %fusion.4 = f32[12,136,512]{2,1,0:T(8,128)S(1)} fusion(f32[12,136,512]{2,1,0:T(8,128)S(1)} %slice.643, f32[12,138,512]{2,1,0:T(8,128)S(1)} %pad_maximum_fusion, f32[4,138,512]{2,1,0:T(8,128)S(1)} %collective-permute-done.3, f32[4,5,512]{2,1,0:T(8,128)S(1)} %collective-permute-done.1, f32[4,138,512]{2,1,0:T(8,128)S(1)} %collective-permute-done.2, ...), kind=kLoop, calls=%fused_computation.9 | loop fusion | flops 15876096 | bytes 17327712 | tf_op jit(solution)/shard_map/jit(_where)/select_n | solution.py:130
  48.5 2.6 %fusion.11 = f32[10,134,512]{2,1,0:T(8,128)S(1)} fusion(f32[10,134,512]{2,1,0:T(8,128)S(1)} %slice.649, f32[12,136,512]{2,1,0:T(8,128)S(1)} %fusion.4, pred[10,134]{1,0:T(8,128)(4,1)S(1)} %broadcast_and_fusion), kind=kLoop, calls=%fused_computation.31 | loop fusion | flops 6174720 | bytes 16467260 | tf_op jit(solution)/shard_map/jit(_where)/select_n | solution.py:130
  56.0 3.5 %collective-permute-start.6 = (f32[2,13,256]{2,1,0:T(8,128)S(1)}, f32[2,13,256]{2,1,0:T(8,128)S(1)}, u32[]{:S(2)}, u32[]{:S(2)}) collective-permute-start(f32[2,13,256]{2,1,0:T(8,128)S(1)} %get-tuple-element.52), channel_id=1, source_target_pairs={{0,1},{1,2},{2,3},{4,5},{5,6},{6,7},{8,9},{9,10},{10,11},{12,13},{... | collective-permute-start | bytes 79880 | tf_op jit(solution)/shard_map/ppermute | solution.py:116
  61.4 2.8 %collective-permute-done.7 = f32[2,13,256]{2,1,0:T(8,128)S(1)} collective-permute-done((f32[2,13,256]{2,1,0:T(8,128)S(1)}, f32[2,13,256]{2,1,0:T(8,128)S(1)}, u32[]{:S(2)}, u32[]{:S(2)}) %collective-permute-start.7) | collective-permute-done | bytes 26656 | tf_op jit(solution)/shard_map/ppermute | solution.py:117
  64.2 8.5 %collective-permute-start.10 = (f32[2,90,256]{2,1,0:T(8,128)S(1)}, f32[2,90,256]{2,1,0:T(8,128)S(1)}, u32[]{:S(2)}, u32[]{:S(2)}) collective-permute-start(f32[2,90,256]{2,1,0:T(8,128)S(1)} %pad_maximum_fusion.20), channel_id=1, source_target_pairs={{0,12},{4,16},{8,20},{12,24},{16,28},{20,32},{24,36},{28,40},{32,4... | collective-permute-start | bytes 552968 | tf_op jit(solution)/shard_map/ppermute | solution.py:116
  72.7 3.3 %collective-permute-start.15 = (f32[1,90,256]{2,1,0:T(8,128)S(1)}, f32[1,90,256]{2,1,0:T(8,128)S(1)}, u32[]{:S(2)}, u32[]{:S(2)}) collective-permute-start(f32[1,90,256]{2,1,0:T(8,128)S(1)} %get-tuple-element.18), channel_id=1, source_target_pairs={{0,16},{4,20},{8,24},{12,28},{16,32},{20,36},{24,40},{28,44},{32,4... | collective-permute-start | bytes 276488 | tf_op jit(solution)/shard_map/ppermute | solution.py:116
  76.0 3.1 %collective-permute-start.11 = (f32[2,90,256]{2,1,0:T(8,128)S(1)}, f32[2,90,256]{2,1,0:T(8,128)S(1)}, u32[]{:S(2)}, u32[]{:S(2)}) collective-permute-start(f32[2,90,256]{2,1,0:T(8,128)S(1)} %pad_maximum_fusion.20), channel_id=1, source_target_pairs={{0,8},{4,12},{8,16},{12,20},{16,24},{20,28},{24,32},{28,36},{32,40... | collective-permute-start | bytes 552968 | tf_op jit(solution)/shard_map/ppermute | solution.py:116
  81.2 2.3 %collective-permute-start.9 = (f32[2,90,256]{2,1,0:T(8,128)S(1)}, f32[2,90,256]{2,1,0:T(8,128)S(1)}, u32[]{:S(2)}, u32[]{:S(2)}) collective-permute-start(f32[2,90,256]{2,1,0:T(8,128)S(1)} %pad_maximum_fusion.20), channel_id=1, source_target_pairs={{4,0},{8,4},{12,8},{16,12},{20,16},{24,20},{28,24},{32,28},{36,32}... | collective-permute-start | bytes 552968 | tf_op jit(solution)/shard_map/ppermute | solution.py:117
  88.5 3.8 %collective-permute-done.12 = f32[2,90,256]{2,1,0:T(8,128)S(1)} collective-permute-done((f32[2,90,256]{2,1,0:T(8,128)S(1)}, f32[2,90,256]{2,1,0:T(8,128)S(1)}, u32[]{:S(2)}, u32[]{:S(2)}) %collective-permute-start.12) | collective-permute-done | bytes 184352 | tf_op jit(solution)/shard_map/ppermute | solution.py:117
  92.4 2.8 %collective-permute-done.13 = f32[2,90,256]{2,1,0:T(8,128)S(1)} collective-permute-done((f32[2,90,256]{2,1,0:T(8,128)S(1)}, f32[2,90,256]{2,1,0:T(8,128)S(1)}, u32[]{:S(2)}, u32[]{:S(2)}) %collective-permute-start.13) | collective-permute-done | bytes 184352 | tf_op jit(solution)/shard_map/ppermute | solution.py:117
  101.0 2.1 %reduce_sum.28 = f32[5,84,256]{2,1,0:T(8,128)} reduce(f32[5,2,84,256]{3,2,1,0:T(8,128)} %bitcast.73, f32[]{:T(128)} %constant.297.clone.1), dimensions={1}, to_apply=%region_1.2 | reduce | flops 107520 | bytes 1290244 | tf_op jit(solution)/shard_map/reduce_sum | solution.py:59
  108.5 12.1 %collective-permute-start.21 = (f32[1,74,256]{2,1,0:T(8,128)S(1)}, f32[1,74,256]{2,1,0:T(8,128)}, u32[]{:S(2)}, u32[]{:S(2)}) collective-permute-start(f32[1,74,256]{2,1,0:T(8,128)S(1)} %bitcast.75), channel_id=1, source_target_pairs={{0,12},{4,16},{8,20},{12,24},{16,28},{20,32},{24,36},{28,40},{32,4... | collective-permute-start | bytes 227336 | tf_op jit(solution)/shard_map/ppermute | solution.py:116
  123.8 2.9 %slice.661 = f32[6,130,512]{2,1,0:T(8,128)} slice(f32[8,132,512]{2,1,0:T(8,128)} %copy-done.1), slice={[1:7], [1:131], [0:512]} | slice | bytes 3194880 | tf_op jit(solution)/shard_map/slice | solution.py:134
  128.6 2.4 %collective-permute-start.17 = (f32[2,74,256]{2,1,0:T(8,128)}, f32[2,74,256]{2,1,0:T(8,128)S(1)}, u32[]{:S(2)}, u32[]{:S(2)}) collective-permute-start(f32[2,74,256]{2,1,0:T(8,128)} %reshape.894), channel_id=1, source_target_pairs={{4,0},{8,4},{12,8},{16,12},{20,16},{24,20},{28,24},{32,28},{36,32}... | collective-permute-start | bytes 454664 | tf_op jit(solution)/shard_map/ppermute | solution.py:117
  135.7 3.6 %collective-permute-done.19 = f32[2,74,256]{2,1,0:T(8,128)S(1)} collective-permute-done((f32[2,74,256]{2,1,0:T(8,128)}, f32[2,74,256]{2,1,0:T(8,128)S(1)}, u32[]{:S(2)}, u32[]{:S(2)}) %collective-permute-start.19) | collective-permute-done | bytes 151584 | tf_op jit(solution)/shard_map/ppermute | solution.py:117
  142.7 2.4 %fusion.93 = f32[6,68,256]{2,1,0:T(8,128)} fusion(f32[10,72,256]{2,1,0:T(8,128)S(1)} %fusion.78, f32[2,74,256]{2,1,0:T(8,128)S(1)} %collective-permute-done.17, f32[2,74,256]{2,1,0:T(8,128)} %reshape.894, f32[2,74,256]{2,1,0:T(8,128)S(1)} %collective-permute-done.16, f32[12,86,256]{2,1,0:T(8,128)} %copy-done.4, f32[14,88,256]{2,1,0:T(8,128)} %copy-done.3, ...), kind=kLoop, calls=%fused_computation.196 | loop fusion | flops 1775616 | bytes 3514368 | tf_op jit(solution)/shard_map/add | solution.py:182
  155.7 3.1 %fusion.32 = (f32[6,130,512]{2,1,0:T(8,128)S(1)}, f32[6,130,512]{2,1,0:T(8,128)S(1)}) fusion(f32[6,130,512]{2,1,0:T(8,128)S(1)} %slice.742, f32[8,132,512]{2,1,0:T(8,128)S(1)} %fusion.20, pred[6,130]{1,0:T(8,128)(4,1)S(1)} %copy-done.25, f32[6,130,512]{2,1,0:T(8,128)S(1)} %copy-done.8, f32[8,132,512]{2,1,0:T(8,128)S(1)} %copy-done.2), kind=kLoop, calls=%fused_computation.70 | loop fusion | flops 7188480 | bytes 19170060 | tf_op jit(solution)/shard_map/jit(_where)/select_n | solution.py:130
  161.2 2.6 %fusion.61 = f32[4,128,512]{2,1,0:T(8,128)S(1)} fusion(f32[8,132,512]{2,1,0:T(8,128)S(1)} %fusion.20, f32[10,134,512]{2,1,0:T(8,128)S(1)} %slice_multiply_fusion, f32[4,128,512]{2,1,0:T(8,128)S(1)} %get-tuple-element.60, f32[10,134,512]{2,1,0:T(8,128)} %copy-done, f32[4,128,512]{2,1,0:T(8,128)S(1)} %copy-done.6, f32[12,136,512]{2,1,0:T(8,128)S(1)} %fusion.4, ...), kind=kLoop, calls=%fused_computation.138 | loop fusion | flops 3407872 | bytes 11534336 | tf_op jit(solution)/shard_map/sub | solution.py:212
  171.0 17.3 %collective-permute-done.27 = f32[128,512]{1,0:T(8,128)S(1)} collective-permute-done((f32[128,512]{1,0:T(8,128)S(1)}, f32[128,512]{1,0:T(8,128)S(1)}, u32[]{:S(2)}, u32[]{:S(2)}) %collective-permute-start.27) | collective-permute-done | bytes 262176 | tf_op jit(solution)/shard_map/ppermute | solution.py:253
  (247 shorter events, 81.1 us)
Async XLA Ops:
  1.5 8.9 %collective-permute-start = (f32[4,5,512]{2,1,0:T(8,128)S(1)}, f32[4,5,512]{2,1,0:T(8,128)S(1)}, u32[]{:S(2)}, u32[]{:S(2)}) collective-permute-start(f32[4,5,512]{2,1,0:T(8,128)S(1)} %get-tuple-element.10), channel_id=1, source_target_pairs={{0,1},{1,2},{2,3},{4,5},{5,6},{6,7},{8,9},{9,10},{10,11},{12,13},{... | collective-permute-start | bytes 122888 | tf_op jit(solution)/shard_map/ppermute | solution.py:116
  5.9 5.2 %collective-permute-start.1 = (f32[4,5,512]{2,1,0:T(8,128)S(1)}, f32[4,5,512]{2,1,0:T(8,128)S(1)}, u32[]{:S(2)}, u32[]{:S(2)}) collective-permute-start(f32[4,5,512]{2,1,0:T(8,128)S(1)} %get-tuple-element.11), channel_id=1, source_target_pairs={{1,0},{2,1},{3,2},{5,4},{6,5},{7,6},{9,8},{10,9},{11,10},{13,12},{... | collective-permute-start | bytes 122888 | tf_op jit(solution)/shard_map/ppermute | solution.py:117
  12.5 21.3 %collective-permute-start.2 = (f32[4,138,512]{2,1,0:T(8,128)S(1)}, f32[4,138,512]{2,1,0:T(8,128)S(1)}, u32[]{:S(2)}, u32[]{:S(2)}) collective-permute-start(f32[4,138,512]{2,1,0:T(8,128)S(1)} %pad_maximum_fusion.10), channel_id=1, source_target_pairs={{0,4},{4,8},{8,12},{12,16},{16,20},{20,24},{24,28},{28,32},{32,36}... | collective-permute-start | bytes 3391496 | tf_op jit(solution)/shard_map/ppermute | solution.py:116
  17.5 20.7 %collective-permute-start.3 = (f32[4,138,512]{2,1,0:T(8,128)S(1)}, f32[4,138,512]{2,1,0:T(8,128)S(1)}, u32[]{:S(2)}, u32[]{:S(2)}) collective-permute-start(f32[4,138,512]{2,1,0:T(8,128)S(1)} %pad_maximum_fusion.10), channel_id=1, source_target_pairs={{4,0},{8,4},{12,8},{16,12},{20,16},{24,20},{28,24},{32,28},{36,32}... | collective-permute-start | bytes 3391496 | tf_op jit(solution)/shard_map/ppermute | solution.py:117
  20.3 19.0 %collective-permute-start.4 = (f32[1,138,512]{2,1,0:T(8,128)S(1)}, f32[1,138,512]{2,1,0:T(8,128)S(1)}, u32[]{:S(2)}, u32[]{:S(2)}) collective-permute-start(f32[1,138,512]{2,1,0:T(8,128)S(1)} %get-tuple-element.8), channel_id=1, source_target_pairs={{8,0},{12,4},{16,8},{20,12},{24,16},{28,20},{32,24},{36,28},{40,32... | collective-permute-start | bytes 847880 | tf_op jit(solution)/shard_map/ppermute | solution.py:117
  21.6 17.8 %collective-permute-start.5 = (f32[1,138,512]{2,1,0:T(8,128)S(1)}, f32[1,138,512]{2,1,0:T(8,128)S(1)}, u32[]{:S(2)}, u32[]{:S(2)}) collective-permute-start(f32[1,138,512]{2,1,0:T(8,128)S(1)} %get-tuple-element.9), channel_id=1, source_target_pairs={{0,8},{4,12},{8,16},{12,20},{16,24},{20,28},{24,32},{28,36},{32,40... | collective-permute-start | bytes 847880 | tf_op jit(solution)/shard_map/ppermute | solution.py:116
  56.0 5.4 %collective-permute-start.6 = (f32[2,13,256]{2,1,0:T(8,128)S(1)}, f32[2,13,256]{2,1,0:T(8,128)S(1)}, u32[]{:S(2)}, u32[]{:S(2)}) collective-permute-start(f32[2,13,256]{2,1,0:T(8,128)S(1)} %get-tuple-element.52), channel_id=1, source_target_pairs={{0,1},{1,2},{2,3},{4,5},{5,6},{6,7},{8,9},{9,10},{10,11},{12,13},{... | collective-permute-start | bytes 79880 | tf_op jit(solution)/shard_map/ppermute | solution.py:116
  59.5 4.7 %collective-permute-start.7 = (f32[2,13,256]{2,1,0:T(8,128)S(1)}, f32[2,13,256]{2,1,0:T(8,128)S(1)}, u32[]{:S(2)}, u32[]{:S(2)}) collective-permute-start(f32[2,13,256]{2,1,0:T(8,128)S(1)} %get-tuple-element.53), channel_id=1, source_target_pairs={{1,0},{2,1},{3,2},{5,4},{6,5},{7,6},{9,8},{10,9},{11,10},{13,12},{... | collective-permute-start | bytes 79880 | tf_op jit(solution)/shard_map/ppermute | solution.py:117
  64.2 20.6 %collective-permute-start.10 = (f32[2,90,256]{2,1,0:T(8,128)S(1)}, f32[2,90,256]{2,1,0:T(8,128)S(1)}, u32[]{:S(2)}, u32[]{:S(2)}) collective-permute-start(f32[2,90,256]{2,1,0:T(8,128)S(1)} %pad_maximum_fusion.20), channel_id=1, source_target_pairs={{0,12},{4,16},{8,20},{12,24},{16,28},{20,32},{24,36},{28,40},{32,4... | collective-permute-start | bytes 552968 | tf_op jit(solution)/shard_map/ppermute | solution.py:116
  72.7 10.8 %collective-permute-start.15 = (f32[1,90,256]{2,1,0:T(8,128)S(1)}, f32[1,90,256]{2,1,0:T(8,128)S(1)}, u32[]{:S(2)}, u32[]{:S(2)}) collective-permute-start(f32[1,90,256]{2,1,0:T(8,128)S(1)} %get-tuple-element.18), channel_id=1, source_target_pairs={{0,16},{4,20},{8,24},{12,28},{16,32},{20,36},{24,40},{28,44},{32,4... | collective-permute-start | bytes 276488 | tf_op jit(solution)/shard_map/ppermute | solution.py:116
  76.0 10.2 %collective-permute-start.11 = (f32[2,90,256]{2,1,0:T(8,128)S(1)}, f32[2,90,256]{2,1,0:T(8,128)S(1)}, u32[]{:S(2)}, u32[]{:S(2)}) collective-permute-start(f32[2,90,256]{2,1,0:T(8,128)S(1)} %pad_maximum_fusion.20), channel_id=1, source_target_pairs={{0,8},{4,12},{8,16},{12,20},{16,24},{20,28},{24,32},{28,36},{32,40... | collective-permute-start | bytes 552968 | tf_op jit(solution)/shard_map/ppermute | solution.py:116
  79.1 8.6 %collective-permute-start.8 = (f32[2,90,256]{2,1,0:T(8,128)S(1)}, f32[2,90,256]{2,1,0:T(8,128)S(1)}, u32[]{:S(2)}, u32[]{:S(2)}) collective-permute-start(f32[2,90,256]{2,1,0:T(8,128)S(1)} %pad_maximum_fusion.20), channel_id=1, source_target_pairs={{0,4},{4,8},{8,12},{12,16},{16,20},{20,24},{24,28},{28,32},{32,36}... | collective-permute-start | bytes 552968 | tf_op jit(solution)/shard_map/ppermute | solution.py:116
  81.2 7.3 %collective-permute-start.9 = (f32[2,90,256]{2,1,0:T(8,128)S(1)}, f32[2,90,256]{2,1,0:T(8,128)S(1)}, u32[]{:S(2)}, u32[]{:S(2)}) collective-permute-start(f32[2,90,256]{2,1,0:T(8,128)S(1)} %pad_maximum_fusion.20), channel_id=1, source_target_pairs={{4,0},{8,4},{12,8},{16,12},{20,16},{24,20},{28,24},{32,28},{36,32}... | collective-permute-start | bytes 552968 | tf_op jit(solution)/shard_map/ppermute | solution.py:117
  83.5 8.8 %collective-permute-start.12 = (f32[2,90,256]{2,1,0:T(8,128)S(1)}, f32[2,90,256]{2,1,0:T(8,128)S(1)}, u32[]{:S(2)}, u32[]{:S(2)}) collective-permute-start(f32[2,90,256]{2,1,0:T(8,128)S(1)} %pad_maximum_fusion.20), channel_id=1, source_target_pairs={{8,0},{12,4},{16,8},{20,12},{24,16},{28,20},{32,24},{36,28},{40,32... | collective-permute-start | bytes 552968 | tf_op jit(solution)/shard_map/ppermute | solution.py:117
  84.8 10.4 %collective-permute-start.13 = (f32[2,90,256]{2,1,0:T(8,128)S(1)}, f32[2,90,256]{2,1,0:T(8,128)S(1)}, u32[]{:S(2)}, u32[]{:S(2)}) collective-permute-start(f32[2,90,256]{2,1,0:T(8,128)S(1)} %pad_maximum_fusion.20), channel_id=1, source_target_pairs={{12,0},{16,4},{20,8},{24,12},{28,16},{32,20},{36,24},{40,28},{44,3... | collective-permute-start | bytes 552968 | tf_op jit(solution)/shard_map/ppermute | solution.py:117
  86.2 10.8 %collective-permute-start.14 = (f32[1,90,256]{2,1,0:T(8,128)S(1)}, f32[1,90,256]{2,1,0:T(8,128)S(1)}, u32[]{:S(2)}, u32[]{:S(2)}) collective-permute-start(f32[1,90,256]{2,1,0:T(8,128)S(1)} %get-tuple-element.17), channel_id=1, source_target_pairs={{16,0},{20,4},{24,8},{28,12},{32,16},{36,20},{40,24},{44,28},{48,3... | collective-permute-start | bytes 276488 | tf_op jit(solution)/shard_map/ppermute | solution.py:117
  108.5 23.8 %collective-permute-start.21 = (f32[1,74,256]{2,1,0:T(8,128)S(1)}, f32[1,74,256]{2,1,0:T(8,128)}, u32[]{:S(2)}, u32[]{:S(2)}) collective-permute-start(f32[1,74,256]{2,1,0:T(8,128)S(1)} %bitcast.75), channel_id=1, source_target_pairs={{0,12},{4,16},{8,20},{12,24},{16,28},{20,32},{24,36},{28,40},{32,4... | collective-permute-start | bytes 227336 | tf_op jit(solution)/shard_map/ppermute | solution.py:116
  121.3 13.2 %collective-permute-start.18 = (f32[2,74,256]{2,1,0:T(8,128)}, f32[2,74,256]{2,1,0:T(8,128)}, u32[]{:S(2)}, u32[]{:S(2)}) collective-permute-start(f32[2,74,256]{2,1,0:T(8,128)} %reshape.894), channel_id=1, source_target_pairs={{0,8},{4,12},{8,16},{12,20},{16,24},{20,28},{24,32},{28,36},{32,40... | collective-permute-start | bytes 454664 | tf_op jit(solution)/shard_map/ppermute | solution.py:116
  126.7 8.8 %collective-permute-start.16 = (f32[2,74,256]{2,1,0:T(8,128)}, f32[2,74,256]{2,1,0:T(8,128)S(1)}, u32[]{:S(2)}, u32[]{:S(2)}) collective-permute-start(f32[2,74,256]{2,1,0:T(8,128)} %reshape.894), channel_id=1, source_target_pairs={{0,4},{4,8},{8,12},{12,16},{16,20},{20,24},{24,28},{28,32},{32,36}... | collective-permute-start | bytes 454664 | tf_op jit(solution)/shard_map/ppermute | solution.py:116
  128.6 7.0 %collective-permute-start.17 = (f32[2,74,256]{2,1,0:T(8,128)}, f32[2,74,256]{2,1,0:T(8,128)S(1)}, u32[]{:S(2)}, u32[]{:S(2)}) collective-permute-start(f32[2,74,256]{2,1,0:T(8,128)} %reshape.894), channel_id=1, source_target_pairs={{4,0},{8,4},{12,8},{16,12},{20,16},{24,20},{28,24},{32,28},{36,32}... | collective-permute-start | bytes 454664 | tf_op jit(solution)/shard_map/ppermute | solution.py:117
  131.0 8.2 %collective-permute-start.19 = (f32[2,74,256]{2,1,0:T(8,128)}, f32[2,74,256]{2,1,0:T(8,128)S(1)}, u32[]{:S(2)}, u32[]{:S(2)}) collective-permute-start(f32[2,74,256]{2,1,0:T(8,128)} %reshape.894), channel_id=1, source_target_pairs={{8,0},{12,4},{16,8},{20,12},{24,16},{28,20},{32,24},{36,28},{40,32... | collective-permute-start | bytes 454664 | tf_op jit(solution)/shard_map/ppermute | solution.py:117
  132.3 8.0 %collective-permute-start.20 = (f32[1,74,256]{2,1,0:T(8,128)S(1)}, f32[1,74,256]{2,1,0:T(8,128)S(1)}, u32[]{:S(2)}, u32[]{:S(2)}) collective-permute-start(f32[1,74,256]{2,1,0:T(8,128)S(1)} %bitcast.76), channel_id=1, source_target_pairs={{12,0},{16,4},{20,8},{24,12},{28,16},{32,20},{36,24},{40,28},{44,3... | collective-permute-start | bytes 227336 | tf_op jit(solution)/shard_map/ppermute | solution.py:117
  169.6 18.8 %collective-permute-start.27 = (f32[128,512]{1,0:T(8,128)S(1)}, f32[128,512]{1,0:T(8,128)S(1)}, u32[]{:S(2)}, u32[]{:S(2)}) collective-permute-start(f32[128,512]{1,0:T(8,128)S(1)} %get-tuple-element.5), channel_id=1, source_target_pairs={{0,24},{32,56},{64,88},{96,120},{124,100},{92,68},{60,36},{28,4},{... | collective-permute-start | bytes 786440 | tf_op jit(solution)/shard_map/ppermute | solution.py:253
  191.8 4.8 %collective-permute-start.29 = (f32[1,128,128]{2,1,0:T(8,128)S(1)}, f32[1,128,128]{2,1,0:T(8,128)S(1)}, u32[]{:S(2)}, u32[]{:S(2)}) collective-permute-start(f32[1,128,128]{2,1,0:T(8,128)S(1)} %get-tuple-element.12), channel_id=1, source_target_pairs={{0,1},{1,2},{2,3},{3,0},{4,5},{5,6},{6,7},{7,4},{8,9},{9,10},{10,1... | collective-permute-start | bytes 196616 | tf_op jit(solution)/shard_map/ppermute | solution.py:266
  (40 other events, 270.2 us)

commit v12 on v9

--- a/solution.py
+++ b/solution.py
@@ -57,9 +57,7 @@
 def children_sum(field):
     x_cells, y_cells, z_cells = field.shape
     paired = field.reshape(x_cells // 2, 2, y_cells, z_cells).sum(axis=1)
-    flat = paired.reshape(x_cells // 2 * y_cells, z_cells)
-    paired = jnp.dot(flat, pair_matrix(z_cells), precision=lax.Precision.HIGHEST)
-    paired = paired.reshape(x_cells // 2, y_cells, z_cells // 2)
+    paired = jnp.dot(paired, pair_matrix(z_cells), precision=lax.Precision.HIGHEST)
     to_rows = pair_matrix(y_cells).T
     planes = [
         jnp.dot(to_rows, paired[i], precision=lax.Precision.HIGHEST)
@@ -70,9 +68,7 @@
 
 def prolong(field):
     x_cells, y_cells, z_cells = field.shape
-    flat = field.reshape(x_cells * y_cells, z_cells)
-    wide = jnp.dot(flat, pair_matrix(2 * z_cells).T, precision=lax.Precision.HIGHEST)
-    wide = wide.reshape(x_cells, y_cells, 2 * z_cells)
+    wide = jnp.dot(field, pair_matrix(2 * z_cells).T, precision=lax.Precision.HIGHEST)
     to_rows = pair_matrix(2 * y_cells)
     planes = [
         jnp.dot(to_rows, wide[i], precision=lax.Precision.HIGHEST)

time: 198 us -> 192 us (0.970)
  local copies, waits for them, and re-layouts: 23.3 us -> 18.5 us
  other arithmetic: 37.3 us -> 35.1 us
    reshape x2 -> x0, local copies, waits for them, and re-layouts: 3.64 us -> none  [the longest x1 1.83 us: prolong(): flat = field.reshape(x_cells * y_cells, z_cells)]
    add x1 -> x0, other arithmetic: 2.41 us -> none  [medium_cycle(): grad_medium + coefficient(1) * crop(stage, width, width, 2, 2, block_x, b...]
    unnamed x83 -> x79, local copies, waits for them, and re-layouts: 10.3 us -> 10.4 us
where the time goes in v12:
time: 192 us; the launch traced here: 190 us
  starting transfers between devices  76.6 us (40%)
  waiting for transfers between devices  47.7 us (25%)
  other arithmetic  35.1 us (18%)
  local copies, waits for them, and re-layouts  18.5 us (10%)
  matrix products  10.3 us (5%)
  between operations  2.23 us (1%)
    ppermute x11, starting transfers between devices, extend(): lows.insert(0, lax.ppermute(low_piece, axis, up))  50.6 us
    ppermute x11, waiting for transfers between devices, extend(): highs.append(lax.ppermute(high_piece, axis, down))  20.4 us
    select_n x14, other arithmetic, masked(): return jnp.where(keep, field, 0.0)  20.1 us
    ppermute x7, waiting for transfers between devices, spread_faces(): got = lax.ppermute(sent, 'slab', low_pairs + high_pairs)  18.6 us
    ppermute x11, starting transfers between devices, extend(): highs.append(lax.ppermute(high_piece, axis, down))  17.2 us
    unnamed x79, local copies, waits for them, and re-layouts  10.4 us
    ppermute x11, waiting for transfers between devices, extend(): lows.insert(0, lax.ppermute(low_piece, axis, up))  6.09 us
    ppermute x7, starting transfers between devices, spread_faces(): got = lax.ppermute(sent, 'slab', low_pairs + high_pairs)  4.98 us
  transfers between devices with their start and end apart: 32, of which 16 were waited for; matrix products, arithmetic and copies ran while one was open for 7% of the time, Pallas kernels for 0%

profile of v12, /device:TPU:1, one launch (start us, length us, event | category | flops | bytes accessed | tf_op | source)
XLA Modules:
  0.0 190.4 jit_solution(8817408777560774989)
XLA Ops:
  0.6 4.7 %collective-permute-start.1 = (f32[4,128,512]{2,1,0:T(8,128)}, f32[4,128,512]{2,1,0:T(8,128)S(1)}, u32[]{:S(2)}, u32[]{:S(2)}) collective-permute-start(f32[4,128,512]{2,1,0:T(8,128)} %param.4), channel_id=1, source_target_pairs={{0,4},{4,8},{8,12},{12,16},{16,20},{20,24},{24,28},{28,32},{32,36}... | collective-permute-start | bytes 3145736 | tf_op jit(solution)/shard_map/ppermute | solution.py:112
  9.2 3.9 %collective-permute-start = (f32[1,128,512]{2,1,0:T(8,128)}, f32[1,128,512]{2,1,0:T(8,128)}, u32[]{:S(2)}, u32[]{:S(2)}) collective-permute-start(f32[1,128,512]{2,1,0:T(8,128)} %get-tuple-element.11), channel_id=1, source_target_pairs={{0,8},{4,12},{8,16},{12,20},{16,24},{20,28},{24,32},{28,36},{32,40... | collective-permute-start | bytes 786440 | tf_op jit(solution)/shard_map/ppermute | solution.py:112
  18.6 4.5 %collective-permute-done = f32[1,128,512]{2,1,0:T(8,128)} collective-permute-done((f32[1,128,512]{2,1,0:T(8,128)}, f32[1,128,512]{2,1,0:T(8,128)}, u32[]{:S(2)}, u32[]{:S(2)}) %collective-permute-start) | collective-permute-done | bytes 262176 | tf_op jit(solution)/shard_map/ppermute | solution.py:112
  26.5 3.6 %collective-permute-start.4 = (f32[14,5,512]{2,1,0:T(8,128)S(1)}, f32[14,5,512]{2,1,0:T(8,128)S(1)}, u32[]{:S(2)}, u32[]{:S(2)}) collective-permute-start(f32[14,5,512]{2,1,0:T(8,128)S(1)} %get-tuple-element.8), channel_id=1, source_target_pairs={{0,1},{1,2},{2,3},{4,5},{5,6},{6,7},{8,9},{9,10},{10,11},{12,13},{... | collective-permute-start | bytes 430088 | tf_op jit(solution)/shard_map/ppermute | solution.py:112
  33.0 4.0 %collective-permute-done.5 = f32[14,5,512]{2,1,0:T(8,128)S(1)} collective-permute-done((f32[14,5,512]{2,1,0:T(8,128)S(1)}, f32[14,5,512]{2,1,0:T(8,128)S(1)}, u32[]{:S(2)}, u32[]{:S(2)}) %collective-permute-start.5) | collective-permute-done | bytes 143392 | tf_op jit(solution)/shard_map/ppermute | solution.py:113
  37.0 2.8 %pad_maximum_fusion = f32[14,138,512]{2,1,0:T(8,128)S(1)} fusion(f32[14,5,512]{2,1,0:T(8,128)S(1)} %collective-permute-done.5, f32[14,128,512]{2,1,0:T(8,128)} %copy-done.8, f32[14,5,512]{2,1,0:T(8,128)S(1)} %collective-permute-done.4), kind=kLoop, calls=%fused_computation.2 | loop fusion | flops 1978368 | bytes 7913472 | tf_op jit(solution)/shard_map/concatenate | solution.py:115
  40.4 3.1 %fusion.4 = f32[12,136,512]{2,1,0:T(8,128)S(1)} fusion(f32[12,136,512]{2,1,0:T(8,128)S(1)} %slice.627, f32[14,138,512]{2,1,0:T(8,128)S(1)} %pad_maximum_fusion, pred[12,136]{1,0:T(8,128)(4,1)S(1)} %broadcast_and_fusion.1), kind=kLoop, calls=%fused_computation.9 | loop fusion | flops 7520256 | bytes 20055648 | tf_op jit(solution)/shard_map/jit(_where)/select_n | solution.py:126
  43.9 2.6 %fusion.9 = f32[10,134,512]{2,1,0:T(8,128)S(1)} fusion(f32[10,134,512]{2,1,0:T(8,128)S(1)} %slice.633, f32[12,136,512]{2,1,0:T(8,128)S(1)} %fusion.4, pred[10,134]{1,0:T(8,128)(4,1)S(1)} %broadcast_and_fusion), kind=kLoop, calls=%fused_computation.21 | loop fusion | flops 6174720 | bytes 16467260 | tf_op jit(solution)/shard_map/jit(_where)/select_n | solution.py:126
  51.4 3.7 %collective-permute-start.6 = (f32[2,13,256]{2,1,0:T(8,128)S(1)}, f32[2,13,256]{2,1,0:T(8,128)S(1)}, u32[]{:S(2)}, u32[]{:S(2)}) collective-permute-start(f32[2,13,256]{2,1,0:T(8,128)S(1)} %get-tuple-element.52), channel_id=1, source_target_pairs={{0,1},{1,2},{2,3},{4,5},{5,6},{6,7},{8,9},{9,10},{10,11},{12,13},{... | collective-permute-start | bytes 79880 | tf_op jit(solution)/shard_map/ppermute | solution.py:112
  57.0 2.7 %collective-permute-done.7 = f32[2,13,256]{2,1,0:T(8,128)S(1)} collective-permute-done((f32[2,13,256]{2,1,0:T(8,128)S(1)}, f32[2,13,256]{2,1,0:T(8,128)S(1)}, u32[]{:S(2)}, u32[]{:S(2)}) %collective-permute-start.7) | collective-permute-done | bytes 26656 | tf_op jit(solution)/shard_map/ppermute | solution.py:113
  59.7 10.4 %collective-permute-start.10 = (f32[2,90,256]{2,1,0:T(8,128)S(1)}, f32[2,90,256]{2,1,0:T(8,128)S(1)}, u32[]{:S(2)}, u32[]{:S(2)}) collective-permute-start(f32[2,90,256]{2,1,0:T(8,128)S(1)} %pad_maximum_fusion.16), channel_id=1, source_target_pairs={{0,12},{4,16},{8,20},{12,24},{16,28},{20,32},{24,36},{28,40},{32,4... | collective-permute-start | bytes 552968 | tf_op jit(solution)/shard_map/ppermute | solution.py:112
  70.1 3.9 %collective-permute-start.15 = (f32[1,90,256]{2,1,0:T(8,128)S(1)}, f32[1,90,256]{2,1,0:T(8,128)S(1)}, u32[]{:S(2)}, u32[]{:S(2)}) collective-permute-start(f32[1,90,256]{2,1,0:T(8,128)S(1)} %get-tuple-element.18), channel_id=1, source_target_pairs={{0,16},{4,20},{8,24},{12,28},{16,32},{20,36},{24,40},{28,44},{32,4... | collective-permute-start | bytes 276488 | tf_op jit(solution)/shard_map/ppermute | solution.py:112
  74.1 2.5 %collective-permute-start.11 = (f32[2,90,256]{2,1,0:T(8,128)S(1)}, f32[2,90,256]{2,1,0:T(8,128)S(1)}, u32[]{:S(2)}, u32[]{:S(2)}) collective-permute-start(f32[2,90,256]{2,1,0:T(8,128)S(1)} %pad_maximum_fusion.16), channel_id=1, source_target_pairs={{0,8},{4,12},{8,16},{12,20},{16,24},{20,28},{24,32},{28,36},{32,40... | collective-permute-start | bytes 552968 | tf_op jit(solution)/shard_map/ppermute | solution.py:112
  78.6 2.3 %collective-permute-start.9 = (f32[2,90,256]{2,1,0:T(8,128)S(1)}, f32[2,90,256]{2,1,0:T(8,128)S(1)}, u32[]{:S(2)}, u32[]{:S(2)}) collective-permute-start(f32[2,90,256]{2,1,0:T(8,128)S(1)} %pad_maximum_fusion.16), channel_id=1, source_target_pairs={{4,0},{8,4},{12,8},{16,12},{20,16},{24,20},{28,24},{32,28},{36,32}... | collective-permute-start | bytes 552968 | tf_op jit(solution)/shard_map/ppermute | solution.py:113
  86.0 3.8 %collective-permute-done.12 = f32[2,90,256]{2,1,0:T(8,128)S(1)} collective-permute-done((f32[2,90,256]{2,1,0:T(8,128)S(1)}, f32[2,90,256]{2,1,0:T(8,128)S(1)}, u32[]{:S(2)}, u32[]{:S(2)}) %collective-permute-start.12) | collective-permute-done | bytes 184352 | tf_op jit(solution)/shard_map/ppermute | solution.py:113
  89.8 2.8 %collective-permute-done.13 = f32[2,90,256]{2,1,0:T(8,128)S(1)} collective-permute-done((f32[2,90,256]{2,1,0:T(8,128)S(1)}, f32[2,90,256]{2,1,0:T(8,128)S(1)}, u32[]{:S(2)}, u32[]{:S(2)}) %collective-permute-start.13) | collective-permute-done | bytes 184352 | tf_op jit(solution)/shard_map/ppermute | solution.py:113
  104.7 12.1 %collective-permute-start.21 = (f32[1,74,256]{2,1,0:T(8,128)S(1)}, f32[1,74,256]{2,1,0:T(8,128)}, u32[]{:S(2)}, u32[]{:S(2)}) collective-permute-start(f32[1,74,256]{2,1,0:T(8,128)S(1)} %bitcast.118), channel_id=1, source_target_pairs={{0,12},{4,16},{8,20},{12,24},{16,28},{20,32},{24,36},{28,40},{32,4... | collective-permute-start | bytes 227336 | tf_op jit(solution)/shard_map/ppermute | solution.py:112
  123.6 2.4 %collective-permute-start.17 = (f32[2,74,256]{2,1,0:T(8,128)}, f32[2,74,256]{2,1,0:T(8,128)S(1)}, u32[]{:S(2)}, u32[]{:S(2)}) collective-permute-start(f32[2,74,256]{2,1,0:T(8,128)} %reshape.856), channel_id=1, source_target_pairs={{4,0},{8,4},{12,8},{16,12},{20,16},{24,20},{28,24},{32,28},{36,32}... | collective-permute-start | bytes 454664 | tf_op jit(solution)/shard_map/ppermute | solution.py:113
  130.6 3.6 %collective-permute-done.19 = f32[2,74,256]{2,1,0:T(8,128)S(1)} collective-permute-done((f32[2,74,256]{2,1,0:T(8,128)}, f32[2,74,256]{2,1,0:T(8,128)S(1)}, u32[]{:S(2)}, u32[]{:S(2)}) %collective-permute-start.19) | collective-permute-done | bytes 151584 | tf_op jit(solution)/shard_map/ppermute | solution.py:113
  137.7 2.2 %fusion.83 = f32[6,68,512]{2,1,0:T(8,128)S(1)} fusion(f32[10,72,256]{2,1,0:T(8,128)S(1)} %fusion.76, f32[2,74,256]{2,1,0:T(8,128)S(1)} %collective-permute-done.17, f32[2,74,256]{2,1,0:T(8,128)} %reshape.856, f32[2,74,256]{2,1,0:T(8,128)S(1)} %collective-permute-done.16, f32[12,86,256]{2,1,0:T(8,128)} %copy-done.4, f32[14,88,256]{2,1,0:T(8,128)} %copy-done.3, ...), kind=kOutput, calls=%fused_computation.173 | convolution fusion | flops 643635200 | bytes 4130816 | tf_op jit(solution)/shard_map/dot_general | solution.py:71
  147.1 3.1 %fusion.30 = (f32[6,130,512]{2,1,0:T(8,128)S(1)}, f32[6,130,512]{2,1,0:T(8,128)S(1)}) fusion(f32[6,130,512]{2,1,0:T(8,128)S(1)} %slice.726, f32[8,132,512]{2,1,0:T(8,128)S(1)} %fusion.18, pred[6,130]{1,0:T(8,128)(4,1)S(1)} %copy-done.25, f32[6,130,512]{2,1,0:T(8,128)S(1)} %slice.645, f32[8,132,512]{2,1,0:T(8,128)S(1)} %copy-done.2), kind=kLoop, calls=%fused_computation.60 | loop fusion | flops 7188480 | bytes 19170060 | tf_op jit(solution)/shard_map/jit(_where)/select_n | solution.py:126
  152.7 2.6 %fusion.59 = f32[4,128,512]{2,1,0:T(8,128)S(1)} fusion(f32[8,132,512]{2,1,0:T(8,128)S(1)} %fusion.18, f32[10,134,512]{2,1,0:T(8,128)S(1)} %slice_multiply_fusion, f32[4,128,512]{2,1,0:T(8,128)S(1)} %get-tuple-element.60, f32[10,134,512]{2,1,0:T(8,128)} %copy-done, f32[4,128,512]{2,1,0:T(8,128)S(1)} %copy-done.7, f32[12,136,512]{2,1,0:T(8,128)S(1)} %fusion.4, ...), kind=kLoop, calls=%fused_computation.127 | loop fusion | flops 3407872 | bytes 11534336 | tf_op jit(solution)/shard_map/sub | solution.py:208
  162.4 17.3 %collective-permute-done.27 = f32[128,512]{1,0:T(8,128)S(1)} collective-permute-done((f32[128,512]{1,0:T(8,128)S(1)}, f32[128,512]{1,0:T(8,128)S(1)}, u32[]{:S(2)}, u32[]{:S(2)}) %collective-permute-start.27) | collective-permute-done | bytes 262176 | tf_op jit(solution)/shard_map/ppermute | solution.py:249
  184.8 2.3 %collective-permute-start.31 = (f32[1,128,128]{2,1,0:T(8,128)S(1)}, f32[1,128,128]{2,1,0:T(8,128)S(1)}, u32[]{:S(2)}, u32[]{:S(2)}) collective-permute-start(f32[1,128,128]{2,1,0:T(8,128)S(1)} %get-tuple-element.13), channel_id=1, source_target_pairs={{0,3},{1,0},{2,1},{3,2},{4,7},{5,4},{6,5},{7,6},{8,11},{9,8},{10,9... | collective-permute-start | bytes 196616 | tf_op jit(solution)/shard_map/ppermute | solution.py:262
  (246 shorter events, 81.2 us)
Async XLA Ops:
  0.6 23.4 %collective-permute-start.1 = (f32[4,128,512]{2,1,0:T(8,128)}, f32[4,128,512]{2,1,0:T(8,128)S(1)}, u32[]{:S(2)}, u32[]{:S(2)}) collective-permute-start(f32[4,128,512]{2,1,0:T(8,128)} %param.4), channel_id=1, source_target_pairs={{0,4},{4,8},{8,12},{12,16},{16,20},{20,24},{24,28},{28,32},{32,36}... | collective-permute-start | bytes 3145736 | tf_op jit(solution)/shard_map/ppermute | solution.py:112
  5.4 19.1 %collective-permute-start.2 = (f32[4,128,512]{2,1,0:T(8,128)}, f32[4,128,512]{2,1,0:T(8,128)S(1)}, u32[]{:S(2)}, u32[]{:S(2)}) collective-permute-start(f32[4,128,512]{2,1,0:T(8,128)} %param.4), channel_id=1, source_target_pairs={{4,0},{8,4},{12,8},{16,12},{20,16},{24,20},{28,24},{32,28},{36,32}... | collective-permute-start | bytes 3145736 | tf_op jit(solution)/shard_map/ppermute | solution.py:113
  9.2 13.9 %collective-permute-start = (f32[1,128,512]{2,1,0:T(8,128)}, f32[1,128,512]{2,1,0:T(8,128)}, u32[]{:S(2)}, u32[]{:S(2)}) collective-permute-start(f32[1,128,512]{2,1,0:T(8,128)} %get-tuple-element.11), channel_id=1, source_target_pairs={{0,8},{4,12},{8,16},{12,20},{16,24},{20,28},{24,32},{28,36},{32,40... | collective-permute-start | bytes 786440 | tf_op jit(solution)/shard_map/ppermute | solution.py:112
  13.1 11.5 %collective-permute-start.3 = (f32[1,128,512]{2,1,0:T(8,128)}, f32[1,128,512]{2,1,0:T(8,128)S(1)}, u32[]{:S(2)}, u32[]{:S(2)}) collective-permute-start(f32[1,128,512]{2,1,0:T(8,128)} %get-tuple-element.10), channel_id=1, source_target_pairs={{8,0},{12,4},{16,8},{20,12},{24,16},{28,20},{32,24},{36,28},{40,32... | collective-permute-start | bytes 786440 | tf_op jit(solution)/shard_map/ppermute | solution.py:113
  26.5 6.5 %collective-permute-start.4 = (f32[14,5,512]{2,1,0:T(8,128)S(1)}, f32[14,5,512]{2,1,0:T(8,128)S(1)}, u32[]{:S(2)}, u32[]{:S(2)}) collective-permute-start(f32[14,5,512]{2,1,0:T(8,128)S(1)} %get-tuple-element.8), channel_id=1, source_target_pairs={{0,1},{1,2},{2,3},{4,5},{5,6},{6,7},{8,9},{9,10},{10,11},{12,13},{... | collective-permute-start | bytes 430088 | tf_op jit(solution)/shard_map/ppermute | solution.py:112
  30.0 6.9 %collective-permute-start.5 = (f32[14,5,512]{2,1,0:T(8,128)S(1)}, f32[14,5,512]{2,1,0:T(8,128)S(1)}, u32[]{:S(2)}, u32[]{:S(2)}) collective-permute-start(f32[14,5,512]{2,1,0:T(8,128)S(1)} %get-tuple-element.9), channel_id=1, source_target_pairs={{1,0},{2,1},{3,2},{5,4},{6,5},{7,6},{9,8},{10,9},{11,10},{13,12},{... | collective-permute-start | bytes 430088 | tf_op jit(solution)/shard_map/ppermute | solution.py:113
  51.4 5.6 %collective-permute-start.6 = (f32[2,13,256]{2,1,0:T(8,128)S(1)}, f32[2,13,256]{2,1,0:T(8,128)S(1)}, u32[]{:S(2)}, u32[]{:S(2)}) collective-permute-start(f32[2,13,256]{2,1,0:T(8,128)S(1)} %get-tuple-element.52), channel_id=1, source_target_pairs={{0,1},{1,2},{2,3},{4,5},{5,6},{6,7},{8,9},{9,10},{10,11},{12,13},{... | collective-permute-start | bytes 79880 | tf_op jit(solution)/shard_map/ppermute | solution.py:112
  59.7 22.5 %collective-permute-start.10 = (f32[2,90,256]{2,1,0:T(8,128)S(1)}, f32[2,90,256]{2,1,0:T(8,128)S(1)}, u32[]{:S(2)}, u32[]{:S(2)}) collective-permute-start(f32[2,90,256]{2,1,0:T(8,128)S(1)} %pad_maximum_fusion.16), channel_id=1, source_target_pairs={{0,12},{4,16},{8,20},{12,24},{16,28},{20,32},{24,36},{28,40},{32,4... | collective-permute-start | bytes 552968 | tf_op jit(solution)/shard_map/ppermute | solution.py:112
  70.1 10.8 %collective-permute-start.15 = (f32[1,90,256]{2,1,0:T(8,128)S(1)}, f32[1,90,256]{2,1,0:T(8,128)S(1)}, u32[]{:S(2)}, u32[]{:S(2)}) collective-permute-start(f32[1,90,256]{2,1,0:T(8,128)S(1)} %get-tuple-element.18), channel_id=1, source_target_pairs={{0,16},{4,20},{8,24},{12,28},{16,32},{20,36},{24,40},{28,44},{32,4... | collective-permute-start | bytes 276488 | tf_op jit(solution)/shard_map/ppermute | solution.py:112
  74.1 9.5 %collective-permute-start.11 = (f32[2,90,256]{2,1,0:T(8,128)S(1)}, f32[2,90,256]{2,1,0:T(8,128)S(1)}, u32[]{:S(2)}, u32[]{:S(2)}) collective-permute-start(f32[2,90,256]{2,1,0:T(8,128)S(1)} %pad_maximum_fusion.16), channel_id=1, source_target_pairs={{0,8},{4,12},{8,16},{12,20},{16,24},{20,28},{24,32},{28,36},{32,40... | collective-permute-start | bytes 552968 | tf_op jit(solution)/shard_map/ppermute | solution.py:112
  76.6 8.6 %collective-permute-start.8 = (f32[2,90,256]{2,1,0:T(8,128)S(1)}, f32[2,90,256]{2,1,0:T(8,128)S(1)}, u32[]{:S(2)}, u32[]{:S(2)}) collective-permute-start(f32[2,90,256]{2,1,0:T(8,128)S(1)} %pad_maximum_fusion.16), channel_id=1, source_target_pairs={{0,4},{4,8},{8,12},{12,16},{16,20},{20,24},{24,28},{28,32},{32,36}... | collective-permute-start | bytes 552968 | tf_op jit(solution)/shard_map/ppermute | solution.py:112
  78.6 7.3 %collective-permute-start.9 = (f32[2,90,256]{2,1,0:T(8,128)S(1)}, f32[2,90,256]{2,1,0:T(8,128)S(1)}, u32[]{:S(2)}, u32[]{:S(2)}) collective-permute-start(f32[2,90,256]{2,1,0:T(8,128)S(1)} %pad_maximum_fusion.16), channel_id=1, source_target_pairs={{4,0},{8,4},{12,8},{16,12},{20,16},{24,20},{28,24},{32,28},{36,32}... | collective-permute-start | bytes 552968 | tf_op jit(solution)/shard_map/ppermute | solution.py:113
  80.9 8.8 %collective-permute-start.12 = (f32[2,90,256]{2,1,0:T(8,128)S(1)}, f32[2,90,256]{2,1,0:T(8,128)S(1)}, u32[]{:S(2)}, u32[]{:S(2)}) collective-permute-start(f32[2,90,256]{2,1,0:T(8,128)S(1)} %pad_maximum_fusion.16), channel_id=1, source_target_pairs={{8,0},{12,4},{16,8},{20,12},{24,16},{28,20},{32,24},{36,28},{40,32... | collective-permute-start | bytes 552968 | tf_op jit(solution)/shard_map/ppermute | solution.py:113
  82.3 10.4 %collective-permute-start.13 = (f32[2,90,256]{2,1,0:T(8,128)S(1)}, f32[2,90,256]{2,1,0:T(8,128)S(1)}, u32[]{:S(2)}, u32[]{:S(2)}) collective-permute-start(f32[2,90,256]{2,1,0:T(8,128)S(1)} %pad_maximum_fusion.16), channel_id=1, source_target_pairs={{12,0},{16,4},{20,8},{24,12},{28,16},{32,20},{36,24},{40,28},{44,3... | collective-permute-start | bytes 552968 | tf_op jit(solution)/shard_map/ppermute | solution.py:113
  83.6 10.8 %collective-permute-start.14 = (f32[1,90,256]{2,1,0:T(8,128)S(1)}, f32[1,90,256]{2,1,0:T(8,128)S(1)}, u32[]{:S(2)}, u32[]{:S(2)}) collective-permute-start(f32[1,90,256]{2,1,0:T(8,128)S(1)} %get-tuple-element.17), channel_id=1, source_target_pairs={{16,0},{20,4},{24,8},{28,12},{32,16},{36,20},{40,24},{44,28},{48,3... | collective-permute-start | bytes 276488 | tf_op jit(solution)/shard_map/ppermute | solution.py:113
  104.7 22.6 %collective-permute-start.21 = (f32[1,74,256]{2,1,0:T(8,128)S(1)}, f32[1,74,256]{2,1,0:T(8,128)}, u32[]{:S(2)}, u32[]{:S(2)}) collective-permute-start(f32[1,74,256]{2,1,0:T(8,128)S(1)} %bitcast.118), channel_id=1, source_target_pairs={{0,12},{4,16},{8,20},{12,24},{16,28},{20,32},{24,36},{28,40},{32,4... | collective-permute-start | bytes 227336 | tf_op jit(solution)/shard_map/ppermute | solution.py:112
  117.5 12.0 %collective-permute-start.18 = (f32[2,74,256]{2,1,0:T(8,128)}, f32[2,74,256]{2,1,0:T(8,128)}, u32[]{:S(2)}, u32[]{:S(2)}) collective-permute-start(f32[2,74,256]{2,1,0:T(8,128)} %reshape.856), channel_id=1, source_target_pairs={{0,8},{4,12},{8,16},{12,20},{16,24},{20,28},{24,32},{28,36},{32,40... | collective-permute-start | bytes 454664 | tf_op jit(solution)/shard_map/ppermute | solution.py:112
  121.6 8.8 %collective-permute-start.16 = (f32[2,74,256]{2,1,0:T(8,128)}, f32[2,74,256]{2,1,0:T(8,128)S(1)}, u32[]{:S(2)}, u32[]{:S(2)}) collective-permute-start(f32[2,74,256]{2,1,0:T(8,128)} %reshape.856), channel_id=1, source_target_pairs={{0,4},{4,8},{8,12},{12,16},{16,20},{20,24},{24,28},{28,32},{32,36}... | collective-permute-start | bytes 454664 | tf_op jit(solution)/shard_map/ppermute | solution.py:112
  123.6 7.0 %collective-permute-start.17 = (f32[2,74,256]{2,1,0:T(8,128)}, f32[2,74,256]{2,1,0:T(8,128)S(1)}, u32[]{:S(2)}, u32[]{:S(2)}) collective-permute-start(f32[2,74,256]{2,1,0:T(8,128)} %reshape.856), channel_id=1, source_target_pairs={{4,0},{8,4},{12,8},{16,12},{20,16},{24,20},{28,24},{32,28},{36,32}... | collective-permute-start | bytes 454664 | tf_op jit(solution)/shard_map/ppermute | solution.py:113
  126.0 8.2 %collective-permute-start.19 = (f32[2,74,256]{2,1,0:T(8,128)}, f32[2,74,256]{2,1,0:T(8,128)S(1)}, u32[]{:S(2)}, u32[]{:S(2)}) collective-permute-start(f32[2,74,256]{2,1,0:T(8,128)} %reshape.856), channel_id=1, source_target_pairs={{8,0},{12,4},{16,8},{20,12},{24,16},{28,20},{32,24},{36,28},{40,32... | collective-permute-start | bytes 454664 | tf_op jit(solution)/shard_map/ppermute | solution.py:113
  127.3 8.0 %collective-permute-start.20 = (f32[1,74,256]{2,1,0:T(8,128)S(1)}, f32[1,74,256]{2,1,0:T(8,128)S(1)}, u32[]{:S(2)}, u32[]{:S(2)}) collective-permute-start(f32[1,74,256]{2,1,0:T(8,128)S(1)} %bitcast.119), channel_id=1, source_target_pairs={{12,0},{16,4},{20,8},{24,12},{28,16},{32,20},{36,24},{40,28},{44,3... | collective-permute-start | bytes 227336 | tf_op jit(solution)/shard_map/ppermute | solution.py:113
  161.0 18.8 %collective-permute-start.27 = (f32[128,512]{1,0:T(8,128)S(1)}, f32[128,512]{1,0:T(8,128)S(1)}, u32[]{:S(2)}, u32[]{:S(2)}) collective-permute-start(f32[128,512]{1,0:T(8,128)S(1)} %get-tuple-element.5), channel_id=1, source_target_pairs={{0,24},{32,56},{64,88},{96,120},{124,100},{92,68},{60,36},{28,4},{... | collective-permute-start | bytes 786440 | tf_op jit(solution)/shard_map/ppermute | solution.py:249
  183.3 4.8 %collective-permute-start.29 = (f32[1,128,128]{2,1,0:T(8,128)S(1)}, f32[1,128,128]{2,1,0:T(8,128)S(1)}, u32[]{:S(2)}, u32[]{:S(2)}) collective-permute-start(f32[1,128,128]{2,1,0:T(8,128)S(1)} %get-tuple-element.12), channel_id=1, source_target_pairs={{0,1},{1,2},{2,3},{3,0},{4,5},{5,6},{6,7},{7,4},{8,9},{9,10},{10,1... | collective-permute-start | bytes 196616 | tf_op jit(solution)/shard_map/ppermute | solution.py:262
  184.8 4.9 %collective-permute-start.31 = (f32[1,128,128]{2,1,0:T(8,128)S(1)}, f32[1,128,128]{2,1,0:T(8,128)S(1)}, u32[]{:S(2)}, u32[]{:S(2)}) collective-permute-start(f32[1,128,128]{2,1,0:T(8,128)S(1)} %get-tuple-element.13), channel_id=1, source_target_pairs={{0,3},{1,0},{2,1},{3,2},{4,7},{5,4},{6,5},{7,6},{8,11},{9,8},{10,9... | collective-permute-start | bytes 196616 | tf_op jit(solution)/shard_map/ppermute | solution.py:262
  (39 other events, 221.6 us)

commit v13 on v12

--- a/solution.py
+++ b/solution.py
@@ -56,8 +56,8 @@
 
 def children_sum(field):
     x_cells, y_cells, z_cells = field.shape
-    paired = field.reshape(x_cells // 2, 2, y_cells, z_cells).sum(axis=1)
-    paired = jnp.dot(paired, pair_matrix(z_cells), precision=lax.Precision.HIGHEST)
+    paired = jnp.dot(field, pair_matrix(z_cells), precision=lax.Precision.HIGHEST)
+    paired = paired.reshape(x_cells // 2, 2, y_cells, z_cells // 2).sum(axis=1)
     to_rows = pair_matrix(y_cells).T
     planes = [
         jnp.dot(to_rows, paired[i], precision=lax.Precision.HIGHEST)

time: 192 us -> 195 us (1.016)
  matrix products: 10.3 us -> 14.4 us
    dot_general x7, matrix products: 2.02 us -> 5.95 us  [children_sum(): jnp.dot(to_rows, paired[i], precision=lax.Precision.HIGHEST)]
    unnamed x79 -> x81, local copies, waits for them, and re-layouts: 10.4 us -> 10.5 us
where the time goes in v13:
time: 195 us; the launch traced here: 193 us
  starting transfers between devices  76.6 us (39%)
  waiting for transfers between devices  47.9 us (25%)
  other arithmetic  33.7 us (17%)
  local copies, waits for them, and re-layouts  18.6 us (10%)
  matrix products  14.4 us (7%)
  between operations  2.22 us (1%)
    ppermute x11, starting transfers between devices, extend(): lows.insert(0, lax.ppermute(low_piece, axis, up))  50.5 us
    ppermute x11, waiting for transfers between devices, extend(): highs.append(lax.ppermute(high_piece, axis, down))  20.4 us
    select_n x14, other arithmetic, masked(): return jnp.where(keep, field, 0.0)  19.2 us
    ppermute x7, waiting for transfers between devices, spread_faces(): got = lax.ppermute(sent, 'slab', low_pairs + high_pairs)  18.6 us
    ppermute x11, starting transfers between devices, extend(): highs.append(lax.ppermute(high_piece, axis, down))  17.2 us
    unnamed x81, local copies, waits for them, and re-layouts  10.5 us
    ppermute x11, waiting for transfers between devices, extend(): lows.insert(0, lax.ppermute(low_piece, axis, up))  6.26 us
    dot_general x7, matrix products, children_sum(): jnp.dot(to_rows, paired[i], precision=lax.Precision.HIGHEST)  5.95 us
  transfers between devices with their start and end apart: 32, of which 16 were waited for; matrix products, arithmetic and copies ran while one was open for 7% of the time, Pallas kernels for 0%

profile of v13, /device:TPU:1, one launch (start us, length us, event | category | flops | bytes accessed | tf_op | source)
XLA Modules:
  0.0 193.4 jit_solution(11878704652091085241)
XLA Ops:
  0.6 4.7 %collective-permute-start.1 = (f32[4,128,512]{2,1,0:T(8,128)}, f32[4,128,512]{2,1,0:T(8,128)S(1)}, u32[]{:S(2)}, u32[]{:S(2)}) collective-permute-start(f32[4,128,512]{2,1,0:T(8,128)} %param.4), channel_id=1, source_target_pairs={{0,4},{4,8},{8,12},{12,16},{16,20},{20,24},{24,28},{28,32},{32,36}... | collective-permute-start | bytes 3145736 | tf_op jit(solution)/shard_map/ppermute | solution.py:112
  9.2 3.9 %collective-permute-start = (f32[1,128,512]{2,1,0:T(8,128)}, f32[1,128,512]{2,1,0:T(8,128)}, u32[]{:S(2)}, u32[]{:S(2)}) collective-permute-start(f32[1,128,512]{2,1,0:T(8,128)} %get-tuple-element.11), channel_id=1, source_target_pairs={{0,8},{4,12},{8,16},{12,20},{16,24},{20,28},{24,32},{28,36},{32,40... | collective-permute-start | bytes 786440 | tf_op jit(solution)/shard_map/ppermute | solution.py:112
  18.4 4.6 %collective-permute-done = f32[1,128,512]{2,1,0:T(8,128)} collective-permute-done((f32[1,128,512]{2,1,0:T(8,128)}, f32[1,128,512]{2,1,0:T(8,128)}, u32[]{:S(2)}, u32[]{:S(2)}) %collective-permute-start) | collective-permute-done | bytes 262176 | tf_op jit(solution)/shard_map/ppermute | solution.py:112
  26.5 3.6 %collective-permute-start.4 = (f32[14,5,512]{2,1,0:T(8,128)S(1)}, f32[14,5,512]{2,1,0:T(8,128)S(1)}, u32[]{:S(2)}, u32[]{:S(2)}) collective-permute-start(f32[14,5,512]{2,1,0:T(8,128)S(1)} %get-tuple-element.8), channel_id=1, source_target_pairs={{0,1},{1,2},{2,3},{4,5},{5,6},{6,7},{8,9},{9,10},{10,11},{12,13},{... | collective-permute-start | bytes 430088 | tf_op jit(solution)/shard_map/ppermute | solution.py:112
  33.0 4.0 %collective-permute-done.5 = f32[14,5,512]{2,1,0:T(8,128)S(1)} collective-permute-done((f32[14,5,512]{2,1,0:T(8,128)S(1)}, f32[14,5,512]{2,1,0:T(8,128)S(1)}, u32[]{:S(2)}, u32[]{:S(2)}) %collective-permute-start.5) | collective-permute-done | bytes 143392 | tf_op jit(solution)/shard_map/ppermute | solution.py:113
  37.0 2.8 %pad_maximum_fusion = f32[14,138,512]{2,1,0:T(8,128)S(1)} fusion(f32[14,5,512]{2,1,0:T(8,128)S(1)} %collective-permute-done.5, f32[14,128,512]{2,1,0:T(8,128)} %copy-done.9, f32[14,5,512]{2,1,0:T(8,128)S(1)} %collective-permute-done.4), kind=kLoop, calls=%fused_computation.2 | loop fusion | flops 1978368 | bytes 7913472 | tf_op jit(solution)/shard_map/concatenate | solution.py:115
  40.4 3.1 %fusion.4 = f32[12,136,512]{2,1,0:T(8,128)S(1)} fusion(f32[12,136,512]{2,1,0:T(8,128)S(1)} %slice.627, f32[14,138,512]{2,1,0:T(8,128)S(1)} %pad_maximum_fusion, pred[12,136]{1,0:T(8,128)(4,1)S(1)} %broadcast_and_fusion.1), kind=kLoop, calls=%fused_computation.9 | loop fusion | flops 7520256 | bytes 20055648 | tf_op jit(solution)/shard_map/jit(_where)/select_n | solution.py:126
  43.9 2.6 %fusion.9 = f32[10,134,512]{2,1,0:T(8,128)S(1)} fusion(f32[10,134,512]{2,1,0:T(8,128)S(1)} %slice.633, f32[12,136,512]{2,1,0:T(8,128)S(1)} %fusion.4, pred[10,134]{1,0:T(8,128)(4,1)S(1)} %broadcast_and_fusion), kind=kLoop, calls=%fused_computation.21 | loop fusion | flops 6174720 | bytes 16467260 | tf_op jit(solution)/shard_map/jit(_where)/select_n | solution.py:126
  51.5 3.7 %collective-permute-start.6 = (f32[2,13,256]{2,1,0:T(8,128)S(1)}, f32[2,13,256]{2,1,0:T(8,128)S(1)}, u32[]{:S(2)}, u32[]{:S(2)}) collective-permute-start(f32[2,13,256]{2,1,0:T(8,128)S(1)} %get-tuple-element.52), channel_id=1, source_target_pairs={{0,1},{1,2},{2,3},{4,5},{5,6},{6,7},{8,9},{9,10},{10,11},{12,13},{... | collective-permute-start | bytes 79880 | tf_op jit(solution)/shard_map/ppermute | solution.py:112
  57.1 2.7 %collective-permute-done.7 = f32[2,13,256]{2,1,0:T(8,128)S(1)} collective-permute-done((f32[2,13,256]{2,1,0:T(8,128)S(1)}, f32[2,13,256]{2,1,0:T(8,128)S(1)}, u32[]{:S(2)}, u32[]{:S(2)}) %collective-permute-start.7) | collective-permute-done | bytes 26656 | tf_op jit(solution)/shard_map/ppermute | solution.py:113
  59.9 10.4 %collective-permute-start.10 = (f32[2,90,256]{2,1,0:T(8,128)S(1)}, f32[2,90,256]{2,1,0:T(8,128)S(1)}, u32[]{:S(2)}, u32[]{:S(2)}) collective-permute-start(f32[2,90,256]{2,1,0:T(8,128)S(1)} %pad_maximum_fusion.15), channel_id=1, source_target_pairs={{0,12},{4,16},{8,20},{12,24},{16,28},{20,32},{24,36},{28,40},{32,4... | collective-permute-start | bytes 552968 | tf_op jit(solution)/shard_map/ppermute | solution.py:112
  70.3 3.9 %collective-permute-start.15 = (f32[1,90,256]{2,1,0:T(8,128)S(1)}, f32[1,90,256]{2,1,0:T(8,128)S(1)}, u32[]{:S(2)}, u32[]{:S(2)}) collective-permute-start(f32[1,90,256]{2,1,0:T(8,128)S(1)} %get-tuple-element.18), channel_id=1, source_target_pairs={{0,16},{4,20},{8,24},{12,28},{16,32},{20,36},{24,40},{28,44},{32,4... | collective-permute-start | bytes 276488 | tf_op jit(solution)/shard_map/ppermute | solution.py:112
  74.2 2.5 %collective-permute-start.11 = (f32[2,90,256]{2,1,0:T(8,128)S(1)}, f32[2,90,256]{2,1,0:T(8,128)S(1)}, u32[]{:S(2)}, u32[]{:S(2)}) collective-permute-start(f32[2,90,256]{2,1,0:T(8,128)S(1)} %pad_maximum_fusion.15), channel_id=1, source_target_pairs={{0,8},{4,12},{8,16},{12,20},{16,24},{20,28},{24,32},{28,36},{32,40... | collective-permute-start | bytes 552968 | tf_op jit(solution)/shard_map/ppermute | solution.py:112
  78.7 2.3 %collective-permute-start.9 = (f32[2,90,256]{2,1,0:T(8,128)S(1)}, f32[2,90,256]{2,1,0:T(8,128)S(1)}, u32[]{:S(2)}, u32[]{:S(2)}) collective-permute-start(f32[2,90,256]{2,1,0:T(8,128)S(1)} %pad_maximum_fusion.15), channel_id=1, source_target_pairs={{4,0},{8,4},{12,8},{16,12},{20,16},{24,20},{28,24},{32,28},{36,32}... | collective-permute-start | bytes 552968 | tf_op jit(solution)/shard_map/ppermute | solution.py:113
  86.1 3.8 %collective-permute-done.12 = f32[2,90,256]{2,1,0:T(8,128)S(1)} collective-permute-done((f32[2,90,256]{2,1,0:T(8,128)S(1)}, f32[2,90,256]{2,1,0:T(8,128)S(1)}, u32[]{:S(2)}, u32[]{:S(2)}) %collective-permute-start.12) | collective-permute-done | bytes 184352 | tf_op jit(solution)/shard_map/ppermute | solution.py:113
  89.9 2.8 %collective-permute-done.13 = f32[2,90,256]{2,1,0:T(8,128)S(1)} collective-permute-done((f32[2,90,256]{2,1,0:T(8,128)S(1)}, f32[2,90,256]{2,1,0:T(8,128)S(1)}, u32[]{:S(2)}, u32[]{:S(2)}) %collective-permute-start.13) | collective-permute-done | bytes 184352 | tf_op jit(solution)/shard_map/ppermute | solution.py:113
  107.7 12.1 %collective-permute-start.21 = (f32[1,74,256]{2,1,0:T(8,128)S(1)}, f32[1,74,256]{2,1,0:T(8,128)}, u32[]{:S(2)}, u32[]{:S(2)}) collective-permute-start(f32[1,74,256]{2,1,0:T(8,128)S(1)} %bitcast.119), channel_id=1, source_target_pairs={{0,12},{4,16},{8,20},{12,24},{16,28},{20,32},{24,36},{28,40},{32,4... | collective-permute-start | bytes 227336 | tf_op jit(solution)/shard_map/ppermute | solution.py:112
  126.6 2.4 %collective-permute-start.17 = (f32[2,74,256]{2,1,0:T(8,128)}, f32[2,74,256]{2,1,0:T(8,128)S(1)}, u32[]{:S(2)}, u32[]{:S(2)}) collective-permute-start(f32[2,74,256]{2,1,0:T(8,128)} %reshape.856), channel_id=1, source_target_pairs={{4,0},{8,4},{12,8},{16,12},{20,16},{24,20},{28,24},{32,28},{36,32}... | collective-permute-start | bytes 454664 | tf_op jit(solution)/shard_map/ppermute | solution.py:113
  133.7 3.6 %collective-permute-done.19 = f32[2,74,256]{2,1,0:T(8,128)S(1)} collective-permute-done((f32[2,74,256]{2,1,0:T(8,128)}, f32[2,74,256]{2,1,0:T(8,128)S(1)}, u32[]{:S(2)}, u32[]{:S(2)}) %collective-permute-start.19) | collective-permute-done | bytes 151584 | tf_op jit(solution)/shard_map/ppermute | solution.py:113
  140.7 2.2 %fusion.85 = f32[6,68,512]{2,1,0:T(8,128)S(1)} fusion(f32[10,72,256]{2,1,0:T(8,128)S(1)} %fusion.78, f32[2,74,256]{2,1,0:T(8,128)S(1)} %collective-permute-done.17, f32[2,74,256]{2,1,0:T(8,128)} %reshape.856, f32[2,74,256]{2,1,0:T(8,128)S(1)} %collective-permute-done.16, f32[12,86,256]{2,1,0:T(8,128)} %copy-done.4, f32[14,88,256]{2,1,0:T(8,128)} %copy-done.3, ...), kind=kOutput, calls=%fused_computation.175 | convolution fusion | flops 643635200 | bytes 4130816 | tf_op jit(solution)/shard_map/dot_general | solution.py:71
  150.1 3.1 %fusion.30 = (f32[6,130,512]{2,1,0:T(8,128)S(1)}, f32[6,130,512]{2,1,0:T(8,128)S(1)}) fusion(f32[6,130,512]{2,1,0:T(8,128)S(1)} %slice.726, f32[8,132,512]{2,1,0:T(8,128)S(1)} %fusion.18, pred[6,130]{1,0:T(8,128)(4,1)S(1)} %copy-done.26, f32[6,130,512]{2,1,0:T(8,128)S(1)} %slice.645, f32[8,132,512]{2,1,0:T(8,128)S(1)} %copy-done.2), kind=kLoop, calls=%fused_computation.60 | loop fusion | flops 7188480 | bytes 19170060 | tf_op jit(solution)/shard_map/jit(_where)/select_n | solution.py:126
  155.6 2.6 %fusion.59 = f32[4,128,512]{2,1,0:T(8,128)S(1)} fusion(f32[8,132,512]{2,1,0:T(8,128)S(1)} %fusion.18, f32[10,134,512]{2,1,0:T(8,128)S(1)} %slice_multiply_fusion, f32[4,128,512]{2,1,0:T(8,128)S(1)} %get-tuple-element.60, f32[10,134,512]{2,1,0:T(8,128)} %copy-done, f32[4,128,512]{2,1,0:T(8,128)S(1)} %copy-done.8, f32[12,136,512]{2,1,0:T(8,128)S(1)} %fusion.4, ...), kind=kLoop, calls=%fused_computation.127 | loop fusion | flops 3407872 | bytes 11534336 | tf_op jit(solution)/shard_map/sub | solution.py:208
  165.4 17.3 %collective-permute-done.27 = f32[128,512]{1,0:T(8,128)S(1)} collective-permute-done((f32[128,512]{1,0:T(8,128)S(1)}, f32[128,512]{1,0:T(8,128)S(1)}, u32[]{:S(2)}, u32[]{:S(2)}) %collective-permute-start.27) | collective-permute-done | bytes 262176 | tf_op jit(solution)/shard_map/ppermute | solution.py:249
  187.8 2.3 %collective-permute-start.31 = (f32[1,128,128]{2,1,0:T(8,128)S(1)}, f32[1,128,128]{2,1,0:T(8,128)S(1)}, u32[]{:S(2)}, u32[]{:S(2)}) collective-permute-start(f32[1,128,128]{2,1,0:T(8,128)S(1)} %get-tuple-element.13), channel_id=1, source_target_pairs={{0,3},{1,0},{2,1},{3,2},{4,7},{5,4},{6,5},{7,6},{8,11},{9,8},{10,9... | collective-permute-start | bytes 196616 | tf_op jit(solution)/shard_map/ppermute | solution.py:262
  (246 shorter events, 84.1 us)
Async XLA Ops:
  0.6 23.4 %collective-permute-start.1 = (f32[4,128,512]{2,1,0:T(8,128)}, f32[4,128,512]{2,1,0:T(8,128)S(1)}, u32[]{:S(2)}, u32[]{:S(2)}) collective-permute-start(f32[4,128,512]{2,1,0:T(8,128)} %param.4), channel_id=1, source_target_pairs={{0,4},{4,8},{8,12},{12,16},{16,20},{20,24},{24,28},{28,32},{32,36}... | collective-permute-start | bytes 3145736 | tf_op jit(solution)/shard_map/ppermute | solution.py:112
  5.4 19.1 %collective-permute-start.2 = (f32[4,128,512]{2,1,0:T(8,128)}, f32[4,128,512]{2,1,0:T(8,128)S(1)}, u32[]{:S(2)}, u32[]{:S(2)}) collective-permute-start(f32[4,128,512]{2,1,0:T(8,128)} %param.4), channel_id=1, source_target_pairs={{4,0},{8,4},{12,8},{16,12},{20,16},{24,20},{28,24},{32,28},{36,32}... | collective-permute-start | bytes 3145736 | tf_op jit(solution)/shard_map/ppermute | solution.py:113
  9.2 13.9 %collective-permute-start = (f32[1,128,512]{2,1,0:T(8,128)}, f32[1,128,512]{2,1,0:T(8,128)}, u32[]{:S(2)}, u32[]{:S(2)}) collective-permute-start(f32[1,128,512]{2,1,0:T(8,128)} %get-tuple-element.11), channel_id=1, source_target_pairs={{0,8},{4,12},{8,16},{12,20},{16,24},{20,28},{24,32},{28,36},{32,40... | collective-permute-start | bytes 786440 | tf_op jit(solution)/shard_map/ppermute | solution.py:112
  13.0 11.5 %collective-permute-start.3 = (f32[1,128,512]{2,1,0:T(8,128)}, f32[1,128,512]{2,1,0:T(8,128)S(1)}, u32[]{:S(2)}, u32[]{:S(2)}) collective-permute-start(f32[1,128,512]{2,1,0:T(8,128)} %get-tuple-element.10), channel_id=1, source_target_pairs={{8,0},{12,4},{16,8},{20,12},{24,16},{28,20},{32,24},{36,28},{40,32... | collective-permute-start | bytes 786440 | tf_op jit(solution)/shard_map/ppermute | solution.py:113
  26.5 6.5 %collective-permute-start.4 = (f32[14,5,512]{2,1,0:T(8,128)S(1)}, f32[14,5,512]{2,1,0:T(8,128)S(1)}, u32[]{:S(2)}, u32[]{:S(2)}) collective-permute-start(f32[14,5,512]{2,1,0:T(8,128)S(1)} %get-tuple-element.8), channel_id=1, source_target_pairs={{0,1},{1,2},{2,3},{4,5},{5,6},{6,7},{8,9},{9,10},{10,11},{12,13},{... | collective-permute-start | bytes 430088 | tf_op jit(solution)/shard_map/ppermute | solution.py:112
  30.0 6.9 %collective-permute-start.5 = (f32[14,5,512]{2,1,0:T(8,128)S(1)}, f32[14,5,512]{2,1,0:T(8,128)S(1)}, u32[]{:S(2)}, u32[]{:S(2)}) collective-permute-start(f32[14,5,512]{2,1,0:T(8,128)S(1)} %get-tuple-element.9), channel_id=1, source_target_pairs={{1,0},{2,1},{3,2},{5,4},{6,5},{7,6},{9,8},{10,9},{11,10},{13,12},{... | collective-permute-start | bytes 430088 | tf_op jit(solution)/shard_map/ppermute | solution.py:113
  51.5 5.6 %collective-permute-start.6 = (f32[2,13,256]{2,1,0:T(8,128)S(1)}, f32[2,13,256]{2,1,0:T(8,128)S(1)}, u32[]{:S(2)}, u32[]{:S(2)}) collective-permute-start(f32[2,13,256]{2,1,0:T(8,128)S(1)} %get-tuple-element.52), channel_id=1, source_target_pairs={{0,1},{1,2},{2,3},{4,5},{5,6},{6,7},{8,9},{9,10},{10,11},{12,13},{... | collective-permute-start | bytes 79880 | tf_op jit(solution)/shard_map/ppermute | solution.py:112
  59.9 22.5 %collective-permute-start.10 = (f32[2,90,256]{2,1,0:T(8,128)S(1)}, f32[2,90,256]{2,1,0:T(8,128)S(1)}, u32[]{:S(2)}, u32[]{:S(2)}) collective-permute-start(f32[2,90,256]{2,1,0:T(8,128)S(1)} %pad_maximum_fusion.15), channel_id=1, source_target_pairs={{0,12},{4,16},{8,20},{12,24},{16,28},{20,32},{24,36},{28,40},{32,4... | collective-permute-start | bytes 552968 | tf_op jit(solution)/shard_map/ppermute | solution.py:112
  70.3 10.8 %collective-permute-start.15 = (f32[1,90,256]{2,1,0:T(8,128)S(1)}, f32[1,90,256]{2,1,0:T(8,128)S(1)}, u32[]{:S(2)}, u32[]{:S(2)}) collective-permute-start(f32[1,90,256]{2,1,0:T(8,128)S(1)} %get-tuple-element.18), channel_id=1, source_target_pairs={{0,16},{4,20},{8,24},{12,28},{16,32},{20,36},{24,40},{28,44},{32,4... | collective-permute-start | bytes 276488 | tf_op jit(solution)/shard_map/ppermute | solution.py:112
  74.2 9.6 %collective-permute-start.11 = (f32[2,90,256]{2,1,0:T(8,128)S(1)}, f32[2,90,256]{2,1,0:T(8,128)S(1)}, u32[]{:S(2)}, u32[]{:S(2)}) collective-permute-start(f32[2,90,256]{2,1,0:T(8,128)S(1)} %pad_maximum_fusion.15), channel_id=1, source_target_pairs={{0,8},{4,12},{8,16},{12,20},{16,24},{20,28},{24,32},{28,36},{32,40... | collective-permute-start | bytes 552968 | tf_op jit(solution)/shard_map/ppermute | solution.py:112
  76.7 8.6 %collective-permute-start.8 = (f32[2,90,256]{2,1,0:T(8,128)S(1)}, f32[2,90,256]{2,1,0:T(8,128)S(1)}, u32[]{:S(2)}, u32[]{:S(2)}) collective-permute-start(f32[2,90,256]{2,1,0:T(8,128)S(1)} %pad_maximum_fusion.15), channel_id=1, source_target_pairs={{0,4},{4,8},{8,12},{12,16},{16,20},{20,24},{24,28},{28,32},{32,36}... | collective-permute-start | bytes 552968 | tf_op jit(solution)/shard_map/ppermute | solution.py:112
  78.7 7.3 %collective-permute-start.9 = (f32[2,90,256]{2,1,0:T(8,128)S(1)}, f32[2,90,256]{2,1,0:T(8,128)S(1)}, u32[]{:S(2)}, u32[]{:S(2)}) collective-permute-start(f32[2,90,256]{2,1,0:T(8,128)S(1)} %pad_maximum_fusion.15), channel_id=1, source_target_pairs={{4,0},{8,4},{12,8},{16,12},{20,16},{24,20},{28,24},{32,28},{36,32}... | collective-permute-start | bytes 552968 | tf_op jit(solution)/shard_map/ppermute | solution.py:113
  81.0 8.8 %collective-permute-start.12 = (f32[2,90,256]{2,1,0:T(8,128)S(1)}, f32[2,90,256]{2,1,0:T(8,128)S(1)}, u32[]{:S(2)}, u32[]{:S(2)}) collective-permute-start(f32[2,90,256]{2,1,0:T(8,128)S(1)} %pad_maximum_fusion.15), channel_id=1, source_target_pairs={{8,0},{12,4},{16,8},{20,12},{24,16},{28,20},{32,24},{36,28},{40,32... | collective-permute-start | bytes 552968 | tf_op jit(solution)/shard_map/ppermute | solution.py:113
  82.4 10.4 %collective-permute-start.13 = (f32[2,90,256]{2,1,0:T(8,128)S(1)}, f32[2,90,256]{2,1,0:T(8,128)S(1)}, u32[]{:S(2)}, u32[]{:S(2)}) collective-permute-start(f32[2,90,256]{2,1,0:T(8,128)S(1)} %pad_maximum_fusion.15), channel_id=1, source_target_pairs={{12,0},{16,4},{20,8},{24,12},{28,16},{32,20},{36,24},{40,28},{44,3... | collective-permute-start | bytes 552968 | tf_op jit(solution)/shard_map/ppermute | solution.py:113
  83.7 10.8 %collective-permute-start.14 = (f32[1,90,256]{2,1,0:T(8,128)S(1)}, f32[1,90,256]{2,1,0:T(8,128)S(1)}, u32[]{:S(2)}, u32[]{:S(2)}) collective-permute-start(f32[1,90,256]{2,1,0:T(8,128)S(1)} %get-tuple-element.17), channel_id=1, source_target_pairs={{16,0},{20,4},{24,8},{28,12},{32,16},{36,20},{40,24},{44,28},{48,3... | collective-permute-start | bytes 276488 | tf_op jit(solution)/shard_map/ppermute | solution.py:113
  107.7 22.6 %collective-permute-start.21 = (f32[1,74,256]{2,1,0:T(8,128)S(1)}, f32[1,74,256]{2,1,0:T(8,128)}, u32[]{:S(2)}, u32[]{:S(2)}) collective-permute-start(f32[1,74,256]{2,1,0:T(8,128)S(1)} %bitcast.119), channel_id=1, source_target_pairs={{0,12},{4,16},{8,20},{12,24},{16,28},{20,32},{24,36},{28,40},{32,4... | collective-permute-start | bytes 227336 | tf_op jit(solution)/shard_map/ppermute | solution.py:112
  120.5 12.0 %collective-permute-start.18 = (f32[2,74,256]{2,1,0:T(8,128)}, f32[2,74,256]{2,1,0:T(8,128)}, u32[]{:S(2)}, u32[]{:S(2)}) collective-permute-start(f32[2,74,256]{2,1,0:T(8,128)} %reshape.856), channel_id=1, source_target_pairs={{0,8},{4,12},{8,16},{12,20},{16,24},{20,28},{24,32},{28,36},{32,40... | collective-permute-start | bytes 454664 | tf_op jit(solution)/shard_map/ppermute | solution.py:112
  124.7 8.8 %collective-permute-start.16 = (f32[2,74,256]{2,1,0:T(8,128)}, f32[2,74,256]{2,1,0:T(8,128)S(1)}, u32[]{:S(2)}, u32[]{:S(2)}) collective-permute-start(f32[2,74,256]{2,1,0:T(8,128)} %reshape.856), channel_id=1, source_target_pairs={{0,4},{4,8},{8,12},{12,16},{16,20},{20,24},{24,28},{28,32},{32,36}... | collective-permute-start | bytes 454664 | tf_op jit(solution)/shard_map/ppermute | solution.py:112
  126.6 7.0 %collective-permute-start.17 = (f32[2,74,256]{2,1,0:T(8,128)}, f32[2,74,256]{2,1,0:T(8,128)S(1)}, u32[]{:S(2)}, u32[]{:S(2)}) collective-permute-start(f32[2,74,256]{2,1,0:T(8,128)} %reshape.856), channel_id=1, source_target_pairs={{4,0},{8,4},{12,8},{16,12},{20,16},{24,20},{28,24},{32,28},{36,32}... | collective-permute-start | bytes 454664 | tf_op jit(solution)/shard_map/ppermute | solution.py:113
  129.0 8.2 %collective-permute-start.19 = (f32[2,74,256]{2,1,0:T(8,128)}, f32[2,74,256]{2,1,0:T(8,128)S(1)}, u32[]{:S(2)}, u32[]{:S(2)}) collective-permute-start(f32[2,74,256]{2,1,0:T(8,128)} %reshape.856), channel_id=1, source_target_pairs={{8,0},{12,4},{16,8},{20,12},{24,16},{28,20},{32,24},{36,28},{40,32... | collective-permute-start | bytes 454664 | tf_op jit(solution)/shard_map/ppermute | solution.py:113
  130.3 8.0 %collective-permute-start.20 = (f32[1,74,256]{2,1,0:T(8,128)S(1)}, f32[1,74,256]{2,1,0:T(8,128)S(1)}, u32[]{:S(2)}, u32[]{:S(2)}) collective-permute-start(f32[1,74,256]{2,1,0:T(8,128)S(1)} %bitcast.120), channel_id=1, source_target_pairs={{12,0},{16,4},{20,8},{24,12},{28,16},{32,20},{36,24},{40,28},{44,3... | collective-permute-start | bytes 227336 | tf_op jit(solution)/shard_map/ppermute | solution.py:113
  164.0 18.8 %collective-permute-start.27 = (f32[128,512]{1,0:T(8,128)S(1)}, f32[128,512]{1,0:T(8,128)S(1)}, u32[]{:S(2)}, u32[]{:S(2)}) collective-permute-start(f32[128,512]{1,0:T(8,128)S(1)} %get-tuple-element.5), channel_id=1, source_target_pairs={{0,24},{32,56},{64,88},{96,120},{124,100},{92,68},{60,36},{28,4},{... | collective-permute-start | bytes 786440 | tf_op jit(solution)/shard_map/ppermute | solution.py:249
  186.3 4.8 %collective-permute-start.29 = (f32[1,128,128]{2,1,0:T(8,128)S(1)}, f32[1,128,128]{2,1,0:T(8,128)S(1)}, u32[]{:S(2)}, u32[]{:S(2)}) collective-permute-start(f32[1,128,128]{2,1,0:T(8,128)S(1)} %get-tuple-element.12), channel_id=1, source_target_pairs={{0,1},{1,2},{2,3},{3,0},{4,5},{5,6},{6,7},{7,4},{8,9},{9,10},{10,1... | collective-permute-start | bytes 196616 | tf_op jit(solution)/shard_map/ppermute | solution.py:262
  187.8 4.9 %collective-permute-start.31 = (f32[1,128,128]{2,1,0:T(8,128)S(1)}, f32[1,128,128]{2,1,0:T(8,128)S(1)}, u32[]{:S(2)}, u32[]{:S(2)}) collective-permute-start(f32[1,128,128]{2,1,0:T(8,128)S(1)} %get-tuple-element.13), channel_id=1, source_target_pairs={{0,3},{1,0},{2,1},{3,2},{4,7},{5,4},{6,5},{7,6},{8,11},{9,8},{10,9... | collective-permute-start | bytes 196616 | tf_op jit(solution)/shard_map/ppermute | solution.py:262
  (40 other events, 246.1 us)

commit v14 on v12

--- a/solution.py
+++ b/solution.py
@@ -70,11 +70,8 @@
     x_cells, y_cells, z_cells = field.shape
     wide = jnp.dot(field, pair_matrix(2 * z_cells).T, precision=lax.Precision.HIGHEST)
     to_rows = pair_matrix(2 * y_cells)
-    planes = [
-        jnp.dot(to_rows, wide[i], precision=lax.Precision.HIGHEST)
-        for i in range(x_cells)
-    ]
-    return jnp.repeat(jnp.stack(planes), 2, axis=0)
+    planes = jnp.einsum("jy,xyz->xjz", to_rows, wide, precision=lax.Precision.HIGHEST)
+    return jnp.repeat(planes, 2, axis=0)
 
 
 def source_rows(seg_rows, owners, offsets, tile_size):

time: 192 us -> 191 us (level)
  no operation moved by 1% of the time
where the time goes in v14:
time: 191 us; the launch traced here: 190 us
  starting transfers between devices  76.6 us (40%)
  waiting for transfers between devices  48.4 us (25%)
  other arithmetic  35.8 us (19%)
  local copies, waits for them, and re-layouts  17.9 us (9%)
  matrix products  8.67 us (5%)
  between operations  2.2 us (1%)
    ppermute x11, starting transfers between devices, extend(): lows.insert(0, lax.ppermute(low_piece, axis, up))  50.6 us
    ppermute x11, waiting for transfers between devices, extend(): highs.append(lax.ppermute(high_piece, axis, down))  21.2 us
    select_n x14, other arithmetic, masked(): return jnp.where(keep, field, 0.0)  20.1 us
    ppermute x7, waiting for transfers between devices, spread_faces(): got = lax.ppermute(sent, 'slab', low_pairs + high_pairs)  18.5 us
    ppermute x11, starting transfers between devices, extend(): highs.append(lax.ppermute(high_piece, axis, down))  17.2 us
    unnamed x79, local copies, waits for them, and re-layouts  10.4 us
    ppermute x11, waiting for transfers between devices, extend(): lows.insert(0, lax.ppermute(low_piece, axis, up))  6.1 us
    ppermute x7, starting transfers between devices, spread_faces(): got = lax.ppermute(sent, 'slab', low_pairs + high_pairs)  4.98 us
  transfers between devices with their start and end apart: 32, of which 16 were waited for; matrix products, arithmetic and copies ran while one was open for 7% of the time, Pallas kernels for 0%

profile of v14, /device:TPU:1, one launch (start us, length us, event | category | flops | bytes accessed | tf_op | source)
XLA Modules:
  0.0 189.6 jit_solution(3866658839491700737)
XLA Ops:
  0.6 4.7 %collective-permute-start.1 = (f32[4,128,512]{2,1,0:T(8,128)}, f32[4,128,512]{2,1,0:T(8,128)S(1)}, u32[]{:S(2)}, u32[]{:S(2)}) collective-permute-start(f32[4,128,512]{2,1,0:T(8,128)} %param.4), channel_id=1, source_target_pairs={{0,4},{4,8},{8,12},{12,16},{16,20},{20,24},{24,28},{28,32},{32,36}... | collective-permute-start | bytes 3145736 | tf_op jit(solution)/shard_map/ppermute | solution.py:109
  9.2 3.9 %collective-permute-start = (f32[1,128,512]{2,1,0:T(8,128)}, f32[1,128,512]{2,1,0:T(8,128)}, u32[]{:S(2)}, u32[]{:S(2)}) collective-permute-start(f32[1,128,512]{2,1,0:T(8,128)} %get-tuple-element.11), channel_id=1, source_target_pairs={{0,8},{4,12},{8,16},{12,20},{16,24},{20,28},{24,32},{28,36},{32,40... | collective-permute-start | bytes 786440 | tf_op jit(solution)/shard_map/ppermute | solution.py:109
  18.5 4.5 %collective-permute-done = f32[1,128,512]{2,1,0:T(8,128)} collective-permute-done((f32[1,128,512]{2,1,0:T(8,128)}, f32[1,128,512]{2,1,0:T(8,128)}, u32[]{:S(2)}, u32[]{:S(2)}) %collective-permute-start) | collective-permute-done | bytes 262176 | tf_op jit(solution)/shard_map/ppermute | solution.py:109
  26.5 3.6 %collective-permute-start.4 = (f32[14,5,512]{2,1,0:T(8,128)S(1)}, f32[14,5,512]{2,1,0:T(8,128)S(1)}, u32[]{:S(2)}, u32[]{:S(2)}) collective-permute-start(f32[14,5,512]{2,1,0:T(8,128)S(1)} %get-tuple-element.8), channel_id=1, source_target_pairs={{0,1},{1,2},{2,3},{4,5},{5,6},{6,7},{8,9},{9,10},{10,11},{12,13},{... | collective-permute-start | bytes 430088 | tf_op jit(solution)/shard_map/ppermute | solution.py:109
  33.0 4.0 %collective-permute-done.5 = f32[14,5,512]{2,1,0:T(8,128)S(1)} collective-permute-done((f32[14,5,512]{2,1,0:T(8,128)S(1)}, f32[14,5,512]{2,1,0:T(8,128)S(1)}, u32[]{:S(2)}, u32[]{:S(2)}) %collective-permute-start.5) | collective-permute-done | bytes 143392 | tf_op jit(solution)/shard_map/ppermute | solution.py:110
  37.0 2.8 %pad_maximum_fusion = f32[14,138,512]{2,1,0:T(8,128)S(1)} fusion(f32[14,5,512]{2,1,0:T(8,128)S(1)} %collective-permute-done.5, f32[14,128,512]{2,1,0:T(8,128)} %copy-done.8, f32[14,5,512]{2,1,0:T(8,128)S(1)} %collective-permute-done.4), kind=kLoop, calls=%fused_computation.2 | loop fusion | flops 1978368 | bytes 7913472 | tf_op jit(solution)/shard_map/concatenate | solution.py:112
  40.4 3.1 %fusion.4 = f32[12,136,512]{2,1,0:T(8,128)S(1)} fusion(f32[12,136,512]{2,1,0:T(8,128)S(1)} %slice.600, f32[14,138,512]{2,1,0:T(8,128)S(1)} %pad_maximum_fusion, pred[12,136]{1,0:T(8,128)(4,1)S(1)} %broadcast_and_fusion.1), kind=kLoop, calls=%fused_computation.9 | loop fusion | flops 7520256 | bytes 20055648 | tf_op jit(solution)/shard_map/jit(_where)/select_n | solution.py:123
  43.9 2.6 %fusion.9 = f32[10,134,512]{2,1,0:T(8,128)S(1)} fusion(f32[10,134,512]{2,1,0:T(8,128)S(1)} %slice.606, f32[12,136,512]{2,1,0:T(8,128)S(1)} %fusion.4, pred[10,134]{1,0:T(8,128)(4,1)S(1)} %broadcast_and_fusion), kind=kLoop, calls=%fused_computation.21 | loop fusion | flops 6174720 | bytes 16467260 | tf_op jit(solution)/shard_map/jit(_where)/select_n | solution.py:123
  51.4 3.7 %collective-permute-start.6 = (f32[2,13,256]{2,1,0:T(8,128)S(1)}, f32[2,13,256]{2,1,0:T(8,128)S(1)}, u32[]{:S(2)}, u32[]{:S(2)}) collective-permute-start(f32[2,13,256]{2,1,0:T(8,128)S(1)} %get-tuple-element.52), channel_id=1, source_target_pairs={{0,1},{1,2},{2,3},{4,5},{5,6},{6,7},{8,9},{9,10},{10,11},{12,13},{... | collective-permute-start | bytes 79880 | tf_op jit(solution)/shard_map/ppermute | solution.py:109
  56.4 3.3 %collective-permute-done.7 = f32[2,13,256]{2,1,0:T(8,128)S(1)} collective-permute-done((f32[2,13,256]{2,1,0:T(8,128)S(1)}, f32[2,13,256]{2,1,0:T(8,128)S(1)}, u32[]{:S(2)}, u32[]{:S(2)}) %collective-permute-start.7) | collective-permute-done | bytes 26656 | tf_op jit(solution)/shard_map/ppermute | solution.py:110
  59.7 10.4 %collective-permute-start.10 = (f32[2,90,256]{2,1,0:T(8,128)S(1)}, f32[2,90,256]{2,1,0:T(8,128)S(1)}, u32[]{:S(2)}, u32[]{:S(2)}) collective-permute-start(f32[2,90,256]{2,1,0:T(8,128)S(1)} %pad_maximum_fusion.16), channel_id=1, source_target_pairs={{0,12},{4,16},{8,20},{12,24},{16,28},{20,32},{24,36},{28,40},{32,4... | collective-permute-start | bytes 552968 | tf_op jit(solution)/shard_map/ppermute | solution.py:109
  70.1 3.9 %collective-permute-start.15 = (f32[1,90,256]{2,1,0:T(8,128)S(1)}, f32[1,90,256]{2,1,0:T(8,128)S(1)}, u32[]{:S(2)}, u32[]{:S(2)}) collective-permute-start(f32[1,90,256]{2,1,0:T(8,128)S(1)} %get-tuple-element.18), channel_id=1, source_target_pairs={{0,16},{4,20},{8,24},{12,28},{16,32},{20,36},{24,40},{28,44},{32,4... | collective-permute-start | bytes 276488 | tf_op jit(solution)/shard_map/ppermute | solution.py:109
  74.1 2.5 %collective-permute-start.11 = (f32[2,90,256]{2,1,0:T(8,128)S(1)}, f32[2,90,256]{2,1,0:T(8,128)S(1)}, u32[]{:S(2)}, u32[]{:S(2)}) collective-permute-start(f32[2,90,256]{2,1,0:T(8,128)S(1)} %pad_maximum_fusion.16), channel_id=1, source_target_pairs={{0,8},{4,12},{8,16},{12,20},{16,24},{20,28},{24,32},{28,36},{32,40... | collective-permute-start | bytes 552968 | tf_op jit(solution)/shard_map/ppermute | solution.py:109
  78.6 2.3 %collective-permute-start.9 = (f32[2,90,256]{2,1,0:T(8,128)S(1)}, f32[2,90,256]{2,1,0:T(8,128)S(1)}, u32[]{:S(2)}, u32[]{:S(2)}) collective-permute-start(f32[2,90,256]{2,1,0:T(8,128)S(1)} %pad_maximum_fusion.16), channel_id=1, source_target_pairs={{4,0},{8,4},{12,8},{16,12},{20,16},{24,20},{28,24},{32,28},{36,32}... | collective-permute-start | bytes 552968 | tf_op jit(solution)/shard_map/ppermute | solution.py:110
  86.0 3.8 %collective-permute-done.12 = f32[2,90,256]{2,1,0:T(8,128)S(1)} collective-permute-done((f32[2,90,256]{2,1,0:T(8,128)S(1)}, f32[2,90,256]{2,1,0:T(8,128)S(1)}, u32[]{:S(2)}, u32[]{:S(2)}) %collective-permute-start.12) | collective-permute-done | bytes 184352 | tf_op jit(solution)/shard_map/ppermute | solution.py:110
  89.8 2.8 %collective-permute-done.13 = f32[2,90,256]{2,1,0:T(8,128)S(1)} collective-permute-done((f32[2,90,256]{2,1,0:T(8,128)S(1)}, f32[2,90,256]{2,1,0:T(8,128)S(1)}, u32[]{:S(2)}, u32[]{:S(2)}) %collective-permute-start.13) | collective-permute-done | bytes 184352 | tf_op jit(solution)/shard_map/ppermute | solution.py:110
  104.7 12.1 %collective-permute-start.21 = (f32[1,74,256]{2,1,0:T(8,128)}, f32[1,74,256]{2,1,0:T(8,128)}, u32[]{:S(2)}, u32[]{:S(2)}) collective-permute-start(f32[1,74,256]{2,1,0:T(8,128)} %get-tuple-element.57), channel_id=1, source_target_pairs={{0,12},{4,16},{8,20},{12,24},{16,28},{20,32},{24,36},{28,40},{32,4... | collective-permute-start | bytes 227336 | tf_op jit(solution)/shard_map/ppermute | solution.py:109
  123.6 2.4 %collective-permute-start.17 = (f32[2,74,256]{2,1,0:T(8,128)}, f32[2,74,256]{2,1,0:T(8,128)S(1)}, u32[]{:S(2)}, u32[]{:S(2)}) collective-permute-start(f32[2,74,256]{2,1,0:T(8,128)} %reshape.862), channel_id=1, source_target_pairs={{4,0},{8,4},{12,8},{16,12},{20,16},{24,20},{28,24},{32,28},{36,32}... | collective-permute-start | bytes 454664 | tf_op jit(solution)/shard_map/ppermute | solution.py:110
  130.7 3.6 %collective-permute-done.19 = f32[2,74,256]{2,1,0:T(8,128)S(1)} collective-permute-done((f32[2,74,256]{2,1,0:T(8,128)}, f32[2,74,256]{2,1,0:T(8,128)S(1)}, u32[]{:S(2)}, u32[]{:S(2)}) %collective-permute-start.19) | collective-permute-done | bytes 151584 | tf_op jit(solution)/shard_map/ppermute | solution.py:110
  138.0 2.2 %fusion.77 = f32[6,68,512]{2,1,0:T(8,128)S(1)} fusion(f32[10,72,256]{2,1,0:T(8,128)S(1)} %fusion.70, f32[2,74,256]{2,1,0:T(8,128)S(1)} %collective-permute-done.17, f32[2,74,256]{2,1,0:T(8,128)} %reshape.862, f32[2,74,256]{2,1,0:T(8,128)S(1)} %collective-permute-done.16, f32[12,86,256]{2,1,0:T(8,128)} %copy-done.4, f32[14,88,256]{2,1,0:T(8,128)} %copy-done.3, ...), kind=kOutput, calls=%fused_computation.162 | convolution fusion | flops 643635200 | bytes 4130816 | tf_op jit(solution)/shard_map/dot_general | solution.py:71
  146.3 3.1 %fusion.30 = (f32[6,130,512]{2,1,0:T(8,128)S(1)}, f32[6,130,512]{2,1,0:T(8,128)S(1)}) fusion(f32[6,130,512]{2,1,0:T(8,128)S(1)} %slice.693, f32[8,132,512]{2,1,0:T(8,128)S(1)} %fusion.18, pred[6,130]{1,0:T(8,128)(4,1)S(1)} %copy-done.24, f32[6,130,512]{2,1,0:T(8,128)S(1)} %slice.618, f32[8,132,512]{2,1,0:T(8,128)S(1)} %copy-done.2), kind=kLoop, calls=%fused_computation.60 | loop fusion | flops 7188480 | bytes 19170060 | tf_op jit(solution)/shard_map/jit(_where)/select_n | solution.py:123
  152.0 2.6 %fusion.53 = f32[4,128,512]{2,1,0:T(8,128)S(1)} fusion(f32[8,132,512]{2,1,0:T(8,128)S(1)} %fusion.18, f32[10,134,512]{2,1,0:T(8,128)S(1)} %slice_multiply_fusion, f32[4,128,512]{2,1,0:T(8,128)S(1)} %get-tuple-element.62, f32[10,134,512]{2,1,0:T(8,128)} %copy-done, f32[4,128,512]{2,1,0:T(8,128)S(1)} %copy-done.7, f32[12,136,512]{2,1,0:T(8,128)S(1)} %fusion.4, ...), kind=kLoop, calls=%fused_computation.116 | loop fusion | flops 3407872 | bytes 11534336 | tf_op jit(solution)/shard_map/sub | solution.py:205
  161.7 17.2 %collective-permute-done.27 = f32[128,512]{1,0:T(8,128)S(1)} collective-permute-done((f32[128,512]{1,0:T(8,128)S(1)}, f32[128,512]{1,0:T(8,128)S(1)}, u32[]{:S(2)}, u32[]{:S(2)}) %collective-permute-start.27) | collective-permute-done | bytes 262176 | tf_op jit(solution)/shard_map/ppermute | solution.py:246
  184.0 2.3 %collective-permute-start.31 = (f32[1,128,128]{2,1,0:T(8,128)S(1)}, f32[1,128,128]{2,1,0:T(8,128)S(1)}, u32[]{:S(2)}, u32[]{:S(2)}) collective-permute-start(f32[1,128,128]{2,1,0:T(8,128)S(1)} %get-tuple-element.13), channel_id=1, source_target_pairs={{0,3},{1,0},{2,1},{3,2},{4,7},{5,4},{6,5},{7,6},{8,11},{9,8},{10,9... | collective-permute-start | bytes 196616 | tf_op jit(solution)/shard_map/ppermute | solution.py:259
  (241 shorter events, 79.9 us)
Async XLA Ops:
  0.6 23.4 %collective-permute-start.1 = (f32[4,128,512]{2,1,0:T(8,128)}, f32[4,128,512]{2,1,0:T(8,128)S(1)}, u32[]{:S(2)}, u32[]{:S(2)}) collective-permute-start(f32[4,128,512]{2,1,0:T(8,128)} %param.4), channel_id=1, source_target_pairs={{0,4},{4,8},{8,12},{12,16},{16,20},{20,24},{24,28},{28,32},{32,36}... | collective-permute-start | bytes 3145736 | tf_op jit(solution)/shard_map/ppermute | solution.py:109
  5.4 19.1 %collective-permute-start.2 = (f32[4,128,512]{2,1,0:T(8,128)}, f32[4,128,512]{2,1,0:T(8,128)S(1)}, u32[]{:S(2)}, u32[]{:S(2)}) collective-permute-start(f32[4,128,512]{2,1,0:T(8,128)} %param.4), channel_id=1, source_target_pairs={{4,0},{8,4},{12,8},{16,12},{20,16},{24,20},{28,24},{32,28},{36,32}... | collective-permute-start | bytes 3145736 | tf_op jit(solution)/shard_map/ppermute | solution.py:110
  9.2 13.9 %collective-permute-start = (f32[1,128,512]{2,1,0:T(8,128)}, f32[1,128,512]{2,1,0:T(8,128)}, u32[]{:S(2)}, u32[]{:S(2)}) collective-permute-start(f32[1,128,512]{2,1,0:T(8,128)} %get-tuple-element.11), channel_id=1, source_target_pairs={{0,8},{4,12},{8,16},{12,20},{16,24},{20,28},{24,32},{28,36},{32,40... | collective-permute-start | bytes 786440 | tf_op jit(solution)/shard_map/ppermute | solution.py:109
  13.1 11.5 %collective-permute-start.3 = (f32[1,128,512]{2,1,0:T(8,128)}, f32[1,128,512]{2,1,0:T(8,128)S(1)}, u32[]{:S(2)}, u32[]{:S(2)}) collective-permute-start(f32[1,128,512]{2,1,0:T(8,128)} %get-tuple-element.10), channel_id=1, source_target_pairs={{8,0},{12,4},{16,8},{20,12},{24,16},{28,20},{32,24},{36,28},{40,32... | collective-permute-start | bytes 786440 | tf_op jit(solution)/shard_map/ppermute | solution.py:110
  26.5 6.5 %collective-permute-start.4 = (f32[14,5,512]{2,1,0:T(8,128)S(1)}, f32[14,5,512]{2,1,0:T(8,128)S(1)}, u32[]{:S(2)}, u32[]{:S(2)}) collective-permute-start(f32[14,5,512]{2,1,0:T(8,128)S(1)} %get-tuple-element.8), channel_id=1, source_target_pairs={{0,1},{1,2},{2,3},{4,5},{5,6},{6,7},{8,9},{9,10},{10,11},{12,13},{... | collective-permute-start | bytes 430088 | tf_op jit(solution)/shard_map/ppermute | solution.py:109
  30.0 6.9 %collective-permute-start.5 = (f32[14,5,512]{2,1,0:T(8,128)S(1)}, f32[14,5,512]{2,1,0:T(8,128)S(1)}, u32[]{:S(2)}, u32[]{:S(2)}) collective-permute-start(f32[14,5,512]{2,1,0:T(8,128)S(1)} %get-tuple-element.9), channel_id=1, source_target_pairs={{1,0},{2,1},{3,2},{5,4},{6,5},{7,6},{9,8},{10,9},{11,10},{13,12},{... | collective-permute-start | bytes 430088 | tf_op jit(solution)/shard_map/ppermute | solution.py:110
  51.4 5.0 %collective-permute-start.6 = (f32[2,13,256]{2,1,0:T(8,128)S(1)}, f32[2,13,256]{2,1,0:T(8,128)S(1)}, u32[]{:S(2)}, u32[]{:S(2)}) collective-permute-start(f32[2,13,256]{2,1,0:T(8,128)S(1)} %get-tuple-element.52), channel_id=1, source_target_pairs={{0,1},{1,2},{2,3},{4,5},{5,6},{6,7},{8,9},{9,10},{10,11},{12,13},{... | collective-permute-start | bytes 79880 | tf_op jit(solution)/shard_map/ppermute | solution.py:109
  59.7 22.5 %collective-permute-start.10 = (f32[2,90,256]{2,1,0:T(8,128)S(1)}, f32[2,90,256]{2,1,0:T(8,128)S(1)}, u32[]{:S(2)}, u32[]{:S(2)}) collective-permute-start(f32[2,90,256]{2,1,0:T(8,128)S(1)} %pad_maximum_fusion.16), channel_id=1, source_target_pairs={{0,12},{4,16},{8,20},{12,24},{16,28},{20,32},{24,36},{28,40},{32,4... | collective-permute-start | bytes 552968 | tf_op jit(solution)/shard_map/ppermute | solution.py:109
  70.1 10.8 %collective-permute-start.15 = (f32[1,90,256]{2,1,0:T(8,128)S(1)}, f32[1,90,256]{2,1,0:T(8,128)S(1)}, u32[]{:S(2)}, u32[]{:S(2)}) collective-permute-start(f32[1,90,256]{2,1,0:T(8,128)S(1)} %get-tuple-element.18), channel_id=1, source_target_pairs={{0,16},{4,20},{8,24},{12,28},{16,32},{20,36},{24,40},{28,44},{32,4... | collective-permute-start | bytes 276488 | tf_op jit(solution)/shard_map/ppermute | solution.py:109
  74.1 9.5 %collective-permute-start.11 = (f32[2,90,256]{2,1,0:T(8,128)S(1)}, f32[2,90,256]{2,1,0:T(8,128)S(1)}, u32[]{:S(2)}, u32[]{:S(2)}) collective-permute-start(f32[2,90,256]{2,1,0:T(8,128)S(1)} %pad_maximum_fusion.16), channel_id=1, source_target_pairs={{0,8},{4,12},{8,16},{12,20},{16,24},{20,28},{24,32},{28,36},{32,40... | collective-permute-start | bytes 552968 | tf_op jit(solution)/shard_map/ppermute | solution.py:109
  76.6 8.6 %collective-permute-start.8 = (f32[2,90,256]{2,1,0:T(8,128)S(1)}, f32[2,90,256]{2,1,0:T(8,128)S(1)}, u32[]{:S(2)}, u32[]{:S(2)}) collective-permute-start(f32[2,90,256]{2,1,0:T(8,128)S(1)} %pad_maximum_fusion.16), channel_id=1, source_target_pairs={{0,4},{4,8},{8,12},{12,16},{16,20},{20,24},{24,28},{28,32},{32,36}... | collective-permute-start | bytes 552968 | tf_op jit(solution)/shard_map/ppermute | solution.py:109
  78.6 7.3 %collective-permute-start.9 = (f32[2,90,256]{2,1,0:T(8,128)S(1)}, f32[2,90,256]{2,1,0:T(8,128)S(1)}, u32[]{:S(2)}, u32[]{:S(2)}) collective-permute-start(f32[2,90,256]{2,1,0:T(8,128)S(1)} %pad_maximum_fusion.16), channel_id=1, source_target_pairs={{4,0},{8,4},{12,8},{16,12},{20,16},{24,20},{28,24},{32,28},{36,32}... | collective-permute-start | bytes 552968 | tf_op jit(solution)/shard_map/ppermute | solution.py:110
  80.9 8.8 %collective-permute-start.12 = (f32[2,90,256]{2,1,0:T(8,128)S(1)}, f32[2,90,256]{2,1,0:T(8,128)S(1)}, u32[]{:S(2)}, u32[]{:S(2)}) collective-permute-start(f32[2,90,256]{2,1,0:T(8,128)S(1)} %pad_maximum_fusion.16), channel_id=1, source_target_pairs={{8,0},{12,4},{16,8},{20,12},{24,16},{28,20},{32,24},{36,28},{40,32... | collective-permute-start | bytes 552968 | tf_op jit(solution)/shard_map/ppermute | solution.py:110
  82.3 10.4 %collective-permute-start.13 = (f32[2,90,256]{2,1,0:T(8,128)S(1)}, f32[2,90,256]{2,1,0:T(8,128)S(1)}, u32[]{:S(2)}, u32[]{:S(2)}) collective-permute-start(f32[2,90,256]{2,1,0:T(8,128)S(1)} %pad_maximum_fusion.16), channel_id=1, source_target_pairs={{12,0},{16,4},{20,8},{24,12},{28,16},{32,20},{36,24},{40,28},{44,3... | collective-permute-start | bytes 552968 | tf_op jit(solution)/shard_map/ppermute | solution.py:110
  83.6 10.8 %collective-permute-start.14 = (f32[1,90,256]{2,1,0:T(8,128)S(1)}, f32[1,90,256]{2,1,0:T(8,128)S(1)}, u32[]{:S(2)}, u32[]{:S(2)}) collective-permute-start(f32[1,90,256]{2,1,0:T(8,128)S(1)} %get-tuple-element.17), channel_id=1, source_target_pairs={{16,0},{20,4},{24,8},{28,12},{32,16},{36,20},{40,24},{44,28},{48,3... | collective-permute-start | bytes 276488 | tf_op jit(solution)/shard_map/ppermute | solution.py:110
  104.7 22.6 %collective-permute-start.21 = (f32[1,74,256]{2,1,0:T(8,128)}, f32[1,74,256]{2,1,0:T(8,128)}, u32[]{:S(2)}, u32[]{:S(2)}) collective-permute-start(f32[1,74,256]{2,1,0:T(8,128)} %get-tuple-element.57), channel_id=1, source_target_pairs={{0,12},{4,16},{8,20},{12,24},{16,28},{20,32},{24,36},{28,40},{32,4... | collective-permute-start | bytes 227336 | tf_op jit(solution)/shard_map/ppermute | solution.py:109
  117.5 12.1 %collective-permute-start.18 = (f32[2,74,256]{2,1,0:T(8,128)}, f32[2,74,256]{2,1,0:T(8,128)}, u32[]{:S(2)}, u32[]{:S(2)}) collective-permute-start(f32[2,74,256]{2,1,0:T(8,128)} %reshape.862), channel_id=1, source_target_pairs={{0,8},{4,12},{8,16},{12,20},{16,24},{20,28},{24,32},{28,36},{32,40... | collective-permute-start | bytes 454664 | tf_op jit(solution)/shard_map/ppermute | solution.py:109
  121.7 8.8 %collective-permute-start.16 = (f32[2,74,256]{2,1,0:T(8,128)}, f32[2,74,256]{2,1,0:T(8,128)S(1)}, u32[]{:S(2)}, u32[]{:S(2)}) collective-permute-start(f32[2,74,256]{2,1,0:T(8,128)} %reshape.862), channel_id=1, source_target_pairs={{0,4},{4,8},{8,12},{12,16},{16,20},{20,24},{24,28},{28,32},{32,36}... | collective-permute-start | bytes 454664 | tf_op jit(solution)/shard_map/ppermute | solution.py:109
  123.6 7.0 %collective-permute-start.17 = (f32[2,74,256]{2,1,0:T(8,128)}, f32[2,74,256]{2,1,0:T(8,128)S(1)}, u32[]{:S(2)}, u32[]{:S(2)}) collective-permute-start(f32[2,74,256]{2,1,0:T(8,128)} %reshape.862), channel_id=1, source_target_pairs={{4,0},{8,4},{12,8},{16,12},{20,16},{24,20},{28,24},{32,28},{36,32}... | collective-permute-start | bytes 454664 | tf_op jit(solution)/shard_map/ppermute | solution.py:110
  126.0 8.2 %collective-permute-start.19 = (f32[2,74,256]{2,1,0:T(8,128)}, f32[2,74,256]{2,1,0:T(8,128)S(1)}, u32[]{:S(2)}, u32[]{:S(2)}) collective-permute-start(f32[2,74,256]{2,1,0:T(8,128)} %reshape.862), channel_id=1, source_target_pairs={{8,0},{12,4},{16,8},{20,12},{24,16},{28,20},{32,24},{36,28},{40,32... | collective-permute-start | bytes 454664 | tf_op jit(solution)/shard_map/ppermute | solution.py:110
  127.4 8.2 %collective-permute-start.20 = (f32[1,74,256]{2,1,0:T(8,128)}, f32[1,74,256]{2,1,0:T(8,128)S(1)}, u32[]{:S(2)}, u32[]{:S(2)}) collective-permute-start(f32[1,74,256]{2,1,0:T(8,128)} %get-tuple-element.57), channel_id=1, source_target_pairs={{12,0},{16,4},{20,8},{24,12},{28,16},{32,20},{36,24},{40,28},{44,3... | collective-permute-start | bytes 227336 | tf_op jit(solution)/shard_map/ppermute | solution.py:110
  160.3 18.6 %collective-permute-start.27 = (f32[128,512]{1,0:T(8,128)S(1)}, f32[128,512]{1,0:T(8,128)S(1)}, u32[]{:S(2)}, u32[]{:S(2)}) collective-permute-start(f32[128,512]{1,0:T(8,128)S(1)} %get-tuple-element.5), channel_id=1, source_target_pairs={{0,24},{32,56},{64,88},{96,120},{124,100},{92,68},{60,36},{28,4},{... | collective-permute-start | bytes 786440 | tf_op jit(solution)/shard_map/ppermute | solution.py:246
  182.4 4.8 %collective-permute-start.29 = (f32[1,128,128]{2,1,0:T(8,128)S(1)}, f32[1,128,128]{2,1,0:T(8,128)S(1)}, u32[]{:S(2)}, u32[]{:S(2)}) collective-permute-start(f32[1,128,128]{2,1,0:T(8,128)S(1)} %get-tuple-element.12), channel_id=1, source_target_pairs={{0,1},{1,2},{2,3},{3,0},{4,5},{5,6},{6,7},{7,4},{8,9},{9,10},{10,1... | collective-permute-start | bytes 196616 | tf_op jit(solution)/shard_map/ppermute | solution.py:259
  184.0 4.9 %collective-permute-start.31 = (f32[1,128,128]{2,1,0:T(8,128)S(1)}, f32[1,128,128]{2,1,0:T(8,128)S(1)}, u32[]{:S(2)}, u32[]{:S(2)}) collective-permute-start(f32[1,128,128]{2,1,0:T(8,128)S(1)} %get-tuple-element.13), channel_id=1, source_target_pairs={{0,3},{1,0},{2,1},{3,2},{4,7},{5,4},{6,5},{7,6},{8,11},{9,8},{10,9... | collective-permute-start | bytes 196616 | tf_op jit(solution)/shard_map/ppermute | solution.py:259
  (39 other events, 222.6 us)

commit v15 on v14

--- a/solution.py
+++ b/solution.py
@@ -59,11 +59,7 @@
     paired = field.reshape(x_cells // 2, 2, y_cells, z_cells).sum(axis=1)
     paired = jnp.dot(paired, pair_matrix(z_cells), precision=lax.Precision.HIGHEST)
     to_rows = pair_matrix(y_cells).T
-    planes = [
-        jnp.dot(to_rows, paired[i], precision=lax.Precision.HIGHEST)
-        for i in range(x_cells // 2)
-    ]
-    return jnp.stack(planes)
+    return jnp.einsum("jy,xyz->xjz", to_rows, paired, precision=lax.Precision.HIGHEST)
 
 
 def prolong(field):

time: 191 us -> 188 us (0.984)
    unnamed x79 -> x85, local copies, waits for them, and re-layouts: 10.4 us -> 9.87 us
  transfers between devices with their start and end apart: 32 -> 32, of which waited for: 16 -> 16; matrix products, arithmetic and copies ran while one was open for 7% -> 8% of each run, Pallas kernels for 0% -> 0%
where the time goes in v15:
time: 188 us; the launch traced here: 187 us
  starting transfers between devices  76.4 us (41%)
  waiting for transfers between devices  47.5 us (25%)
  other arithmetic  36 us (19%)
  local copies, waits for them, and re-layouts  18 us (10%)
  matrix products  7.1 us (4%)
  between operations  2.14 us (1%)
    ppermute x11, starting transfers between devices, extend(): lows.insert(0, lax.ppermute(low_piece, axis, up))  50.5 us
    ppermute x11, waiting for transfers between devices, extend(): highs.append(lax.ppermute(high_piece, axis, down))  21.1 us
    select_n x14, other arithmetic, masked(): return jnp.where(keep, field, 0.0)  20.1 us
    ppermute x7, waiting for transfers between devices, spread_faces(): got = lax.ppermute(sent, 'slab', low_pairs + high_pairs)  18.7 us
    ppermute x11, starting transfers between devices, extend(): highs.append(lax.ppermute(high_piece, axis, down))  17 us
    unnamed x85, local copies, waits for them, and re-layouts  9.87 us
    ppermute x11, waiting for transfers between devices, extend(): lows.insert(0, lax.ppermute(low_piece, axis, up))  5.06 us
    ppermute x7, starting transfers between devices, spread_faces(): got = lax.ppermute(sent, 'slab', low_pairs + high_pairs)  4.98 us
  transfers between devices with their start and end apart: 32, of which 16 were waited for; matrix products, arithmetic and copies ran while one was open for 8% of the time, Pallas kernels for 0%

profile of v15, /device:TPU:1, one launch (start us, length us, event | category | flops | bytes accessed | tf_op | source)
XLA Modules:
  0.0 187.1 jit_solution(9295364976306465432)
XLA Ops:
  0.6 4.7 %collective-permute-start.1 = (f32[4,128,512]{2,1,0:T(8,128)}, f32[4,128,512]{2,1,0:T(8,128)S(1)}, u32[]{:S(2)}, u32[]{:S(2)}) collective-permute-start(f32[4,128,512]{2,1,0:T(8,128)} %param.4), channel_id=1, source_target_pairs={{0,4},{4,8},{8,12},{12,16},{16,20},{20,24},{24,28},{28,32},{32,36}... | collective-permute-start | bytes 3145736 | tf_op jit(solution)/shard_map/ppermute | solution.py:105
  9.1 3.9 %collective-permute-start = (f32[1,128,512]{2,1,0:T(8,128)}, f32[1,128,512]{2,1,0:T(8,128)}, u32[]{:S(2)}, u32[]{:S(2)}) collective-permute-start(f32[1,128,512]{2,1,0:T(8,128)} %get-tuple-element.11), channel_id=1, source_target_pairs={{0,8},{4,12},{8,16},{12,20},{16,24},{20,28},{24,32},{28,36},{32,40... | collective-permute-start | bytes 786440 | tf_op jit(solution)/shard_map/ppermute | solution.py:105
  19.0 4.0 %collective-permute-done = f32[1,128,512]{2,1,0:T(8,128)} collective-permute-done((f32[1,128,512]{2,1,0:T(8,128)}, f32[1,128,512]{2,1,0:T(8,128)}, u32[]{:S(2)}, u32[]{:S(2)}) %collective-permute-start) | collective-permute-done | bytes 262176 | tf_op jit(solution)/shard_map/ppermute | solution.py:105
  24.7 3.6 %collective-permute-start.4 = (f32[14,5,512]{2,1,0:T(8,128)S(1)}, f32[14,5,512]{2,1,0:T(8,128)S(1)}, u32[]{:S(2)}, u32[]{:S(2)}) collective-permute-start(f32[14,5,512]{2,1,0:T(8,128)S(1)} %get-tuple-element.8), channel_id=1, source_target_pairs={{0,1},{1,2},{2,3},{4,5},{5,6},{6,7},{8,9},{9,10},{10,11},{12,13},{... | collective-permute-start | bytes 430088 | tf_op jit(solution)/shard_map/ppermute | solution.py:105
  31.2 4.0 %collective-permute-done.5 = f32[14,5,512]{2,1,0:T(8,128)S(1)} collective-permute-done((f32[14,5,512]{2,1,0:T(8,128)S(1)}, f32[14,5,512]{2,1,0:T(8,128)S(1)}, u32[]{:S(2)}, u32[]{:S(2)}) %collective-permute-start.5) | collective-permute-done | bytes 143392 | tf_op jit(solution)/shard_map/ppermute | solution.py:106
  36.7 3.1 %fusion.4 = f32[12,136,512]{2,1,0:T(8,128)S(1)} fusion(f32[12,136,512]{2,1,0:T(8,128)S(1)} %slice.567, f32[14,138,512]{2,1,0:T(8,128)S(1)} %pad_maximum_fusion, pred[12,136]{1,0:T(8,128)(4,1)S(1)} %broadcast_and_fusion.1), kind=kLoop, calls=%fused_computation.9 | loop fusion | flops 7520256 | bytes 20055648 | tf_op jit(solution)/shard_map/jit(_where)/select_n | solution.py:119
  40.3 2.6 %fusion.9 = f32[10,134,512]{2,1,0:T(8,128)S(1)} fusion(f32[10,134,512]{2,1,0:T(8,128)S(1)} %slice.573, f32[12,136,512]{2,1,0:T(8,128)S(1)} %fusion.4, pred[10,134]{1,0:T(8,128)(4,1)S(1)} %broadcast_and_fusion), kind=kLoop, calls=%fused_computation.21 | loop fusion | flops 6174720 | bytes 16467260 | tf_op jit(solution)/shard_map/jit(_where)/select_n | solution.py:119
  49.3 3.6 %collective-permute-start.6 = (f32[2,13,256]{2,1,0:T(8,128)}, f32[2,13,256]{2,1,0:T(8,128)S(1)}, u32[]{:S(2)}, u32[]{:S(2)}) collective-permute-start(f32[2,13,256]{2,1,0:T(8,128)} %get-tuple-element.52), channel_id=1, source_target_pairs={{0,1},{1,2},{2,3},{4,5},{5,6},{6,7},{8,9},{9,10},{10,11},{12,13},{... | collective-permute-start | bytes 79880 | tf_op jit(solution)/shard_map/ppermute | solution.py:105
  54.8 3.0 %collective-permute-done.7 = f32[2,13,256]{2,1,0:T(8,128)S(1)} collective-permute-done((f32[2,13,256]{2,1,0:T(8,128)}, f32[2,13,256]{2,1,0:T(8,128)S(1)}, u32[]{:S(2)}, u32[]{:S(2)}) %collective-permute-start.7) | collective-permute-done | bytes 26656 | tf_op jit(solution)/shard_map/ppermute | solution.py:106
  57.9 10.4 %collective-permute-start.10 = (f32[2,90,256]{2,1,0:T(8,128)S(1)}, f32[2,90,256]{2,1,0:T(8,128)S(1)}, u32[]{:S(2)}, u32[]{:S(2)}) collective-permute-start(f32[2,90,256]{2,1,0:T(8,128)S(1)} %pad_maximum_fusion.13), channel_id=1, source_target_pairs={{0,12},{4,16},{8,20},{12,24},{16,28},{20,32},{24,36},{28,40},{32,4... | collective-permute-start | bytes 552968 | tf_op jit(solution)/shard_map/ppermute | solution.py:105
  68.3 3.9 %collective-permute-start.15 = (f32[1,90,256]{2,1,0:T(8,128)S(1)}, f32[1,90,256]{2,1,0:T(8,128)S(1)}, u32[]{:S(2)}, u32[]{:S(2)}) collective-permute-start(f32[1,90,256]{2,1,0:T(8,128)S(1)} %get-tuple-element.18), channel_id=1, source_target_pairs={{0,16},{4,20},{8,24},{12,28},{16,32},{20,36},{24,40},{28,44},{32,4... | collective-permute-start | bytes 276488 | tf_op jit(solution)/shard_map/ppermute | solution.py:105
  72.7 2.5 %collective-permute-start.11 = (f32[2,90,256]{2,1,0:T(8,128)S(1)}, f32[2,90,256]{2,1,0:T(8,128)S(1)}, u32[]{:S(2)}, u32[]{:S(2)}) collective-permute-start(f32[2,90,256]{2,1,0:T(8,128)S(1)} %pad_maximum_fusion.13), channel_id=1, source_target_pairs={{0,8},{4,12},{8,16},{12,20},{16,24},{20,28},{24,32},{28,36},{32,40... | collective-permute-start | bytes 552968 | tf_op jit(solution)/shard_map/ppermute | solution.py:105
  77.2 2.3 %collective-permute-start.9 = (f32[2,90,256]{2,1,0:T(8,128)S(1)}, f32[2,90,256]{2,1,0:T(8,128)S(1)}, u32[]{:S(2)}, u32[]{:S(2)}) collective-permute-start(f32[2,90,256]{2,1,0:T(8,128)S(1)} %pad_maximum_fusion.13), channel_id=1, source_target_pairs={{4,0},{8,4},{12,8},{16,12},{20,16},{24,20},{28,24},{32,28},{36,32}... | collective-permute-start | bytes 552968 | tf_op jit(solution)/shard_map/ppermute | solution.py:106
  84.6 3.8 %collective-permute-done.12 = f32[2,90,256]{2,1,0:T(8,128)S(1)} collective-permute-done((f32[2,90,256]{2,1,0:T(8,128)S(1)}, f32[2,90,256]{2,1,0:T(8,128)S(1)}, u32[]{:S(2)}, u32[]{:S(2)}) %collective-permute-start.12) | collective-permute-done | bytes 184352 | tf_op jit(solution)/shard_map/ppermute | solution.py:106
  88.4 2.8 %collective-permute-done.13 = f32[2,90,256]{2,1,0:T(8,128)S(1)} collective-permute-done((f32[2,90,256]{2,1,0:T(8,128)S(1)}, f32[2,90,256]{2,1,0:T(8,128)S(1)}, u32[]{:S(2)}, u32[]{:S(2)}) %collective-permute-start.13) | collective-permute-done | bytes 184352 | tf_op jit(solution)/shard_map/ppermute | solution.py:106
  96.9 2.1 %reduce_sum.28 = f32[5,84,256]{2,1,0:T(8,128)} reduce(f32[5,2,84,256]{3,2,1,0:T(8,128)} %bitcast.63, f32[]{:T(128)} %constant.297.clone.1), dimensions={1}, to_apply=%region_1.2 | reduce | flops 107520 | bytes 1290244 | tf_op jit(solution)/shard_map/reduce_sum | solution.py:59
  102.1 12.1 %collective-permute-start.21 = (f32[1,74,256]{2,1,0:T(8,128)}, f32[1,74,256]{2,1,0:T(8,128)}, u32[]{:S(2)}, u32[]{:S(2)}) collective-permute-start(f32[1,74,256]{2,1,0:T(8,128)} %get-tuple-element.57), channel_id=1, source_target_pairs={{0,12},{4,16},{8,20},{12,24},{16,28},{20,32},{24,36},{28,40},{32,4... | collective-permute-start | bytes 227336 | tf_op jit(solution)/shard_map/ppermute | solution.py:105
  121.0 2.4 %collective-permute-start.17 = (f32[2,74,256]{2,1,0:T(8,128)}, f32[2,74,256]{2,1,0:T(8,128)S(1)}, u32[]{:S(2)}, u32[]{:S(2)}) collective-permute-start(f32[2,74,256]{2,1,0:T(8,128)} %reshape.862), channel_id=1, source_target_pairs={{4,0},{8,4},{12,8},{16,12},{20,16},{24,20},{28,24},{32,28},{36,32}... | collective-permute-start | bytes 454664 | tf_op jit(solution)/shard_map/ppermute | solution.py:106
  128.1 3.6 %collective-permute-done.19 = f32[2,74,256]{2,1,0:T(8,128)S(1)} collective-permute-done((f32[2,74,256]{2,1,0:T(8,128)}, f32[2,74,256]{2,1,0:T(8,128)S(1)}, u32[]{:S(2)}, u32[]{:S(2)}) %collective-permute-start.19) | collective-permute-done | bytes 151584 | tf_op jit(solution)/shard_map/ppermute | solution.py:106
  135.4 2.2 %fusion.77 = f32[6,68,512]{2,1,0:T(8,128)S(1)} fusion(f32[10,72,256]{2,1,0:T(8,128)S(1)} %fusion.70, f32[2,74,256]{2,1,0:T(8,128)S(1)} %collective-permute-done.17, f32[2,74,256]{2,1,0:T(8,128)} %reshape.862, f32[2,74,256]{2,1,0:T(8,128)S(1)} %collective-permute-done.16, f32[12,86,256]{2,1,0:T(8,128)} %copy-done.4, f32[14,88,256]{2,1,0:T(8,128)} %copy-done.3, ...), kind=kOutput, calls=%fused_computation.157 | convolution fusion | flops 643530752 | bytes 4130816 | tf_op jit(solution)/shard_map/dot_general | solution.py:67
  143.8 3.1 %fusion.30 = (f32[6,130,512]{2,1,0:T(8,128)S(1)}, f32[6,130,512]{2,1,0:T(8,128)S(1)}) fusion(f32[6,130,512]{2,1,0:T(8,128)S(1)} %slice.653, f32[8,132,512]{2,1,0:T(8,128)S(1)} %fusion.18, pred[6,130]{1,0:T(8,128)(4,1)S(1)} %copy-done.23, f32[6,130,512]{2,1,0:T(8,128)S(1)} %slice.585, f32[8,132,512]{2,1,0:T(8,128)S(1)} %copy-done.2), kind=kLoop, calls=%fused_computation.60 | loop fusion | flops 7188480 | bytes 19170060 | tf_op jit(solution)/shard_map/jit(_where)/select_n | solution.py:119
  149.3 2.6 %fusion.53 = f32[4,128,512]{2,1,0:T(8,128)S(1)} fusion(f32[8,132,512]{2,1,0:T(8,128)S(1)} %fusion.18, f32[10,134,512]{2,1,0:T(8,128)S(1)} %slice_multiply_fusion, f32[4,128,512]{2,1,0:T(8,128)S(1)} %get-tuple-element.62, f32[10,134,512]{2,1,0:T(8,128)} %copy-done, f32[4,128,512]{2,1,0:T(8,128)S(1)} %copy-done.7, f32[12,136,512]{2,1,0:T(8,128)S(1)} %fusion.4, ...), kind=kLoop, calls=%fused_computation.111 | loop fusion | flops 3407872 | bytes 11534336 | tf_op jit(solution)/shard_map/sub | solution.py:201
  159.1 17.4 %collective-permute-done.27 = f32[128,512]{1,0:T(8,128)S(1)} collective-permute-done((f32[128,512]{1,0:T(8,128)S(1)}, f32[128,512]{1,0:T(8,128)S(1)}, u32[]{:S(2)}, u32[]{:S(2)}) %collective-permute-start.27) | collective-permute-done | bytes 262176 | tf_op jit(solution)/shard_map/ppermute | solution.py:242
  181.5 2.3 %collective-permute-start.31 = (f32[1,128,128]{2,1,0:T(8,128)S(1)}, f32[1,128,128]{2,1,0:T(8,128)S(1)}, u32[]{:S(2)}, u32[]{:S(2)}) collective-permute-start(f32[1,128,128]{2,1,0:T(8,128)S(1)} %get-tuple-element.13), channel_id=1, source_target_pairs={{0,3},{1,0},{2,1},{3,2},{4,7},{5,4},{6,5},{7,6},{8,11},{9,8},{10,9... | collective-permute-start | bytes 196616 | tf_op jit(solution)/shard_map/ppermute | solution.py:255
  (240 shorter events, 78.8 us)
Async XLA Ops:
  0.6 23.4 %collective-permute-start.1 = (f32[4,128,512]{2,1,0:T(8,128)}, f32[4,128,512]{2,1,0:T(8,128)S(1)}, u32[]{:S(2)}, u32[]{:S(2)}) collective-permute-start(f32[4,128,512]{2,1,0:T(8,128)} %param.4), channel_id=1, source_target_pairs={{0,4},{4,8},{8,12},{12,16},{16,20},{20,24},{24,28},{28,32},{32,36}... | collective-permute-start | bytes 3145736 | tf_op jit(solution)/shard_map/ppermute | solution.py:105
  5.4 19.1 %collective-permute-start.2 = (f32[4,128,512]{2,1,0:T(8,128)}, f32[4,128,512]{2,1,0:T(8,128)S(1)}, u32[]{:S(2)}, u32[]{:S(2)}) collective-permute-start(f32[4,128,512]{2,1,0:T(8,128)} %param.4), channel_id=1, source_target_pairs={{4,0},{8,4},{12,8},{16,12},{20,16},{24,20},{28,24},{32,28},{36,32}... | collective-permute-start | bytes 3145736 | tf_op jit(solution)/shard_map/ppermute | solution.py:106
  9.1 13.9 %collective-permute-start = (f32[1,128,512]{2,1,0:T(8,128)}, f32[1,128,512]{2,1,0:T(8,128)}, u32[]{:S(2)}, u32[]{:S(2)}) collective-permute-start(f32[1,128,512]{2,1,0:T(8,128)} %get-tuple-element.11), channel_id=1, source_target_pairs={{0,8},{4,12},{8,16},{12,20},{16,24},{20,28},{24,32},{28,36},{32,40... | collective-permute-start | bytes 786440 | tf_op jit(solution)/shard_map/ppermute | solution.py:105
  13.1 11.5 %collective-permute-start.3 = (f32[1,128,512]{2,1,0:T(8,128)}, f32[1,128,512]{2,1,0:T(8,128)S(1)}, u32[]{:S(2)}, u32[]{:S(2)}) collective-permute-start(f32[1,128,512]{2,1,0:T(8,128)} %get-tuple-element.10), channel_id=1, source_target_pairs={{8,0},{12,4},{16,8},{20,12},{24,16},{28,20},{32,24},{36,28},{40,32... | collective-permute-start | bytes 786440 | tf_op jit(solution)/shard_map/ppermute | solution.py:106
  24.7 6.5 %collective-permute-start.4 = (f32[14,5,512]{2,1,0:T(8,128)S(1)}, f32[14,5,512]{2,1,0:T(8,128)S(1)}, u32[]{:S(2)}, u32[]{:S(2)}) collective-permute-start(f32[14,5,512]{2,1,0:T(8,128)S(1)} %get-tuple-element.8), channel_id=1, source_target_pairs={{0,1},{1,2},{2,3},{4,5},{5,6},{6,7},{8,9},{9,10},{10,11},{12,13},{... | collective-permute-start | bytes 430088 | tf_op jit(solution)/shard_map/ppermute | solution.py:105
  28.2 6.9 %collective-permute-start.5 = (f32[14,5,512]{2,1,0:T(8,128)S(1)}, f32[14,5,512]{2,1,0:T(8,128)S(1)}, u32[]{:S(2)}, u32[]{:S(2)}) collective-permute-start(f32[14,5,512]{2,1,0:T(8,128)S(1)} %get-tuple-element.9), channel_id=1, source_target_pairs={{1,0},{2,1},{3,2},{5,4},{6,5},{7,6},{9,8},{10,9},{11,10},{13,12},{... | collective-permute-start | bytes 430088 | tf_op jit(solution)/shard_map/ppermute | solution.py:106
  49.3 5.5 %collective-permute-start.6 = (f32[2,13,256]{2,1,0:T(8,128)}, f32[2,13,256]{2,1,0:T(8,128)S(1)}, u32[]{:S(2)}, u32[]{:S(2)}) collective-permute-start(f32[2,13,256]{2,1,0:T(8,128)} %get-tuple-element.52), channel_id=1, source_target_pairs={{0,1},{1,2},{2,3},{4,5},{5,6},{6,7},{8,9},{9,10},{10,11},{12,13},{... | collective-permute-start | bytes 79880 | tf_op jit(solution)/shard_map/ppermute | solution.py:105
  53.0 4.9 %collective-permute-start.7 = (f32[2,13,256]{2,1,0:T(8,128)}, f32[2,13,256]{2,1,0:T(8,128)S(1)}, u32[]{:S(2)}, u32[]{:S(2)}) collective-permute-start(f32[2,13,256]{2,1,0:T(8,128)} %get-tuple-element.53), channel_id=1, source_target_pairs={{1,0},{2,1},{3,2},{5,4},{6,5},{7,6},{9,8},{10,9},{11,10},{13,12},{... | collective-permute-start | bytes 79880 | tf_op jit(solution)/shard_map/ppermute | solution.py:106
  57.9 23.0 %collective-permute-start.10 = (f32[2,90,256]{2,1,0:T(8,128)S(1)}, f32[2,90,256]{2,1,0:T(8,128)S(1)}, u32[]{:S(2)}, u32[]{:S(2)}) collective-permute-start(f32[2,90,256]{2,1,0:T(8,128)S(1)} %pad_maximum_fusion.13), channel_id=1, source_target_pairs={{0,12},{4,16},{8,20},{12,24},{16,28},{20,32},{24,36},{28,40},{32,4... | collective-permute-start | bytes 552968 | tf_op jit(solution)/shard_map/ppermute | solution.py:105
  68.3 11.3 %collective-permute-start.15 = (f32[1,90,256]{2,1,0:T(8,128)S(1)}, f32[1,90,256]{2,1,0:T(8,128)S(1)}, u32[]{:S(2)}, u32[]{:S(2)}) collective-permute-start(f32[1,90,256]{2,1,0:T(8,128)S(1)} %get-tuple-element.18), channel_id=1, source_target_pairs={{0,16},{4,20},{8,24},{12,28},{16,32},{20,36},{24,40},{28,44},{32,4... | collective-permute-start | bytes 276488 | tf_op jit(solution)/shard_map/ppermute | solution.py:105
  72.7 9.5 %collective-permute-start.11 = (f32[2,90,256]{2,1,0:T(8,128)S(1)}, f32[2,90,256]{2,1,0:T(8,128)S(1)}, u32[]{:S(2)}, u32[]{:S(2)}) collective-permute-start(f32[2,90,256]{2,1,0:T(8,128)S(1)} %pad_maximum_fusion.13), channel_id=1, source_target_pairs={{0,8},{4,12},{8,16},{12,20},{16,24},{20,28},{24,32},{28,36},{32,40... | collective-permute-start | bytes 552968 | tf_op jit(solution)/shard_map/ppermute | solution.py:105
  75.2 8.4 %collective-permute-start.8 = (f32[2,90,256]{2,1,0:T(8,128)S(1)}, f32[2,90,256]{2,1,0:T(8,128)S(1)}, u32[]{:S(2)}, u32[]{:S(2)}) collective-permute-start(f32[2,90,256]{2,1,0:T(8,128)S(1)} %pad_maximum_fusion.13), channel_id=1, source_target_pairs={{0,4},{4,8},{8,12},{12,16},{16,20},{20,24},{24,28},{28,32},{32,36}... | collective-permute-start | bytes 552968 | tf_op jit(solution)/shard_map/ppermute | solution.py:105
  77.2 7.3 %collective-permute-start.9 = (f32[2,90,256]{2,1,0:T(8,128)S(1)}, f32[2,90,256]{2,1,0:T(8,128)S(1)}, u32[]{:S(2)}, u32[]{:S(2)}) collective-permute-start(f32[2,90,256]{2,1,0:T(8,128)S(1)} %pad_maximum_fusion.13), channel_id=1, source_target_pairs={{4,0},{8,4},{12,8},{16,12},{20,16},{24,20},{28,24},{32,28},{36,32}... | collective-permute-start | bytes 552968 | tf_op jit(solution)/shard_map/ppermute | solution.py:106
  79.5 8.8 %collective-permute-start.12 = (f32[2,90,256]{2,1,0:T(8,128)S(1)}, f32[2,90,256]{2,1,0:T(8,128)S(1)}, u32[]{:S(2)}, u32[]{:S(2)}) collective-permute-start(f32[2,90,256]{2,1,0:T(8,128)S(1)} %pad_maximum_fusion.13), channel_id=1, source_target_pairs={{8,0},{12,4},{16,8},{20,12},{24,16},{28,20},{32,24},{36,28},{40,32... | collective-permute-start | bytes 552968 | tf_op jit(solution)/shard_map/ppermute | solution.py:106
  80.9 10.4 %collective-permute-start.13 = (f32[2,90,256]{2,1,0:T(8,128)S(1)}, f32[2,90,256]{2,1,0:T(8,128)S(1)}, u32[]{:S(2)}, u32[]{:S(2)}) collective-permute-start(f32[2,90,256]{2,1,0:T(8,128)S(1)} %pad_maximum_fusion.13), channel_id=1, source_target_pairs={{12,0},{16,4},{20,8},{24,12},{28,16},{32,20},{36,24},{40,28},{44,3... | collective-permute-start | bytes 552968 | tf_op jit(solution)/shard_map/ppermute | solution.py:106
  82.2 10.8 %collective-permute-start.14 = (f32[1,90,256]{2,1,0:T(8,128)S(1)}, f32[1,90,256]{2,1,0:T(8,128)S(1)}, u32[]{:S(2)}, u32[]{:S(2)}) collective-permute-start(f32[1,90,256]{2,1,0:T(8,128)S(1)} %get-tuple-element.17), channel_id=1, source_target_pairs={{16,0},{20,4},{24,8},{28,12},{32,16},{36,20},{40,24},{44,28},{48,3... | collective-permute-start | bytes 276488 | tf_op jit(solution)/shard_map/ppermute | solution.py:106
  102.1 22.6 %collective-permute-start.21 = (f32[1,74,256]{2,1,0:T(8,128)}, f32[1,74,256]{2,1,0:T(8,128)}, u32[]{:S(2)}, u32[]{:S(2)}) collective-permute-start(f32[1,74,256]{2,1,0:T(8,128)} %get-tuple-element.57), channel_id=1, source_target_pairs={{0,12},{4,16},{8,20},{12,24},{16,28},{20,32},{24,36},{28,40},{32,4... | collective-permute-start | bytes 227336 | tf_op jit(solution)/shard_map/ppermute | solution.py:105
  114.9 12.1 %collective-permute-start.18 = (f32[2,74,256]{2,1,0:T(8,128)}, f32[2,74,256]{2,1,0:T(8,128)}, u32[]{:S(2)}, u32[]{:S(2)}) collective-permute-start(f32[2,74,256]{2,1,0:T(8,128)} %reshape.862), channel_id=1, source_target_pairs={{0,8},{4,12},{8,16},{12,20},{16,24},{20,28},{24,32},{28,36},{32,40... | collective-permute-start | bytes 454664 | tf_op jit(solution)/shard_map/ppermute | solution.py:105
  119.1 8.8 %collective-permute-start.16 = (f32[2,74,256]{2,1,0:T(8,128)}, f32[2,74,256]{2,1,0:T(8,128)S(1)}, u32[]{:S(2)}, u32[]{:S(2)}) collective-permute-start(f32[2,74,256]{2,1,0:T(8,128)} %reshape.862), channel_id=1, source_target_pairs={{0,4},{4,8},{8,12},{12,16},{16,20},{20,24},{24,28},{28,32},{32,36}... | collective-permute-start | bytes 454664 | tf_op jit(solution)/shard_map/ppermute | solution.py:105
  121.0 7.0 %collective-permute-start.17 = (f32[2,74,256]{2,1,0:T(8,128)}, f32[2,74,256]{2,1,0:T(8,128)S(1)}, u32[]{:S(2)}, u32[]{:S(2)}) collective-permute-start(f32[2,74,256]{2,1,0:T(8,128)} %reshape.862), channel_id=1, source_target_pairs={{4,0},{8,4},{12,8},{16,12},{20,16},{24,20},{28,24},{32,28},{36,32}... | collective-permute-start | bytes 454664 | tf_op jit(solution)/shard_map/ppermute | solution.py:106
  123.5 8.2 %collective-permute-start.19 = (f32[2,74,256]{2,1,0:T(8,128)}, f32[2,74,256]{2,1,0:T(8,128)S(1)}, u32[]{:S(2)}, u32[]{:S(2)}) collective-permute-start(f32[2,74,256]{2,1,0:T(8,128)} %reshape.862), channel_id=1, source_target_pairs={{8,0},{12,4},{16,8},{20,12},{24,16},{28,20},{32,24},{36,28},{40,32... | collective-permute-start | bytes 454664 | tf_op jit(solution)/shard_map/ppermute | solution.py:106
  124.8 8.2 %collective-permute-start.20 = (f32[1,74,256]{2,1,0:T(8,128)}, f32[1,74,256]{2,1,0:T(8,128)S(1)}, u32[]{:S(2)}, u32[]{:S(2)}) collective-permute-start(f32[1,74,256]{2,1,0:T(8,128)} %get-tuple-element.57), channel_id=1, source_target_pairs={{12,0},{16,4},{20,8},{24,12},{28,16},{32,20},{36,24},{40,28},{44,3... | collective-permute-start | bytes 227336 | tf_op jit(solution)/shard_map/ppermute | solution.py:106
  157.7 18.8 %collective-permute-start.27 = (f32[128,512]{1,0:T(8,128)S(1)}, f32[128,512]{1,0:T(8,128)S(1)}, u32[]{:S(2)}, u32[]{:S(2)}) collective-permute-start(f32[128,512]{1,0:T(8,128)S(1)} %get-tuple-element.5), channel_id=1, source_target_pairs={{0,24},{32,56},{64,88},{96,120},{124,100},{92,68},{60,36},{28,4},{... | collective-permute-start | bytes 786440 | tf_op jit(solution)/shard_map/ppermute | solution.py:242
  181.5 4.9 %collective-permute-start.31 = (f32[1,128,128]{2,1,0:T(8,128)S(1)}, f32[1,128,128]{2,1,0:T(8,128)S(1)}, u32[]{:S(2)}, u32[]{:S(2)}) collective-permute-start(f32[1,128,128]{2,1,0:T(8,128)S(1)} %get-tuple-element.13), channel_id=1, source_target_pairs={{0,3},{1,0},{2,1},{3,2},{4,7},{5,4},{6,5},{7,6},{8,11},{9,8},{10,9... | collective-permute-start | bytes 196616 | tf_op jit(solution)/shard_map/ppermute | solution.py:255
  (42 other events, 223.9 us)
